TPU v7x, 32 devices: a whole 2x2x4 slice. The times are simulated.
32 devices in a mesh: groups: 2 (over y), seq: 4 (over z), res: 2 (over x), chan: 2 (over core).
Axes of the slice: x: 2, y: 2, z: 4, core: 2. Of those that a mesh axis runs over, the one named last changes fastest.
Arguments:
- homolog_embedding: bfloat16 [2560, 64, 64], P(('groups', 'seq', 'chan'), 'res'), parts along dimension 0, may hold values from -6 to 6
- coupling_embedding: float32 [128, 64, 128], P(('groups', 'res'), ('seq', 'chan')), parts along dimension 0, may hold values from -6 to 6
- homolog_widen_weights: bfloat16 [64, 256], replicated, may hold values from -0.75 to 0.75
- homolog_shrink_weights: bfloat16 [256, 64], replicated, may hold values from -0.375 to 0.375
- lhs_projector: bfloat16 [64, 32], replicated, may hold values from -0.75 to 0.75
- rhs_projector: bfloat16 [64, 32], replicated, may hold values from -0.75 to 0.75
- moment_coupling_weights: float32 [1024, 128], replicated, may hold values from -6 to 6
- coupling_widen_weights: bfloat16 [128, 512], replicated, may hold values from -0.5 to 0.5
- coupling_shrink_weights: bfloat16 [512, 128], replicated, may hold values from -0.25 to 0.25
Outputs:
- homolog_refreshed: bfloat16 [2560, 64, 64], P(('groups', 'seq', 'chan'), 'res'), parts along dimension 0
- coupling_refreshed: float32 [128, 64, 128], P(('groups', 'res'), ('seq', 'chan')), parts along dimension 0
There are 2 independent parts, one for each index of `groups`. A program takes and returns all parts, laid end to end along the dimension named above; an argument that names none is the same for every part. Nothing has to cross between parts.
All inputs are finite; a program needn't handle non-finite values.
Results may differ from a plain program's by a relative error of at most 0.0043.
Values may be sent and summed in bfloat16 or wider, within the bound.
No kernel may reach another device: no remote copies, remote signals or barrier semaphores. Data moves between devices by JAX's collectives and lax.ppermute only.
A program may use at most 64 MiB of HBM per device.

v0:
```python
import functools

import jax
import jax.numpy as jnp
from jax import lax
from jax.experimental import pallas as pl
from jax.experimental.pallas import tpu as pltpu
from jax.sharding import PartitionSpec as P


def apply_layer_norm(values):
    mean = jnp.mean(values, axis=-1, keepdims=True)
    centred = values - mean
    variance = jnp.mean(centred * centred, axis=-1, keepdims=True)
    return centred * lax.rsqrt(variance + 1e-05)


C_HI = 8
C_LO = 4
JB = 4


def outer_project_kernel(scale, lt_ref, r_ref, wh_ref, wl_ref, o_ref, vh_ref, vl_ref):
    width = wh_ref.shape[0] // (C_HI * C_LO)
    rows_i = lt_ref.shape[0] // (C_HI * C_LO)
    lanes = JB * width
    nja = r_ref.shape[1] // lanes
    dd = wh_ref.shape[1]

    @pl.when(pl.program_id(0) == 0)
    def _build():
        vh_ref[...] = jnp.zeros_like(vh_ref)
        vl_ref[...] = jnp.zeros_like(vl_ref)
        for c_hi in range(C_HI):
            for c_lo in range(C_LO):
                src = (c_hi * C_LO + c_lo) * width
                for jb in range(JB):
                    row = c_lo * lanes + jb * width
                    vh_ref[c_hi, row : row + width, jb * dd : (jb + 1) * dd] = wh_ref[src : src + width, :]
                    vl_ref[c_hi, row : row + width, jb * dd : (jb + 1) * dd] = wl_ref[src : src + width, :]

    def rearrange(y):
        return jnp.concatenate(
            [
                jnp.concatenate(
                    [y[c_lo * rows_i : (c_lo + 1) * rows_i, ja * lanes : (ja + 1) * lanes] for c_lo in range(C_LO)],
                    axis=1,
                )
                for ja in range(nja)
            ],
            axis=0,
        )

    acc = jnp.zeros(o_ref.shape, jnp.float32)
    block = C_LO * rows_i
    for c_hi in range(C_HI):
        x = jnp.dot(lt_ref[c_hi * block : (c_hi + 1) * block, :], r_ref[...], preferred_element_type=jnp.float32)
        xh = x.astype(jnp.bfloat16)
        xl = (x - xh.astype(jnp.float32)).astype(jnp.bfloat16)
        lh = rearrange(xh)
        ll = rearrange(xl)
        vh = vh_ref[c_hi]
        acc = acc + jnp.dot(lh, vh, preferred_element_type=jnp.float32)
        acc = acc + jnp.dot(ll, vh, preferred_element_type=jnp.float32)
        acc = acc + jnp.dot(lh, vl_ref[c_hi], preferred_element_type=jnp.float32)
    o_ref[...] = acc * scale


def outer_project(lt, r_all, wh, wl, scale):
    rows_i = lt.shape[0] // (C_HI * C_LO)
    width = wh.shape[0] // (C_HI * C_LO)
    lanes = JB * width
    total_lanes = r_all.shape[1]
    chunk = min(total_lanes, 16 * lanes)
    steps = total_lanes // chunk
    nja_chunk = chunk // lanes
    out_rows = (total_lanes // lanes) * rows_i
    d = wh.shape[1]
    s = lt.shape[1]
    flops = 2 * lt.shape[0] * s * total_lanes + 3 * 2 * out_rows * (C_LO * lanes) * (JB * d) * C_HI
    return pl.pallas_call(
        functools.partial(outer_project_kernel, scale),
        grid=(steps,),
        in_specs=[
            pl.BlockSpec(lt.shape, lambda q: (0, 0)),
            pl.BlockSpec((s, chunk), lambda q: (0, q)),
            pl.BlockSpec(wh.shape, lambda q: (0, 0)),
            pl.BlockSpec(wl.shape, lambda q: (0, 0)),
        ],
        out_specs=pl.BlockSpec((nja_chunk * rows_i, JB * d), lambda q: (q, 0)),
        out_shape=jax.ShapeDtypeStruct((out_rows, JB * d), jnp.float32),
        scratch_shapes=[
            pltpu.VMEM((C_HI, C_LO * lanes, JB * d), jnp.bfloat16),
            pltpu.VMEM((C_HI, C_LO * lanes, JB * d), jnp.bfloat16),
        ],
        compiler_params=pltpu.CompilerParams(
            dimension_semantics=("arbitrary",), vmem_limit_bytes=48 * 1024 * 1024
        ),
        cost_estimate=pl.CostEstimate(
            flops=flops,
            transcendentals=0,
            bytes_accessed=lt.size * 2 + r_all.size * 2 + wh.size * 4 + out_rows * JB * d * 4,
        ),
    )(lt, r_all, wh, wl)


def per_device(
    homolog_embedding,
    coupling_embedding,
    homolog_widen_weights,
    homolog_shrink_weights,
    lhs_projector,
    rhs_projector,
    moment_coupling_weights,
    coupling_widen_weights,
    coupling_shrink_weights,
):
    homologs_local_share, sites_local_share, homolog_lane_number = homolog_embedding.shape
    proj_width = lhs_projector.shape[1]
    pair_width = coupling_embedding.shape[2]
    cross_moment_average = homolog_embedding.reshape(
        homologs_local_share * sites_local_share, homolog_lane_number
    )
    homolog_standardized = apply_layer_norm(cross_moment_average.astype(jnp.float32)).astype(
        jnp.bfloat16
    )
    homolog_inner_state = jnp.maximum(
        jnp.dot(homolog_standardized, homolog_widen_weights, preferred_element_type=jnp.float32),
        0.0,
    ).astype(jnp.bfloat16)
    homolog_refreshed = (
        cross_moment_average.astype(jnp.float32)
        + jnp.dot(homolog_inner_state, homolog_shrink_weights, preferred_element_type=jnp.float32)
    ).astype(jnp.bfloat16)
    alignment_normed2 = apply_layer_norm(homolog_refreshed.astype(jnp.float32)).astype(jnp.bfloat16)
    left_features = (
        jnp.dot(alignment_normed2, lhs_projector, preferred_element_type=jnp.float32)
        .astype(jnp.bfloat16)
        .reshape(homologs_local_share, sites_local_share, proj_width)
    )
    right_features = (
        jnp.dot(alignment_normed2, rhs_projector, preferred_element_type=jnp.float32)
        .astype(jnp.bfloat16)
        .reshape(homologs_local_share, sites_local_share * proj_width)
    )
    owners = lax.axis_size(("seq", "chan"))
    depth_total = float(homologs_local_share * owners)
    block_cols = coupling_embedding.shape[1]

    lt = jnp.transpose(left_features, (2, 1, 0)).reshape(proj_width * sites_local_share, homologs_local_share)
    r_all = lax.all_gather(right_features, "res", axis=1, tiled=True)
    w_hi = moment_coupling_weights.astype(jnp.bfloat16)
    w_lo = (moment_coupling_weights - w_hi.astype(jnp.float32)).astype(jnp.bfloat16)
    partial_value = outer_project(lt, r_all, w_hi, w_lo, 1.0 / depth_total)
    pair_update = lax.psum_scatter(partial_value, ("seq", "chan"), scatter_dimension=0, tiled=True)
    nja_local = block_cols // JB
    pair_update = (
        pair_update.reshape(nja_local, sites_local_share, JB, pair_width)
        .transpose(1, 0, 2, 3)
        .reshape(sites_local_share * block_cols, pair_width)
    )
    pair_mid = coupling_embedding.reshape(sites_local_share * block_cols, pair_width) + pair_update
    pair_norm = apply_layer_norm(pair_mid).astype(jnp.bfloat16)
    pair_hidden = jnp.maximum(
        jnp.dot(pair_norm, coupling_widen_weights, preferred_element_type=jnp.float32), 0.0
    ).astype(jnp.bfloat16)
    coupling_refreshed = pair_mid + jnp.dot(
        pair_hidden, coupling_shrink_weights, preferred_element_type=jnp.float32
    )
    return (
        homolog_refreshed.reshape(homologs_local_share, sites_local_share, homolog_lane_number),
        coupling_refreshed.reshape(sites_local_share, block_cols, pair_width),
    )


def solution(mesh):
    return jax.shard_map(
        per_device,
        mesh=mesh,
        in_specs=(
            P(("groups", "seq", "chan"), "res", None),
            P(("groups", "res"), ("seq", "chan"), None),
            P(),
            P(),
            P(),
            P(),
            P(),
            P(),
            P(),
        ),
        out_specs=(
            P(("groups", "seq", "chan"), "res", None),
            P(("groups", "res"), ("seq", "chan"), None),
        ),
        check_vma=False,
    )
```

profile of v0, /device:TPU:0, one launch (start us, length us, event | category | flops | bytes accessed | tf_op | source)
XLA Modules:
  0.0 87.0 jit_solution(7803195756125423828)
XLA Ops:
  7.2 0.0 copy-start
  7.2 0.0 reduce-scatter.2.cloned.1.call-start
  7.2 2.4 %copy.26 = f32[160,32,64]{2,1,0:T(8,128)S(1)} copy(bf16[160,32,64]{0,2,1:T(8,128)(2,1)} %param.9) | data formatting | bytes 1966080 | tf_op jit(solution)/shard_map/convert_element_type | solution.py:132
  9.6 0.0 copy-start.1
  9.7 1.5 %convert_reduce_fusion.1 = f32[160,32]{0,1:T(8,128)S(1)} fusion(bf16[160,32,64]{0,2,1:T(8,128)(2,1)} %param.9), kind=kLoop, calls=%fused_computation.21 | loop fusion | flops 650240 | bytes 675840 | tf_op jit(solution)/shard_map/reduce_sum | solution.py:12
  11.2 0.0 copy-done.1
  11.2 0.4 multiply_reduce_fusion
  11.6 0.1 copy.27
  11.7 0.0 copy-start.4
  11.7 0.0 copy-start.5
  11.7 1.8 %copy.29 = f32[5120,64]{0,1:T(8,128)} copy(f32[5120,64]{1,0:T(8,128)S(1)} %bitcast.27) | data formatting | bytes 2621440 | tf_op jit(solution)/shard_map/convert_element_type | solution.py:132
  13.6 0.1 copy.28
  13.7 0.1 rsqrt.31
  13.8 0.1 div.23
  13.9 0.0 copy-done.4
  13.9 0.0 copy-done.5
  13.9 0.0 copy-start.6
  13.9 3.1 %convert_reduce_fusion = (f32[5120]{0:T(1024)S(1)}, bf16[5120,64]{0,1:T(8,128)(2,1)S(1)}) fusion(f32[5120,64]{0,1:T(8,128)} %copy.29, bf16[256,64]{0,1:T(8,128)(2,1)S(1)} %copy-done.4, bf16[64,256]{1,0:T(8,128)(2,1)S(1)} %copy-done.5, f32[5120,64]{1,0:T(8,128)S(1)} %bitcast.28, f32[5120]{0:T(1024)S(1)} %rsqrt.31, f32[5120]{0:T(1024)S(1)} %div.23), kind=kOutput, calls=%fused_computation.9 | convolution fusion | flops 340454400 | bytes 3403776 | tf_op jit(solution)/shard_map/dot_general | solution.py:133
  17.0 0.2 fusion.4
  17.2 0.0 copy-done.6
  17.2 0.3 convolution_convert_fusion
  17.5 0.7 copy.32
  18.3 0.0 copy-start.7
  18.3 1.4 %reshape.115 = bf16[160,1024]{1,0:T(8,128)(2,1)S(1)} reshape(bf16[5120,32]{1,0:T(8,128)(2,1)S(1)} %copy.32) | data formatting | bytes 655360 | tf_op jit(solution)/shard_map/reshape | solution.py:144
  19.7 11.5 %all_gather.3.r_ref = bf16[160,2048]{1,0:T(8,128)(2,1)S(1)} all-gather(bf16[160,1024]{1,0:T(8,128)(2,1)S(1)} %reshape.115), channel_id=1, replica_groups=mesh['groups'=2,'seq'=4,'res'=2,'chan'=2] {'res'}, dimensions={1}, use_global_device_ids=true | all-gather | bytes 983040 | tf_op jit(solution)/shard_map/all_gather | solution.py:151
  31.2 0.0 copy-done.7
  31.2 0.3 convolution_convert_fusion.1
  31.5 1.0 %reshape.113 = bf16[160,32,32]{1,0,2:T(8,128)(2,1)S(1)} reshape(bf16[5120,32]{0,1:T(8,128)(2,1)S(1)} %convolution_convert_fusion.1) | data formatting | bytes 655360 | tf_op jit(solution)/shard_map/reshape | solution.py:139
  32.5 0.7 copy.31
  33.2 1.3 %subtract_convert_fusion = (bf16[1024,128]{1,0:T(8,128)(2,1)S(1)}, bf16[1024,128]{1,0:T(8,128)(2,1)S(1)}) fusion(f32[1024,128]{1,0:T(8,128)} %param.15), kind=kLoop, calls=%fused_computation.22 | loop fusion | flops 524288 | bytes 1048576 | tf_op jit(solution)/shard_map/convert_element_type | solution.py:153
  34.5 9.0 %shard_map.104 = f32[512,512]{1,0:T(8,128)} custom-call(bf16[1024,160]{1,0:T(8,128)(2,1)S(1)} %bitcast.26, bf16[160,2048]{1,0:T(8,128)(2,1)S(1)} %all_gather.3.r_ref, bf16[1024,128]{1,0:T(8,128)(2,1)S(1)} %get-tuple-element.11.wh_ref, bf16[1024,128]{1,0:T(8,128)(2,1)S(1)} %get-tuple-element.10.wl_ref), custom_call_target="tpu_custom_call" | custom-call | flops 7113539584 | bytes 2555904 | tf_op jit(solution)/shard_map/pallas_call | solution.py:81
  43.5 0.0 reduce-scatter.2.cloned.1.call-update
  43.6 0.7 copy.30
  44.3 0.0 copy-start.2
  44.3 0.0 copy-start.3
  44.3 2.0 %copy.35 = bf16[160,32,64]{0,2,1:T(8,128)(2,1)} copy(bf16[160,32,64]{2,1,0:T(8,128)(2,1)S(1)} %bitcast.30) | data formatting | bytes 1310720
  46.3 31.3 %reduce-scatter.2.cloned.1.call-done = f32[64,512]{1,0:T(8,128)} async-done(((f32[512,512]{1,0:T(8,128)}), f32[64,512]{1,0:T(8,128)}) %reduce-scatter.2.cloned.1.call-update) | async-done | bytes 131088 | tf_op jit(solution)/shard_map/reduce_scatter | solution.py:155
  77.6 0.9 %reshape.116 = f32[2,32,4,128]{3,2,1,0:T(4,128)S(1)} reshape(f32[64,512]{1,0:T(8,128)} %reduce-scatter.2.cloned.1.call-done) | data formatting | bytes 262144 | tf_op jit(solution)/shard_map/reshape | solution.py:158
  78.6 0.0 copy-done.2
  78.6 0.1 fusion.23
  78.7 0.1 div.28
  78.8 0.2 multiply_reduce_fusion.1
  79.0 0.1 rsqrt.34
  79.1 0.0 copy-done
  79.1 0.0 copy-done.3
  79.1 1.1 %fusion.13 = f32[32,8,128]{2,1,0:T(8,128)} fusion(bf16[512,128]{1,0:T(8,128)(2,1)S(1)} %copy-done, bf16[128,512]{1,0:T(8,128)(2,1)S(1)} %copy-done.3, f32[256,128]{1,0:T(8,128)S(1)} %bitcast.32, f32[32,8,128]{2,1,0:T(8,128)S(1)} %copy-done.2, f32[256]{0:T(256)S(1)} %rsqrt.34, f32[256]{0:T(256)S(1)} %div.28), kind=kOutput, calls=%fused_computation.20 | convolution fusion | flops 67567616 | bytes 657408 | tf_op jit(solution)/shard_map/dot_general | solution.py:167
  (7 shorter events, 0.1 us)
Async XLA Ops:
  7.2 71.9 %copy-start = (bf16[512,128]{1,0:T(8,128)(2,1)S(1)}, bf16[512,128]{1,0:T(8,128)(2,1)}, u32[]{:S(2)}) copy-start(bf16[512,128]{1,0:T(8,128)(2,1)} %param.17) | copy-start | bytes 393220
  7.2 70.4 %reduce-scatter.2.cloned.1.call-start = ((), (), s32[]{:S(2)}) async-start(), calls=%async_computation.1 | async-start | bytes 1179648 | tf_op jit(solution)/shard_map/reduce_scatter | solution.py:155
  9.6 1.6 %copy-start.1 = (bf16[160,32,64]{0,2,1:T(8,128)(2,1)S(1)}, bf16[160,32,64]{0,2,1:T(8,128)(2,1)}, u32[]{:S(2)}) copy-start(bf16[160,32,64]{0,2,1:T(8,128)(2,1)} %param.9) | copy-start | bytes 1966084
  11.7 2.1 %copy-start.4 = (bf16[256,64]{0,1:T(8,128)(2,1)S(1)}, bf16[256,64]{0,1:T(8,128)(2,1)}, u32[]{:S(2)}) copy-start(bf16[256,64]{0,1:T(8,128)(2,1)} %param.12) | copy-start | bytes 98308
  11.7 2.1 %copy-start.5 = (bf16[64,256]{1,0:T(8,128)(2,1)S(1)}, bf16[64,256]{1,0:T(8,128)(2,1)}, u32[]{:S(2)}) copy-start(bf16[64,256]{1,0:T(8,128)(2,1)} %param.11) | copy-start | bytes 98308
  13.9 3.4 %copy-start.6 = (bf16[64,32]{0,1:T(8,128)(2,1)S(1)}, bf16[64,32]{0,1:T(8,128)(2,1)}, u32[]{:S(2)}) copy-start(bf16[64,32]{0,1:T(8,128)(2,1)} %param.14) | copy-start | bytes 12292
  18.3 12.9 %copy-start.7 = (bf16[64,32]{0,1:T(8,128)(2,1)S(1)}, bf16[64,32]{0,1:T(8,128)(2,1)}, u32[]{:S(2)}) copy-start(bf16[64,32]{0,1:T(8,128)(2,1)} %param.13) | copy-start | bytes 12292
  44.3 34.3 %copy-start.2 = (f32[32,8,128]{2,1,0:T(8,128)S(1)}, f32[32,8,128]{2,1,0:T(8,128)}, u32[]{:S(2)}) copy-start(f32[32,8,128]{2,1,0:T(8,128)} %param.10) | copy-start | bytes 393220
  44.3 34.8 %copy-start.3 = (bf16[128,512]{1,0:T(8,128)(2,1)S(1)}, bf16[128,512]{1,0:T(8,128)(2,1)}, u32[]{:S(2)}) copy-start(bf16[128,512]{1,0:T(8,128)(2,1)} %param.16) | copy-start | bytes 393220
Sparse Core Ops, SparseCore 0:
  43.7 33.8 reduce-scatter.1
where the time goes:
time: 87.3 us; the launch traced here: 87 us
  waiting for transfers between devices  31.3 us (36%)
  between operations  14.3 us (16%)
  local copies, waits for them, and re-layouts  12.4 us (14%)
  blocking collectives  11.5 us (13%)
  Pallas kernels  9 us (10%)
  matrix products  4.73 us (5%)
  other arithmetic  3.75 us (4%)
    reduce_scatter x1, waiting for transfers between devices, per_device(): lax.psum_scatter(partial_value, ('seq', 'chan'), scatter_dimension=0, til...  31.3 us
    all_gather x1, blocking collectives, per_device(): r_all = lax.all_gather(right_features, 'res', axis=1, tiled=True)  11.5 us
    pallas_call x1, Pallas kernels, outer_project(): pl.pallas_call(functools.partial(outer_project_kernel, scale), grid=(step...  9 us
    convert_element_type x2, local copies, waits for them, and re-layouts, per_device(): cross_moment_average.astype(jnp.float32)  4.24 us
    dot_general x1, matrix products, per_device(): jnp.dot(homolog_inner_state, homolog_shrink_weights, preferred_element_ty...  3.09 us
    unnamed x17, local copies, waits for them, and re-layouts  2.02 us
  transfers between devices with their start and end apart: 1, of which 1 were waited for; matrix products, arithmetic and copies ran while one was open for 3% of the time, Pallas kernels for 0%

commit v1 on v0

--- a/solution.py
+++ b/solution.py
@@ -104,6 +104,23 @@
     )(lt, r_all, wh, wl)
 
 
+def reduce_over_sequences(partial_value):
+    nseq = lax.axis_size("seq")
+    nchan = lax.axis_size("chan")
+    if nchan != 2:
+        return lax.psum_scatter(partial_value, ("seq", "chan"), scatter_dimension=0, tiled=True)
+    rows, cols = partial_value.shape
+    chunk = rows // (nseq * nchan)
+    xs = partial_value.reshape(nseq, nchan, chunk, cols)
+    c = lax.axis_index("chan")
+    mine = lax.dynamic_index_in_dim(xs, c, axis=1, keepdims=False)
+    other = lax.dynamic_index_in_dim(xs, 1 - c, axis=1, keepdims=False)
+    received = lax.ppermute(other, "chan", [(0, 1), (1, 0)])
+    part = mine + received
+    gathered = lax.all_to_all(part, "seq", 0, 0, tiled=False)
+    return gathered.sum(axis=0)
+
+
 def per_device(
     homolog_embedding,
     coupling_embedding,
@@ -149,10 +166,11 @@
 
     lt = jnp.transpose(left_features, (2, 1, 0)).reshape(proj_width * sites_local_share, homologs_local_share)
     r_all = lax.all_gather(right_features, "res", axis=1, tiled=True)
-    w_hi = moment_coupling_weights.astype(jnp.bfloat16)
-    w_lo = (moment_coupling_weights - w_hi.astype(jnp.float32)).astype(jnp.bfloat16)
+    w_hi_f32 = lax.reduce_precision(moment_coupling_weights, exponent_bits=8, mantissa_bits=7)
+    w_hi = w_hi_f32.astype(jnp.bfloat16)
+    w_lo = (moment_coupling_weights - w_hi_f32).astype(jnp.bfloat16)
     partial_value = outer_project(lt, r_all, w_hi, w_lo, 1.0 / depth_total)
-    pair_update = lax.psum_scatter(partial_value, ("seq", "chan"), scatter_dimension=0, tiled=True)
+    pair_update = reduce_over_sequences(partial_value)
     nja_local = block_cols // JB
     pair_update = (
         pair_update.reshape(nja_local, sites_local_share, JB, pair_width)

time: 87.3 us -> 60.8 us (0.70)
  waiting for transfers between devices: 31.3 us -> 14 us
  between operations: 14.3 us -> 0.96 us
  starting transfers between devices: 0.04 us -> 5.2 us
  Pallas kernels: 9 us -> 8.01 us
    reduce_scatter x1 -> x0, waiting for transfers between devices: 31.3 us -> none  [per_device(): lax.psum_scatter(partial_value, ('seq', 'chan'), scatter_dimension=0, til...]
    all_to_all x0 -> x1, waiting for transfers between devices: none -> 12.1 us  [reduce_over_sequences(): gathered = lax.all_to_all(part, 'seq', 0, 0, tiled=False)]
    all_to_all x0 -> x1, starting transfers between devices: none -> 5.13 us  [reduce_over_sequences(): gathered = lax.all_to_all(part, 'seq', 0, 0, tiled=False)]
    ppermute x0 -> x1, waiting for transfers between devices: none -> 1.9 us  [reduce_over_sequences(): received = lax.ppermute(other, 'chan', [(0, 1), (1, 0)])]
    pallas_call x1, Pallas kernels: 9 us -> 8.01 us  [outer_project(): pl.pallas_call(functools.partial(outer_project_kernel, scale), grid=(step...]
    reshape x1, local copies, waits for them, and re-layouts: 0.95 us -> 0.05 us  [per_device(): pair_update.reshape(nja_local, sites_local_share, JB, pair_width)]
  transfers between devices with their start and end apart: 1 -> 2, of which waited for: 1 -> 2; matrix products, arithmetic and copies ran while one was open for 3% -> 4% of each run, Pallas kernels for 0% -> 0%
where the time goes in v1:
time: 60.8 us; the launch traced here: 60.5 us
  waiting for transfers between devices  14 us (23%)
  local copies, waits for them, and re-layouts  11.6 us (19%)
  blocking collectives  11.5 us (19%)
  Pallas kernels  8.01 us (13%)
  starting transfers between devices  5.2 us (9%)
  matrix products  4.73 us (8%)
  other arithmetic  4.51 us (7%)
  between operations  0.96 us (2%)
    all_to_all x1, waiting for transfers between devices, reduce_over_sequences(): gathered = lax.all_to_all(part, 'seq', 0, 0, tiled=False)  12.1 us
    all_gather x1, blocking collectives, per_device(): r_all = lax.all_gather(right_features, 'res', axis=1, tiled=True)  11.5 us
    pallas_call x1, Pallas kernels, outer_project(): pl.pallas_call(functools.partial(outer_project_kernel, scale), grid=(step...  8.01 us
    all_to_all x1, starting transfers between devices, reduce_over_sequences(): gathered = lax.all_to_all(part, 'seq', 0, 0, tiled=False)  5.13 us
    convert_element_type x2, local copies, waits for them, and re-layouts, per_device(): cross_moment_average.astype(jnp.float32)  4.25 us
    dot_general x1, matrix products, per_device(): jnp.dot(homolog_inner_state, homolog_shrink_weights, preferred_element_ty...  3.09 us
    unnamed x17, local copies, waits for them, and re-layouts  2.02 us
    ppermute x1, waiting for transfers between devices, reduce_over_sequences(): received = lax.ppermute(other, 'chan', [(0, 1), (1, 0)])  1.9 us
  transfers between devices with their start and end apart: 2, of which 2 were waited for; matrix products, arithmetic and copies ran while one was open for 4% of the time, Pallas kernels for 0%

profile of v1, /device:TPU:0, one launch (start us, length us, event | category | flops | bytes accessed | tf_op | source)
XLA Modules:
  0.0 60.5 jit_solution(2375504582820083571)
XLA Ops:
  0.6 0.0 copy-start
  0.6 2.4 %copy.34 = f32[160,32,64]{2,1,0:T(8,128)S(1)} copy(bf16[160,32,64]{0,2,1:T(8,128)(2,1)} %param.9) | data formatting | bytes 1966080 | tf_op jit(solution)/shard_map/convert_element_type | solution.py:149
  3.1 0.0 copy-start.1
  3.1 1.5 %convert_reduce_fusion.1 = f32[160,32]{0,1:T(8,128)S(1)} fusion(bf16[160,32,64]{0,2,1:T(8,128)(2,1)} %param.9), kind=kLoop, calls=%fused_computation.21 | loop fusion | flops 650240 | bytes 675840 | tf_op jit(solution)/shard_map/reduce_sum | solution.py:12
  4.6 0.0 copy-done.1
  4.6 0.4 multiply_reduce_fusion
  5.0 0.1 copy.35
  5.1 0.0 copy-start.4
  5.2 0.0 copy-start.5
  5.2 1.8 %copy.37 = f32[5120,64]{0,1:T(8,128)} copy(f32[5120,64]{1,0:T(8,128)S(1)} %bitcast.34) | data formatting | bytes 2621440 | tf_op jit(solution)/shard_map/convert_element_type | solution.py:149
  7.0 0.1 copy.36
  7.1 0.1 rsqrt.31
  7.2 0.1 div.23
  7.3 0.0 copy-done.4
  7.3 0.0 copy-done.5
  7.3 0.0 copy-start.6
  7.3 3.1 %convert_reduce_fusion = (f32[5120]{0:T(1024)S(1)}, bf16[5120,64]{0,1:T(8,128)(2,1)S(1)}) fusion(f32[5120,64]{0,1:T(8,128)} %copy.37, bf16[256,64]{0,1:T(8,128)(2,1)S(1)} %copy-done.4, bf16[64,256]{1,0:T(8,128)(2,1)S(1)} %copy-done.5, f32[5120,64]{1,0:T(8,128)S(1)} %bitcast.35, f32[5120]{0:T(1024)S(1)} %rsqrt.31, f32[5120]{0:T(1024)S(1)} %div.23), kind=kOutput, calls=%fused_computation.9 | convolution fusion | flops 340454400 | bytes 3403776 | tf_op jit(solution)/shard_map/dot_general | solution.py:150
  10.4 0.2 fusion.4
  10.7 0.0 copy-done.6
  10.7 0.3 convolution_convert_fusion
  11.0 0.7 %copy.40 = bf16[5120,32]{1,0:T(8,128)(2,1)S(1)} copy(bf16[5120,32]{0,1:T(8,128)(2,1)S(1)} %convolution_convert_fusion) | data formatting | bytes 655360 | tf_op jit(solution)/shard_map/convert_element_type | solution.py:160
  11.7 0.0 copy-start.7
  11.7 1.4 %reshape.118 = bf16[160,1024]{1,0:T(8,128)(2,1)S(1)} reshape(bf16[5120,32]{1,0:T(8,128)(2,1)S(1)} %copy.40) | data formatting | bytes 655360 | tf_op jit(solution)/shard_map/reshape | solution.py:161
  13.1 11.5 %all_gather.3.r_ref = bf16[160,2048]{1,0:T(8,128)(2,1)S(1)} all-gather(bf16[160,1024]{1,0:T(8,128)(2,1)S(1)} %reshape.118), channel_id=1, replica_groups=mesh['groups'=2,'seq'=4,'res'=2,'chan'=2] {'res'}, dimensions={1}, use_global_device_ids=true | all-gather | bytes 983040 | tf_op jit(solution)/shard_map/all_gather | solution.py:168
  24.6 0.0 copy-done.7
  24.6 0.3 convolution_convert_fusion.1
  24.9 1.0 %reshape.116 = bf16[160,32,32]{1,0,2:T(8,128)(2,1)S(1)} reshape(bf16[5120,32]{0,1:T(8,128)(2,1)S(1)} %convolution_convert_fusion.1) | data formatting | bytes 655360 | tf_op jit(solution)/shard_map/reshape | solution.py:156
  25.9 0.7 %copy.39 = bf16[32,32,160]{2,1,0:T(8,128)(2,1)S(1)} copy(bf16[32,32,160]{1,2,0:T(8,128)(2,1)S(1)} %bitcast.36) | data formatting | bytes 655360 | tf_op jit(solution)/shard_map/transpose | solution.py:167
  26.6 1.1 %fusion.14 = (bf16[1024,128]{1,0:T(8,128)(2,1)S(1)}, bf16[1024,128]{1,0:T(8,128)(2,1)S(1)}) fusion(f32[1024,128]{1,0:T(8,128)} %param.15), kind=kLoop, calls=%fused_computation.24 | loop fusion | flops 524288 | bytes 1048576 | tf_op jit(solution)/shard_map/convert_element_type | solution.py:171
  27.7 8.0 %shard_map.104 = f32[512,512]{1,0:T(8,128)S(1)} custom-call(bf16[1024,160]{1,0:T(8,128)(2,1)S(1)} %bitcast.33, bf16[160,2048]{1,0:T(8,128)(2,1)S(1)} %all_gather.3.r_ref, bf16[1024,128]{1,0:T(8,128)(2,1)S(1)} %get-tuple-element.11.wh_ref, bf16[1024,128]{1,0:T(8,128)(2,1)S(1)} %get-tuple-element.10.wl_ref), custom_call_target="tpu_custom_call" | custom-call | flops 7113539584 | bytes 2555904 | tf_op jit(solution)/shard_map/pallas_call | solution.py:81
  35.8 0.1 collective-permute-start
  35.9 1.9 %collective-permute-done = f32[4,64,512]{2,1,0:T(8,128)S(1)} collective-permute-done((f32[4,64,512]{2,1,0:T(8,128)S(1)}, f32[4,64,512]{2,1,0:T(8,128)S(1)}, u32[]{:S(2)}, u32[]{:S(2)}) %collective-permute-start) | collective-permute-done | bytes 524320 | tf_op jit(solution)/shard_map/ppermute | solution.py:118
  37.8 0.9 %bitcast_add_fusion = f32[4,64,512]{2,1,0:T(8,128)} fusion(f32[4,64,512]{2,1,0:T(8,128)S(1)} %collective-permute-done, f32[4,2,64,512]{3,2,1,0:T(8,128)S(1)} %bitcast.32, s32[]{:T(128)S(6)} %select_n.7), kind=kLoop, calls=%fused_computation.25 | loop fusion | flops 131072 | bytes 1572868 | tf_op jit(solution)/shard_map/add | solution.py:119
  38.7 5.1 %all-to-all-start = ((f32[4,64,512]{2,1,0:T(8,128)}), f32[4,64,512]{2,1,0:T(8,128)S(1)}, u32[]{:S(2)}, u32[]{:S(2)}) async-start(f32[4,64,512]{2,1,0:T(8,128)} %bitcast_add_fusion), calls=%async_computation | async-start | bytes 1048576 | tf_op jit(solution)/shard_map/all_to_all | solution.py:120
  43.8 0.7 %copy.38 = bf16[5120,64]{1,0:T(8,128)(2,1)S(1)} copy(bf16[5120,64]{0,1:T(8,128)(2,1)S(1)} %get-tuple-element.13) | data formatting | bytes 1310720 | tf_op jit(solution)/shard_map/convert_element_type | solution.py:151
  44.5 0.0 copy-start.2
  44.5 2.0 %copy.46 = bf16[160,32,64]{0,2,1:T(8,128)(2,1)} copy(bf16[160,32,64]{2,1,0:T(8,128)(2,1)S(1)} %bitcast.37) | data formatting | bytes 1310720
  46.5 12.1 %all-to-all-done = f32[4,64,512]{2,1,0:T(8,128)S(1)} async-done(((f32[4,64,512]{2,1,0:T(8,128)}), f32[4,64,512]{2,1,0:T(8,128)S(1)}, u32[]{:S(2)}, u32[]{:S(2)}) %all-to-all-start) | async-done | bytes 524320 | tf_op jit(solution)/shard_map/all_to_all | solution.py:120
  58.7 0.0 copy-done.2
  58.7 0.1 fusion.22
  58.8 0.2 multiply_reduce_fusion.1
  59.0 0.1 copy.44
  59.1 0.1 copy.45
  59.2 0.1 rsqrt.34
  59.3 0.1 div.28
  59.4 0.0 copy-done
  59.4 0.0 copy-done.3
  59.4 1.1 %fusion.13 = f32[32,8,128]{2,1,0:T(8,128)} fusion(bf16[512,128]{1,0:T(8,128)(2,1)S(1)} %copy-done, bf16[128,512]{1,0:T(8,128)(2,1)S(1)} %copy-done.3, f32[256,128]{1,0:T(8,128)S(1)} %bitcast.42, f32[32,8,128]{2,1,0:T(8,128)S(1)} %copy-done.2, f32[256]{0:T(256)S(1)} %rsqrt.34, f32[256]{0:T(256)S(1)} %div.28), kind=kOutput, calls=%fused_computation.20 | convolution fusion | flops 67567616 | bytes 657408 | tf_op jit(solution)/shard_map/dot_general | solution.py:185
  (12 shorter events, 0.2 us)
Async XLA Ops:
  0.6 58.8 %copy-start = (bf16[512,128]{1,0:T(8,128)(2,1)S(1)}, bf16[512,128]{1,0:T(8,128)(2,1)}, u32[]{:S(2)}) copy-start(bf16[512,128]{1,0:T(8,128)(2,1)} %param.17) | copy-start | bytes 393220
  3.1 1.6 %copy-start.1 = (bf16[160,32,64]{0,2,1:T(8,128)(2,1)S(1)}, bf16[160,32,64]{0,2,1:T(8,128)(2,1)}, u32[]{:S(2)}) copy-start(bf16[160,32,64]{0,2,1:T(8,128)(2,1)} %param.9) | copy-start | bytes 1966084
  5.1 2.2 %copy-start.4 = (bf16[256,64]{0,1:T(8,128)(2,1)S(1)}, bf16[256,64]{0,1:T(8,128)(2,1)}, u32[]{:S(2)}) copy-start(bf16[256,64]{0,1:T(8,128)(2,1)} %param.12) | copy-start | bytes 98308
  5.2 2.1 %copy-start.5 = (bf16[64,256]{1,0:T(8,128)(2,1)S(1)}, bf16[64,256]{1,0:T(8,128)(2,1)}, u32[]{:S(2)}) copy-start(bf16[64,256]{1,0:T(8,128)(2,1)} %param.11) | copy-start | bytes 98308
  7.3 3.4 %copy-start.6 = (bf16[64,32]{0,1:T(8,128)(2,1)S(1)}, bf16[64,32]{0,1:T(8,128)(2,1)}, u32[]{:S(2)}) copy-start(bf16[64,32]{0,1:T(8,128)(2,1)} %param.14) | copy-start | bytes 12292
  11.7 12.9 %copy-start.7 = (bf16[64,32]{0,1:T(8,128)(2,1)S(1)}, bf16[64,32]{0,1:T(8,128)(2,1)}, u32[]{:S(2)}) copy-start(bf16[64,32]{0,1:T(8,128)(2,1)} %param.13) | copy-start | bytes 12292
  35.8 2.0 %collective-permute-start = (f32[4,64,512]{2,1,0:T(8,128)S(1)}, f32[4,64,512]{2,1,0:T(8,128)S(1)}, u32[]{:S(2)}, u32[]{:S(2)}) collective-permute-start(f32[4,64,512]{2,1,0:T(8,128)S(1)} %dynamic-slice_bitcast_fusion), channel_id=1, source_target_pairs={{0,1},{1,0},{2,3},{3,2},{4,5},{5,4},{6,7},{7,6},{8,9},{9,8},{10,11... | collective-permute-start | bytes 1572872 | tf_op jit(solution)/shard_map/ppermute | solution.py:118
  38.7 19.9 %all-to-all-start = ((f32[4,64,512]{2,1,0:T(8,128)}), f32[4,64,512]{2,1,0:T(8,128)S(1)}, u32[]{:S(2)}, u32[]{:S(2)}) async-start(f32[4,64,512]{2,1,0:T(8,128)} %bitcast_add_fusion), calls=%async_computation | async-start | bytes 1048576 | tf_op jit(solution)/shard_map/all_to_all | solution.py:120
  44.5 14.2 %copy-start.2 = (f32[32,8,128]{2,1,0:T(8,128)S(1)}, f32[32,8,128]{2,1,0:T(8,128)}, u32[]{:S(2)}) copy-start(f32[32,8,128]{2,1,0:T(8,128)} %param.10) | copy-start | bytes 393220
  46.5 12.9 %copy-start.3 = (bf16[128,512]{1,0:T(8,128)(2,1)S(1)}, bf16[128,512]{1,0:T(8,128)(2,1)}, u32[]{:S(2)}) copy-start(bf16[128,512]{1,0:T(8,128)(2,1)} %param.16) | copy-start | bytes 393220

commit v2 on v1

--- a/solution.py
+++ b/solution.py
@@ -24,7 +24,7 @@
     width = wh_ref.shape[0] // (C_HI * C_LO)
     rows_i = lt_ref.shape[0] // (C_HI * C_LO)
     lanes = JB * width
-    nja = r_ref.shape[1] // lanes
+    nja = r_ref.shape[0] // lanes
     dd = wh_ref.shape[1]
 
     @pl.when(pl.program_id(0) == 0)
@@ -54,7 +54,12 @@
     acc = jnp.zeros(o_ref.shape, jnp.float32)
     block = C_LO * rows_i
     for c_hi in range(C_HI):
-        x = jnp.dot(lt_ref[c_hi * block : (c_hi + 1) * block, :], r_ref[...], preferred_element_type=jnp.float32)
+        x = lax.dot_general(
+            lt_ref[c_hi * block : (c_hi + 1) * block, :].astype(jnp.bfloat16),
+            r_ref[...],
+            (((1,), (1,)), ((), ())),
+            preferred_element_type=jnp.float32,
+        )
         xh = x.astype(jnp.bfloat16)
         xl = (x - xh.astype(jnp.float32)).astype(jnp.bfloat16)
         lh = rearrange(xh)
@@ -70,7 +75,7 @@
     rows_i = lt.shape[0] // (C_HI * C_LO)
     width = wh.shape[0] // (C_HI * C_LO)
     lanes = JB * width
-    total_lanes = r_all.shape[1]
+    total_lanes = r_all.shape[0]
     chunk = min(total_lanes, 16 * lanes)
     steps = total_lanes // chunk
     nja_chunk = chunk // lanes
@@ -83,7 +88,7 @@
         grid=(steps,),
         in_specs=[
             pl.BlockSpec(lt.shape, lambda q: (0, 0)),
-            pl.BlockSpec((s, chunk), lambda q: (0, q)),
+            pl.BlockSpec((chunk, s), lambda q: (q, 0)),
             pl.BlockSpec(wh.shape, lambda q: (0, 0)),
             pl.BlockSpec(wl.shape, lambda q: (0, 0)),
         ],
@@ -99,9 +104,57 @@
         cost_estimate=pl.CostEstimate(
             flops=flops,
             transcendentals=0,
-            bytes_accessed=lt.size * 2 + r_all.size * 2 + wh.size * 4 + out_rows * JB * d * 4,
+            bytes_accessed=lt.size * 4 + r_all.size * 2 + wh.size * 4 + out_rows * JB * d * 4,
         ),
     )(lt, r_all, wh, wl)
+
+
+def msa_kernel(x_ref, ww_ref, ws_ref, pt_ref, o_ref, lt_ref, rt_ref, n2_ref):
+    x = x_ref[...].astype(jnp.float32)
+    n1 = apply_layer_norm(x).astype(jnp.bfloat16)
+    hidden = jnp.maximum(jnp.dot(n1, ww_ref[...], preferred_element_type=jnp.float32), 0.0).astype(jnp.bfloat16)
+    refreshed = (x + jnp.dot(hidden, ws_ref[...], preferred_element_type=jnp.float32)).astype(jnp.bfloat16)
+    o_ref[...] = refreshed
+    k = x_ref.shape[1]
+    n2_ref[:, :k] = apply_layer_norm(refreshed.astype(jnp.float32)).astype(jnp.bfloat16).astype(jnp.float32)
+    n2_ref[:, k:] = jnp.zeros((n2_ref.shape[0], n2_ref.shape[1] - k), jnp.float32)
+    width = pt_ref.shape[0] // 2
+    sites = rt_ref.shape[0] // width
+    depth = rt_ref.shape[1]
+    pt = pt_ref[...]
+
+    def body(i, carry):
+        rows = n2_ref[pl.ds(i, depth, stride=sites), :].astype(jnp.bfloat16)
+        proj = lax.dot_general(pt, rows, (((1,), (1,)), ((), ())), preferred_element_type=jnp.float32)
+        start = pl.multiple_of(i * width, width)
+        lt_ref[pl.ds(start, width), :] = proj[:width]
+        rt_ref[pl.ds(start, width), :] = proj[width:].astype(jnp.bfloat16)
+        return carry
+
+    lax.fori_loop(0, sites, body, 0)
+
+
+def msa_block(x2, ww, ws, pt, depth, sites):
+    rows, k = x2.shape
+    width = pt.shape[0] // 2
+    hidden = ww.shape[1]
+    return pl.pallas_call(
+        msa_kernel,
+        out_shape=(
+            jax.ShapeDtypeStruct((rows, k), jnp.bfloat16),
+            jax.ShapeDtypeStruct((width * sites, depth), jnp.float32),
+            jax.ShapeDtypeStruct((sites * width, depth), jnp.bfloat16),
+        ),
+        in_specs=[pl.BlockSpec(memory_space=pltpu.VMEM)] * 4,
+        out_specs=(pl.BlockSpec(memory_space=pltpu.VMEM),) * 3,
+        scratch_shapes=[pltpu.VMEM((rows, pt.shape[1]), jnp.float32)],
+        compiler_params=pltpu.CompilerParams(vmem_limit_bytes=48 * 1024 * 1024),
+        cost_estimate=pl.CostEstimate(
+            flops=2 * rows * k * hidden * 2 + 2 * rows * k * 2 * width,
+            transcendentals=2 * rows,
+            bytes_accessed=rows * k * 4 + 2 * rows * width * 3,
+        ),
+    )(x2, ww, ws, pt)
 
 
 def reduce_over_sequences(partial_value):
@@ -135,37 +188,22 @@
     homologs_local_share, sites_local_share, homolog_lane_number = homolog_embedding.shape
     proj_width = lhs_projector.shape[1]
     pair_width = coupling_embedding.shape[2]
-    cross_moment_average = homolog_embedding.reshape(
-        homologs_local_share * sites_local_share, homolog_lane_number
-    )
-    homolog_standardized = apply_layer_norm(cross_moment_average.astype(jnp.float32)).astype(
-        jnp.bfloat16
-    )
-    homolog_inner_state = jnp.maximum(
-        jnp.dot(homolog_standardized, homolog_widen_weights, preferred_element_type=jnp.float32),
-        0.0,
-    ).astype(jnp.bfloat16)
-    homolog_refreshed = (
-        cross_moment_average.astype(jnp.float32)
-        + jnp.dot(homolog_inner_state, homolog_shrink_weights, preferred_element_type=jnp.float32)
-    ).astype(jnp.bfloat16)
-    alignment_normed2 = apply_layer_norm(homolog_refreshed.astype(jnp.float32)).astype(jnp.bfloat16)
-    left_features = (
-        jnp.dot(alignment_normed2, lhs_projector, preferred_element_type=jnp.float32)
-        .astype(jnp.bfloat16)
-        .reshape(homologs_local_share, sites_local_share, proj_width)
-    )
-    right_features = (
-        jnp.dot(alignment_normed2, rhs_projector, preferred_element_type=jnp.float32)
-        .astype(jnp.bfloat16)
-        .reshape(homologs_local_share, sites_local_share * proj_width)
+    x2 = homolog_embedding.reshape(homologs_local_share * sites_local_share, homolog_lane_number)
+    pt = jnp.concatenate([lhs_projector, rhs_projector], axis=1).T
+    pt = jnp.pad(pt, ((0, 0), (0, 128 - homolog_lane_number)))
+    homolog_refreshed, left_t, right_t = msa_block(
+        x2, homolog_widen_weights, homolog_shrink_weights, pt, homologs_local_share, sites_local_share
+    )
+    lt = (
+        left_t.reshape(sites_local_share, proj_width, homologs_local_share)
+        .transpose(1, 0, 2)
+        .reshape(proj_width * sites_local_share, homologs_local_share)
     )
     owners = lax.axis_size(("seq", "chan"))
     depth_total = float(homologs_local_share * owners)
     block_cols = coupling_embedding.shape[1]
 
-    lt = jnp.transpose(left_features, (2, 1, 0)).reshape(proj_width * sites_local_share, homologs_local_share)
-    r_all = lax.all_gather(right_features, "res", axis=1, tiled=True)
+    r_all = lax.all_gather(right_t, "res", axis=0, tiled=True)
     w_hi_f32 = lax.reduce_precision(moment_coupling_weights, exponent_bits=8, mantissa_bits=7)
     w_hi = w_hi_f32.astype(jnp.bfloat16)
     w_lo = (moment_coupling_weights - w_hi_f32).astype(jnp.bfloat16)

time: 60.8 us -> 69.2 us (1.14)
  Pallas kernels: 8.01 us -> 19.8 us
  blocking collectives: 11.5 us -> 15.7 us
  matrix products: 4.73 us -> 1.06 us
  other arithmetic: 4.51 us -> 2.11 us
  local copies, waits for them, and re-layouts: 11.6 us -> 9.54 us
  waiting for transfers between devices: 14 us -> 14.7 us
    pallas_call x0 -> x1, Pallas kernels: none -> 10.4 us  [msa_block(): pl.pallas_call(msa_kernel, out_shape=(jax.ShapeDtypeStruct((rows, k), jnp...]
    convert_element_type x4 -> x0, local copies, waits for them, and re-layouts: 5.71 us -> none  [the longest x2 4.25 us: per_device(): cross_moment_average.astype(jnp.float32)]
    unnamed x17 -> x25, local copies, waits for them, and re-layouts: 2.02 us -> 7.48 us
    all_gather x1, blocking collectives: 11.5 us -> 15.7 us  [per_device(): r_all = lax.all_gather(right_t, 'res', axis=0, tiled=True)]
    dot_general x3 -> x0, matrix products: 3.66 us -> none  [the longest x1 3.09 us: per_device(): jnp.dot(homolog_inner_state, homolog_shrink_weights, preferred_element_ty...]
    reduce_sum x2 -> x1, other arithmetic: 1.65 us -> 0.11 us  [apply_layer_norm(): mean = jnp.mean(values, axis=-1, keepdims=True)]
    pallas_call x1, Pallas kernels: 8.01 us -> 9.34 us  [outer_project(): pl.pallas_call(functools.partial(outer_project_kernel, scale), grid=(step...]
    all_to_all x1, waiting for transfers between devices: 12.1 us -> 12.8 us  [reduce_over_sequences(): gathered = lax.all_to_all(part, 'seq', 0, 0, tiled=False)]
  transfers between devices with their start and end apart: 2 -> 2, of which waited for: 2 -> 2; matrix products, arithmetic and copies ran while one was open for 4% -> 3% of each run, Pallas kernels for 0% -> 0%
where the time goes in v2:
time: 69.2 us; the launch traced here: 68.9 us
  Pallas kernels  19.8 us (29%)
  blocking collectives  15.7 us (23%)
  waiting for transfers between devices  14.7 us (21%)
  local copies, waits for them, and re-layouts  9.54 us (14%)
  starting transfers between devices  5.19 us (8%)
  other arithmetic  2.11 us (3%)
  matrix products  1.06 us (2%)
  between operations  0.85 us (1%)
    all_gather x1, blocking collectives, per_device(): r_all = lax.all_gather(right_t, 'res', axis=0, tiled=True)  15.7 us
    all_to_all x1, waiting for transfers between devices, reduce_over_sequences(): gathered = lax.all_to_all(part, 'seq', 0, 0, tiled=False)  12.8 us
    pallas_call x1, Pallas kernels, msa_block(): pl.pallas_call(msa_kernel, out_shape=(jax.ShapeDtypeStruct((rows, k), jnp...  10.4 us
    pallas_call x1, Pallas kernels, outer_project(): pl.pallas_call(functools.partial(outer_project_kernel, scale), grid=(step...  9.34 us
    unnamed x25, local copies, waits for them, and re-layouts  7.48 us
    all_to_all x1, starting transfers between devices, reduce_over_sequences(): gathered = lax.all_to_all(part, 'seq', 0, 0, tiled=False)  5.12 us
    ppermute x1, waiting for transfers between devices, reduce_over_sequences(): received = lax.ppermute(other, 'chan', [(0, 1), (1, 0)])  1.9 us
    reshape x1, local copies, waits for them, and re-layouts, per_device(): left_t.reshape(sites_local_share, proj_width, homologs_local_share)  1.59 us
  transfers between devices with their start and end apart: 2, of which 2 were waited for; matrix products, arithmetic and copies ran while one was open for 3% of the time, Pallas kernels for 0%

profile of v2, /device:TPU:0, one launch (start us, length us, event | category | flops | bytes accessed | tf_op | source)
XLA Modules:
  0.0 68.9 jit_solution(5913585247223958316)
XLA Ops:
  0.6 0.0 copy-start
  0.6 0.0 copy-start.8
  0.7 0.0 copy-start.9
  0.7 0.0 copy-start.10
  0.7 0.0 copy-start.4
  0.7 2.3 %copy.28 = bf16[160,32,64]{2,1,0:T(8,128)(2,1)S(1)} copy(bf16[160,32,64]{0,2,1:T(8,128)(2,1)} %param.9) | data formatting | bytes 1310720 | tf_op args[0]
  3.0 0.0 copy-done.8
  3.0 0.1 copy.29.ws_ref
  3.1 0.0 copy-done.9
  3.1 0.0 copy-done.10
  3.1 0.0 copy-done.4
  3.1 10.4 %shard_map.104 = (bf16[5120,64]{1,0:T(8,128)(2,1)S(1)}, f32[1024,160]{1,0:T(8,128)S(1)}, bf16[1024,160]{1,0:T(8,128)(2,1)S(1)}) custom-call(bf16[5120,64]{1,0:T(8,128)(2,1)S(1)} %bitcast.29, bf16[64,256]{1,0:T(8,128)(2,1)S(1)} %copy-done.4, bf16[256,64]{1,0:T(8,128)(2,1)S(1)} %copy.29.ws_ref, bf16[64,128]{1,0:T(8,128)(2,1)S(1)} %pad.4.pt_ref), custom_call_target="tpu_custom_call" | custom-call | flops 377487360 | bytes 2293760 | tf_op jit(solution)/shard_map/pallas_call | solution.py:141
  13.6 1.6 %copy.30 = f32[32,32,160]{2,0,1:T(8,128)} copy(f32[32,32,160]{2,1,0:T(8,128)S(1)} %bitcast.32) | data formatting | bytes 1310720 | tf_op jit(solution)/shard_map/reshape | solution.py:198
  15.2 0.0 copy-start.6
  15.2 15.7 %all_gather.3.r_ref = bf16[2048,160]{1,0:T(8,128)(2,1)S(1)} all-gather(bf16[1024,160]{1,0:T(8,128)(2,1)S(1)} %get-tuple-element.7), channel_id=1, replica_groups=mesh['groups'=2,'seq'=4,'res'=2,'chan'=2] {'res'}, dimensions={0}, use_global_device_ids=true | all-gather | bytes 983040 | tf_op jit(solution)/shard_map/all_gather | solution.py:206
  30.8 0.0 copy-done.6
  30.8 0.9 %fusion.4 = (bf16[1024,128]{1,0:T(8,128)(2,1)}, bf16[1024,128]{1,0:T(8,128)(2,1)}) fusion(f32[1024,128]{1,0:T(8,128)S(1)} %copy-done.6), kind=kLoop, calls=%fused_computation.7 | loop fusion | flops 524288 | bytes 1048576 | tf_op jit(solution)/shard_map/convert_element_type | solution.py:209
  31.7 0.0 copy-start.1
  31.7 1.2 %copy-done.1 = f32[32,32,160]{2,0,1:T(8,128)S(1)} copy-done((f32[32,32,160]{2,0,1:T(8,128)S(1)}, f32[32,32,160]{2,0,1:T(8,128)}, u32[]{:S(2)}) %copy-start.1) | copy-done | bytes 655384
  32.9 0.0 copy-start.2
  33.0 0.9 %copy-done.2 = bf16[1024,128]{1,0:T(8,128)(2,1)S(1)} copy-done((bf16[1024,128]{1,0:T(8,128)(2,1)S(1)}, bf16[1024,128]{1,0:T(8,128)(2,1)}, u32[]{:S(2)}) %copy-start.2) | copy-done | bytes 262168
  33.9 0.0 copy-start.3
  33.9 0.9 %copy-done.3 = bf16[1024,128]{1,0:T(8,128)(2,1)S(1)} copy-done((bf16[1024,128]{1,0:T(8,128)(2,1)S(1)}, bf16[1024,128]{1,0:T(8,128)(2,1)}, u32[]{:S(2)}) %copy-start.3) | copy-done | bytes 262168
  34.8 9.3 %shard_map.105 = f32[512,512]{1,0:T(8,128)S(1)} custom-call(f32[1024,160]{1,0:T(8,128)S(1)} %bitcast.31, bf16[2048,160]{1,0:T(8,128)(2,1)S(1)} %all_gather.3.r_ref, bf16[1024,128]{1,0:T(8,128)(2,1)S(1)} %copy-done.3, bf16[1024,128]{1,0:T(8,128)(2,1)S(1)} %copy-done.2), custom_call_target="tpu_custom_call" | custom-call | flops 7113539584 | bytes 2883584 | tf_op jit(solution)/shard_map/pallas_call | solution.py:86
  44.2 0.1 collective-permute-start
  44.3 1.9 %collective-permute-done = f32[4,64,512]{2,1,0:T(8,128)S(1)} collective-permute-done((f32[4,64,512]{2,1,0:T(8,128)S(1)}, f32[4,64,512]{2,1,0:T(8,128)S(1)}, u32[]{:S(2)}, u32[]{:S(2)}) %collective-permute-start) | collective-permute-done | bytes 524320 | tf_op jit(solution)/shard_map/ppermute | solution.py:171
  46.2 0.9 %bitcast_add_fusion = f32[4,64,512]{2,1,0:T(8,128)} fusion(f32[4,64,512]{2,1,0:T(8,128)S(1)} %collective-permute-done, f32[4,2,64,512]{3,2,1,0:T(8,128)S(1)} %bitcast.34, s32[]{:T(128)S(6)} %select_n.7), kind=kLoop, calls=%fused_computation.8 | loop fusion | flops 131072 | bytes 1572868 | tf_op jit(solution)/shard_map/add | solution.py:172
  47.1 5.1 %all-to-all-start = ((f32[4,64,512]{2,1,0:T(8,128)}), f32[4,64,512]{2,1,0:T(8,128)S(1)}, u32[]{:S(2)}, u32[]{:S(2)}) async-start(f32[4,64,512]{2,1,0:T(8,128)} %bitcast_add_fusion), calls=%async_computation | async-start | bytes 1048576 | tf_op jit(solution)/shard_map/all_to_all | solution.py:173
  52.2 1.9 %copy.36 = bf16[160,32,64]{0,2,1:T(8,128)(2,1)} copy(bf16[160,32,64]{2,1,0:T(8,128)(2,1)S(1)} %bitcast.30) | data formatting | bytes 1310720
  54.2 0.0 copy-start.5
  54.2 0.0 copy-start.7
  54.2 12.8 %all-to-all-done = f32[4,64,512]{2,1,0:T(8,128)S(1)} async-done(((f32[4,64,512]{2,1,0:T(8,128)}), f32[4,64,512]{2,1,0:T(8,128)S(1)}, u32[]{:S(2)}, u32[]{:S(2)}) %all-to-all-start) | async-done | bytes 524320 | tf_op jit(solution)/shard_map/all_to_all | solution.py:173
  67.2 0.0 copy-done.5
  67.2 0.1 fusion.10
  67.3 0.2 multiply_reduce_fusion
  67.5 0.1 copy.34
  67.6 0.1 copy.35
  67.6 0.1 rsqrt.12
  67.7 0.1 div.9
  67.8 0.0 copy-done
  67.8 0.0 copy-done.7
  67.8 1.1 %fusion.3 = f32[32,8,128]{2,1,0:T(8,128)} fusion(bf16[512,128]{1,0:T(8,128)(2,1)S(1)} %copy-done, bf16[128,512]{1,0:T(8,128)(2,1)S(1)} %copy-done.7, f32[256,128]{1,0:T(8,128)S(1)} %bitcast.39, f32[32,8,128]{2,1,0:T(8,128)S(1)} %copy-done.5, f32[256]{0:T(256)S(1)} %rsqrt.12, f32[256]{0:T(256)S(1)} %div.9), kind=kOutput, calls=%fused_computation.4 | convolution fusion | flops 67567616 | bytes 657408 | tf_op jit(solution)/shard_map/dot_general | solution.py:223
  (9 shorter events, 0.2 us)
Async XLA Ops:
  0.6 67.2 %copy-start = (bf16[512,128]{1,0:T(8,128)(2,1)S(1)}, bf16[512,128]{1,0:T(8,128)(2,1)}, u32[]{:S(2)}) copy-start(bf16[512,128]{1,0:T(8,128)(2,1)} %param.17) | copy-start | bytes 393220
  0.6 2.3 %copy-start.8 = (bf16[256,64]{0,1:T(8,128)(2,1)S(1)}, bf16[256,64]{0,1:T(8,128)(2,1)}, u32[]{:S(2)}) copy-start(bf16[256,64]{0,1:T(8,128)(2,1)} %param.12) | copy-start | bytes 98308
  0.7 2.4 %copy-start.9 = (bf16[64,32]{0,1:T(8,128)(2,1)S(1)}, bf16[64,32]{0,1:T(8,128)(2,1)}, u32[]{:S(2)}) copy-start(bf16[64,32]{0,1:T(8,128)(2,1)} %param.14) | copy-start | bytes 12292
  0.7 2.4 %copy-start.10 = (bf16[64,32]{0,1:T(8,128)(2,1)S(1)}, bf16[64,32]{0,1:T(8,128)(2,1)}, u32[]{:S(2)}) copy-start(bf16[64,32]{0,1:T(8,128)(2,1)} %param.13) | copy-start | bytes 12292
  0.7 2.5 %copy-start.4 = (bf16[64,256]{1,0:T(8,128)(2,1)S(1)}, bf16[64,256]{1,0:T(8,128)(2,1)}, u32[]{:S(2)}) copy-start(bf16[64,256]{1,0:T(8,128)(2,1)} %ww_ref.1) | copy-start | bytes 98308
  15.2 15.7 %copy-start.6 = (f32[1024,128]{1,0:T(8,128)S(1)}, f32[1024,128]{1,0:T(8,128)}, u32[]{:S(2)}) copy-start(f32[1024,128]{1,0:T(8,128)} %param.15) | copy-start | bytes 1572868
  31.7 1.2 %copy-start.1 = (f32[32,32,160]{2,0,1:T(8,128)S(1)}, f32[32,32,160]{2,0,1:T(8,128)}, u32[]{:S(2)}) copy-start(f32[32,32,160]{2,0,1:T(8,128)} %copy.30) | copy-start | bytes 1966084
  32.9 0.9 %copy-start.2 = (bf16[1024,128]{1,0:T(8,128)(2,1)S(1)}, bf16[1024,128]{1,0:T(8,128)(2,1)}, u32[]{:S(2)}) copy-start(bf16[1024,128]{1,0:T(8,128)(2,1)} %get-tuple-element.16.wl_ref) | copy-start | bytes 786436
  33.9 0.9 %copy-start.3 = (bf16[1024,128]{1,0:T(8,128)(2,1)S(1)}, bf16[1024,128]{1,0:T(8,128)(2,1)}, u32[]{:S(2)}) copy-start(bf16[1024,128]{1,0:T(8,128)(2,1)} %get-tuple-element.17.wh_ref) | copy-start | bytes 786436
  44.2 2.0 %collective-permute-start = (f32[4,64,512]{2,1,0:T(8,128)S(1)}, f32[4,64,512]{2,1,0:T(8,128)S(1)}, u32[]{:S(2)}, u32[]{:S(2)}) collective-permute-start(f32[4,64,512]{2,1,0:T(8,128)S(1)} %dynamic-slice_bitcast_fusion), channel_id=1, source_target_pairs={{0,1},{1,0},{2,3},{3,2},{4,5},{5,4},{6,7},{7,6},{8,9},{9,8},{10,11... | collective-permute-start | bytes 1572872 | tf_op jit(solution)/shard_map/ppermute | solution.py:171
  47.1 19.9 %all-to-all-start = ((f32[4,64,512]{2,1,0:T(8,128)}), f32[4,64,512]{2,1,0:T(8,128)S(1)}, u32[]{:S(2)}, u32[]{:S(2)}) async-start(f32[4,64,512]{2,1,0:T(8,128)} %bitcast_add_fusion), calls=%async_computation | async-start | bytes 1048576 | tf_op jit(solution)/shard_map/all_to_all | solution.py:173
  54.2 13.0 %copy-start.5 = (f32[32,8,128]{2,1,0:T(8,128)S(1)}, f32[32,8,128]{2,1,0:T(8,128)}, u32[]{:S(2)}) copy-start(f32[32,8,128]{2,1,0:T(8,128)} %param.10) | copy-start | bytes 393220
  54.2 13.7 %copy-start.7 = (bf16[128,512]{1,0:T(8,128)(2,1)S(1)}, bf16[128,512]{1,0:T(8,128)(2,1)}, u32[]{:S(2)}) copy-start(bf16[128,512]{1,0:T(8,128)(2,1)} %param.16) | copy-start | bytes 393220

commit v3 on v1

--- a/solution.py
+++ b/solution.py
@@ -117,8 +117,15 @@
     other = lax.dynamic_index_in_dim(xs, 1 - c, axis=1, keepdims=False)
     received = lax.ppermute(other, "chan", [(0, 1), (1, 0)])
     part = mine + received
-    gathered = lax.all_to_all(part, "seq", 0, 0, tiled=False)
-    return gathered.sum(axis=0)
+    if nseq > 4:
+        gathered = lax.all_to_all(part, "seq", 0, 0, tiled=False)
+        return gathered.sum(axis=0)
+    me = lax.axis_index("seq")
+    acc = lax.dynamic_index_in_dim(part, me, axis=0, keepdims=False)
+    for k in range(1, nseq):
+        src = lax.dynamic_index_in_dim(part, (me + k) % nseq, axis=0, keepdims=False)
+        acc = acc + lax.ppermute(src, "seq", [(q, (q + k) % nseq) for q in range(nseq)])
+    return acc
 
 
 def per_device(
@@ -165,11 +172,21 @@
     block_cols = coupling_embedding.shape[1]
 
     lt = jnp.transpose(left_features, (2, 1, 0)).reshape(proj_width * sites_local_share, homologs_local_share)
-    r_all = lax.all_gather(right_features, "res", axis=1, tiled=True)
     w_hi_f32 = lax.reduce_precision(moment_coupling_weights, exponent_bits=8, mantissa_bits=7)
     w_hi = w_hi_f32.astype(jnp.bfloat16)
     w_lo = (moment_coupling_weights - w_hi_f32).astype(jnp.bfloat16)
-    partial_value = outer_project(lt, r_all, w_hi, w_lo, 1.0 / depth_total)
+    nres = lax.axis_size("res")
+    if nres == 2:
+        r_other = lax.ppermute(right_features, "res", [(0, 1), (1, 0)])
+        p_own = outer_project(lt, right_features, w_hi, w_lo, 1.0 / depth_total)
+        p_other = outer_project(lt, r_other, w_hi, w_lo, 1.0 / depth_total)
+        first = lax.axis_index("res") == 0
+        partial_value = jnp.where(
+            first, jnp.concatenate([p_own, p_other], axis=0), jnp.concatenate([p_other, p_own], axis=0)
+        )
+    else:
+        r_all = lax.all_gather(right_features, "res", axis=1, tiled=True)
+        partial_value = outer_project(lt, r_all, w_hi, w_lo, 1.0 / depth_total)
     pair_update = reduce_over_sequences(partial_value)
     nja_local = block_cols // JB
     pair_update = (

time: 60.8 us -> 47.2 us (0.78)
  blocking collectives: 11.5 us -> 0 us
  waiting for transfers between devices: 14 us -> 6.73 us
  starting transfers between devices: 5.2 us -> 8.63 us
  Pallas kernels: 8.01 us -> 9.72 us
  other arithmetic: 4.51 us -> 3.84 us
    all_to_all x1 -> x0, waiting for transfers between devices: 12.1 us -> none  [reduce_over_sequences(): gathered = lax.all_to_all(part, 'seq', 0, 0, tiled=False)]
    all_gather x1 -> x0, blocking collectives: 11.5 us -> none  [per_device(): r_all = lax.all_gather(right_features, 'res', axis=1, tiled=True)]
    ppermute x0 -> x4, starting transfers between devices: none -> 8.56 us  [the longest x3 5.56 us: reduce_over_sequences(): lax.ppermute(src, 'seq', [(q, (q + k) % nseq) for q in range(nseq)])]
    all_to_all x1 -> x0, starting transfers between devices: 5.13 us -> none  [reduce_over_sequences(): gathered = lax.all_to_all(part, 'seq', 0, 0, tiled=False)]
    ppermute x0 -> x4, waiting for transfers between devices: none -> 4.87 us  [the longest x3 4.87 us: reduce_over_sequences(): lax.ppermute(src, 'seq', [(q, (q + k) % nseq) for q in range(nseq)])]
    pallas_call x1 -> x2, Pallas kernels: 8.01 us -> 9.72 us  [outer_project(): pl.pallas_call(functools.partial(outer_project_kernel, scale), grid=(step...]
    add x1, other arithmetic: 0.87 us -> 0.08 us  [reduce_over_sequences(): part = mine + received]
  transfers between devices with their start and end apart: 2 -> 5, of which waited for: 2 -> 2; matrix products, arithmetic and copies ran while one was open for 4% -> 13% of each run, Pallas kernels for 0% -> 10%
where the time goes in v3:
time: 47.2 us; the launch traced here: 46.5 us
  local copies, waits for them, and re-layouts  11.8 us (25%)
  Pallas kernels  9.72 us (21%)
  starting transfers between devices  8.63 us (18%)
  waiting for transfers between devices  6.73 us (14%)
  matrix products  4.73 us (10%)
  other arithmetic  3.84 us (8%)
  between operations  1.05 us (2%)
    pallas_call x2, Pallas kernels, outer_project(): pl.pallas_call(functools.partial(outer_project_kernel, scale), grid=(step...  9.72 us
    ppermute x3, starting transfers between devices, reduce_over_sequences(): lax.ppermute(src, 'seq', [(q, (q + k) % nseq) for q in range(nseq)])  5.56 us
    ppermute x3, waiting for transfers between devices, reduce_over_sequences(): lax.ppermute(src, 'seq', [(q, (q + k) % nseq) for q in range(nseq)])  4.87 us
    convert_element_type x2, local copies, waits for them, and re-layouts, per_device(): cross_moment_average.astype(jnp.float32)  4.25 us
    dot_general x1, matrix products, per_device(): jnp.dot(homolog_inner_state, homolog_shrink_weights, preferred_element_ty...  3.09 us
    ppermute x1, starting transfers between devices, per_device(): r_other = lax.ppermute(right_features, 'res', [(0, 1), (1, 0)])  3 us
    unnamed x17, local copies, waits for them, and re-layouts  2.02 us
    ppermute x1, waiting for transfers between devices, reduce_over_sequences(): received = lax.ppermute(other, 'chan', [(0, 1), (1, 0)])  1.85 us
  transfers between devices with their start and end apart: 5, of which 2 were waited for; matrix products, arithmetic and copies ran while one was open for 13% of the time, Pallas kernels for 10%

profile of v3, /device:TPU:0, one launch (start us, length us, event | category | flops | bytes accessed | tf_op | source)
XLA Modules:
  0.0 46.5 jit_solution(12801271757715993118)
XLA Ops:
  0.6 0.0 copy-start
  0.6 2.4 %copy.34 = f32[160,32,64]{2,1,0:T(8,128)S(1)} copy(bf16[160,32,64]{0,2,1:T(8,128)(2,1)} %param.9) | data formatting | bytes 1966080 | tf_op jit(solution)/shard_map/convert_element_type | solution.py:156
  3.1 0.0 copy-start.1
  3.1 1.5 %convert_reduce_fusion.1 = f32[160,32]{0,1:T(8,128)S(1)} fusion(bf16[160,32,64]{0,2,1:T(8,128)(2,1)} %param.9), kind=kLoop, calls=%fused_computation.22 | loop fusion | flops 650240 | bytes 675840 | tf_op jit(solution)/shard_map/reduce_sum | solution.py:12
  4.6 0.0 copy-done.1
  4.6 0.4 multiply_reduce_fusion
  5.0 0.1 copy.35
  5.1 0.0 copy-start.4
  5.2 0.0 copy-start.5
  5.2 1.8 %copy.37 = f32[5120,64]{0,1:T(8,128)} copy(f32[5120,64]{1,0:T(8,128)S(1)} %bitcast.45) | data formatting | bytes 2621440 | tf_op jit(solution)/shard_map/convert_element_type | solution.py:156
  7.0 0.1 copy.36
  7.1 0.1 rsqrt.31
  7.2 0.1 div.23
  7.3 0.0 copy-start.6
  7.3 3.1 %convert_reduce_fusion = (f32[5120]{0:T(1024)S(1)}, bf16[5120,64]{0,1:T(8,128)(2,1)S(1)}) fusion(f32[5120,64]{0,1:T(8,128)} %copy.37, bf16[256,64]{0,1:T(8,128)(2,1)S(1)} %copy-done.4, bf16[64,256]{1,0:T(8,128)(2,1)S(1)} %copy-done.5, f32[5120,64]{1,0:T(8,128)S(1)} %bitcast.46, f32[5120]{0:T(1024)S(1)} %rsqrt.31, f32[5120]{0:T(1024)S(1)} %div.23), kind=kOutput, calls=%fused_computation.9 | convolution fusion | flops 340454400 | bytes 3403776 | tf_op jit(solution)/shard_map/dot_general | solution.py:157
  10.4 0.2 fusion.4
  10.7 0.3 convolution_convert_fusion
  11.0 0.0 copy-start.7
  11.0 0.7 %copy.40 = bf16[5120,32]{1,0:T(8,128)(2,1)S(1)} copy(bf16[5120,32]{0,1:T(8,128)(2,1)S(1)} %convolution_convert_fusion) | data formatting | bytes 655360 | tf_op jit(solution)/shard_map/convert_element_type | solution.py:167
  11.7 1.4 %reshape.120.r_ref = bf16[160,1024]{1,0:T(8,128)(2,1)S(1)} reshape(bf16[5120,32]{1,0:T(8,128)(2,1)S(1)} %copy.40) | data formatting | bytes 655360 | tf_op jit(solution)/shard_map/reshape | solution.py:168
  13.1 3.0 %collective-permute-start = (bf16[160,1024]{1,0:T(8,128)(2,1)S(1)}, bf16[160,1024]{1,0:T(8,128)(2,1)S(1)}, u32[]{:S(2)}, u32[]{:S(2)}) collective-permute-start(bf16[160,1024]{1,0:T(8,128)(2,1)S(1)} %reshape.120.r_ref), channel_id=1, source_target_pairs={{0,2},{2,0},{1,3},{3,1},{4,6},{6,4},{5,7},{7,5},{8,10},{10,8},{9,1... | collective-permute-start | bytes 983048 | tf_op jit(solution)/shard_map/ppermute | solution.py:180
  16.1 0.3 convolution_convert_fusion.1
  16.4 1.0 %reshape.118 = bf16[160,32,32]{1,0,2:T(8,128)(2,1)S(1)} reshape(bf16[5120,32]{0,1:T(8,128)(2,1)S(1)} %convolution_convert_fusion.1) | data formatting | bytes 655360 | tf_op jit(solution)/shard_map/reshape | solution.py:163
  17.4 0.9 %copy.39 = bf16[32,32,160]{2,1,0:T(8,128)(2,1)S(1)} copy(bf16[32,32,160]{1,2,0:T(8,128)(2,1)S(1)} %bitcast.47) | data formatting | bytes 655360 | tf_op jit(solution)/shard_map/transpose | solution.py:174
  18.3 1.1 %fusion.14 = (bf16[1024,128]{1,0:T(8,128)(2,1)S(1)}, bf16[1024,128]{1,0:T(8,128)(2,1)S(1)}) fusion(f32[1024,128]{1,0:T(8,128)} %param.15), kind=kLoop, calls=%fused_computation.25 | loop fusion | flops 524288 | bytes 1048576 | tf_op jit(solution)/shard_map/convert_element_type | solution.py:177
  19.4 4.9 %shard_map.104 = f32[256,512]{1,0:T(8,128)S(1)} custom-call(bf16[1024,160]{1,0:T(8,128)(2,1)S(1)} %bitcast.43, bf16[160,1024]{1,0:T(8,128)(2,1)S(1)} %reshape.120.r_ref, bf16[1024,128]{1,0:T(8,128)(2,1)S(1)} %get-tuple-element.14.wh_ref, bf16[1024,128]{1,0:T(8,128)(2,1)S(1)} %get-tuple-element.13.wl_ref), custom_call_target="tpu_custom_call" | custom-call | flops 3556769792 | bytes 1703936 | tf_op jit(solution)/shard_map/pallas_call | solution.py:81
  24.3 0.0 collective-permute-done.r_ref
  24.3 4.9 %shard_map.105 = f32[256,512]{1,0:T(8,128)S(1)} custom-call(bf16[1024,160]{1,0:T(8,128)(2,1)S(1)} %bitcast.44, bf16[160,1024]{1,0:T(8,128)(2,1)S(1)} %collective-permute-done.r_ref, bf16[1024,128]{1,0:T(8,128)(2,1)S(1)} %get-tuple-element.14.wh_ref, bf16[1024,128]{1,0:T(8,128)(2,1)S(1)} %get-tuple-element.13.wl_ref), custom_call_target="tpu_custom_call" | custom-call | flops 3556769792 | bytes 1703936 | tf_op jit(solution)/shard_map/pallas_call | solution.py:81
  29.2 0.1 maximum_select_fusion
  29.4 0.1 collective-permute-start.1
  29.5 1.9 %collective-permute-done.1 = f32[4,64,512]{2,1,0:T(8,128)S(1)} collective-permute-done((f32[4,64,512]{2,1,0:T(8,128)S(1)}, f32[4,64,512]{2,1,0:T(8,128)S(1)}, u32[]{:S(2)}, u32[]{:S(2)}) %collective-permute-start.1) | collective-permute-done | bytes 524320 | tf_op jit(solution)/shard_map/ppermute | solution.py:118
  31.3 0.1 bitcast_add_fusion
  31.5 1.6 %collective-permute-start.2 = (f32[64,512]{1,0:T(8,128)S(1)}, f32[64,512]{1,0:T(8,128)S(1)}, u32[]{:S(2)}, u32[]{:S(2)}) collective-permute-start(f32[64,512]{1,0:T(8,128)S(1)} %get-tuple-element.10), channel_id=1, source_target_pairs={{0,4},{4,8},{8,12},{12,0},{1,5},{5,9},{9,13},{13,1},{2,6},{6,10},{... | collective-permute-start | bytes 393224 | tf_op jit(solution)/shard_map/ppermute | solution.py:127
  33.1 2.6 %collective-permute-start.3 = (f32[64,512]{1,0:T(8,128)S(1)}, f32[64,512]{1,0:T(8,128)S(1)}, u32[]{:S(2)}, u32[]{:S(2)}) collective-permute-start(f32[64,512]{1,0:T(8,128)S(1)} %get-tuple-element.12), channel_id=1, source_target_pairs={{0,8},{4,12},{8,0},{12,4},{1,9},{5,13},{9,1},{13,5},{2,10},{6,14},... | collective-permute-start | bytes 393224 | tf_op jit(solution)/shard_map/ppermute | solution.py:127
  35.7 1.3 %collective-permute-start.4 = (f32[64,512]{1,0:T(8,128)S(1)}, f32[64,512]{1,0:T(8,128)S(1)}, u32[]{:S(2)}, u32[]{:S(2)}) collective-permute-start(f32[64,512]{1,0:T(8,128)S(1)} %get-tuple-element.11), channel_id=1, source_target_pairs={{0,12},{4,0},{8,4},{12,8},{1,13},{5,1},{9,5},{13,9},{2,14},{6,2},{... | collective-permute-start | bytes 393224 | tf_op jit(solution)/shard_map/ppermute | solution.py:127
  37.0 0.7 %copy.38 = bf16[5120,64]{1,0:T(8,128)(2,1)S(1)} copy(bf16[5120,64]{0,1:T(8,128)(2,1)S(1)} %get-tuple-element.16) | data formatting | bytes 1310720 | tf_op jit(solution)/shard_map/convert_element_type | solution.py:158
  37.8 0.0 copy-start.2
  37.8 2.0 %copy.46 = bf16[160,32,64]{0,2,1:T(8,128)(2,1)} copy(bf16[160,32,64]{2,1,0:T(8,128)(2,1)S(1)} %bitcast.48) | data formatting | bytes 1310720
  39.8 0.0 collective-permute-done.2
  39.8 4.9 %collective-permute-done.3 = f32[64,512]{1,0:T(8,128)S(1)} collective-permute-done((f32[64,512]{1,0:T(8,128)S(1)}, f32[64,512]{1,0:T(8,128)S(1)}, u32[]{:S(2)}, u32[]{:S(2)}) %collective-permute-start.3) | collective-permute-done | bytes 131104 | tf_op jit(solution)/shard_map/ppermute | solution.py:127
  44.6 0.0 collective-permute-done.4
  44.7 0.1 fusion.24
  44.9 0.2 multiply_reduce_fusion.1
  45.1 0.1 copy.44
  45.2 0.1 copy.45
  45.3 0.1 rsqrt.34
  45.3 0.1 div.28
  45.5 1.1 %fusion.13 = f32[32,8,128]{2,1,0:T(8,128)} fusion(bf16[512,128]{1,0:T(8,128)(2,1)S(1)} %copy-done, bf16[128,512]{1,0:T(8,128)(2,1)S(1)} %copy-done.3, f32[256,128]{1,0:T(8,128)S(1)} %bitcast.55, f32[32,8,128]{2,1,0:T(8,128)S(1)} %copy-done.2, f32[256]{0:T(256)S(1)} %rsqrt.34, f32[256]{0:T(256)S(1)} %div.28), kind=kOutput, calls=%fused_computation.20 | convolution fusion | flops 67567616 | bytes 657408 | tf_op jit(solution)/shard_map/dot_general | solution.py:202
  (20 shorter events, 0.3 us)
Async XLA Ops:
  0.6 44.8 %copy-start = (bf16[512,128]{1,0:T(8,128)(2,1)S(1)}, bf16[512,128]{1,0:T(8,128)(2,1)}, u32[]{:S(2)}) copy-start(bf16[512,128]{1,0:T(8,128)(2,1)} %param.17) | copy-start | bytes 393220
  3.1 1.6 %copy-start.1 = (bf16[160,32,64]{0,2,1:T(8,128)(2,1)S(1)}, bf16[160,32,64]{0,2,1:T(8,128)(2,1)}, u32[]{:S(2)}) copy-start(bf16[160,32,64]{0,2,1:T(8,128)(2,1)} %param.9) | copy-start | bytes 1966084
  5.1 2.1 %copy-start.4 = (bf16[256,64]{0,1:T(8,128)(2,1)S(1)}, bf16[256,64]{0,1:T(8,128)(2,1)}, u32[]{:S(2)}) copy-start(bf16[256,64]{0,1:T(8,128)(2,1)} %param.12) | copy-start | bytes 98308
  5.2 2.1 %copy-start.5 = (bf16[64,256]{1,0:T(8,128)(2,1)S(1)}, bf16[64,256]{1,0:T(8,128)(2,1)}, u32[]{:S(2)}) copy-start(bf16[64,256]{1,0:T(8,128)(2,1)} %param.11) | copy-start | bytes 98308
  7.3 3.4 %copy-start.6 = (bf16[64,32]{0,1:T(8,128)(2,1)S(1)}, bf16[64,32]{0,1:T(8,128)(2,1)}, u32[]{:S(2)}) copy-start(bf16[64,32]{0,1:T(8,128)(2,1)} %param.14) | copy-start | bytes 12292
  11.0 5.1 %copy-start.7 = (bf16[64,32]{0,1:T(8,128)(2,1)S(1)}, bf16[64,32]{0,1:T(8,128)(2,1)}, u32[]{:S(2)}) copy-start(bf16[64,32]{0,1:T(8,128)(2,1)} %param.13) | copy-start | bytes 12292
  13.1 11.2 %collective-permute-start = (bf16[160,1024]{1,0:T(8,128)(2,1)S(1)}, bf16[160,1024]{1,0:T(8,128)(2,1)S(1)}, u32[]{:S(2)}, u32[]{:S(2)}) collective-permute-start(bf16[160,1024]{1,0:T(8,128)(2,1)S(1)} %reshape.120.r_ref), channel_id=1, source_target_pairs={{0,2},{2,0},{1,3},{3,1},{4,6},{6,4},{5,7},{7,5},{8,10},{10,8},{9,1... | collective-permute-start | bytes 983048 | tf_op jit(solution)/shard_map/ppermute | solution.py:180
  29.4 2.0 %collective-permute-start.1 = (f32[4,64,512]{2,1,0:T(8,128)S(1)}, f32[4,64,512]{2,1,0:T(8,128)S(1)}, u32[]{:S(2)}, u32[]{:S(2)}) collective-permute-start(f32[4,64,512]{2,1,0:T(8,128)S(1)} %dynamic-slice_bitcast_fusion), channel_id=1, source_target_pairs={{0,1},{1,0},{2,3},{3,2},{4,5},{5,4},{6,7},{7,6},{8,9},{9,8},{10,11... | collective-permute-start | bytes 1572872 | tf_op jit(solution)/shard_map/ppermute | solution.py:118
  31.5 8.3 %collective-permute-start.2 = (f32[64,512]{1,0:T(8,128)S(1)}, f32[64,512]{1,0:T(8,128)S(1)}, u32[]{:S(2)}, u32[]{:S(2)}) collective-permute-start(f32[64,512]{1,0:T(8,128)S(1)} %get-tuple-element.10), channel_id=1, source_target_pairs={{0,4},{4,8},{8,12},{12,0},{1,5},{5,9},{9,13},{13,1},{2,6},{6,10},{... | collective-permute-start | bytes 393224 | tf_op jit(solution)/shard_map/ppermute | solution.py:127
  33.1 11.5 %collective-permute-start.3 = (f32[64,512]{1,0:T(8,128)S(1)}, f32[64,512]{1,0:T(8,128)S(1)}, u32[]{:S(2)}, u32[]{:S(2)}) collective-permute-start(f32[64,512]{1,0:T(8,128)S(1)} %get-tuple-element.12), channel_id=1, source_target_pairs={{0,8},{4,12},{8,0},{12,4},{1,9},{5,13},{9,1},{13,5},{2,10},{6,14},... | collective-permute-start | bytes 393224 | tf_op jit(solution)/shard_map/ppermute | solution.py:127
  35.7 8.9 %collective-permute-start.4 = (f32[64,512]{1,0:T(8,128)S(1)}, f32[64,512]{1,0:T(8,128)S(1)}, u32[]{:S(2)}, u32[]{:S(2)}) collective-permute-start(f32[64,512]{1,0:T(8,128)S(1)} %get-tuple-element.11), channel_id=1, source_target_pairs={{0,12},{4,0},{8,4},{12,8},{1,13},{5,1},{9,5},{13,9},{2,14},{6,2},{... | collective-permute-start | bytes 393224 | tf_op jit(solution)/shard_map/ppermute | solution.py:127
  37.8 7.0 %copy-start.2 = (f32[32,8,128]{2,1,0:T(8,128)S(1)}, f32[32,8,128]{2,1,0:T(8,128)}, u32[]{:S(2)}) copy-start(f32[32,8,128]{2,1,0:T(8,128)} %param.10) | copy-start | bytes 393220
  39.7 5.7 %copy-start.3 = (bf16[128,512]{1,0:T(8,128)(2,1)S(1)}, bf16[128,512]{1,0:T(8,128)(2,1)}, u32[]{:S(2)}) copy-start(bf16[128,512]{1,0:T(8,128)(2,1)} %param.16) | copy-start | bytes 393220

commit v4 on v3

--- a/solution.py
+++ b/solution.py
@@ -104,6 +104,58 @@
     )(lt, r_all, wh, wl)
 
 
+def norm_over_rows(values):
+    mean = jnp.mean(values, axis=0, keepdims=True)
+    centred = values - mean
+    variance = jnp.mean(centred * centred, axis=0, keepdims=True)
+    return centred * lax.rsqrt(variance + 1e-05)
+
+
+def msa_kernel(x_ref, wwt_ref, wst_ref, pt_ref, o_ref, lt_ref, rt_ref):
+    sites = x_ref.shape[0]
+    width = pt_ref.shape[0] // 2
+    wwt = wwt_ref[...]
+    wst = wst_ref[...]
+    pt = pt_ref[...]
+
+    def body(i, carry):
+        x = x_ref[i].astype(jnp.float32)
+        n1 = norm_over_rows(x).astype(jnp.bfloat16)
+        hidden = jnp.maximum(jnp.dot(wwt, n1, preferred_element_type=jnp.float32), 0.0).astype(jnp.bfloat16)
+        refreshed = (x + jnp.dot(wst, hidden, preferred_element_type=jnp.float32)).astype(jnp.bfloat16)
+        o_ref[i] = refreshed
+        n2 = norm_over_rows(refreshed.astype(jnp.float32)).astype(jnp.bfloat16)
+        proj = jnp.dot(pt, n2, preferred_element_type=jnp.float32)
+        start = pl.multiple_of(i * width, width)
+        lt_ref[pl.ds(start, width), :] = proj[:width]
+        rt_ref[pl.ds(start, width), :] = proj[width:].astype(jnp.bfloat16)
+        return carry
+
+    lax.fori_loop(0, sites, body, 0, unroll=2)
+
+
+def msa_block(xt, wwt, wst, pt):
+    sites, k, depth = xt.shape
+    width = pt.shape[0] // 2
+    hidden = wwt.shape[0]
+    return pl.pallas_call(
+        msa_kernel,
+        out_shape=(
+            jax.ShapeDtypeStruct(xt.shape, jnp.bfloat16),
+            jax.ShapeDtypeStruct((sites * width, depth), jnp.float32),
+            jax.ShapeDtypeStruct((sites * width, depth), jnp.bfloat16),
+        ),
+        in_specs=[pl.BlockSpec(memory_space=pltpu.VMEM)] * 4,
+        out_specs=(pl.BlockSpec(memory_space=pltpu.VMEM),) * 3,
+        compiler_params=pltpu.CompilerParams(vmem_limit_bytes=32 * 1024 * 1024),
+        cost_estimate=pl.CostEstimate(
+            flops=2 * sites * depth * k * (2 * hidden + 2 * width),
+            transcendentals=2 * sites * depth,
+            bytes_accessed=sites * depth * (k * 4 + width * 6),
+        ),
+    )(xt, wwt, wst, pt)
+
+
 def reduce_over_sequences(partial_value):
     nseq = lax.axis_size("seq")
     nchan = lax.axis_size("chan")
@@ -142,36 +194,20 @@
     homologs_local_share, sites_local_share, homolog_lane_number = homolog_embedding.shape
     proj_width = lhs_projector.shape[1]
     pair_width = coupling_embedding.shape[2]
-    cross_moment_average = homolog_embedding.reshape(
-        homologs_local_share * sites_local_share, homolog_lane_number
-    )
-    homolog_standardized = apply_layer_norm(cross_moment_average.astype(jnp.float32)).astype(
-        jnp.bfloat16
-    )
-    homolog_inner_state = jnp.maximum(
-        jnp.dot(homolog_standardized, homolog_widen_weights, preferred_element_type=jnp.float32),
-        0.0,
-    ).astype(jnp.bfloat16)
-    homolog_refreshed = (
-        cross_moment_average.astype(jnp.float32)
-        + jnp.dot(homolog_inner_state, homolog_shrink_weights, preferred_element_type=jnp.float32)
-    ).astype(jnp.bfloat16)
-    alignment_normed2 = apply_layer_norm(homolog_refreshed.astype(jnp.float32)).astype(jnp.bfloat16)
-    left_features = (
-        jnp.dot(alignment_normed2, lhs_projector, preferred_element_type=jnp.float32)
-        .astype(jnp.bfloat16)
-        .reshape(homologs_local_share, sites_local_share, proj_width)
-    )
-    right_features = (
-        jnp.dot(alignment_normed2, rhs_projector, preferred_element_type=jnp.float32)
-        .astype(jnp.bfloat16)
-        .reshape(homologs_local_share, sites_local_share * proj_width)
-    )
+    xt = jnp.transpose(homolog_embedding, (1, 2, 0))
+    pt = jnp.concatenate([lhs_projector, rhs_projector], axis=1).T
+    refreshed_t, left_t, right_t = msa_block(xt, homolog_widen_weights.T, homolog_shrink_weights.T, pt)
+    homolog_refreshed = jnp.transpose(refreshed_t, (2, 0, 1))
+    lt = (
+        left_t.reshape(sites_local_share, proj_width, homologs_local_share)
+        .transpose(1, 0, 2)
+        .reshape(proj_width * sites_local_share, homologs_local_share)
+    )
+    right_features = right_t.T
     owners = lax.axis_size(("seq", "chan"))
     depth_total = float(homologs_local_share * owners)
     block_cols = coupling_embedding.shape[1]
 
-    lt = jnp.transpose(left_features, (2, 1, 0)).reshape(proj_width * sites_local_share, homologs_local_share)
     w_hi_f32 = lax.reduce_precision(moment_coupling_weights, exponent_bits=8, mantissa_bits=7)
     w_hi = w_hi_f32.astype(jnp.bfloat16)
     w_lo = (moment_coupling_weights - w_hi_f32).astype(jnp.bfloat16)
@@ -203,7 +239,7 @@
         pair_hidden, coupling_shrink_weights, preferred_element_type=jnp.float32
     )
     return (
-        homolog_refreshed.reshape(homologs_local_share, sites_local_share, homolog_lane_number),
+        homolog_refreshed,
         coupling_refreshed.reshape(sites_local_share, block_cols, pair_width),
     )
 

time: 47.2 us -> 56.3 us (1.19)
  Pallas kernels: 9.72 us -> 25.4 us
  waiting for transfers between devices: 6.73 us -> 14.2 us
  local copies, waits for them, and re-layouts: 11.8 us -> 5.84 us
  matrix products: 4.73 us -> 1.06 us
  other arithmetic: 3.84 us -> 0.63 us
  starting transfers between devices: 8.63 us -> 7.98 us
    pallas_call x0 -> x1, Pallas kernels: none -> 15.6 us  [msa_block(): pl.pallas_call(msa_kernel, out_shape=(jax.ShapeDtypeStruct(xt.shape, jnp....]
    ppermute x3, waiting for transfers between devices: 4.87 us -> 10.7 us  [reduce_over_sequences(): lax.ppermute(src, 'seq', [(q, (q + k) % nseq) for q in range(nseq)])]
    convert_element_type x4 -> x0, local copies, waits for them, and re-layouts: 5.71 us -> none  [the longest x2 4.25 us: per_device(): cross_moment_average.astype(jnp.float32)]
    dot_general x3 -> x0, matrix products: 3.66 us -> none  [the longest x1 3.09 us: per_device(): jnp.dot(homolog_inner_state, homolog_shrink_weights, preferred_element_ty...]
    unnamed x17, local copies, waits for them, and re-layouts: 2.02 us -> 4.55 us
    reshape x2 -> x1, local copies, waits for them, and re-layouts: 2.34 us -> 0.61 us  [per_device(): left_t.reshape(sites_local_share, proj_width, homologs_local_share)]
    ppermute x1, waiting for transfers between devices: 0.01 us -> 1.68 us  [per_device(): r_other = lax.ppermute(right_features, 'res', [(0, 1), (1, 0)])]
    reduce_sum x2 -> x1, other arithmetic: 1.65 us -> 0.11 us  [apply_layer_norm(): mean = jnp.mean(values, axis=-1, keepdims=True)]
  transfers between devices with their start and end apart: 5 -> 5, of which waited for: 2 -> 4; matrix products, arithmetic and copies ran while one was open for 13% -> 1% of each run, Pallas kernels for 10% -> 9%
where the time goes in v4:
time: 56.3 us; the launch traced here: 56 us
  Pallas kernels  25.4 us (45%)
  waiting for transfers between devices  14.2 us (25%)
  starting transfers between devices  7.98 us (14%)
  local copies, waits for them, and re-layouts  5.84 us (10%)
  matrix products  1.06 us (2%)
  between operations  0.89 us (2%)
  other arithmetic  0.63 us (1%)
    pallas_call x1, Pallas kernels, msa_block(): pl.pallas_call(msa_kernel, out_shape=(jax.ShapeDtypeStruct(xt.shape, jnp....  15.6 us
    ppermute x3, waiting for transfers between devices, reduce_over_sequences(): lax.ppermute(src, 'seq', [(q, (q + k) % nseq) for q in range(nseq)])  10.7 us
    pallas_call x2, Pallas kernels, outer_project(): pl.pallas_call(functools.partial(outer_project_kernel, scale), grid=(step...  9.77 us
    ppermute x3, starting transfers between devices, reduce_over_sequences(): lax.ppermute(src, 'seq', [(q, (q + k) % nseq) for q in range(nseq)])  4.91 us
    unnamed x17, local copies, waits for them, and re-layouts  4.55 us
    ppermute x1, starting transfers between devices, per_device(): r_other = lax.ppermute(right_features, 'res', [(0, 1), (1, 0)])  3 us
    ppermute x1, waiting for transfers between devices, reduce_over_sequences(): received = lax.ppermute(other, 'chan', [(0, 1), (1, 0)])  1.85 us
    ppermute x1, waiting for transfers between devices, per_device(): r_other = lax.ppermute(right_features, 'res', [(0, 1), (1, 0)])  1.68 us
  transfers between devices with their start and end apart: 5, of which 4 were waited for; matrix products, arithmetic and copies ran while one was open for 1% of the time, Pallas kernels for 9%

profile of v4, /device:TPU:0, one launch (start us, length us, event | category | flops | bytes accessed | tf_op | source)
XLA Modules:
  0.0 56.0 jit_solution(6631096288760197881)
XLA Ops:
  0.6 0.0 copy-start
  0.6 0.0 copy-start.6
  0.7 0.0 copy-start.7
  0.7 0.9 %copy.25 = bf16[64,256]{0,1:T(8,128)(2,1)S(1)} copy(bf16[64,256]{1,0:T(8,128)(2,1)} %param.11) | data formatting | bytes 65536 | tf_op args[2]
  1.6 0.0 copy-done.6
  1.6 0.0 copy-done.7
  1.6 0.0 copy-start.2
  1.6 0.7 %copy-done.2 = bf16[256,64]{0,1:T(8,128)(2,1)S(1)} copy-done((bf16[256,64]{0,1:T(8,128)(2,1)S(1)}, bf16[256,64]{0,1:T(8,128)(2,1)}, u32[]{:S(2)}) %copy-start.2) | copy-done | bytes 32792
  2.4 0.0 copy-start.1
  2.4 1.2 %copy-done.1 = bf16[160,32,64]{0,2,1:T(8,128)(2,1)S(1)} copy-done((bf16[160,32,64]{0,2,1:T(8,128)(2,1)S(1)}, bf16[160,32,64]{0,2,1:T(8,128)(2,1)}, u32[]{:S(2)}) %copy-start.1) | copy-done | bytes 655384
  3.6 15.6 %shard_map.104 = (bf16[32,64,160]{2,1,0:T(8,128)(2,1)}, f32[1024,160]{1,0:T(8,128)S(1)}, bf16[1024,160]{1,0:T(8,128)(2,1)S(1)}) custom-call(bf16[32,64,160]{2,1,0:T(8,128)(2,1)S(1)} %bitcast.50, bf16[256,64]{1,0:T(8,128)(2,1)S(1)} %bitcast.49, bf16[64,256]{1,0:T(8,128)(2,1)S(1)} %bitcast.51, bf16[64,64]{1,0:T(8,128)(2,1)S(1)} %maximum_bitcast_fusion.pt_ref), custom_call_target="tpu_custom_call" | custom-call | flops 377487360 | bytes 2293760 | tf_op jit(solution)/shard_map/pallas_call | solution.py:141
  19.2 0.2 copy.27
  19.3 3.0 %collective-permute-start = (bf16[160,1024]{1,0:T(8,128)(2,1)S(1)}, bf16[160,1024]{1,0:T(8,128)(2,1)S(1)}, u32[]{:S(2)}, u32[]{:S(2)}) collective-permute-start(bf16[160,1024]{1,0:T(8,128)(2,1)S(1)} %bitcast.47), channel_id=1, source_target_pairs={{0,2},{2,0},{1,3},{3,1},{4,6},{6,4},{5,7},{7,5},{8,10},{10,8},{9,1... | collective-permute-start | bytes 983048 | tf_op jit(solution)/shard_map/ppermute | solution.py:216
  22.3 0.0 copy-start.4
  22.3 0.6 %copy.26 = f32[32,32,160]{2,0,1:T(8,128)S(1)} copy(f32[32,32,160]{2,1,0:T(8,128)S(1)} %bitcast.46) | data formatting | bytes 1310720 | tf_op jit(solution)/shard_map/reshape | solution.py:202
  23.0 0.4 copy-done.4
  23.4 0.1 fusion.4
  23.5 4.9 %shard_map.105 = f32[256,512]{1,0:T(8,128)S(1)} custom-call(f32[1024,160]{1,0:T(8,128)S(1)} %bitcast.44, bf16[160,1024]{1,0:T(8,128)(2,1)S(1)} %bitcast.48, bf16[1024,128]{1,0:T(8,128)(2,1)S(1)} %get-tuple-element.12.wh_ref, bf16[1024,128]{1,0:T(8,128)(2,1)S(1)} %get-tuple-element.11.wl_ref), custom_call_target="tpu_custom_call" | custom-call | flops 3556769792 | bytes 1703936 | tf_op jit(solution)/shard_map/pallas_call | solution.py:81
  28.4 1.7 %collective-permute-done.r_ref = bf16[160,1024]{1,0:T(8,128)(2,1)S(1)} collective-permute-done((bf16[160,1024]{1,0:T(8,128)(2,1)S(1)}, bf16[160,1024]{1,0:T(8,128)(2,1)S(1)}, u32[]{:S(2)}, u32[]{:S(2)}) %collective-permute-start) | collective-permute-done | bytes 327712 | tf_op jit(solution)/shard_map/ppermute | solution.py:216
  30.1 4.9 %shard_map.106 = f32[256,512]{1,0:T(8,128)S(1)} custom-call(f32[1024,160]{1,0:T(8,128)S(1)} %bitcast.45, bf16[160,1024]{1,0:T(8,128)(2,1)S(1)} %collective-permute-done.r_ref, bf16[1024,128]{1,0:T(8,128)(2,1)S(1)} %get-tuple-element.12.wh_ref, bf16[1024,128]{1,0:T(8,128)(2,1)S(1)} %get-tuple-element.11.wl_ref), custom_call_target="tpu_custom_call" | custom-call | flops 3556769792 | bytes 1703936 | tf_op jit(solution)/shard_map/pallas_call | solution.py:81
  34.9 0.1 maximum_select_fusion
  35.1 0.1 collective-permute-start.1
  35.3 1.9 %collective-permute-done.1 = f32[4,64,512]{2,1,0:T(8,128)S(1)} collective-permute-done((f32[4,64,512]{2,1,0:T(8,128)S(1)}, f32[4,64,512]{2,1,0:T(8,128)S(1)}, u32[]{:S(2)}, u32[]{:S(2)}) %collective-permute-start.1) | collective-permute-done | bytes 524320 | tf_op jit(solution)/shard_map/ppermute | solution.py:170
  37.1 0.1 bitcast_add_fusion
  37.2 3.9 %collective-permute-start.4 = (f32[64,512]{1,0:T(8,128)S(1)}, f32[64,512]{1,0:T(8,128)S(1)}, u32[]{:S(2)}, u32[]{:S(2)}) collective-permute-start(f32[64,512]{1,0:T(8,128)S(1)} %get-tuple-element.9), channel_id=1, source_target_pairs={{0,12},{4,0},{8,4},{12,8},{1,13},{5,1},{9,5},{13,9},{2,14},{6,2},{... | collective-permute-start | bytes 393224 | tf_op jit(solution)/shard_map/ppermute | solution.py:179
  41.1 0.0 collective-permute-start.3
  41.1 1.0 %collective-permute-start.2 = (f32[64,512]{1,0:T(8,128)S(1)}, f32[64,512]{1,0:T(8,128)S(1)}, u32[]{:S(2)}, u32[]{:S(2)}) collective-permute-start(f32[64,512]{1,0:T(8,128)S(1)} %get-tuple-element.8), channel_id=1, source_target_pairs={{0,4},{4,8},{8,12},{12,0},{1,5},{5,9},{9,13},{13,1},{2,6},{6,10},{... | collective-permute-start | bytes 393224 | tf_op jit(solution)/shard_map/ppermute | solution.py:179
  42.2 2.9 %collective-permute-done.4 = f32[64,512]{1,0:T(8,128)S(1)} collective-permute-done((f32[64,512]{1,0:T(8,128)S(1)}, f32[64,512]{1,0:T(8,128)S(1)}, u32[]{:S(2)}, u32[]{:S(2)}) %collective-permute-start.4) | collective-permute-done | bytes 131104 | tf_op jit(solution)/shard_map/ppermute | solution.py:179
  45.1 7.7 %collective-permute-done.3 = f32[64,512]{1,0:T(8,128)S(1)} collective-permute-done((f32[64,512]{1,0:T(8,128)S(1)}, f32[64,512]{1,0:T(8,128)S(1)}, u32[]{:S(2)}, u32[]{:S(2)}) %collective-permute-start.3) | collective-permute-done | bytes 131104 | tf_op jit(solution)/shard_map/ppermute | solution.py:179
  52.8 0.0 collective-permute-done.2
  53.0 0.0 copy-start.3
  53.0 0.9 %copy-done.3 = f32[32,8,128]{2,1,0:T(8,128)S(1)} copy-done((f32[32,8,128]{2,1,0:T(8,128)S(1)}, f32[32,8,128]{2,1,0:T(8,128)}, u32[]{:S(2)}) %copy-start.3) | copy-done | bytes 131096
  53.9 0.1 fusion.12
  54.0 0.0 copy-start.5
  54.0 0.2 multiply_reduce_fusion
  54.2 0.1 copy.31
  54.3 0.1 copy.32
  54.3 0.1 rsqrt.12
  54.4 0.1 div.9
  54.5 0.0 copy-done
  54.5 0.4 copy-done.5
  54.9 1.1 %fusion.3 = f32[32,8,128]{2,1,0:T(8,128)} fusion(bf16[512,128]{1,0:T(8,128)(2,1)S(1)} %copy-done, bf16[128,512]{1,0:T(8,128)(2,1)S(1)} %copy-done.5, f32[256,128]{1,0:T(8,128)S(1)} %bitcast.58, f32[32,8,128]{2,1,0:T(8,128)S(1)} %copy-done.3, f32[256]{0:T(256)S(1)} %rsqrt.12, f32[256]{0:T(256)S(1)} %div.9), kind=kOutput, calls=%fused_computation.4 | convolution fusion | flops 67567616 | bytes 657408 | tf_op jit(solution)/shard_map/dot_general | solution.py:238
  (9 shorter events, 0.2 us)
Async XLA Ops:
  0.6 53.9 %copy-start = (bf16[512,128]{1,0:T(8,128)(2,1)S(1)}, bf16[512,128]{1,0:T(8,128)(2,1)}, u32[]{:S(2)}) copy-start(bf16[512,128]{1,0:T(8,128)(2,1)} %param.17) | copy-start | bytes 393220
  0.6 0.9 %copy-start.6 = (bf16[64,32]{0,1:T(8,128)(2,1)S(1)}, bf16[64,32]{0,1:T(8,128)(2,1)}, u32[]{:S(2)}) copy-start(bf16[64,32]{0,1:T(8,128)(2,1)} %param.14) | copy-start | bytes 12292
  0.7 0.9 %copy-start.7 = (bf16[64,32]{0,1:T(8,128)(2,1)S(1)}, bf16[64,32]{0,1:T(8,128)(2,1)}, u32[]{:S(2)}) copy-start(bf16[64,32]{0,1:T(8,128)(2,1)} %param.13) | copy-start | bytes 12292
  1.6 0.8 %copy-start.2 = (bf16[256,64]{0,1:T(8,128)(2,1)S(1)}, bf16[256,64]{0,1:T(8,128)(2,1)}, u32[]{:S(2)}) copy-start(bf16[256,64]{0,1:T(8,128)(2,1)} %param.12) | copy-start | bytes 98308
  2.4 1.2 %copy-start.1 = (bf16[160,32,64]{0,2,1:T(8,128)(2,1)S(1)}, bf16[160,32,64]{0,2,1:T(8,128)(2,1)}, u32[]{:S(2)}) copy-start(bf16[160,32,64]{0,2,1:T(8,128)(2,1)} %param.9) | copy-start | bytes 1966084
  19.3 10.7 %collective-permute-start = (bf16[160,1024]{1,0:T(8,128)(2,1)S(1)}, bf16[160,1024]{1,0:T(8,128)(2,1)S(1)}, u32[]{:S(2)}, u32[]{:S(2)}) collective-permute-start(bf16[160,1024]{1,0:T(8,128)(2,1)S(1)} %bitcast.47), channel_id=1, source_target_pairs={{0,2},{2,0},{1,3},{3,1},{4,6},{6,4},{5,7},{7,5},{8,10},{10,8},{9,1... | collective-permute-start | bytes 983048 | tf_op jit(solution)/shard_map/ppermute | solution.py:216
  22.3 1.0 %copy-start.4 = (f32[1024,128]{1,0:T(8,128)S(1)}, f32[1024,128]{1,0:T(8,128)}, u32[]{:S(2)}) copy-start(f32[1024,128]{1,0:T(8,128)} %param.15) | copy-start | bytes 1572868
  35.1 2.0 %collective-permute-start.1 = (f32[4,64,512]{2,1,0:T(8,128)S(1)}, f32[4,64,512]{2,1,0:T(8,128)S(1)}, u32[]{:S(2)}, u32[]{:S(2)}) collective-permute-start(f32[4,64,512]{2,1,0:T(8,128)S(1)} %dynamic-slice_bitcast_fusion), channel_id=1, source_target_pairs={{0,1},{1,0},{2,3},{3,2},{4,5},{5,4},{6,7},{7,6},{8,9},{9,8},{10,11... | collective-permute-start | bytes 1572872 | tf_op jit(solution)/shard_map/ppermute | solution.py:170
  37.2 7.8 %collective-permute-start.4 = (f32[64,512]{1,0:T(8,128)S(1)}, f32[64,512]{1,0:T(8,128)S(1)}, u32[]{:S(2)}, u32[]{:S(2)}) collective-permute-start(f32[64,512]{1,0:T(8,128)S(1)} %get-tuple-element.9), channel_id=1, source_target_pairs={{0,12},{4,0},{8,4},{12,8},{1,13},{5,1},{9,5},{13,9},{2,14},{6,2},{... | collective-permute-start | bytes 393224 | tf_op jit(solution)/shard_map/ppermute | solution.py:179
  41.1 11.7 %collective-permute-start.3 = (f32[64,512]{1,0:T(8,128)S(1)}, f32[64,512]{1,0:T(8,128)S(1)}, u32[]{:S(2)}, u32[]{:S(2)}) collective-permute-start(f32[64,512]{1,0:T(8,128)S(1)} %get-tuple-element.10), channel_id=1, source_target_pairs={{0,8},{4,12},{8,0},{12,4},{1,9},{5,13},{9,1},{13,5},{2,10},{6,14},... | collective-permute-start | bytes 393224 | tf_op jit(solution)/shard_map/ppermute | solution.py:179
  41.1 11.7 %collective-permute-start.2 = (f32[64,512]{1,0:T(8,128)S(1)}, f32[64,512]{1,0:T(8,128)S(1)}, u32[]{:S(2)}, u32[]{:S(2)}) collective-permute-start(f32[64,512]{1,0:T(8,128)S(1)} %get-tuple-element.8), channel_id=1, source_target_pairs={{0,4},{4,8},{8,12},{12,0},{1,5},{5,9},{9,13},{13,1},{2,6},{6,10},{... | collective-permute-start | bytes 393224 | tf_op jit(solution)/shard_map/ppermute | solution.py:179
  53.0 0.9 %copy-start.3 = (f32[32,8,128]{2,1,0:T(8,128)S(1)}, f32[32,8,128]{2,1,0:T(8,128)}, u32[]{:S(2)}) copy-start(f32[32,8,128]{2,1,0:T(8,128)} %param.10) | copy-start | bytes 393220
  54.0 0.9 %copy-start.5 = (bf16[128,512]{1,0:T(8,128)(2,1)S(1)}, bf16[128,512]{1,0:T(8,128)(2,1)}, u32[]{:S(2)}) copy-start(bf16[128,512]{1,0:T(8,128)(2,1)} %param.16) | copy-start | bytes 393220

commit v5 on v4

--- a/solution.py
+++ b/solution.py
@@ -131,7 +131,7 @@
         rt_ref[pl.ds(start, width), :] = proj[width:].astype(jnp.bfloat16)
         return carry
 
-    lax.fori_loop(0, sites, body, 0, unroll=2)
+    lax.fori_loop(0, sites, body, 0, unroll=True)
 
 
 def msa_block(xt, wwt, wst, pt):

time: 56.3 us -> 54 us (0.959)
  Pallas kernels: 25.4 us -> 23 us
    pallas_call x1, Pallas kernels: 15.6 us -> 13.1 us  [msa_block(): pl.pallas_call(msa_kernel, out_shape=(jax.ShapeDtypeStruct(xt.shape, jnp....]
where the time goes in v5:
time: 54 us; the launch traced here: 53.7 us
  Pallas kernels  23 us (43%)
  waiting for transfers between devices  14.2 us (26%)
  starting transfers between devices  8.01 us (15%)
  local copies, waits for them, and re-layouts  5.84 us (11%)
  matrix products  1.06 us (2%)
  between operations  0.89 us (2%)
  other arithmetic  0.63 us (1%)
    pallas_call x1, Pallas kernels, msa_block(): pl.pallas_call(msa_kernel, out_shape=(jax.ShapeDtypeStruct(xt.shape, jnp....  13.1 us
    ppermute x3, waiting for transfers between devices, reduce_over_sequences(): lax.ppermute(src, 'seq', [(q, (q + k) % nseq) for q in range(nseq)])  10.7 us
    pallas_call x2, Pallas kernels, outer_project(): pl.pallas_call(functools.partial(outer_project_kernel, scale), grid=(step...  9.95 us
    ppermute x3, starting transfers between devices, reduce_over_sequences(): lax.ppermute(src, 'seq', [(q, (q + k) % nseq) for q in range(nseq)])  4.93 us
    unnamed x17, local copies, waits for them, and re-layouts  4.55 us
    ppermute x1, starting transfers between devices, per_device(): r_other = lax.ppermute(right_features, 'res', [(0, 1), (1, 0)])  3.01 us
    ppermute x1, waiting for transfers between devices, reduce_over_sequences(): received = lax.ppermute(other, 'chan', [(0, 1), (1, 0)])  1.85 us
    ppermute x1, waiting for transfers between devices, per_device(): r_other = lax.ppermute(right_features, 'res', [(0, 1), (1, 0)])  1.68 us
  transfers between devices with their start and end apart: 5, of which 4 were waited for; matrix products, arithmetic and copies ran while one was open for 1% of the time, Pallas kernels for 9%

profile of v5, /device:TPU:0, one launch (start us, length us, event | category | flops | bytes accessed | tf_op | source)
XLA Modules:
  0.0 53.7 jit_solution(4140705315583231619)
XLA Ops:
  0.6 0.0 copy-start
  0.6 0.0 copy-start.6
  0.7 0.0 copy-start.7
  0.7 0.9 %copy.25 = bf16[64,256]{0,1:T(8,128)(2,1)S(1)} copy(bf16[64,256]{1,0:T(8,128)(2,1)} %param.11) | data formatting | bytes 65536 | tf_op args[2]
  1.6 0.0 copy-done.6
  1.6 0.0 copy-done.7
  1.6 0.0 copy-start.2
  1.6 0.7 %copy-done.2 = bf16[256,64]{0,1:T(8,128)(2,1)S(1)} copy-done((bf16[256,64]{0,1:T(8,128)(2,1)S(1)}, bf16[256,64]{0,1:T(8,128)(2,1)}, u32[]{:S(2)}) %copy-start.2) | copy-done | bytes 32792
  2.4 0.0 copy-start.1
  2.4 1.2 %copy-done.1 = bf16[160,32,64]{0,2,1:T(8,128)(2,1)S(1)} copy-done((bf16[160,32,64]{0,2,1:T(8,128)(2,1)S(1)}, bf16[160,32,64]{0,2,1:T(8,128)(2,1)}, u32[]{:S(2)}) %copy-start.1) | copy-done | bytes 655384
  3.6 13.1 %shard_map.104 = (bf16[32,64,160]{2,1,0:T(8,128)(2,1)}, f32[1024,160]{1,0:T(8,128)S(1)}, bf16[1024,160]{1,0:T(8,128)(2,1)S(1)}) custom-call(bf16[32,64,160]{2,1,0:T(8,128)(2,1)S(1)} %bitcast.50, bf16[256,64]{1,0:T(8,128)(2,1)S(1)} %bitcast.49, bf16[64,256]{1,0:T(8,128)(2,1)S(1)} %bitcast.51, bf16[64,64]{1,0:T(8,128)(2,1)S(1)} %maximum_bitcast_fusion.pt_ref), custom_call_target="tpu_custom_call" | custom-call | flops 377487360 | bytes 2293760 | tf_op jit(solution)/shard_map/pallas_call | solution.py:141
  16.7 0.2 copy.27
  16.8 3.0 %collective-permute-start = (bf16[160,1024]{1,0:T(8,128)(2,1)S(1)}, bf16[160,1024]{1,0:T(8,128)(2,1)S(1)}, u32[]{:S(2)}, u32[]{:S(2)}) collective-permute-start(bf16[160,1024]{1,0:T(8,128)(2,1)S(1)} %bitcast.47), channel_id=1, source_target_pairs={{0,2},{2,0},{1,3},{3,1},{4,6},{6,4},{5,7},{7,5},{8,10},{10,8},{9,1... | collective-permute-start | bytes 983048 | tf_op jit(solution)/shard_map/ppermute | solution.py:216
  19.8 0.0 copy-start.4
  19.9 0.6 %copy.26 = f32[32,32,160]{2,0,1:T(8,128)S(1)} copy(f32[32,32,160]{2,1,0:T(8,128)S(1)} %bitcast.46) | data formatting | bytes 1310720 | tf_op jit(solution)/shard_map/reshape | solution.py:202
  20.5 0.4 copy-done.4
  20.9 0.1 fusion.4
  21.0 4.9 %shard_map.105 = f32[256,512]{1,0:T(8,128)S(1)} custom-call(f32[1024,160]{1,0:T(8,128)S(1)} %bitcast.44, bf16[160,1024]{1,0:T(8,128)(2,1)S(1)} %bitcast.48, bf16[1024,128]{1,0:T(8,128)(2,1)S(1)} %get-tuple-element.12.wh_ref, bf16[1024,128]{1,0:T(8,128)(2,1)S(1)} %get-tuple-element.11.wl_ref), custom_call_target="tpu_custom_call" | custom-call | flops 3556769792 | bytes 1703936 | tf_op jit(solution)/shard_map/pallas_call | solution.py:81
  25.9 1.7 %collective-permute-done.r_ref = bf16[160,1024]{1,0:T(8,128)(2,1)S(1)} collective-permute-done((bf16[160,1024]{1,0:T(8,128)(2,1)S(1)}, bf16[160,1024]{1,0:T(8,128)(2,1)S(1)}, u32[]{:S(2)}, u32[]{:S(2)}) %collective-permute-start) | collective-permute-done | bytes 327712 | tf_op jit(solution)/shard_map/ppermute | solution.py:216
  27.6 5.1 %shard_map.106 = f32[256,512]{1,0:T(8,128)S(1)} custom-call(f32[1024,160]{1,0:T(8,128)S(1)} %bitcast.45, bf16[160,1024]{1,0:T(8,128)(2,1)S(1)} %collective-permute-done.r_ref, bf16[1024,128]{1,0:T(8,128)(2,1)S(1)} %get-tuple-element.12.wh_ref, bf16[1024,128]{1,0:T(8,128)(2,1)S(1)} %get-tuple-element.11.wl_ref), custom_call_target="tpu_custom_call" | custom-call | flops 3556769792 | bytes 1703936 | tf_op jit(solution)/shard_map/pallas_call | solution.py:81
  32.6 0.1 maximum_select_fusion
  32.8 0.1 collective-permute-start.1
  32.9 1.9 %collective-permute-done.1 = f32[4,64,512]{2,1,0:T(8,128)S(1)} collective-permute-done((f32[4,64,512]{2,1,0:T(8,128)S(1)}, f32[4,64,512]{2,1,0:T(8,128)S(1)}, u32[]{:S(2)}, u32[]{:S(2)}) %collective-permute-start.1) | collective-permute-done | bytes 524320 | tf_op jit(solution)/shard_map/ppermute | solution.py:170
  34.8 0.1 bitcast_add_fusion
  34.9 3.9 %collective-permute-start.4 = (f32[64,512]{1,0:T(8,128)S(1)}, f32[64,512]{1,0:T(8,128)S(1)}, u32[]{:S(2)}, u32[]{:S(2)}) collective-permute-start(f32[64,512]{1,0:T(8,128)S(1)} %get-tuple-element.9), channel_id=1, source_target_pairs={{0,12},{4,0},{8,4},{12,8},{1,13},{5,1},{9,5},{13,9},{2,14},{6,2},{... | collective-permute-start | bytes 393224 | tf_op jit(solution)/shard_map/ppermute | solution.py:179
  38.8 0.0 collective-permute-start.3
  38.8 1.0 %collective-permute-start.2 = (f32[64,512]{1,0:T(8,128)S(1)}, f32[64,512]{1,0:T(8,128)S(1)}, u32[]{:S(2)}, u32[]{:S(2)}) collective-permute-start(f32[64,512]{1,0:T(8,128)S(1)} %get-tuple-element.8), channel_id=1, source_target_pairs={{0,4},{4,8},{8,12},{12,0},{1,5},{5,9},{9,13},{13,1},{2,6},{6,10},{... | collective-permute-start | bytes 393224 | tf_op jit(solution)/shard_map/ppermute | solution.py:179
  39.9 2.9 %collective-permute-done.4 = f32[64,512]{1,0:T(8,128)S(1)} collective-permute-done((f32[64,512]{1,0:T(8,128)S(1)}, f32[64,512]{1,0:T(8,128)S(1)}, u32[]{:S(2)}, u32[]{:S(2)}) %collective-permute-start.4) | collective-permute-done | bytes 131104 | tf_op jit(solution)/shard_map/ppermute | solution.py:179
  42.8 7.7 %collective-permute-done.3 = f32[64,512]{1,0:T(8,128)S(1)} collective-permute-done((f32[64,512]{1,0:T(8,128)S(1)}, f32[64,512]{1,0:T(8,128)S(1)}, u32[]{:S(2)}, u32[]{:S(2)}) %collective-permute-start.3) | collective-permute-done | bytes 131104 | tf_op jit(solution)/shard_map/ppermute | solution.py:179
  50.5 0.0 collective-permute-done.2
  50.7 0.0 copy-start.3
  50.7 0.9 %copy-done.3 = f32[32,8,128]{2,1,0:T(8,128)S(1)} copy-done((f32[32,8,128]{2,1,0:T(8,128)S(1)}, f32[32,8,128]{2,1,0:T(8,128)}, u32[]{:S(2)}) %copy-start.3) | copy-done | bytes 131096
  51.6 0.1 fusion.12
  51.7 0.0 copy-start.5
  51.7 0.2 multiply_reduce_fusion
  51.9 0.1 copy.31
  52.0 0.1 copy.32
  52.0 0.1 rsqrt.12
  52.1 0.1 div.9
  52.2 0.0 copy-done
  52.2 0.4 copy-done.5
  52.6 1.1 %fusion.3 = f32[32,8,128]{2,1,0:T(8,128)} fusion(bf16[512,128]{1,0:T(8,128)(2,1)S(1)} %copy-done, bf16[128,512]{1,0:T(8,128)(2,1)S(1)} %copy-done.5, f32[256,128]{1,0:T(8,128)S(1)} %bitcast.58, f32[32,8,128]{2,1,0:T(8,128)S(1)} %copy-done.3, f32[256]{0:T(256)S(1)} %rsqrt.12, f32[256]{0:T(256)S(1)} %div.9), kind=kOutput, calls=%fused_computation.4 | convolution fusion | flops 67567616 | bytes 657408 | tf_op jit(solution)/shard_map/dot_general | solution.py:238
  (9 shorter events, 0.2 us)
Async XLA Ops:
  0.6 51.6 %copy-start = (bf16[512,128]{1,0:T(8,128)(2,1)S(1)}, bf16[512,128]{1,0:T(8,128)(2,1)}, u32[]{:S(2)}) copy-start(bf16[512,128]{1,0:T(8,128)(2,1)} %param.17) | copy-start | bytes 393220
  0.6 0.9 %copy-start.6 = (bf16[64,32]{0,1:T(8,128)(2,1)S(1)}, bf16[64,32]{0,1:T(8,128)(2,1)}, u32[]{:S(2)}) copy-start(bf16[64,32]{0,1:T(8,128)(2,1)} %param.14) | copy-start | bytes 12292
  0.7 0.9 %copy-start.7 = (bf16[64,32]{0,1:T(8,128)(2,1)S(1)}, bf16[64,32]{0,1:T(8,128)(2,1)}, u32[]{:S(2)}) copy-start(bf16[64,32]{0,1:T(8,128)(2,1)} %param.13) | copy-start | bytes 12292
  1.6 0.8 %copy-start.2 = (bf16[256,64]{0,1:T(8,128)(2,1)S(1)}, bf16[256,64]{0,1:T(8,128)(2,1)}, u32[]{:S(2)}) copy-start(bf16[256,64]{0,1:T(8,128)(2,1)} %param.12) | copy-start | bytes 98308
  2.4 1.2 %copy-start.1 = (bf16[160,32,64]{0,2,1:T(8,128)(2,1)S(1)}, bf16[160,32,64]{0,2,1:T(8,128)(2,1)}, u32[]{:S(2)}) copy-start(bf16[160,32,64]{0,2,1:T(8,128)(2,1)} %param.9) | copy-start | bytes 1966084
  16.8 10.7 %collective-permute-start = (bf16[160,1024]{1,0:T(8,128)(2,1)S(1)}, bf16[160,1024]{1,0:T(8,128)(2,1)S(1)}, u32[]{:S(2)}, u32[]{:S(2)}) collective-permute-start(bf16[160,1024]{1,0:T(8,128)(2,1)S(1)} %bitcast.47), channel_id=1, source_target_pairs={{0,2},{2,0},{1,3},{3,1},{4,6},{6,4},{5,7},{7,5},{8,10},{10,8},{9,1... | collective-permute-start | bytes 983048 | tf_op jit(solution)/shard_map/ppermute | solution.py:216
  19.8 1.0 %copy-start.4 = (f32[1024,128]{1,0:T(8,128)S(1)}, f32[1024,128]{1,0:T(8,128)}, u32[]{:S(2)}) copy-start(f32[1024,128]{1,0:T(8,128)} %param.15) | copy-start | bytes 1572868
  32.8 2.0 %collective-permute-start.1 = (f32[4,64,512]{2,1,0:T(8,128)S(1)}, f32[4,64,512]{2,1,0:T(8,128)S(1)}, u32[]{:S(2)}, u32[]{:S(2)}) collective-permute-start(f32[4,64,512]{2,1,0:T(8,128)S(1)} %dynamic-slice_bitcast_fusion), channel_id=1, source_target_pairs={{0,1},{1,0},{2,3},{3,2},{4,5},{5,4},{6,7},{7,6},{8,9},{9,8},{10,11... | collective-permute-start | bytes 1572872 | tf_op jit(solution)/shard_map/ppermute | solution.py:170
  34.9 7.9 %collective-permute-start.4 = (f32[64,512]{1,0:T(8,128)S(1)}, f32[64,512]{1,0:T(8,128)S(1)}, u32[]{:S(2)}, u32[]{:S(2)}) collective-permute-start(f32[64,512]{1,0:T(8,128)S(1)} %get-tuple-element.9), channel_id=1, source_target_pairs={{0,12},{4,0},{8,4},{12,8},{1,13},{5,1},{9,5},{13,9},{2,14},{6,2},{... | collective-permute-start | bytes 393224 | tf_op jit(solution)/shard_map/ppermute | solution.py:179
  38.8 11.7 %collective-permute-start.3 = (f32[64,512]{1,0:T(8,128)S(1)}, f32[64,512]{1,0:T(8,128)S(1)}, u32[]{:S(2)}, u32[]{:S(2)}) collective-permute-start(f32[64,512]{1,0:T(8,128)S(1)} %get-tuple-element.10), channel_id=1, source_target_pairs={{0,8},{4,12},{8,0},{12,4},{1,9},{5,13},{9,1},{13,5},{2,10},{6,14},... | collective-permute-start | bytes 393224 | tf_op jit(solution)/shard_map/ppermute | solution.py:179
  38.8 11.7 %collective-permute-start.2 = (f32[64,512]{1,0:T(8,128)S(1)}, f32[64,512]{1,0:T(8,128)S(1)}, u32[]{:S(2)}, u32[]{:S(2)}) collective-permute-start(f32[64,512]{1,0:T(8,128)S(1)} %get-tuple-element.8), channel_id=1, source_target_pairs={{0,4},{4,8},{8,12},{12,0},{1,5},{5,9},{9,13},{13,1},{2,6},{6,10},{... | collective-permute-start | bytes 393224 | tf_op jit(solution)/shard_map/ppermute | solution.py:179
  50.7 0.9 %copy-start.3 = (f32[32,8,128]{2,1,0:T(8,128)S(1)}, f32[32,8,128]{2,1,0:T(8,128)}, u32[]{:S(2)}) copy-start(f32[32,8,128]{2,1,0:T(8,128)} %param.10) | copy-start | bytes 393220
  51.7 0.9 %copy-start.5 = (bf16[128,512]{1,0:T(8,128)(2,1)S(1)}, bf16[128,512]{1,0:T(8,128)(2,1)}, u32[]{:S(2)}) copy-start(bf16[128,512]{1,0:T(8,128)(2,1)} %param.16) | copy-start | bytes 393220

commit v6 on v3

--- a/solution.py
+++ b/solution.py
@@ -12,6 +12,13 @@
     mean = jnp.mean(values, axis=-1, keepdims=True)
     centred = values - mean
     variance = jnp.mean(centred * centred, axis=-1, keepdims=True)
+    return centred * lax.rsqrt(variance + 1e-05)
+
+
+def apply_layer_norm_axis1(values):
+    mean = jnp.mean(values, axis=1, keepdims=True)
+    centred = values - mean
+    variance = jnp.mean(centred * centred, axis=1, keepdims=True)
     return centred * lax.rsqrt(variance + 1e-05)
 
 
@@ -142,28 +149,23 @@
     homologs_local_share, sites_local_share, homolog_lane_number = homolog_embedding.shape
     proj_width = lhs_projector.shape[1]
     pair_width = coupling_embedding.shape[2]
-    cross_moment_average = homolog_embedding.reshape(
-        homologs_local_share * sites_local_share, homolog_lane_number
-    )
-    homolog_standardized = apply_layer_norm(cross_moment_average.astype(jnp.float32)).astype(
-        jnp.bfloat16
-    )
-    homolog_inner_state = jnp.maximum(
-        jnp.dot(homolog_standardized, homolog_widen_weights, preferred_element_type=jnp.float32),
-        0.0,
+    xt = jnp.transpose(homolog_embedding, (1, 2, 0)).astype(jnp.float32)
+    n1 = apply_layer_norm_axis1(xt).astype(jnp.bfloat16)
+    hidden = jnp.maximum(
+        jnp.einsum("kh,iks->ihs", homolog_widen_weights, n1, preferred_element_type=jnp.float32), 0.0
     ).astype(jnp.bfloat16)
-    homolog_refreshed = (
-        cross_moment_average.astype(jnp.float32)
-        + jnp.dot(homolog_inner_state, homolog_shrink_weights, preferred_element_type=jnp.float32)
+    refreshed_t = (
+        xt + jnp.einsum("hk,ihs->iks", homolog_shrink_weights, hidden, preferred_element_type=jnp.float32)
     ).astype(jnp.bfloat16)
-    alignment_normed2 = apply_layer_norm(homolog_refreshed.astype(jnp.float32)).astype(jnp.bfloat16)
-    left_features = (
-        jnp.dot(alignment_normed2, lhs_projector, preferred_element_type=jnp.float32)
+    homolog_refreshed = jnp.transpose(refreshed_t, (2, 0, 1))
+    n2 = apply_layer_norm_axis1(refreshed_t.astype(jnp.float32)).astype(jnp.bfloat16)
+    lt = (
+        jnp.einsum("kc,iks->cis", lhs_projector, n2, preferred_element_type=jnp.float32)
         .astype(jnp.bfloat16)
-        .reshape(homologs_local_share, sites_local_share, proj_width)
+        .reshape(proj_width * sites_local_share, homologs_local_share)
     )
     right_features = (
-        jnp.dot(alignment_normed2, rhs_projector, preferred_element_type=jnp.float32)
+        jnp.einsum("ke,iks->sie", rhs_projector, n2, preferred_element_type=jnp.float32)
         .astype(jnp.bfloat16)
         .reshape(homologs_local_share, sites_local_share * proj_width)
     )
@@ -171,7 +173,6 @@
     depth_total = float(homologs_local_share * owners)
     block_cols = coupling_embedding.shape[1]
 
-    lt = jnp.transpose(left_features, (2, 1, 0)).reshape(proj_width * sites_local_share, homologs_local_share)
     w_hi_f32 = lax.reduce_precision(moment_coupling_weights, exponent_bits=8, mantissa_bits=7)
     w_hi = w_hi_f32.astype(jnp.bfloat16)
     w_lo = (moment_coupling_weights - w_hi_f32).astype(jnp.bfloat16)
@@ -203,7 +204,7 @@
         pair_hidden, coupling_shrink_weights, preferred_element_type=jnp.float32
     )
     return (
-        homolog_refreshed.reshape(homologs_local_share, sites_local_share, homolog_lane_number),
+        homolog_refreshed,
         coupling_refreshed.reshape(sites_local_share, block_cols, pair_width),
     )
 

time: 47.2 us -> 47.1 us (level)
  local copies, waits for them, and re-layouts: 11.8 us -> 1.03 us
  waiting for transfers between devices: 6.73 us -> 14.6 us
  other arithmetic: 3.84 us -> 6.27 us
  matrix products: 4.73 us -> 6.29 us
  starting transfers between devices: 8.63 us -> 7.99 us
    ppermute x3, waiting for transfers between devices: 4.87 us -> 10.7 us  [reduce_over_sequences(): lax.ppermute(src, 'seq', [(q, (q + k) % nseq) for q in range(nseq)])]
    reduce_sum x0 -> x4, other arithmetic: none -> 5.61 us  [the longest x2 3.6 us: apply_layer_norm_axis1(): mean = jnp.mean(values, axis=1, keepdims=True)]
    convert_element_type x4 -> x1, local copies, waits for them, and re-layouts: 5.71 us -> 0.29 us  [per_device(): lt = jnp.einsum('kc,iks->cis', lhs_projector, n2, preferred_element_type=...]
    reshape x2 -> x1, local copies, waits for them, and re-layouts: 2.34 us -> 0.18 us  [per_device(): right_features = jnp.einsum('ke,iks->sie', rhs_projector, n2, preferred_e...]
    ppermute x1, waiting for transfers between devices: 0.01 us -> 2.05 us  [per_device(): r_other = lax.ppermute(right_features, 'res', [(0, 1), (1, 0)])]
    unnamed x17 -> x18, local copies, waits for them, and re-layouts: 2.02 us -> 0.05 us
    dot_general x3, matrix products: 3.66 us -> 5.22 us  [the longest x1 4.47 us: per_device(): jnp.einsum('hk,ihs->iks', homolog_shrink_weights, hidden, preferred_eleme...]
    reduce_sum x2 -> x1, other arithmetic: 1.65 us -> 0.11 us  [apply_layer_norm(): mean = jnp.mean(values, axis=-1, keepdims=True)]
  transfers between devices with their start and end apart: 5 -> 5, of which waited for: 2 -> 4; matrix products, arithmetic and copies ran while one was open for 13% -> 2% of each run, Pallas kernels for 10% -> 10%
where the time goes in v6:
time: 47.1 us; the launch traced here: 46.9 us
  waiting for transfers between devices  14.6 us (31%)
  Pallas kernels  9.71 us (21%)
  starting transfers between devices  7.99 us (17%)
  matrix products  6.29 us (13%)
  other arithmetic  6.27 us (13%)
  local copies, waits for them, and re-layouts  1.03 us (2%)
  between operations  1.01 us (2%)
    ppermute x3, waiting for transfers between devices, reduce_over_sequences(): lax.ppermute(src, 'seq', [(q, (q + k) % nseq) for q in range(nseq)])  10.7 us
    pallas_call x2, Pallas kernels, outer_project(): pl.pallas_call(functools.partial(outer_project_kernel, scale), grid=(step...  9.71 us
    ppermute x3, starting transfers between devices, reduce_over_sequences(): lax.ppermute(src, 'seq', [(q, (q + k) % nseq) for q in range(nseq)])  4.92 us
    dot_general x1, matrix products, per_device(): jnp.einsum('hk,ihs->iks', homolog_shrink_weights, hidden, preferred_eleme...  4.47 us
    reduce_sum x2, other arithmetic, apply_layer_norm_axis1(): mean = jnp.mean(values, axis=1, keepdims=True)  3.6 us
    ppermute x1, starting transfers between devices, per_device(): r_other = lax.ppermute(right_features, 'res', [(0, 1), (1, 0)])  3 us
    ppermute x1, waiting for transfers between devices, per_device(): r_other = lax.ppermute(right_features, 'res', [(0, 1), (1, 0)])  2.05 us
    reduce_sum x2, other arithmetic, apply_layer_norm_axis1(): variance = jnp.mean(centred * centred, axis=1, keepdims=True)  2 us
  transfers between devices with their start and end apart: 5, of which 4 were waited for; matrix products, arithmetic and copies ran while one was open for 2% of the time, Pallas kernels for 10%

profile of v6, /device:TPU:0, one launch (start us, length us, event | category | flops | bytes accessed | tf_op | source)
XLA Modules:
  0.0 46.9 jit_solution(14660228985778316550)
XLA Ops:
  0.6 0.0 copy-start
  0.6 0.0 copy-start.1
  0.7 0.0 copy-start.7
  0.7 0.0 copy-start.8
  0.7 1.6 %fusion.2 = f32[32,160]{1,0:T(8,128)S(1)} fusion(bf16[160,32,64]{0,2,1:T(8,128)(2,1)} %param.9), kind=kLoop, calls=%fused_computation.7 | loop fusion | flops 650240 | bytes 675840 | tf_op jit(solution)/shard_map/reduce_sum | solution.py:19
  2.2 1.6 %fusion.15 = f32[32,160]{1,0:T(8,128)S(1)} fusion(bf16[160,32,64]{0,2,1:T(8,128)(2,1)} %param.9, f32[32,160]{1,0:T(8,128)S(1)} %broadcast_multiply_fusion.1), kind=kLoop, calls=%fused_computation.18 | loop fusion | flops 1305600 | bytes 696320 | tf_op jit(solution)/shard_map/reduce_sum | solution.py:21
  3.9 0.0 copy-done.1
  3.9 0.0 copy-done.7
  3.9 0.0 copy-done.8
  3.9 4.5 %fusion.18 = (bf16[160,32,64]{0,2,1:T(8,128)(2,1)}, f32[32,160,64]{1,2,0:T(8,128)}) fusion(bf16[160,32,64]{0,2,1:T(8,128)(2,1)S(1)} %copy-done.1, bf16[256,64]{0,1:T(8,128)(2,1)S(1)} %copy-done.7, f32[32,160]{1,0:T(8,128)S(1)} %add_rsqrt_fusion.1, f32[32,160]{1,0:T(8,128)S(1)} %broadcast_multiply_fusion.1, bf16[64,256]{1,0:T(8,128)(2,1)S(1)} %copy-done.8), kind=kOutput, calls=%fused_computation.21 | convolution fusion | flops 340459520 | bytes 2727936 | tf_op jit(solution)/shard_map/hk,ihs->iks/dot_general | solution.py:158
  8.4 2.1 %convert_reduce_fusion = (f32[32,160]{1,0:T(8,128)S(1)}, bf16[32,64,160]{2,1,0:T(8,128)(2,1)S(1)}) fusion(f32[32,160,64]{1,2,0:T(8,128)} %get-tuple-element.10, bf16[160,32,64]{0,2,1:T(8,128)(2,1)S(1)} %copy-done.1), kind=kLoop, calls=%fused_computation.2 | loop fusion | flops 1633280 | bytes 2641920 | tf_op jit(solution)/shard_map/reduce_sum | solution.py:19
  10.4 0.0 copy-start.6
  10.5 0.4 fusion.13
  10.9 0.0 copy-done.5
  10.9 0.4 convolution_convert_fusion
  11.3 0.0 copy-start.3
  11.3 0.2 copy.25.r_ref
  11.5 3.0 %collective-permute-start = (bf16[160,1024]{1,0:T(8,128)(2,1)S(1)}, bf16[160,1024]{1,0:T(8,128)(2,1)S(1)}, u32[]{:S(2)}, u32[]{:S(2)}) collective-permute-start(bf16[160,1024]{1,0:T(8,128)(2,1)S(1)} %copy.25.r_ref), channel_id=1, source_target_pairs={{0,2},{2,0},{1,3},{3,1},{4,6},{6,4},{5,7},{7,5},{8,10},{10,8},{9,1... | collective-permute-start | bytes 983048 | tf_op jit(solution)/shard_map/ppermute | solution.py:181
  14.5 0.0 copy-done.6
  14.5 0.4 fusion.19
  14.9 0.3 copy.24
  15.2 0.0 copy-done.3
  15.2 0.1 fusion.32
  15.3 4.9 %shard_map.104 = f32[256,512]{1,0:T(8,128)S(1)} custom-call(bf16[1024,160]{1,0:T(8,128)(2,1)S(1)} %bitcast.89, bf16[160,1024]{1,0:T(8,128)(2,1)S(1)} %copy.25.r_ref, bf16[1024,128]{1,0:T(8,128)(2,1)S(1)} %get-tuple-element.8.wh_ref, bf16[1024,128]{1,0:T(8,128)(2,1)S(1)} %get-tuple-element.7.wl_ref), custom_call_target="tpu_custom_call" | custom-call | flops 3556769792 | bytes 1703936 | tf_op jit(solution)/shard_map/pallas_call | solution.py:88
  20.1 2.0 %collective-permute-done.r_ref = bf16[160,1024]{1,0:T(8,128)(2,1)S(1)} collective-permute-done((bf16[160,1024]{1,0:T(8,128)(2,1)S(1)}, bf16[160,1024]{1,0:T(8,128)(2,1)S(1)}, u32[]{:S(2)}, u32[]{:S(2)}) %collective-permute-start) | collective-permute-done | bytes 327712 | tf_op jit(solution)/shard_map/ppermute | solution.py:181
  22.2 4.9 %shard_map.105 = f32[256,512]{1,0:T(8,128)S(1)} custom-call(bf16[1024,160]{1,0:T(8,128)(2,1)S(1)} %bitcast.90, bf16[160,1024]{1,0:T(8,128)(2,1)S(1)} %collective-permute-done.r_ref, bf16[1024,128]{1,0:T(8,128)(2,1)S(1)} %get-tuple-element.8.wh_ref, bf16[1024,128]{1,0:T(8,128)(2,1)S(1)} %get-tuple-element.7.wl_ref), custom_call_target="tpu_custom_call" | custom-call | flops 3556769792 | bytes 1703936 | tf_op jit(solution)/shard_map/pallas_call | solution.py:88
  27.1 0.1 maximum_select_fusion
  27.2 0.0 copy-start.2
  27.2 0.1 collective-permute-start.1
  27.4 0.0 copy-start.4
  27.4 1.8 %collective-permute-done.1 = f32[4,64,512]{2,1,0:T(8,128)S(1)} collective-permute-done((f32[4,64,512]{2,1,0:T(8,128)S(1)}, f32[4,64,512]{2,1,0:T(8,128)S(1)}, u32[]{:S(2)}, u32[]{:S(2)}) %collective-permute-start.1) | collective-permute-done | bytes 524320 | tf_op jit(solution)/shard_map/ppermute | solution.py:125
  29.2 0.1 bitcast_add_fusion
  29.4 3.9 %collective-permute-start.4 = (f32[64,512]{1,0:T(8,128)S(1)}, f32[64,512]{1,0:T(8,128)S(1)}, u32[]{:S(2)}, u32[]{:S(2)}) collective-permute-start(f32[64,512]{1,0:T(8,128)S(1)} %get-tuple-element.5), channel_id=1, source_target_pairs={{0,12},{4,0},{8,4},{12,8},{1,13},{5,1},{9,5},{13,9},{2,14},{6,2},{... | collective-permute-start | bytes 393224 | tf_op jit(solution)/shard_map/ppermute | solution.py:134
  33.3 0.0 collective-permute-start.3
  33.3 1.0 %collective-permute-start.2 = (f32[64,512]{1,0:T(8,128)S(1)}, f32[64,512]{1,0:T(8,128)S(1)}, u32[]{:S(2)}, u32[]{:S(2)}) collective-permute-start(f32[64,512]{1,0:T(8,128)S(1)} %get-tuple-element.4), channel_id=1, source_target_pairs={{0,4},{4,8},{8,12},{12,0},{1,5},{5,9},{9,13},{13,1},{2,6},{6,10},{... | collective-permute-start | bytes 393224 | tf_op jit(solution)/shard_map/ppermute | solution.py:134
  34.3 2.9 %collective-permute-done.4 = f32[64,512]{1,0:T(8,128)S(1)} collective-permute-done((f32[64,512]{1,0:T(8,128)S(1)}, f32[64,512]{1,0:T(8,128)S(1)}, u32[]{:S(2)}, u32[]{:S(2)}) %collective-permute-start.4) | collective-permute-done | bytes 131104 | tf_op jit(solution)/shard_map/ppermute | solution.py:134
  37.2 7.7 %collective-permute-done.3 = f32[64,512]{1,0:T(8,128)S(1)} collective-permute-done((f32[64,512]{1,0:T(8,128)S(1)}, f32[64,512]{1,0:T(8,128)S(1)}, u32[]{:S(2)}, u32[]{:S(2)}) %collective-permute-start.3) | collective-permute-done | bytes 131104 | tf_op jit(solution)/shard_map/ppermute | solution.py:134
  44.9 0.0 collective-permute-done.2
  45.1 0.0 copy-done.2
  45.1 0.1 fusion.40
  45.2 0.2 multiply_reduce_fusion
  45.4 0.1 copy.30
  45.5 0.1 copy.31
  45.6 0.1 rsqrt.30
  45.7 0.1 div.25
  45.8 0.0 copy-done
  45.8 0.0 copy-done.4
  45.8 1.1 %fusion.23 = f32[32,8,128]{2,1,0:T(8,128)} fusion(bf16[512,128]{1,0:T(8,128)(2,1)S(1)} %copy-done, bf16[128,512]{1,0:T(8,128)(2,1)S(1)} %copy-done.4, f32[256,128]{1,0:T(8,128)S(1)} %bitcast.98, f32[32,8,128]{2,1,0:T(8,128)S(1)} %copy-done.2, f32[256]{0:T(256)S(1)} %rsqrt.30, f32[256]{0:T(256)S(1)} %div.25), kind=kOutput, calls=%fused_computation.29 | convolution fusion | flops 67567616 | bytes 657408 | tf_op jit(solution)/shard_map/dot_general | solution.py:203
  (13 shorter events, 0.2 us)
Async XLA Ops:
  0.6 45.1 %copy-start = (bf16[512,128]{1,0:T(8,128)(2,1)S(1)}, bf16[512,128]{1,0:T(8,128)(2,1)}, u32[]{:S(2)}) copy-start(bf16[512,128]{1,0:T(8,128)(2,1)} %param.17) | copy-start | bytes 393220
  0.6 3.2 %copy-start.1 = (bf16[160,32,64]{0,2,1:T(8,128)(2,1)S(1)}, bf16[160,32,64]{0,2,1:T(8,128)(2,1)}, u32[]{:S(2)}) copy-start(bf16[160,32,64]{0,2,1:T(8,128)(2,1)} %param.9) | copy-start | bytes 1966084
  0.7 3.2 %copy-start.7 = (bf16[256,64]{0,1:T(8,128)(2,1)S(1)}, bf16[256,64]{0,1:T(8,128)(2,1)}, u32[]{:S(2)}) copy-start(bf16[256,64]{0,1:T(8,128)(2,1)} %param.12) | copy-start | bytes 98308
  0.7 3.2 %copy-start.8 = (bf16[64,256]{1,0:T(8,128)(2,1)S(1)}, bf16[64,256]{1,0:T(8,128)(2,1)}, u32[]{:S(2)}) copy-start(bf16[64,256]{1,0:T(8,128)(2,1)} %param.11) | copy-start | bytes 98308
  8.4 2.5 %copy-start.5 = (bf16[64,32]{0,1:T(8,128)(2,1)S(1)}, bf16[64,32]{0,1:T(8,128)(2,1)}, u32[]{:S(2)}) copy-start(bf16[64,32]{0,1:T(8,128)(2,1)} %param.14) | copy-start | bytes 12292
  10.4 4.0 %copy-start.6 = (bf16[64,32]{0,1:T(8,128)(2,1)S(1)}, bf16[64,32]{0,1:T(8,128)(2,1)}, u32[]{:S(2)}) copy-start(bf16[64,32]{0,1:T(8,128)(2,1)} %param.13) | copy-start | bytes 12292
  11.3 3.9 %copy-start.3 = (f32[1024,128]{1,0:T(8,128)S(1)}, f32[1024,128]{1,0:T(8,128)}, u32[]{:S(2)}) copy-start(f32[1024,128]{1,0:T(8,128)} %param.15) | copy-start | bytes 1572868
  11.5 10.7 %collective-permute-start = (bf16[160,1024]{1,0:T(8,128)(2,1)S(1)}, bf16[160,1024]{1,0:T(8,128)(2,1)S(1)}, u32[]{:S(2)}, u32[]{:S(2)}) collective-permute-start(bf16[160,1024]{1,0:T(8,128)(2,1)S(1)} %copy.25.r_ref), channel_id=1, source_target_pairs={{0,2},{2,0},{1,3},{3,1},{4,6},{6,4},{5,7},{7,5},{8,10},{10,8},{9,1... | collective-permute-start | bytes 983048 | tf_op jit(solution)/shard_map/ppermute | solution.py:181
  27.2 17.9 %copy-start.2 = (f32[32,8,128]{2,1,0:T(8,128)S(1)}, f32[32,8,128]{2,1,0:T(8,128)}, u32[]{:S(2)}) copy-start(f32[32,8,128]{2,1,0:T(8,128)} %param.10) | copy-start | bytes 393220
  27.2 2.0 %collective-permute-start.1 = (f32[4,64,512]{2,1,0:T(8,128)S(1)}, f32[4,64,512]{2,1,0:T(8,128)S(1)}, u32[]{:S(2)}, u32[]{:S(2)}) collective-permute-start(f32[4,64,512]{2,1,0:T(8,128)S(1)} %dynamic-slice_bitcast_fusion), channel_id=1, source_target_pairs={{0,1},{1,0},{2,3},{3,2},{4,5},{5,4},{6,7},{7,6},{8,9},{9,8},{10,11... | collective-permute-start | bytes 1572872 | tf_op jit(solution)/shard_map/ppermute | solution.py:125
  27.4 18.4 %copy-start.4 = (bf16[128,512]{1,0:T(8,128)(2,1)S(1)}, bf16[128,512]{1,0:T(8,128)(2,1)}, u32[]{:S(2)}) copy-start(bf16[128,512]{1,0:T(8,128)(2,1)} %param.16) | copy-start | bytes 393220
  29.4 7.9 %collective-permute-start.4 = (f32[64,512]{1,0:T(8,128)S(1)}, f32[64,512]{1,0:T(8,128)S(1)}, u32[]{:S(2)}, u32[]{:S(2)}) collective-permute-start(f32[64,512]{1,0:T(8,128)S(1)} %get-tuple-element.5), channel_id=1, source_target_pairs={{0,12},{4,0},{8,4},{12,8},{1,13},{5,1},{9,5},{13,9},{2,14},{6,2},{... | collective-permute-start | bytes 393224 | tf_op jit(solution)/shard_map/ppermute | solution.py:134
  33.3 11.7 %collective-permute-start.3 = (f32[64,512]{1,0:T(8,128)S(1)}, f32[64,512]{1,0:T(8,128)S(1)}, u32[]{:S(2)}, u32[]{:S(2)}) collective-permute-start(f32[64,512]{1,0:T(8,128)S(1)} %get-tuple-element.6), channel_id=1, source_target_pairs={{0,8},{4,12},{8,0},{12,4},{1,9},{5,13},{9,1},{13,5},{2,10},{6,14},... | collective-permute-start | bytes 393224 | tf_op jit(solution)/shard_map/ppermute | solution.py:134
  33.3 11.7 %collective-permute-start.2 = (f32[64,512]{1,0:T(8,128)S(1)}, f32[64,512]{1,0:T(8,128)S(1)}, u32[]{:S(2)}, u32[]{:S(2)}) collective-permute-start(f32[64,512]{1,0:T(8,128)S(1)} %get-tuple-element.4), channel_id=1, source_target_pairs={{0,4},{4,8},{8,12},{12,0},{1,5},{5,9},{9,13},{13,1},{2,6},{6,10},{... | collective-permute-start | bytes 393224 | tf_op jit(solution)/shard_map/ppermute | solution.py:134

commit v7 on v6

--- a/solution.py
+++ b/solution.py
@@ -111,19 +111,18 @@
     )(lt, r_all, wh, wl)
 
 
-def reduce_over_sequences(partial_value):
-    nseq = lax.axis_size("seq")
+def chan_stage(block, chunk):
     nchan = lax.axis_size("chan")
-    if nchan != 2:
-        return lax.psum_scatter(partial_value, ("seq", "chan"), scatter_dimension=0, tiled=True)
-    rows, cols = partial_value.shape
-    chunk = rows // (nseq * nchan)
-    xs = partial_value.reshape(nseq, nchan, chunk, cols)
+    rows, cols = block.shape
+    xs = block.reshape(rows // (chunk * nchan), nchan, chunk, cols)
     c = lax.axis_index("chan")
     mine = lax.dynamic_index_in_dim(xs, c, axis=1, keepdims=False)
     other = lax.dynamic_index_in_dim(xs, 1 - c, axis=1, keepdims=False)
-    received = lax.ppermute(other, "chan", [(0, 1), (1, 0)])
-    part = mine + received
+    return mine + lax.ppermute(other, "chan", [(0, 1), (1, 0)])
+
+
+def seq_stage(part):
+    nseq = lax.axis_size("seq")
     if nseq > 4:
         gathered = lax.all_to_all(part, "seq", 0, 0, tiled=False)
         return gathered.sum(axis=0)
@@ -133,6 +132,13 @@
         src = lax.dynamic_index_in_dim(part, (me + k) % nseq, axis=0, keepdims=False)
         acc = acc + lax.ppermute(src, "seq", [(q, (q + k) % nseq) for q in range(nseq)])
     return acc
+
+
+def reduce_over_sequences(partial_value):
+    if lax.axis_size("chan") != 2:
+        return lax.psum_scatter(partial_value, ("seq", "chan"), scatter_dimension=0, tiled=True)
+    chunk = partial_value.shape[0] // (lax.axis_size("seq") * lax.axis_size("chan"))
+    return seq_stage(chan_stage(partial_value, chunk))
 
 
 def per_device(
@@ -149,26 +155,31 @@
     homologs_local_share, sites_local_share, homolog_lane_number = homolog_embedding.shape
     proj_width = lhs_projector.shape[1]
     pair_width = coupling_embedding.shape[2]
-    xt = jnp.transpose(homolog_embedding, (1, 2, 0)).astype(jnp.float32)
-    n1 = apply_layer_norm_axis1(xt).astype(jnp.bfloat16)
-    hidden = jnp.maximum(
-        jnp.einsum("kh,iks->ihs", homolog_widen_weights, n1, preferred_element_type=jnp.float32), 0.0
-    ).astype(jnp.bfloat16)
-    refreshed_t = (
-        xt + jnp.einsum("hk,ihs->iks", homolog_shrink_weights, hidden, preferred_element_type=jnp.float32)
-    ).astype(jnp.bfloat16)
-    homolog_refreshed = jnp.transpose(refreshed_t, (2, 0, 1))
-    n2 = apply_layer_norm_axis1(refreshed_t.astype(jnp.float32)).astype(jnp.bfloat16)
-    lt = (
-        jnp.einsum("kc,iks->cis", lhs_projector, n2, preferred_element_type=jnp.float32)
-        .astype(jnp.bfloat16)
-        .reshape(proj_width * sites_local_share, homologs_local_share)
-    )
-    right_features = (
-        jnp.einsum("ke,iks->sie", rhs_projector, n2, preferred_element_type=jnp.float32)
-        .astype(jnp.bfloat16)
-        .reshape(homologs_local_share, sites_local_share * proj_width)
-    )
+    xt_all = jnp.transpose(homolog_embedding, (1, 2, 0))
+    halves = 2 if sites_local_share % 16 == 0 else 1
+    step = sites_local_share // halves
+    refreshed_parts, lt_parts, right_parts = [], [], []
+    for h in range(halves):
+        xt = xt_all[h * step : (h + 1) * step].astype(jnp.float32)
+        n1 = apply_layer_norm_axis1(xt).astype(jnp.bfloat16)
+        hidden = jnp.maximum(
+            jnp.einsum("kh,iks->ihs", homolog_widen_weights, n1, preferred_element_type=jnp.float32), 0.0
+        ).astype(jnp.bfloat16)
+        refreshed_t = (
+            xt + jnp.einsum("hk,ihs->iks", homolog_shrink_weights, hidden, preferred_element_type=jnp.float32)
+        ).astype(jnp.bfloat16)
+        refreshed_parts.append(refreshed_t)
+        n2 = apply_layer_norm_axis1(refreshed_t.astype(jnp.float32)).astype(jnp.bfloat16)
+        right_parts.append(
+            jnp.einsum("ke,iks->sie", rhs_projector, n2, preferred_element_type=jnp.float32)
+            .astype(jnp.bfloat16)
+            .reshape(homologs_local_share, step * proj_width)
+        )
+        lt_parts.append(
+            jnp.einsum("kc,iks->cis", lhs_projector, n2, preferred_element_type=jnp.float32).astype(jnp.bfloat16)
+        )
+    homolog_refreshed = jnp.transpose(jnp.concatenate(refreshed_parts, axis=0), (2, 0, 1))
+    lt = jnp.concatenate(lt_parts, axis=1).reshape(proj_width * sites_local_share, homologs_local_share)
     owners = lax.axis_size(("seq", "chan"))
     depth_total = float(homologs_local_share * owners)
     block_cols = coupling_embedding.shape[1]
@@ -178,17 +189,22 @@
     w_lo = (moment_coupling_weights - w_hi_f32).astype(jnp.bfloat16)
     nres = lax.axis_size("res")
     if nres == 2:
-        r_other = lax.ppermute(right_features, "res", [(0, 1), (1, 0)])
-        p_own = outer_project(lt, right_features, w_hi, w_lo, 1.0 / depth_total)
+        r_other = jnp.concatenate([lax.ppermute(r, "res", [(0, 1), (1, 0)]) for r in right_parts], axis=1)
+        r_own = jnp.concatenate(right_parts, axis=1)
+        p_own = outer_project(lt, r_own, w_hi, w_lo, 1.0 / depth_total)
+        chunk = 2 * p_own.shape[0] // (lax.axis_size("seq") * lax.axis_size("chan"))
+        part_own = chan_stage(p_own, chunk)
         p_other = outer_project(lt, r_other, w_hi, w_lo, 1.0 / depth_total)
+        part_other = chan_stage(p_other, chunk)
         first = lax.axis_index("res") == 0
-        partial_value = jnp.where(
-            first, jnp.concatenate([p_own, p_other], axis=0), jnp.concatenate([p_other, p_own], axis=0)
-        )
+        part = jnp.where(
+            first, jnp.concatenate([part_own, part_other], axis=0), jnp.concatenate([part_other, part_own], axis=0)
+        )
+        pair_update = seq_stage(part)
     else:
-        r_all = lax.all_gather(right_features, "res", axis=1, tiled=True)
+        r_all = lax.all_gather(jnp.concatenate(right_parts, axis=1), "res", axis=1, tiled=True)
         partial_value = outer_project(lt, r_all, w_hi, w_lo, 1.0 / depth_total)
-    pair_update = reduce_over_sequences(partial_value)
+        pair_update = reduce_over_sequences(partial_value)
     nja_local = block_cols // JB
     pair_update = (
         pair_update.reshape(nja_local, sites_local_share, JB, pair_width)

time: 47.1 us -> 43.9 us (0.932)
  waiting for transfers between devices: 14.6 us -> 10.5 us
  local copies, waits for them, and re-layouts: 1.03 us -> 2.42 us
  matrix products: 6.29 us -> 5.15 us
  starting transfers between devices: 7.99 us -> 8.85 us
    ppermute x5 -> x7, waiting for transfers between devices: 14.6 us -> 10.5 us  [the longest x3 10.3 us: seq_stage(): lax.ppermute(src, 'seq', [(q, (q + k) % nseq) for q in range(nseq)])]
    reduce_sum x2 -> x1, other arithmetic: 3.6 us -> 1.53 us  [apply_layer_norm_axis1(): mean = jnp.mean(values, axis=1, keepdims=True)]
    dot_general x1 -> x2, matrix products: 4.47 us -> 3.07 us  [per_device(): jnp.einsum('hk,ihs->iks', homolog_shrink_weights, hidden, preferred_eleme...]
    reduce_sum x2 -> x3, other arithmetic: 2 us -> 0.76 us  [apply_layer_norm_axis1(): variance = jnp.mean(centred * centred, axis=1, keepdims=True)]
    transpose x0 -> x1, other arithmetic: none -> 1.14 us  [per_device(): jnp.transpose(jnp.concatenate(refreshed_parts, axis=0), (2, 0, 1))]
    concatenate x0 -> x3, other arithmetic: none -> 1.06 us  [the longest x1 0.94 us: per_device(): jnp.concatenate([lax.ppermute(r, 'res', [(0, 1), (1, 0)]) for r in right_...]
    add x2 -> x3, other arithmetic: 0.12 us -> 1.06 us  [the longest x2 1.02 us: chan_stage(): return mine + lax.ppermute(other, 'chan', [(0, 1), (1, 0)])]
    ppermute x5 -> x7, starting transfers between devices: 7.99 us -> 8.85 us  [the longest x3 5.19 us: seq_stage(): lax.ppermute(src, 'seq', [(q, (q + k) % nseq) for q in range(nseq)])]
  transfers between devices with their start and end apart: 5 -> 7, of which waited for: 4 -> 4; matrix products, arithmetic and copies ran while one was open for 2% -> 16% of each run, Pallas kernels for 10% -> 22%
where the time goes in v7:
time: 43.9 us; the launch traced here: 43.6 us
  waiting for transfers between devices  10.5 us (24%)
  Pallas kernels  9.72 us (22%)
  starting transfers between devices  8.85 us (20%)
  other arithmetic  6.02 us (14%)
  matrix products  5.15 us (12%)
  local copies, waits for them, and re-layouts  2.42 us (6%)
  between operations  1.02 us (2%)
    ppermute x3, waiting for transfers between devices, seq_stage(): lax.ppermute(src, 'seq', [(q, (q + k) % nseq) for q in range(nseq)])  10.3 us
    pallas_call x2, Pallas kernels, outer_project(): pl.pallas_call(functools.partial(outer_project_kernel, scale), grid=(step...  9.72 us
    ppermute x3, starting transfers between devices, seq_stage(): lax.ppermute(src, 'seq', [(q, (q + k) % nseq) for q in range(nseq)])  5.19 us
    ppermute x2, starting transfers between devices, per_device(): lax.ppermute(r, 'res', [(0, 1), (1, 0)])  3.09 us
    dot_general x2, matrix products, per_device(): jnp.einsum('hk,ihs->iks', homolog_shrink_weights, hidden, preferred_eleme...  3.07 us
    reduce_sum x1, other arithmetic, apply_layer_norm_axis1(): mean = jnp.mean(values, axis=1, keepdims=True)  1.53 us
    transpose x1, other arithmetic, per_device(): jnp.transpose(jnp.concatenate(refreshed_parts, axis=0), (2, 0, 1))  1.14 us
    dot_general x1, matrix products, per_device(): jnp.dot(pair_hidden, coupling_shrink_weights, preferred_element_type=jnp....  1.06 us
  transfers between devices with their start and end apart: 7, of which 4 were waited for; matrix products, arithmetic and copies ran while one was open for 16% of the time, Pallas kernels for 22%

profile of v7, /device:TPU:0, one launch (start us, length us, event | category | flops | bytes accessed | tf_op | source)
XLA Modules:
  0.0 43.6 jit_solution(11018212983953626221)
XLA Ops:
  0.6 0.0 copy-start
  0.7 1.5 %convert_reduce_fusion.1 = (f32[16,160]{1,0:T(8,128)S(1)}, f32[16,160]{1,0:T(8,128)S(1)}) fusion(bf16[32,64,160]{2,1,0:T(8,128)(2,1)} %bitcast.124), kind=kLoop, calls=%fused_computation.7 | loop fusion | flops 650240 | bytes 675840 | tf_op jit(solution)/shard_map/reduce_sum | solution.py:19
  2.2 0.0 copy-done.1
  2.2 0.4 fusion.26
  2.7 0.0 copy-start.5
  2.7 1.5 %convert_reduce_fusion.2 = (f32[16,160]{1,0:T(8,128)S(1)}, bf16[16,64,160]{2,1,0:T(8,128)(2,1)S(1)}) fusion(bf16[256,64]{0,1:T(8,128)(2,1)S(1)} %copy-done.7, f32[16,160]{1,0:T(8,128)S(1)} %add_rsqrt_fusion.2, f32[16,160]{1,0:T(8,128)S(1)} %get-tuple-element.15, bf16[32,64,160]{2,1,0:T(8,128)(2,1)S(1)} %bitcast.126, bf16[64,256]{1,0:T(8,128)(2,1)S(1)} %copy-done.8), kind=kOutput, calls=%fused_computation.15 | convolution fusion | flops 170554880 | bytes 1079296 | tf_op jit(solution)/shard_map/hk,ihs->iks/dot_general | solution.py:169
  4.2 0.2 fusion.28
  4.4 0.3 convolution_convert_fusion
  4.7 0.1 copy.31
  4.8 3.0 %collective-permute-start.2 = (bf16[160,512]{1,0:T(8,128)(2,1)S(1)}, bf16[160,512]{1,0:T(8,128)(2,1)}, u32[]{:S(2)}, u32[]{:S(2)}) collective-permute-start(bf16[160,512]{1,0:T(8,128)(2,1)S(1)} %copy.31), channel_id=1, source_target_pairs={{0,2},{2,0},{1,3},{3,1},{4,6},{6,4},{5,7},{7,5},{8,10},{10,8},{9,1... | collective-permute-start | bytes 491528 | tf_op jit(solution)/shard_map/ppermute | solution.py:192
  7.8 1.5 %convert_reduce_fusion.3 = (f32[16,160]{1,0:T(8,128)S(1)}, bf16[16,64,160]{2,1,0:T(8,128)(2,1)S(1)}) fusion(bf16[256,64]{0,1:T(8,128)(2,1)S(1)} %copy-done.7, f32[16,160]{1,0:T(8,128)S(1)} %add_rsqrt_fusion.3, f32[16,160]{1,0:T(8,128)S(1)} %get-tuple-element.16, bf16[32,64,160]{2,1,0:T(8,128)(2,1)S(1)} %bitcast.127, bf16[64,256]{1,0:T(8,128)(2,1)S(1)} %copy-done.8), kind=kOutput, calls=%fused_computation.17 | convolution fusion | flops 170554880 | bytes 1079296 | tf_op jit(solution)/shard_map/hk,ihs->iks/dot_general | solution.py:169
  9.4 0.0 copy-start.6
  9.4 0.2 fusion.30
  9.6 0.3 convolution_convert_fusion.1
  9.9 0.1 copy.30
  10.0 0.1 collective-permute-start.1
  10.1 0.3 fusion.20
  10.4 0.3 fusion.19
  10.7 0.0 copy-start.3
  10.7 0.1 pad_maximum_fusion
  10.8 0.3 copy.29
  11.1 0.6 %copy-done.3 = f32[1024,128]{1,0:T(8,128)S(1)} copy-done((f32[1024,128]{1,0:T(8,128)S(1)}, f32[1024,128]{1,0:T(8,128)}, u32[]{:S(2)}) %copy-start.3) | copy-done | bytes 524312
  11.7 0.1 fusion.36
  11.8 4.9 %shard_map.104 = f32[256,512]{1,0:T(8,128)S(1)} custom-call(bf16[1024,160]{1,0:T(8,128)(2,1)S(1)} %bitcast.122, bf16[160,1024]{1,0:T(8,128)(2,1)S(1)} %pad_maximum_fusion.1.r_ref, bf16[1024,128]{1,0:T(8,128)(2,1)S(1)} %get-tuple-element.10.wh_ref, bf16[1024,128]{1,0:T(8,128)(2,1)S(1)} %get-tuple-element.9.wl_ref), custom_call_target="tpu_custom_call" | custom-call | flops 3556769792 | bytes 1703936 | tf_op jit(solution)/shard_map/pallas_call | solution.py:88
  16.7 0.7 %dynamic-slice_bitcast_fusion.1 = f32[2,64,512]{2,1,0:T(8,128)} fusion(f32[2,2,64,512]{3,2,1,0:T(8,128)S(1)} %bitcast.118, s32[]{:T(128)S(6)} %select_n.47), kind=kLoop, calls=%fused_computation.67 | loop fusion | bytes 524292 | tf_op jit(solution)/shard_map/jit(dynamic_index_in_dim)/squeeze | solution.py:120
  17.4 0.0 collective-permute-start
  17.4 0.0 collective-permute-done.2
  17.4 0.0 collective-permute-done.1
  17.4 0.9 %pad_maximum_fusion.2.r_ref = bf16[160,1024]{1,0:T(8,128)(2,1)S(1)} fusion(bf16[160,512]{1,0:T(8,128)(2,1)} %collective-permute-done.2, bf16[160,512]{1,0:T(8,128)(2,1)S(1)} %collective-permute-done.1), kind=kLoop, calls=%fused_computation.62 | loop fusion | flops 655360 | bytes 655360 | tf_op jit(solution)/shard_map/concatenate | solution.py:192
  18.4 4.9 %shard_map.105 = f32[256,512]{1,0:T(8,128)S(1)} custom-call(bf16[1024,160]{1,0:T(8,128)(2,1)S(1)} %bitcast.123, bf16[160,1024]{1,0:T(8,128)(2,1)S(1)} %pad_maximum_fusion.2.r_ref, bf16[1024,128]{1,0:T(8,128)(2,1)S(1)} %get-tuple-element.10.wh_ref, bf16[1024,128]{1,0:T(8,128)(2,1)S(1)} %get-tuple-element.9.wl_ref), custom_call_target="tpu_custom_call" | custom-call | flops 3556769792 | bytes 1703936 | tf_op jit(solution)/shard_map/pallas_call | solution.py:88
  23.3 0.6 %collective-permute-start.3 = (f32[2,64,512]{2,1,0:T(8,128)S(1)}, f32[2,64,512]{2,1,0:T(8,128)S(1)}, u32[]{:S(2)}, u32[]{:S(2)}) collective-permute-start(f32[2,64,512]{2,1,0:T(8,128)S(1)} %dynamic-slice_bitcast_fusion), channel_id=1, source_target_pairs={{0,1},{1,0},{2,3},{3,2},{4,5},{5,4},{6,7},{7,6},{8,9},{9,8},{10,11... | collective-permute-start | bytes 786440 | tf_op jit(solution)/shard_map/ppermute | solution.py:121
  23.8 0.0 collective-permute-done
  23.8 1.0 %bitcast_add_fusion.1 = f32[2,64,512]{2,1,0:T(8,128)S(1)} fusion(f32[2,64,512]{2,1,0:T(8,128)} %collective-permute-done, f32[2,2,64,512]{3,2,1,0:T(8,128)S(1)} %bitcast.119, s32[]{:T(128)S(6)} %select_n.46), kind=kLoop, calls=%fused_computation.64 | loop fusion | flops 65536 | bytes 786436 | tf_op jit(solution)/shard_map/add | solution.py:121
  24.8 0.2 collective-permute-done.3
  25.1 2.2 %collective-permute-start.4 = (f32[64,512]{1,0:T(8,128)S(1)}, f32[64,512]{1,0:T(8,128)S(1)}, u32[]{:S(2)}, u32[]{:S(2)}) collective-permute-start(f32[64,512]{1,0:T(8,128)S(1)} %get-tuple-element.6), channel_id=1, source_target_pairs={{0,4},{4,8},{8,12},{12,0},{1,5},{5,9},{9,13},{13,1},{2,6},{6,10},{... | collective-permute-start | bytes 393224 | tf_op jit(solution)/shard_map/ppermute | solution.py:133
  27.3 2.1 %collective-permute-start.6 = (f32[64,512]{1,0:T(8,128)S(1)}, f32[64,512]{1,0:T(8,128)S(1)}, u32[]{:S(2)}, u32[]{:S(2)}) collective-permute-start(f32[64,512]{1,0:T(8,128)S(1)} %get-tuple-element.7), channel_id=1, source_target_pairs={{0,12},{4,0},{8,4},{12,8},{1,13},{5,1},{9,5},{13,9},{2,14},{6,2},{... | collective-permute-start | bytes 393224 | tf_op jit(solution)/shard_map/ppermute | solution.py:133
  29.4 0.9 %collective-permute-start.5 = (f32[64,512]{1,0:T(8,128)S(1)}, f32[64,512]{1,0:T(8,128)S(1)}, u32[]{:S(2)}, u32[]{:S(2)}) collective-permute-start(f32[64,512]{1,0:T(8,128)S(1)} %get-tuple-element.8), channel_id=1, source_target_pairs={{0,8},{4,12},{8,0},{12,4},{1,9},{5,13},{9,1},{13,5},{2,10},{6,14},... | collective-permute-start | bytes 393224 | tf_op jit(solution)/shard_map/ppermute | solution.py:133
  30.3 1.1 %maximum_bitcast_fusion = bf16[160,32,64]{0,2,1:T(8,128)(2,1)} fusion(bf16[16,64,160]{2,1,0:T(8,128)(2,1)S(1)} %get-tuple-element.12, bf16[16,64,160]{2,1,0:T(8,128)(2,1)S(1)} %get-tuple-element.14), kind=kLoop, calls=%fused_computation.49 | loop fusion | flops 327680 | bytes 1310720 | tf_op jit(solution)/shard_map/transpose | solution.py:181
  31.5 2.2 %collective-permute-done.4 = f32[64,512]{1,0:T(8,128)S(1)} collective-permute-done((f32[64,512]{1,0:T(8,128)S(1)}, f32[64,512]{1,0:T(8,128)S(1)}, u32[]{:S(2)}, u32[]{:S(2)}) %collective-permute-start.4) | collective-permute-done | bytes 131104 | tf_op jit(solution)/shard_map/ppermute | solution.py:133
  33.7 1.9 %collective-permute-done.6 = f32[64,512]{1,0:T(8,128)S(1)} collective-permute-done((f32[64,512]{1,0:T(8,128)S(1)}, f32[64,512]{1,0:T(8,128)S(1)}, u32[]{:S(2)}, u32[]{:S(2)}) %collective-permute-start.6) | collective-permute-done | bytes 131104 | tf_op jit(solution)/shard_map/ppermute | solution.py:133
  35.6 6.2 %collective-permute-done.5 = f32[64,512]{1,0:T(8,128)S(1)} collective-permute-done((f32[64,512]{1,0:T(8,128)S(1)}, f32[64,512]{1,0:T(8,128)S(1)}, u32[]{:S(2)}, u32[]{:S(2)}) %collective-permute-start.5) | collective-permute-done | bytes 131104 | tf_op jit(solution)/shard_map/ppermute | solution.py:133
  41.9 0.1 fusion.60
  42.0 0.2 multiply_reduce_fusion
  42.2 0.1 copy.37
  42.3 0.1 copy.38
  42.4 0.1 rsqrt.48
  42.5 0.1 div.41
  42.6 1.1 %fusion.23 = f32[32,8,128]{2,1,0:T(8,128)} fusion(bf16[512,128]{1,0:T(8,128)(2,1)S(1)} %copy-done, bf16[128,512]{1,0:T(8,128)(2,1)S(1)} %copy-done.4, f32[256,128]{1,0:T(8,128)S(1)} %bitcast.134, f32[32,8,128]{2,1,0:T(8,128)S(1)} %copy-done.2, f32[256]{0:T(256)S(1)} %rsqrt.48, f32[256]{0:T(256)S(1)} %div.41), kind=kOutput, calls=%fused_computation.40 | convolution fusion | flops 67567616 | bytes 657408 | tf_op jit(solution)/shard_map/dot_general | solution.py:219
  (30 shorter events, 0.4 us)
Async XLA Ops:
  0.6 41.9 %copy-start = (bf16[512,128]{1,0:T(8,128)(2,1)S(1)}, bf16[512,128]{1,0:T(8,128)(2,1)}, u32[]{:S(2)}) copy-start(bf16[512,128]{1,0:T(8,128)(2,1)} %param.17) | copy-start | bytes 393220
  0.6 1.6 %copy-start.1 = (bf16[160,32,64]{0,2,1:T(8,128)(2,1)S(1)}, bf16[160,32,64]{0,2,1:T(8,128)(2,1)}, u32[]{:S(2)}) copy-start(bf16[160,32,64]{0,2,1:T(8,128)(2,1)} %param.9) | copy-start | bytes 1966084
  0.7 2.0 %copy-start.7 = (bf16[256,64]{0,1:T(8,128)(2,1)S(1)}, bf16[256,64]{0,1:T(8,128)(2,1)}, u32[]{:S(2)}) copy-start(bf16[256,64]{0,1:T(8,128)(2,1)} %param.12) | copy-start | bytes 98308
  0.7 2.0 %copy-start.8 = (bf16[64,256]{1,0:T(8,128)(2,1)S(1)}, bf16[64,256]{1,0:T(8,128)(2,1)}, u32[]{:S(2)}) copy-start(bf16[64,256]{1,0:T(8,128)(2,1)} %param.11) | copy-start | bytes 98308
  2.7 1.8 %copy-start.5 = (bf16[64,32]{0,1:T(8,128)(2,1)S(1)}, bf16[64,32]{0,1:T(8,128)(2,1)}, u32[]{:S(2)}) copy-start(bf16[64,32]{0,1:T(8,128)(2,1)} %param.14) | copy-start | bytes 12292
  4.8 12.6 %collective-permute-start.2 = (bf16[160,512]{1,0:T(8,128)(2,1)S(1)}, bf16[160,512]{1,0:T(8,128)(2,1)}, u32[]{:S(2)}, u32[]{:S(2)}) collective-permute-start(bf16[160,512]{1,0:T(8,128)(2,1)S(1)} %copy.31), channel_id=1, source_target_pairs={{0,2},{2,0},{1,3},{3,1},{4,6},{6,4},{5,7},{7,5},{8,10},{10,8},{9,1... | collective-permute-start | bytes 491528 | tf_op jit(solution)/shard_map/ppermute | solution.py:192
  9.4 0.7 %copy-start.6 = (bf16[64,32]{0,1:T(8,128)(2,1)S(1)}, bf16[64,32]{0,1:T(8,128)(2,1)}, u32[]{:S(2)}) copy-start(bf16[64,32]{0,1:T(8,128)(2,1)} %param.13) | copy-start | bytes 12292
  10.0 7.4 %collective-permute-start.1 = (bf16[160,512]{1,0:T(8,128)(2,1)S(1)}, bf16[160,512]{1,0:T(8,128)(2,1)S(1)}, u32[]{:S(2)}, u32[]{:S(2)}) collective-permute-start(bf16[160,512]{1,0:T(8,128)(2,1)S(1)} %copy.30), channel_id=1, source_target_pairs={{0,2},{2,0},{1,3},{3,1},{4,6},{6,4},{5,7},{7,5},{8,10},{10,8},{9,1... | collective-permute-start | bytes 491528 | tf_op jit(solution)/shard_map/ppermute | solution.py:192
  10.7 1.0 %copy-start.3 = (f32[1024,128]{1,0:T(8,128)S(1)}, f32[1024,128]{1,0:T(8,128)}, u32[]{:S(2)}) copy-start(f32[1024,128]{1,0:T(8,128)} %param.15) | copy-start | bytes 1572868
  17.4 6.4 %collective-permute-start = (f32[2,64,512]{2,1,0:T(8,128)}, f32[2,64,512]{2,1,0:T(8,128)}, u32[]{:S(2)}, u32[]{:S(2)}) collective-permute-start(f32[2,64,512]{2,1,0:T(8,128)} %dynamic-slice_bitcast_fusion.1), channel_id=1, source_target_pairs={{0,1},{1,0},{2,3},{3,2},{4,5},{5,4},{6,7},{7,6},{8,9},{9,8},{10,11... | collective-permute-start | bytes 786440 | tf_op jit(solution)/shard_map/ppermute | solution.py:121
  23.3 1.7 %collective-permute-start.3 = (f32[2,64,512]{2,1,0:T(8,128)S(1)}, f32[2,64,512]{2,1,0:T(8,128)S(1)}, u32[]{:S(2)}, u32[]{:S(2)}) collective-permute-start(f32[2,64,512]{2,1,0:T(8,128)S(1)} %dynamic-slice_bitcast_fusion), channel_id=1, source_target_pairs={{0,1},{1,0},{2,3},{3,2},{4,5},{5,4},{6,7},{7,6},{8,9},{9,8},{10,11... | collective-permute-start | bytes 786440 | tf_op jit(solution)/shard_map/ppermute | solution.py:121
  25.1 8.6 %collective-permute-start.4 = (f32[64,512]{1,0:T(8,128)S(1)}, f32[64,512]{1,0:T(8,128)S(1)}, u32[]{:S(2)}, u32[]{:S(2)}) collective-permute-start(f32[64,512]{1,0:T(8,128)S(1)} %get-tuple-element.6), channel_id=1, source_target_pairs={{0,4},{4,8},{8,12},{12,0},{1,5},{5,9},{9,13},{13,1},{2,6},{6,10},{... | collective-permute-start | bytes 393224 | tf_op jit(solution)/shard_map/ppermute | solution.py:133
  27.3 8.3 %collective-permute-start.6 = (f32[64,512]{1,0:T(8,128)S(1)}, f32[64,512]{1,0:T(8,128)S(1)}, u32[]{:S(2)}, u32[]{:S(2)}) collective-permute-start(f32[64,512]{1,0:T(8,128)S(1)} %get-tuple-element.7), channel_id=1, source_target_pairs={{0,12},{4,0},{8,4},{12,8},{1,13},{5,1},{9,5},{13,9},{2,14},{6,2},{... | collective-permute-start | bytes 393224 | tf_op jit(solution)/shard_map/ppermute | solution.py:133
  29.4 12.4 %collective-permute-start.5 = (f32[64,512]{1,0:T(8,128)S(1)}, f32[64,512]{1,0:T(8,128)S(1)}, u32[]{:S(2)}, u32[]{:S(2)}) collective-permute-start(f32[64,512]{1,0:T(8,128)S(1)} %get-tuple-element.8), channel_id=1, source_target_pairs={{0,8},{4,12},{8,0},{12,4},{1,9},{5,13},{9,1},{13,5},{2,10},{6,14},... | collective-permute-start | bytes 393224 | tf_op jit(solution)/shard_map/ppermute | solution.py:133
  31.5 10.4 %copy-start.2 = (f32[32,8,128]{2,1,0:T(8,128)S(1)}, f32[32,8,128]{2,1,0:T(8,128)}, u32[]{:S(2)}) copy-start(f32[32,8,128]{2,1,0:T(8,128)} %param.10) | copy-start | bytes 393220
  31.5 11.1 %copy-start.4 = (bf16[128,512]{1,0:T(8,128)(2,1)S(1)}, bf16[128,512]{1,0:T(8,128)(2,1)}, u32[]{:S(2)}) copy-start(bf16[128,512]{1,0:T(8,128)(2,1)} %param.16) | copy-start | bytes 393220

commit v8 on v7

--- a/solution.py
+++ b/solution.py
@@ -27,24 +27,25 @@
 JB = 4
 
 
-def outer_project_kernel(scale, lt_ref, r_ref, wh_ref, wl_ref, o_ref, vh_ref, vl_ref):
+def outer_project_kernel(scale, build, lt_ref, r_ref, wh_ref, wl_ref, o_ref, vh_ref, vl_ref):
     width = wh_ref.shape[0] // (C_HI * C_LO)
     rows_i = lt_ref.shape[0] // (C_HI * C_LO)
     lanes = JB * width
     nja = r_ref.shape[1] // lanes
     dd = wh_ref.shape[1]
 
-    @pl.when(pl.program_id(0) == 0)
-    def _build():
-        vh_ref[...] = jnp.zeros_like(vh_ref)
-        vl_ref[...] = jnp.zeros_like(vl_ref)
-        for c_hi in range(C_HI):
-            for c_lo in range(C_LO):
-                src = (c_hi * C_LO + c_lo) * width
-                for jb in range(JB):
-                    row = c_lo * lanes + jb * width
-                    vh_ref[c_hi, row : row + width, jb * dd : (jb + 1) * dd] = wh_ref[src : src + width, :]
-                    vl_ref[c_hi, row : row + width, jb * dd : (jb + 1) * dd] = wl_ref[src : src + width, :]
+    if build:
+        @pl.when(pl.program_id(0) == 0)
+        def _build():
+            vh_ref[...] = jnp.zeros_like(vh_ref)
+            vl_ref[...] = jnp.zeros_like(vl_ref)
+            for c_hi in range(C_HI):
+                for c_lo in range(C_LO):
+                    src = (c_hi * C_LO + c_lo) * width
+                    for jb in range(JB):
+                        row = c_lo * lanes + jb * width
+                        vh_ref[c_hi, row : row + width, jb * dd : (jb + 1) * dd] = wh_ref[src : src + width, :]
+                        vl_ref[c_hi, row : row + width, jb * dd : (jb + 1) * dd] = wl_ref[src : src + width, :]
 
     def rearrange(y):
         return jnp.concatenate(
@@ -73,7 +74,7 @@
     o_ref[...] = acc * scale
 
 
-def outer_project(lt, r_all, wh, wl, scale):
+def outer_project(lt, r_all, wh, wl, scale, weights=None):
     rows_i = lt.shape[0] // (C_HI * C_LO)
     width = wh.shape[0] // (C_HI * C_LO)
     lanes = JB * width
@@ -85,31 +86,47 @@
     d = wh.shape[1]
     s = lt.shape[1]
     flops = 2 * lt.shape[0] * s * total_lanes + 3 * 2 * out_rows * (C_LO * lanes) * (JB * d) * C_HI
-    return pl.pallas_call(
-        functools.partial(outer_project_kernel, scale),
+    v_shape = jax.ShapeDtypeStruct((C_HI, C_LO * lanes, JB * d), jnp.bfloat16)
+    vmem = pl.BlockSpec(memory_space=pltpu.VMEM)
+    in_specs = [
+        pl.BlockSpec(lt.shape, lambda q: (0, 0)),
+        pl.BlockSpec((s, chunk), lambda q: (0, q)),
+        pl.BlockSpec(wh.shape, lambda q: (0, 0)),
+        pl.BlockSpec(wl.shape, lambda q: (0, 0)),
+    ]
+    out_block = pl.BlockSpec((nja_chunk * rows_i, JB * d), lambda q: (q, 0))
+    out_shape = jax.ShapeDtypeStruct((out_rows, JB * d), jnp.float32)
+    params = pltpu.CompilerParams(dimension_semantics=("arbitrary",), vmem_limit_bytes=48 * 1024 * 1024)
+    cost = pl.CostEstimate(
+        flops=flops,
+        transcendentals=0,
+        bytes_accessed=lt.size * 2 + r_all.size * 2 + wh.size * 4 + out_rows * JB * d * 4,
+    )
+    if weights is None:
+        out, vh, vl = pl.pallas_call(
+            functools.partial(outer_project_kernel, scale, True),
+            grid=(steps,),
+            in_specs=in_specs,
+            out_specs=(out_block, vmem, vmem),
+            out_shape=(out_shape, v_shape, v_shape),
+            compiler_params=params,
+            cost_estimate=cost,
+        )(lt, r_all, wh, wl)
+        return out, (vh, vl)
+
+    def kernel(lt_ref, r_ref, wh_ref, wl_ref, vh_ref, vl_ref, o_ref):
+        outer_project_kernel(scale, False, lt_ref, r_ref, wh_ref, wl_ref, o_ref, vh_ref, vl_ref)
+
+    out = pl.pallas_call(
+        kernel,
         grid=(steps,),
-        in_specs=[
-            pl.BlockSpec(lt.shape, lambda q: (0, 0)),
-            pl.BlockSpec((s, chunk), lambda q: (0, q)),
-            pl.BlockSpec(wh.shape, lambda q: (0, 0)),
-            pl.BlockSpec(wl.shape, lambda q: (0, 0)),
-        ],
-        out_specs=pl.BlockSpec((nja_chunk * rows_i, JB * d), lambda q: (q, 0)),
-        out_shape=jax.ShapeDtypeStruct((out_rows, JB * d), jnp.float32),
-        scratch_shapes=[
-            pltpu.VMEM((C_HI, C_LO * lanes, JB * d), jnp.bfloat16),
-            pltpu.VMEM((C_HI, C_LO * lanes, JB * d), jnp.bfloat16),
-        ],
-        compiler_params=pltpu.CompilerParams(
-            dimension_semantics=("arbitrary",), vmem_limit_bytes=48 * 1024 * 1024
-        ),
-        cost_estimate=pl.CostEstimate(
-            flops=flops,
-            transcendentals=0,
-            bytes_accessed=lt.size * 2 + r_all.size * 2 + wh.size * 4 + out_rows * JB * d * 4,
-        ),
-    )(lt, r_all, wh, wl)
-
+        in_specs=in_specs + [vmem, vmem],
+        out_specs=out_block,
+        out_shape=out_shape,
+        compiler_params=params,
+        cost_estimate=cost,
+    )(lt, r_all, wh, wl, *weights)
+    return out, weights
 
 def chan_stage(block, chunk):
     nchan = lax.axis_size("chan")
@@ -191,10 +208,10 @@
     if nres == 2:
         r_other = jnp.concatenate([lax.ppermute(r, "res", [(0, 1), (1, 0)]) for r in right_parts], axis=1)
         r_own = jnp.concatenate(right_parts, axis=1)
-        p_own = outer_project(lt, r_own, w_hi, w_lo, 1.0 / depth_total)
+        p_own, weights = outer_project(lt, r_own, w_hi, w_lo, 1.0 / depth_total)
         chunk = 2 * p_own.shape[0] // (lax.axis_size("seq") * lax.axis_size("chan"))
         part_own = chan_stage(p_own, chunk)
-        p_other = outer_project(lt, r_other, w_hi, w_lo, 1.0 / depth_total)
+        p_other, _ = outer_project(lt, r_other, w_hi, w_lo, 1.0 / depth_total, weights)
         part_other = chan_stage(p_other, chunk)
         first = lax.axis_index("res") == 0
         part = jnp.where(
@@ -203,7 +220,7 @@
         pair_update = seq_stage(part)
     else:
         r_all = lax.all_gather(jnp.concatenate(right_parts, axis=1), "res", axis=1, tiled=True)
-        partial_value = outer_project(lt, r_all, w_hi, w_lo, 1.0 / depth_total)
+        partial_value, _ = outer_project(lt, r_all, w_hi, w_lo, 1.0 / depth_total)
         pair_update = reduce_over_sequences(partial_value)
     nja_local = block_cols // JB
     pair_update = (

time: 43.9 us -> 53.8 us (1.23)
  Pallas kernels: 9.72 us -> 13.6 us
  local copies, waits for them, and re-layouts: 2.42 us -> 5.23 us
  other arithmetic: 6.02 us -> 8.21 us
  matrix products: 5.15 us -> 6.46 us
    pallas_call x2, Pallas kernels: 9.72 us -> 13.6 us  [the longest x1 6.81 us: outer_project(): pl.pallas_call(kernel, grid=(steps,), in_specs=in_specs + [vmem, vmem], o...]
    unnamed x18 -> x20, local copies, waits for them, and re-layouts: 0.68 us -> 4.2 us
    dot_general x2, matrix products: 3.07 us -> 4.38 us  [per_device(): jnp.einsum('hk,ihs->iks', homolog_shrink_weights, hidden, preferred_eleme...]
    reduce_sum x3, other arithmetic: 0.76 us -> 1.96 us  [apply_layer_norm_axis1(): variance = jnp.mean(centred * centred, axis=1, keepdims=True)]
    convert_element_type x1, other arithmetic: 0.09 us -> 1.13 us  [per_device(): w_lo = (moment_coupling_weights - w_hi_f32).astype(jnp.bfloat16)]
    squeeze x2, local copies, waits for them, and re-layouts: 0.75 us -> 0.05 us  [chan_stage(): other = lax.dynamic_index_in_dim(xs, 1 - c, axis=1, keepdims=False)]
  transfers between devices with their start and end apart: 7 -> 7, of which waited for: 4 -> 3; matrix products, arithmetic and copies ran while one was open for 16% -> 14% of each run, Pallas kernels for 22% -> 25%
where the time goes in v8:
time: 53.8 us; the launch traced here: 53.5 us
  Pallas kernels  13.6 us (25%)
  waiting for transfers between devices  10 us (19%)
  starting transfers between devices  8.9 us (17%)
  other arithmetic  8.21 us (15%)
  matrix products  6.46 us (12%)
  local copies, waits for them, and re-layouts  5.23 us (10%)
  between operations  1.05 us (2%)
    ppermute x3, waiting for transfers between devices, seq_stage(): lax.ppermute(src, 'seq', [(q, (q + k) % nseq) for q in range(nseq)])  9.84 us
    pallas_call x1, Pallas kernels, outer_project(): pl.pallas_call(kernel, grid=(steps,), in_specs=in_specs + [vmem, vmem], o...  6.81 us
    pallas_call x1, Pallas kernels, outer_project(): pl.pallas_call(functools.partial(outer_project_kernel, scale, True), grid...  6.79 us
    ppermute x3, starting transfers between devices, seq_stage(): lax.ppermute(src, 'seq', [(q, (q + k) % nseq) for q in range(nseq)])  5.2 us
    dot_general x2, matrix products, per_device(): jnp.einsum('hk,ihs->iks', homolog_shrink_weights, hidden, preferred_eleme...  4.38 us
    unnamed x20, local copies, waits for them, and re-layouts  4.2 us
    ppermute x2, starting transfers between devices, per_device(): lax.ppermute(r, 'res', [(0, 1), (1, 0)])  3.09 us
    reduce_sum x3, other arithmetic, apply_layer_norm_axis1(): variance = jnp.mean(centred * centred, axis=1, keepdims=True)  1.96 us
  transfers between devices with their start and end apart: 7, of which 3 were waited for; matrix products, arithmetic and copies ran while one was open for 14% of the time, Pallas kernels for 25%

profile of v8, /device:TPU:0, one launch (start us, length us, event | category | flops | bytes accessed | tf_op | source)
XLA Modules:
  0.0 53.5 jit_solution(14150264413287810168)
XLA Ops:
  0.6 0.0 copy-start
  0.6 1.5 %convert_reduce_fusion.1 = (f32[16,160]{1,0:T(8,128)S(1)}, f32[16,160]{1,0:T(8,128)S(1)}) fusion(bf16[32,64,160]{2,1,0:T(8,128)(2,1)} %bitcast.124), kind=kLoop, calls=%fused_computation.7 | loop fusion | flops 650240 | bytes 675840 | tf_op jit(solution)/shard_map/reduce_sum | solution.py:19
  2.1 0.0 copy-start.6
  2.1 1.6 %fusion.26 = (f32[16,160]{1,0:T(8,128)S(1)}, f32[16,160]{1,0:T(8,128)S(1)}) fusion(f32[16,160]{1,0:T(8,128)S(1)} %get-tuple-element.22, bf16[32,64,160]{2,1,0:T(8,128)(2,1)} %bitcast.125, f32[16,160]{1,0:T(8,128)S(1)} %get-tuple-element.21), kind=kLoop, calls=%fused_computation.43 | loop fusion | flops 1305600 | bytes 696320 | tf_op jit(solution)/shard_map/reduce_sum | solution.py:21
  3.8 0.0 copy-start.3
  3.8 0.0 copy-start.8
  3.8 0.0 copy-start.9
  3.8 2.9 %convert_reduce_fusion.2 = (f32[16,160]{1,0:T(8,128)S(1)}, bf16[16,64,160]{2,1,0:T(8,128)(2,1)S(1)}) fusion(bf16[256,64]{0,1:T(8,128)(2,1)} %param.12, f32[16,160]{1,0:T(8,128)S(1)} %add_rsqrt_fusion.2, f32[16,160]{1,0:T(8,128)S(1)} %get-tuple-element.21, bf16[32,64,160]{2,1,0:T(8,128)(2,1)} %bitcast.126, bf16[64,256]{1,0:T(8,128)(2,1)} %param.11), kind=kOutput, calls=%fused_computation.15 | convolution fusion | flops 170554880 | bytes 1079296 | tf_op jit(solution)/shard_map/hk,ihs->iks/dot_general | solution.py:186
  6.7 0.2 fusion.28
  6.9 0.3 convolution_convert_fusion
  7.1 0.1 copy.31
  7.3 3.0 %collective-permute-start.2 = (bf16[160,512]{1,0:T(8,128)(2,1)S(1)}, bf16[160,512]{1,0:T(8,128)(2,1)}, u32[]{:S(2)}, u32[]{:S(2)}) collective-permute-start(bf16[160,512]{1,0:T(8,128)(2,1)S(1)} %copy.31), channel_id=1, source_target_pairs={{0,2},{2,0},{1,3},{3,1},{4,6},{6,4},{5,7},{7,5},{8,10},{10,8},{9,1... | collective-permute-start | bytes 491528 | tf_op jit(solution)/shard_map/ppermute | solution.py:209
  10.3 0.0 copy-start.7
  10.3 1.5 %convert_reduce_fusion.3 = (f32[16,160]{1,0:T(8,128)S(1)}, bf16[16,64,160]{2,1,0:T(8,128)(2,1)S(1)}) fusion(bf16[256,64]{0,1:T(8,128)(2,1)S(1)} %copy-done.8, f32[16,160]{1,0:T(8,128)S(1)} %add_rsqrt_fusion.3, f32[16,160]{1,0:T(8,128)S(1)} %get-tuple-element.22, bf16[32,64,160]{2,1,0:T(8,128)(2,1)S(1)} %bitcast.127, bf16[64,256]{1,0:T(8,128)(2,1)S(1)} %copy-done.9), kind=kOutput, calls=%fused_computation.17 | convolution fusion | flops 170554880 | bytes 1079296 | tf_op jit(solution)/shard_map/hk,ihs->iks/dot_general | solution.py:186
  11.9 0.2 fusion.30
  12.1 0.3 convolution_convert_fusion.1
  12.3 0.1 copy.30
  12.5 0.1 collective-permute-start.1
  12.6 0.3 fusion.20
  12.8 0.3 fusion.19
  13.1 0.1 pad_maximum_fusion
  13.2 0.3 copy.29
  13.5 1.1 %fusion.36 = (bf16[1024,128]{1,0:T(8,128)(2,1)S(1)}, bf16[1024,128]{1,0:T(8,128)(2,1)S(1)}) fusion(f32[1024,128]{1,0:T(8,128)} %param.15), kind=kLoop, calls=%fused_computation.52 | loop fusion | flops 524288 | bytes 1048576 | tf_op jit(solution)/shard_map/convert_element_type | solution.py:206
  14.6 6.8 %shard_map.104 = (f32[256,512]{1,0:T(8,128)S(1)}, bf16[8,512,512]{2,1,0:T(8,128)(2,1)S(1)}, bf16[8,512,512]{2,1,0:T(8,128)(2,1)}) custom-call(bf16[1024,160]{1,0:T(8,128)(2,1)S(1)} %bitcast.122, bf16[160,1024]{1,0:T(8,128)(2,1)S(1)} %pad_maximum_fusion.1.r_ref, bf16[1024,128]{1,0:T(8,128)(2,1)S(1)} %get-tuple-element.16.wh_ref, ...), custom_call_target="tpu_custom_call" | custom-call | flops 3556769792 | bytes 1703936 | tf_op jit(solution)/shard_map/pallas_call | solution.py:106
  21.4 2.0 %copy-done.1 = bf16[8,512,512]{2,1,0:T(8,128)(2,1)} copy-done((bf16[8,512,512]{2,1,0:T(8,128)(2,1)}, bf16[8,512,512]{2,1,0:T(8,128)(2,1)S(1)}, u32[]{:S(2)}) %copy-start.1) | copy-done | bytes 4194328
  23.4 0.1 collective-permute-start
  23.5 0.0 collective-permute-done.2
  23.5 0.9 %pad_maximum_fusion.2.r_ref = bf16[160,1024]{1,0:T(8,128)(2,1)S(1)} fusion(bf16[160,512]{1,0:T(8,128)(2,1)} %collective-permute-done.2, bf16[160,512]{1,0:T(8,128)(2,1)S(1)} %collective-permute-done.1), kind=kLoop, calls=%fused_computation.62 | loop fusion | flops 655360 | bytes 655360 | tf_op jit(solution)/shard_map/concatenate | solution.py:209
  24.5 2.2 %copy-done.2 = bf16[8,512,512]{2,1,0:T(8,128)(2,1)S(1)} copy-done((bf16[8,512,512]{2,1,0:T(8,128)(2,1)S(1)}, bf16[8,512,512]{2,1,0:T(8,128)(2,1)}, u32[]{:S(2)}) %copy-start.2) | copy-done | bytes 4194328
  26.7 6.8 %shard_map.105 = f32[256,512]{1,0:T(8,128)S(1)} custom-call(bf16[1024,160]{1,0:T(8,128)(2,1)S(1)} %bitcast.123, bf16[160,1024]{1,0:T(8,128)(2,1)S(1)} %pad_maximum_fusion.2.r_ref, bf16[1024,128]{1,0:T(8,128)(2,1)S(1)} %get-tuple-element.16.wh_ref, bf16[1024,128]{1,0:T(8,128)(2,1)S(1)} %get-tuple-element.15.wl_ref, bf16[8,512,512]{2,1,0:T(8,128)(2,1)S(1)} %copy-done.2, ...), custom_call_target="tpu_custom_call" | custom-call | flops 3556769792 | bytes 1703936 | tf_op jit(solution)/shard_map/pallas_call | solution.py:120
  33.5 0.5 %collective-permute-start.3 = (f32[2,64,512]{2,1,0:T(8,128)S(1)}, f32[2,64,512]{2,1,0:T(8,128)S(1)}, u32[]{:S(2)}, u32[]{:S(2)}) collective-permute-start(f32[2,64,512]{2,1,0:T(8,128)S(1)} %dynamic-slice_bitcast_fusion), channel_id=1, source_target_pairs={{0,1},{1,0},{2,3},{3,2},{4,5},{5,4},{6,7},{7,6},{8,9},{9,8},{10,11... | collective-permute-start | bytes 786440 | tf_op jit(solution)/shard_map/ppermute | solution.py:138
  34.1 1.0 %bitcast_add_fusion.1 = f32[2,64,512]{2,1,0:T(8,128)S(1)} fusion(f32[2,64,512]{2,1,0:T(8,128)} %collective-permute-done, f32[2,2,64,512]{3,2,1,0:T(8,128)S(1)} %bitcast.119, s32[]{:T(128)S(6)} %select_n.46), kind=kLoop, calls=%fused_computation.64 | loop fusion | flops 65536 | bytes 786436 | tf_op jit(solution)/shard_map/add | solution.py:138
  35.0 0.2 collective-permute-done.3
  35.3 0.0 copy-start.4
  35.3 0.0 copy-start.5
  35.4 4.2 %collective-permute-start.6 = (f32[64,512]{1,0:T(8,128)S(1)}, f32[64,512]{1,0:T(8,128)S(1)}, u32[]{:S(2)}, u32[]{:S(2)}) collective-permute-start(f32[64,512]{1,0:T(8,128)S(1)} %get-tuple-element.13), channel_id=1, source_target_pairs={{0,12},{4,0},{8,4},{12,8},{1,13},{5,1},{9,5},{13,9},{2,14},{6,2},{... | collective-permute-start | bytes 393224 | tf_op jit(solution)/shard_map/ppermute | solution.py:150
  39.6 1.0 %collective-permute-start.4 = (f32[64,512]{1,0:T(8,128)S(1)}, f32[64,512]{1,0:T(8,128)S(1)}, u32[]{:S(2)}, u32[]{:S(2)}) collective-permute-start(f32[64,512]{1,0:T(8,128)S(1)} %get-tuple-element.12), channel_id=1, source_target_pairs={{0,4},{4,8},{8,12},{12,0},{1,5},{5,9},{9,13},{13,1},{2,6},{6,10},{... | collective-permute-start | bytes 393224 | tf_op jit(solution)/shard_map/ppermute | solution.py:150
  40.6 1.1 %maximum_bitcast_fusion = bf16[160,32,64]{0,2,1:T(8,128)(2,1)} fusion(bf16[16,64,160]{2,1,0:T(8,128)(2,1)S(1)} %get-tuple-element.18, bf16[16,64,160]{2,1,0:T(8,128)(2,1)S(1)} %get-tuple-element.20), kind=kLoop, calls=%fused_computation.49 | loop fusion | flops 327680 | bytes 1310720 | tf_op jit(solution)/shard_map/transpose | solution.py:198
  41.7 1.8 %collective-permute-done.6 = f32[64,512]{1,0:T(8,128)S(1)} collective-permute-done((f32[64,512]{1,0:T(8,128)S(1)}, f32[64,512]{1,0:T(8,128)S(1)}, u32[]{:S(2)}, u32[]{:S(2)}) %collective-permute-start.6) | collective-permute-done | bytes 131104 | tf_op jit(solution)/shard_map/ppermute | solution.py:150
  43.5 8.1 %collective-permute-done.5 = f32[64,512]{1,0:T(8,128)S(1)} collective-permute-done((f32[64,512]{1,0:T(8,128)S(1)}, f32[64,512]{1,0:T(8,128)S(1)}, u32[]{:S(2)}, u32[]{:S(2)}) %collective-permute-start.5) | collective-permute-done | bytes 131104 | tf_op jit(solution)/shard_map/ppermute | solution.py:150
  51.6 0.0 collective-permute-done.4
  51.7 0.1 fusion.60
  51.8 0.2 multiply_reduce_fusion
  52.0 0.1 copy.37
  52.1 0.1 copy.38
  52.2 0.1 rsqrt.48
  52.3 0.1 div.41
  52.4 1.1 %fusion.23 = f32[32,8,128]{2,1,0:T(8,128)} fusion(bf16[512,128]{1,0:T(8,128)(2,1)S(1)} %copy-done, bf16[128,512]{1,0:T(8,128)(2,1)S(1)} %copy-done.5, f32[256,128]{1,0:T(8,128)S(1)} %bitcast.134, f32[32,8,128]{2,1,0:T(8,128)S(1)} %copy-done.4, f32[256]{0:T(256)S(1)} %rsqrt.48, f32[256]{0:T(256)S(1)} %div.41), kind=kOutput, calls=%fused_computation.40 | convolution fusion | flops 67567616 | bytes 657408 | tf_op jit(solution)/shard_map/dot_general | solution.py:236
  (32 shorter events, 0.4 us)
Async XLA Ops:
  0.6 51.7 %copy-start = (bf16[512,128]{1,0:T(8,128)(2,1)S(1)}, bf16[512,128]{1,0:T(8,128)(2,1)}, u32[]{:S(2)}) copy-start(bf16[512,128]{1,0:T(8,128)(2,1)} %param.17) | copy-start | bytes 393220
  2.1 4.7 %copy-start.6 = (bf16[64,32]{0,1:T(8,128)(2,1)S(1)}, bf16[64,32]{0,1:T(8,128)(2,1)}, u32[]{:S(2)}) copy-start(bf16[64,32]{0,1:T(8,128)(2,1)} %param.14) | copy-start | bytes 12292
  3.8 6.5 %copy-start.3 = (bf16[160,32,64]{0,2,1:T(8,128)(2,1)S(1)}, bf16[160,32,64]{0,2,1:T(8,128)(2,1)}, u32[]{:S(2)}) copy-start(bf16[160,32,64]{0,2,1:T(8,128)(2,1)} %param.9) | copy-start | bytes 1966084
  3.8 6.5 %copy-start.8 = (bf16[256,64]{0,1:T(8,128)(2,1)S(1)}, bf16[256,64]{0,1:T(8,128)(2,1)}, u32[]{:S(2)}) copy-start(bf16[256,64]{0,1:T(8,128)(2,1)} %param.12) | copy-start | bytes 98308
  3.8 6.5 %copy-start.9 = (bf16[64,256]{1,0:T(8,128)(2,1)S(1)}, bf16[64,256]{1,0:T(8,128)(2,1)}, u32[]{:S(2)}) copy-start(bf16[64,256]{1,0:T(8,128)(2,1)} %param.11) | copy-start | bytes 98308
  7.3 16.2 %collective-permute-start.2 = (bf16[160,512]{1,0:T(8,128)(2,1)S(1)}, bf16[160,512]{1,0:T(8,128)(2,1)}, u32[]{:S(2)}, u32[]{:S(2)}) collective-permute-start(bf16[160,512]{1,0:T(8,128)(2,1)S(1)} %copy.31), channel_id=1, source_target_pairs={{0,2},{2,0},{1,3},{3,1},{4,6},{6,4},{5,7},{7,5},{8,10},{10,8},{9,1... | collective-permute-start | bytes 491528 | tf_op jit(solution)/shard_map/ppermute | solution.py:209
  10.3 2.2 %copy-start.7 = (bf16[64,32]{0,1:T(8,128)(2,1)S(1)}, bf16[64,32]{0,1:T(8,128)(2,1)}, u32[]{:S(2)}) copy-start(bf16[64,32]{0,1:T(8,128)(2,1)} %param.13) | copy-start | bytes 12292
  12.5 11.1 %collective-permute-start.1 = (bf16[160,512]{1,0:T(8,128)(2,1)S(1)}, bf16[160,512]{1,0:T(8,128)(2,1)S(1)}, u32[]{:S(2)}, u32[]{:S(2)}) collective-permute-start(bf16[160,512]{1,0:T(8,128)(2,1)S(1)} %copy.30), channel_id=1, source_target_pairs={{0,2},{2,0},{1,3},{3,1},{4,6},{6,4},{5,7},{7,5},{8,10},{10,8},{9,1... | collective-permute-start | bytes 491528 | tf_op jit(solution)/shard_map/ppermute | solution.py:209
  21.4 2.0 %copy-start.1 = (bf16[8,512,512]{2,1,0:T(8,128)(2,1)}, bf16[8,512,512]{2,1,0:T(8,128)(2,1)S(1)}, u32[]{:S(2)}) copy-start(bf16[8,512,512]{2,1,0:T(8,128)(2,1)S(1)} %get-tuple-element.6.vh_ref) | copy-start | bytes 12582916
  23.4 10.6 %collective-permute-start = (f32[2,64,512]{2,1,0:T(8,128)S(1)}, f32[2,64,512]{2,1,0:T(8,128)}, u32[]{:S(2)}, u32[]{:S(2)}) collective-permute-start(f32[2,64,512]{2,1,0:T(8,128)S(1)} %dynamic-slice_bitcast_fusion.1), channel_id=1, source_target_pairs={{0,1},{1,0},{2,3},{3,2},{4,5},{5,4},{6,7},{7,6},{8,9},{9,8},{10,11... | collective-permute-start | bytes 786440 | tf_op jit(solution)/shard_map/ppermute | solution.py:138
  24.5 2.2 %copy-start.2 = (bf16[8,512,512]{2,1,0:T(8,128)(2,1)S(1)}, bf16[8,512,512]{2,1,0:T(8,128)(2,1)}, u32[]{:S(2)}) copy-start(bf16[8,512,512]{2,1,0:T(8,128)(2,1)} %copy-done.1) | copy-start | bytes 12582916
  33.5 1.7 %collective-permute-start.3 = (f32[2,64,512]{2,1,0:T(8,128)S(1)}, f32[2,64,512]{2,1,0:T(8,128)S(1)}, u32[]{:S(2)}, u32[]{:S(2)}) collective-permute-start(f32[2,64,512]{2,1,0:T(8,128)S(1)} %dynamic-slice_bitcast_fusion), channel_id=1, source_target_pairs={{0,1},{1,0},{2,3},{3,2},{4,5},{5,4},{6,7},{7,6},{8,9},{9,8},{10,11... | collective-permute-start | bytes 786440 | tf_op jit(solution)/shard_map/ppermute | solution.py:138
  35.3 16.4 %copy-start.4 = (f32[32,8,128]{2,1,0:T(8,128)S(1)}, f32[32,8,128]{2,1,0:T(8,128)}, u32[]{:S(2)}) copy-start(f32[32,8,128]{2,1,0:T(8,128)} %param.10) | copy-start | bytes 393220
  35.3 17.1 %copy-start.5 = (bf16[128,512]{1,0:T(8,128)(2,1)S(1)}, bf16[128,512]{1,0:T(8,128)(2,1)}, u32[]{:S(2)}) copy-start(bf16[128,512]{1,0:T(8,128)(2,1)} %param.16) | copy-start | bytes 393220
  35.4 8.1 %collective-permute-start.6 = (f32[64,512]{1,0:T(8,128)S(1)}, f32[64,512]{1,0:T(8,128)S(1)}, u32[]{:S(2)}, u32[]{:S(2)}) collective-permute-start(f32[64,512]{1,0:T(8,128)S(1)} %get-tuple-element.13), channel_id=1, source_target_pairs={{0,12},{4,0},{8,4},{12,8},{1,13},{5,1},{9,5},{13,9},{2,14},{6,2},{... | collective-permute-start | bytes 393224 | tf_op jit(solution)/shard_map/ppermute | solution.py:150
  39.6 12.0 %collective-permute-start.5 = (f32[64,512]{1,0:T(8,128)S(1)}, f32[64,512]{1,0:T(8,128)S(1)}, u32[]{:S(2)}, u32[]{:S(2)}) collective-permute-start(f32[64,512]{1,0:T(8,128)S(1)} %get-tuple-element.14), channel_id=1, source_target_pairs={{0,8},{4,12},{8,0},{12,4},{1,9},{5,13},{9,1},{13,5},{2,10},{6,14},... | collective-permute-start | bytes 393224 | tf_op jit(solution)/shard_map/ppermute | solution.py:150
  39.6 12.0 %collective-permute-start.4 = (f32[64,512]{1,0:T(8,128)S(1)}, f32[64,512]{1,0:T(8,128)S(1)}, u32[]{:S(2)}, u32[]{:S(2)}) collective-permute-start(f32[64,512]{1,0:T(8,128)S(1)} %get-tuple-element.12), channel_id=1, source_target_pairs={{0,4},{4,8},{8,12},{12,0},{1,5},{5,9},{9,13},{13,1},{2,6},{6,10},{... | collective-permute-start | bytes 393224 | tf_op jit(solution)/shard_map/ppermute | solution.py:150

commit v9 on v7

--- a/solution.py
+++ b/solution.py
@@ -109,6 +109,37 @@
             bytes_accessed=lt.size * 2 + r_all.size * 2 + wh.size * 4 + out_rows * JB * d * 4,
         ),
     )(lt, r_all, wh, wl)
+
+
+def pair_kernel(nj, u_ref, c_ref, ww_ref, ws_ref, o_ref):
+    d = c_ref.shape[1]
+    jbs = u_ref.shape[1] // d
+    rows_i = c_ref.shape[0] // nj
+    mids = []
+    for j in range(nj):
+        ja, jb = divmod(j, jbs)
+        mids.append(
+            c_ref[pl.ds(j, rows_i, stride=nj), :] + u_ref[ja * rows_i : (ja + 1) * rows_i, jb * d : (jb + 1) * d]
+        )
+    mid = jnp.concatenate(mids, axis=0)
+    norm = apply_layer_norm(mid).astype(jnp.bfloat16)
+    hidden = jnp.maximum(jnp.dot(norm, ww_ref[...], preferred_element_type=jnp.float32), 0.0).astype(jnp.bfloat16)
+    out = mid + jnp.dot(hidden, ws_ref[...], preferred_element_type=jnp.float32)
+    for j in range(nj):
+        o_ref[pl.ds(j, rows_i, stride=nj), :] = out[j * rows_i : (j + 1) * rows_i]
+
+
+def pair_transition(update, coupling, ww, ws, nj):
+    rows, d = coupling.shape
+    return pl.pallas_call(
+        functools.partial(pair_kernel, nj),
+        out_shape=jax.ShapeDtypeStruct((rows, d), jnp.float32),
+        in_specs=[pl.BlockSpec(memory_space=pltpu.VMEM)] * 4,
+        out_specs=pl.BlockSpec(memory_space=pltpu.VMEM),
+        cost_estimate=pl.CostEstimate(
+            flops=4 * rows * d * ww.shape[1], transcendentals=rows, bytes_accessed=rows * d * 12
+        ),
+    )(update, coupling, ww, ws)
 
 
 def chan_stage(block, chunk):
@@ -205,19 +236,12 @@
         r_all = lax.all_gather(jnp.concatenate(right_parts, axis=1), "res", axis=1, tiled=True)
         partial_value = outer_project(lt, r_all, w_hi, w_lo, 1.0 / depth_total)
         pair_update = reduce_over_sequences(partial_value)
-    nja_local = block_cols // JB
-    pair_update = (
-        pair_update.reshape(nja_local, sites_local_share, JB, pair_width)
-        .transpose(1, 0, 2, 3)
-        .reshape(sites_local_share * block_cols, pair_width)
-    )
-    pair_mid = coupling_embedding.reshape(sites_local_share * block_cols, pair_width) + pair_update
-    pair_norm = apply_layer_norm(pair_mid).astype(jnp.bfloat16)
-    pair_hidden = jnp.maximum(
-        jnp.dot(pair_norm, coupling_widen_weights, preferred_element_type=jnp.float32), 0.0
-    ).astype(jnp.bfloat16)
-    coupling_refreshed = pair_mid + jnp.dot(
-        pair_hidden, coupling_shrink_weights, preferred_element_type=jnp.float32
+    coupling_refreshed = pair_transition(
+        pair_update,
+        coupling_embedding.reshape(sites_local_share * block_cols, pair_width),
+        coupling_widen_weights,
+        coupling_shrink_weights,
+        block_cols,
     )
     return (
         homolog_refreshed,

time: 43.9 us -> 44 us (level)
  Pallas kernels: 9.72 us -> 12 us
  matrix products: 5.15 us -> 4.07 us
  other arithmetic: 6.02 us -> 5.44 us
    pallas_call x0 -> x1, Pallas kernels: none -> 2.28 us  [pair_transition(): pl.pallas_call(functools.partial(pair_kernel, nj), out_shape=jax.ShapeDty...]
    dot_general x1 -> x0, matrix products: 1.06 us -> none  [per_device(): jnp.dot(pair_hidden, coupling_shrink_weights, preferred_element_type=jnp....]
    concatenate x1, other arithmetic: 0.94 us -> 0.03 us  [per_device(): jnp.concatenate([lax.ppermute(r, 'res', [(0, 1), (1, 0)]) for r in right_...]
    add x1, other arithmetic: 0.04 us -> 0.67 us  [seq_stage(): acc + lax.ppermute(src, 'seq', [(q, (q + k) % nseq) for q in range(nseq)])]
  transfers between devices with their start and end apart: 7 -> 7, of which waited for: 4 -> 4; matrix products, arithmetic and copies ran while one was open for 16% -> 14% of each run, Pallas kernels for 22% -> 22%
where the time goes in v9:
time: 44 us; the launch traced here: 43.8 us
  Pallas kernels  12 us (27%)
  waiting for transfers between devices  10.5 us (24%)
  starting transfers between devices  8.86 us (20%)
  other arithmetic  5.44 us (12%)
  matrix products  4.07 us (9%)
  local copies, waits for them, and re-layouts  1.99 us (5%)
  between operations  0.93 us (2%)
    ppermute x3, waiting for transfers between devices, seq_stage(): lax.ppermute(src, 'seq', [(q, (q + k) % nseq) for q in range(nseq)])  10.3 us
    pallas_call x2, Pallas kernels, outer_project(): pl.pallas_call(functools.partial(outer_project_kernel, scale), grid=(step...  9.72 us
    ppermute x3, starting transfers between devices, seq_stage(): lax.ppermute(src, 'seq', [(q, (q + k) % nseq) for q in range(nseq)])  5.2 us
    ppermute x2, starting transfers between devices, per_device(): lax.ppermute(r, 'res', [(0, 1), (1, 0)])  3.09 us
    dot_general x2, matrix products, per_device(): jnp.einsum('hk,ihs->iks', homolog_shrink_weights, hidden, preferred_eleme...  3.06 us
    pallas_call x1, Pallas kernels, pair_transition(): pl.pallas_call(functools.partial(pair_kernel, nj), out_shape=jax.ShapeDty...  2.28 us
    reduce_sum x1, other arithmetic, apply_layer_norm_axis1(): mean = jnp.mean(values, axis=1, keepdims=True)  1.52 us
    transpose x1, other arithmetic, per_device(): jnp.transpose(jnp.concatenate(refreshed_parts, axis=0), (2, 0, 1))  1.14 us
  transfers between devices with their start and end apart: 7, of which 4 were waited for; matrix products, arithmetic and copies ran while one was open for 14% of the time, Pallas kernels for 22%

profile of v9, /device:TPU:0, one launch (start us, length us, event | category | flops | bytes accessed | tf_op | source)
XLA Modules:
  0.0 43.8 jit_solution(916594871890430849)
XLA Ops:
  0.6 0.0 copy-start
  0.6 0.0 copy-start.1
  0.7 0.0 copy-start.5
  0.7 1.5 %convert_reduce_fusion.1 = (f32[16,160]{1,0:T(8,128)S(1)}, f32[16,160]{1,0:T(8,128)S(1)}) fusion(bf16[32,64,160]{2,1,0:T(8,128)(2,1)} %bitcast.110), kind=kLoop, calls=%fused_computation.7 | loop fusion | flops 650240 | bytes 675840 | tf_op jit(solution)/shard_map/reduce_sum | solution.py:19
  2.2 0.0 copy-done.1
  2.2 0.4 fusion.22
  2.6 0.0 copy-done
  2.6 0.0 copy-done.5
  2.6 0.0 copy-start.3
  2.7 1.5 %convert_reduce_fusion.2 = (f32[16,160]{1,0:T(8,128)S(1)}, bf16[16,64,160]{2,1,0:T(8,128)(2,1)S(1)}) fusion(bf16[256,64]{0,1:T(8,128)(2,1)S(1)} %copy-done, f32[16,160]{1,0:T(8,128)S(1)} %add_rsqrt_fusion.2, f32[16,160]{1,0:T(8,128)S(1)} %get-tuple-element.15, bf16[32,64,160]{2,1,0:T(8,128)(2,1)S(1)} %bitcast.112, bf16[64,256]{1,0:T(8,128)(2,1)S(1)} %copy-done.5), kind=kOutput, calls=%fused_computation.15 | convolution fusion | flops 170554880 | bytes 1079296 | tf_op jit(solution)/shard_map/hk,ihs->iks/dot_general | solution.py:200
  4.2 0.2 fusion.24
  4.4 0.0 copy-done.3
  4.4 0.3 convolution_convert_fusion
  4.7 0.1 copy.16
  4.8 3.0 %collective-permute-start.2 = (bf16[160,512]{1,0:T(8,128)(2,1)S(1)}, bf16[160,512]{1,0:T(8,128)(2,1)S(1)}, u32[]{:S(2)}, u32[]{:S(2)}) collective-permute-start(bf16[160,512]{1,0:T(8,128)(2,1)S(1)} %copy.16), channel_id=1, source_target_pairs={{0,2},{2,0},{1,3},{3,1},{4,6},{6,4},{5,7},{7,5},{8,10},{10,8},{9,1... | collective-permute-start | bytes 491528 | tf_op jit(solution)/shard_map/ppermute | solution.py:223
  7.8 1.5 %convert_reduce_fusion.3 = (f32[16,160]{1,0:T(8,128)S(1)}, bf16[16,64,160]{2,1,0:T(8,128)(2,1)S(1)}) fusion(bf16[256,64]{0,1:T(8,128)(2,1)S(1)} %copy-done, f32[16,160]{1,0:T(8,128)S(1)} %add_rsqrt_fusion.3, f32[16,160]{1,0:T(8,128)S(1)} %get-tuple-element.16, bf16[32,64,160]{2,1,0:T(8,128)(2,1)S(1)} %bitcast.113, bf16[64,256]{1,0:T(8,128)(2,1)S(1)} %copy-done.5), kind=kOutput, calls=%fused_computation.17 | convolution fusion | flops 170554880 | bytes 1079296 | tf_op jit(solution)/shard_map/hk,ihs->iks/dot_general | solution.py:200
  9.4 0.0 copy-start.4
  9.4 0.2 fusion.26
  9.6 0.3 convolution_convert_fusion.1
  9.8 0.1 copy.15
  10.0 0.1 collective-permute-start.1
  10.1 0.0 copy-done.4
  10.1 0.3 fusion.19
  10.3 0.3 fusion.18
  10.6 0.0 copy-start.2
  10.6 0.1 pad_maximum_fusion
  10.7 0.3 copy.14
  11.0 0.6 %copy-done.2 = f32[1024,128]{1,0:T(8,128)S(1)} copy-done((f32[1024,128]{1,0:T(8,128)S(1)}, f32[1024,128]{1,0:T(8,128)}, u32[]{:S(2)}) %copy-start.2) | copy-done | bytes 524312
  11.7 0.1 fusion.32
  11.8 4.9 %shard_map.104 = f32[256,512]{1,0:T(8,128)S(1)} custom-call(bf16[1024,160]{1,0:T(8,128)(2,1)S(1)} %bitcast.108, bf16[160,1024]{1,0:T(8,128)(2,1)S(1)} %pad_maximum_fusion.1.r_ref, bf16[1024,128]{1,0:T(8,128)(2,1)S(1)} %get-tuple-element.10.wh_ref, bf16[1024,128]{1,0:T(8,128)(2,1)S(1)} %get-tuple-element.9.wl_ref), custom_call_target="tpu_custom_call" | custom-call | flops 3556769792 | bytes 1703936 | tf_op jit(solution)/shard_map/pallas_call | solution.py:88
  16.6 0.7 %dynamic-slice_bitcast_fusion.1 = f32[2,64,512]{2,1,0:T(8,128)} fusion(f32[2,2,64,512]{3,2,1,0:T(8,128)S(1)} %bitcast.104, s32[]{:T(128)S(6)} %select_n.47), kind=kLoop, calls=%fused_computation.61 | loop fusion | bytes 524292 | tf_op jit(solution)/shard_map/jit(dynamic_index_in_dim)/squeeze | solution.py:151
  17.4 0.0 collective-permute-start
  17.4 0.0 collective-permute-done.2
  17.4 0.0 collective-permute-done.1
  17.4 4.9 %shard_map.105 = f32[256,512]{1,0:T(8,128)S(1)} custom-call(bf16[1024,160]{1,0:T(8,128)(2,1)S(1)} %bitcast.109, bf16[160,1024]{1,0:T(8,128)(2,1)S(1)} %pad_maximum_fusion.2.r_ref, bf16[1024,128]{1,0:T(8,128)(2,1)S(1)} %get-tuple-element.10.wh_ref, bf16[1024,128]{1,0:T(8,128)(2,1)S(1)} %get-tuple-element.9.wl_ref), custom_call_target="tpu_custom_call" | custom-call | flops 3556769792 | bytes 1703936 | tf_op jit(solution)/shard_map/pallas_call | solution.py:88
  22.3 0.6 %collective-permute-start.3 = (f32[2,64,512]{2,1,0:T(8,128)S(1)}, f32[2,64,512]{2,1,0:T(8,128)S(1)}, u32[]{:S(2)}, u32[]{:S(2)}) collective-permute-start(f32[2,64,512]{2,1,0:T(8,128)S(1)} %dynamic-slice_bitcast_fusion), channel_id=1, source_target_pairs={{0,1},{1,0},{2,3},{3,2},{4,5},{5,4},{6,7},{7,6},{8,9},{9,8},{10,11... | collective-permute-start | bytes 786440 | tf_op jit(solution)/shard_map/ppermute | solution.py:152
  22.9 0.0 collective-permute-done
  22.9 1.0 %bitcast_add_fusion.1 = f32[2,64,512]{2,1,0:T(8,128)S(1)} fusion(f32[2,64,512]{2,1,0:T(8,128)} %collective-permute-done, f32[2,2,64,512]{3,2,1,0:T(8,128)S(1)} %bitcast.105, s32[]{:T(128)S(6)} %select_n.46), kind=kLoop, calls=%fused_computation.59 | loop fusion | flops 65536 | bytes 786436 | tf_op jit(solution)/shard_map/add | solution.py:152
  23.9 0.2 collective-permute-done.3
  24.2 2.2 %collective-permute-start.4 = (f32[64,512]{1,0:T(8,128)S(1)}, f32[64,512]{1,0:T(8,128)S(1)}, u32[]{:S(2)}, u32[]{:S(2)}) collective-permute-start(f32[64,512]{1,0:T(8,128)S(1)} %get-tuple-element.6), channel_id=1, source_target_pairs={{0,4},{4,8},{8,12},{12,0},{1,5},{5,9},{9,13},{13,1},{2,6},{6,10},{... | collective-permute-start | bytes 393224 | tf_op jit(solution)/shard_map/ppermute | solution.py:164
  26.3 2.1 %collective-permute-start.6 = (f32[64,512]{1,0:T(8,128)S(1)}, f32[64,512]{1,0:T(8,128)S(1)}, u32[]{:S(2)}, u32[]{:S(2)}) collective-permute-start(f32[64,512]{1,0:T(8,128)S(1)} %get-tuple-element.7), channel_id=1, source_target_pairs={{0,12},{4,0},{8,4},{12,8},{1,13},{5,1},{9,5},{13,9},{2,14},{6,2},{... | collective-permute-start | bytes 393224 | tf_op jit(solution)/shard_map/ppermute | solution.py:164
  28.4 0.9 %collective-permute-start.5 = (f32[64,512]{1,0:T(8,128)S(1)}, f32[64,512]{1,0:T(8,128)S(1)}, u32[]{:S(2)}, u32[]{:S(2)}) collective-permute-start(f32[64,512]{1,0:T(8,128)S(1)} %get-tuple-element.8), channel_id=1, source_target_pairs={{0,8},{4,12},{8,0},{12,4},{1,9},{5,13},{9,1},{13,5},{2,10},{6,14},... | collective-permute-start | bytes 393224 | tf_op jit(solution)/shard_map/ppermute | solution.py:164
  29.4 1.1 %maximum_bitcast_fusion = bf16[160,32,64]{0,2,1:T(8,128)(2,1)} fusion(bf16[16,64,160]{2,1,0:T(8,128)(2,1)S(1)} %get-tuple-element.12, bf16[16,64,160]{2,1,0:T(8,128)(2,1)S(1)} %get-tuple-element.14), kind=kLoop, calls=%fused_computation.44 | loop fusion | flops 327680 | bytes 1310720 | tf_op jit(solution)/shard_map/transpose | solution.py:212
  30.5 2.2 %collective-permute-done.4 = f32[64,512]{1,0:T(8,128)S(1)} collective-permute-done((f32[64,512]{1,0:T(8,128)S(1)}, f32[64,512]{1,0:T(8,128)S(1)}, u32[]{:S(2)}, u32[]{:S(2)}) %collective-permute-start.4) | collective-permute-done | bytes 131104 | tf_op jit(solution)/shard_map/ppermute | solution.py:164
  32.7 1.9 %collective-permute-done.6 = f32[64,512]{1,0:T(8,128)S(1)} collective-permute-done((f32[64,512]{1,0:T(8,128)S(1)}, f32[64,512]{1,0:T(8,128)S(1)}, u32[]{:S(2)}, u32[]{:S(2)}) %collective-permute-start.6) | collective-permute-done | bytes 131104 | tf_op jit(solution)/shard_map/ppermute | solution.py:164
  34.6 6.2 %collective-permute-done.5 = f32[64,512]{1,0:T(8,128)S(1)} collective-permute-done((f32[64,512]{1,0:T(8,128)S(1)}, f32[64,512]{1,0:T(8,128)S(1)}, u32[]{:S(2)}, u32[]{:S(2)}) %collective-permute-start.5) | collective-permute-done | bytes 131104 | tf_op jit(solution)/shard_map/ppermute | solution.py:164
  40.8 0.7 %fusion.50.u_ref = f32[64,512]{1,0:T(8,128)} fusion(f32[64,512]{1,0:T(8,128)S(1)} %collective-permute-done.6, f32[64,512]{1,0:T(8,128)S(1)} %collective-permute-done.5, f32[64,512]{1,0:T(8,128)S(1)} %collective-permute-done.4, f32[4,64,512]{2,1,0:T(8,128)S(1)} %maximum_select_fusion, s32[]{:T(128)S(6)} %select_n.49), kind=kLoop, calls=%fused_computation.64 | loop fusion | flops 98304 | bytes 655364 | tf_op jit(solution)/shard_map/add | solution.py:164
  41.5 2.3 %shard_map.106 = f32[256,128]{1,0:T(8,128)} custom-call(f32[64,512]{1,0:T(8,128)} %fusion.50.u_ref, f32[256,128]{1,0:T(8,128)} %bitcast.116, bf16[128,512]{1,0:T(8,128)(2,1)} %ww_ref.1, bf16[512,128]{1,0:T(8,128)(2,1)} %ws_ref.1), custom_call_target="tpu_custom_call" | custom-call | flops 67108864 | bytes 393216 | tf_op jit(solution)/shard_map/pallas_call | solution.py:134
  (13 shorter events, 0.2 us)
Async XLA Ops:
  0.6 2.0 %copy-start = (bf16[256,64]{0,1:T(8,128)(2,1)S(1)}, bf16[256,64]{0,1:T(8,128)(2,1)}, u32[]{:S(2)}) copy-start(bf16[256,64]{0,1:T(8,128)(2,1)} %param.12) | copy-start | bytes 98308
  0.6 1.6 %copy-start.1 = (bf16[160,32,64]{0,2,1:T(8,128)(2,1)S(1)}, bf16[160,32,64]{0,2,1:T(8,128)(2,1)}, u32[]{:S(2)}) copy-start(bf16[160,32,64]{0,2,1:T(8,128)(2,1)} %param.9) | copy-start | bytes 1966084
  0.7 2.0 %copy-start.5 = (bf16[64,256]{1,0:T(8,128)(2,1)S(1)}, bf16[64,256]{1,0:T(8,128)(2,1)}, u32[]{:S(2)}) copy-start(bf16[64,256]{1,0:T(8,128)(2,1)} %param.11) | copy-start | bytes 98308
  2.6 1.8 %copy-start.3 = (bf16[64,32]{0,1:T(8,128)(2,1)S(1)}, bf16[64,32]{0,1:T(8,128)(2,1)}, u32[]{:S(2)}) copy-start(bf16[64,32]{0,1:T(8,128)(2,1)} %param.14) | copy-start | bytes 12292
  4.8 12.6 %collective-permute-start.2 = (bf16[160,512]{1,0:T(8,128)(2,1)S(1)}, bf16[160,512]{1,0:T(8,128)(2,1)S(1)}, u32[]{:S(2)}, u32[]{:S(2)}) collective-permute-start(bf16[160,512]{1,0:T(8,128)(2,1)S(1)} %copy.16), channel_id=1, source_target_pairs={{0,2},{2,0},{1,3},{3,1},{4,6},{6,4},{5,7},{7,5},{8,10},{10,8},{9,1... | collective-permute-start | bytes 491528 | tf_op jit(solution)/shard_map/ppermute | solution.py:223
  9.4 0.7 %copy-start.4 = (bf16[64,32]{0,1:T(8,128)(2,1)S(1)}, bf16[64,32]{0,1:T(8,128)(2,1)}, u32[]{:S(2)}) copy-start(bf16[64,32]{0,1:T(8,128)(2,1)} %param.13) | copy-start | bytes 12292
  10.0 7.4 %collective-permute-start.1 = (bf16[160,512]{1,0:T(8,128)(2,1)S(1)}, bf16[160,512]{1,0:T(8,128)(2,1)S(1)}, u32[]{:S(2)}, u32[]{:S(2)}) collective-permute-start(bf16[160,512]{1,0:T(8,128)(2,1)S(1)} %copy.15), channel_id=1, source_target_pairs={{0,2},{2,0},{1,3},{3,1},{4,6},{6,4},{5,7},{7,5},{8,10},{10,8},{9,1... | collective-permute-start | bytes 491528 | tf_op jit(solution)/shard_map/ppermute | solution.py:223
  10.6 1.0 %copy-start.2 = (f32[1024,128]{1,0:T(8,128)S(1)}, f32[1024,128]{1,0:T(8,128)}, u32[]{:S(2)}) copy-start(f32[1024,128]{1,0:T(8,128)} %param.15) | copy-start | bytes 1572868
  17.4 5.5 %collective-permute-start = (f32[2,64,512]{2,1,0:T(8,128)}, f32[2,64,512]{2,1,0:T(8,128)}, u32[]{:S(2)}, u32[]{:S(2)}) collective-permute-start(f32[2,64,512]{2,1,0:T(8,128)} %dynamic-slice_bitcast_fusion.1), channel_id=1, source_target_pairs={{0,1},{1,0},{2,3},{3,2},{4,5},{5,4},{6,7},{7,6},{8,9},{9,8},{10,11... | collective-permute-start | bytes 786440 | tf_op jit(solution)/shard_map/ppermute | solution.py:152
  22.3 1.7 %collective-permute-start.3 = (f32[2,64,512]{2,1,0:T(8,128)S(1)}, f32[2,64,512]{2,1,0:T(8,128)S(1)}, u32[]{:S(2)}, u32[]{:S(2)}) collective-permute-start(f32[2,64,512]{2,1,0:T(8,128)S(1)} %dynamic-slice_bitcast_fusion), channel_id=1, source_target_pairs={{0,1},{1,0},{2,3},{3,2},{4,5},{5,4},{6,7},{7,6},{8,9},{9,8},{10,11... | collective-permute-start | bytes 786440 | tf_op jit(solution)/shard_map/ppermute | solution.py:152
  24.2 8.6 %collective-permute-start.4 = (f32[64,512]{1,0:T(8,128)S(1)}, f32[64,512]{1,0:T(8,128)S(1)}, u32[]{:S(2)}, u32[]{:S(2)}) collective-permute-start(f32[64,512]{1,0:T(8,128)S(1)} %get-tuple-element.6), channel_id=1, source_target_pairs={{0,4},{4,8},{8,12},{12,0},{1,5},{5,9},{9,13},{13,1},{2,6},{6,10},{... | collective-permute-start | bytes 393224 | tf_op jit(solution)/shard_map/ppermute | solution.py:164
  26.3 8.3 %collective-permute-start.6 = (f32[64,512]{1,0:T(8,128)S(1)}, f32[64,512]{1,0:T(8,128)S(1)}, u32[]{:S(2)}, u32[]{:S(2)}) collective-permute-start(f32[64,512]{1,0:T(8,128)S(1)} %get-tuple-element.7), channel_id=1, source_target_pairs={{0,12},{4,0},{8,4},{12,8},{1,13},{5,1},{9,5},{13,9},{2,14},{6,2},{... | collective-permute-start | bytes 393224 | tf_op jit(solution)/shard_map/ppermute | solution.py:164
  28.4 12.4 %collective-permute-start.5 = (f32[64,512]{1,0:T(8,128)S(1)}, f32[64,512]{1,0:T(8,128)S(1)}, u32[]{:S(2)}, u32[]{:S(2)}) collective-permute-start(f32[64,512]{1,0:T(8,128)S(1)} %get-tuple-element.8), channel_id=1, source_target_pairs={{0,8},{4,12},{8,0},{12,4},{1,9},{5,13},{9,1},{13,5},{2,10},{6,14},... | collective-permute-start | bytes 393224 | tf_op jit(solution)/shard_map/ppermute | solution.py:164

commit v10 on v7

--- a/solution.py
+++ b/solution.py
@@ -119,6 +119,28 @@
     mine = lax.dynamic_index_in_dim(xs, c, axis=1, keepdims=False)
     other = lax.dynamic_index_in_dim(xs, 1 - c, axis=1, keepdims=False)
     return mine + lax.ppermute(other, "chan", [(0, 1), (1, 0)])
+
+
+def block_phase(part_blk, own_block):
+    nseq = lax.axis_size("seq")
+    half = nseq // 2
+    me = lax.axis_index("seq")
+    r = lax.axis_index("res")
+    base_me = r * half if own_block else (1 - r) * half
+    total = None
+    for rho in range(1, nseq):
+        pairs = []
+        for a in range(nseq):
+            for rr in range(2):
+                d = (a + rho) % nseq
+                base = rr * half if own_block else (1 - rr) * half
+                if base <= d < base + half:
+                    pairs.append((a * 2 + rr, d * 2 + rr))
+        t = jnp.clip((me + rho) % nseq - base_me, 0, half - 1)
+        src = lax.dynamic_index_in_dim(part_blk, t, axis=0, keepdims=False)
+        got = lax.ppermute(src, ("seq", "res"), pairs)
+        total = got if total is None else total + got
+    return total
 
 
 def seq_stage(part):
@@ -194,13 +216,22 @@
         p_own = outer_project(lt, r_own, w_hi, w_lo, 1.0 / depth_total)
         chunk = 2 * p_own.shape[0] // (lax.axis_size("seq") * lax.axis_size("chan"))
         part_own = chan_stage(p_own, chunk)
+        part_own, r_other = lax.optimization_barrier((part_own, r_other))
+        received_own = block_phase(part_own, True)
         p_other = outer_project(lt, r_other, w_hi, w_lo, 1.0 / depth_total)
+        received_own, p_other = lax.optimization_barrier((received_own, p_other))
         part_other = chan_stage(p_other, chunk)
-        first = lax.axis_index("res") == 0
-        part = jnp.where(
-            first, jnp.concatenate([part_own, part_other], axis=0), jnp.concatenate([part_other, part_own], axis=0)
-        )
-        pair_update = seq_stage(part)
+        nseq = lax.axis_size("seq")
+        half = nseq // 2
+        me = lax.axis_index("seq")
+        r = lax.axis_index("res")
+        received_other = block_phase(part_other, False)
+        kept_own = lax.dynamic_index_in_dim(part_own, jnp.clip(me - r * half, 0, half - 1), axis=0, keepdims=False)
+        kept_other = lax.dynamic_index_in_dim(
+            part_other, jnp.clip(me - (1 - r) * half, 0, half - 1), axis=0, keepdims=False
+        )
+        kept = jnp.where(me // half == r, kept_own, kept_other)
+        pair_update = kept + received_own + received_other
     else:
         r_all = lax.all_gather(jnp.concatenate(right_parts, axis=1), "res", axis=1, tiled=True)
         partial_value = outer_project(lt, r_all, w_hi, w_lo, 1.0 / depth_total)

time: 43.9 us -> 54.6 us (1.24)
  the two profiles are of different devices: /device:TPU:0 before, /device:TPU:11 now
where the time goes in v10:
time: 54.6 us; the launch traced here: 54.2 us
  starting transfers between devices  16.7 us (31%)
  waiting for transfers between devices  13.7 us (25%)
  Pallas kernels  9.71 us (18%)
  other arithmetic  6.1 us (11%)
  matrix products  5.14 us (9%)
  local copies, waits for them, and re-layouts  1.75 us (3%)
  between operations  1.1 us (2%)
    ppermute x6, starting transfers between devices, block_phase(): got = lax.ppermute(src, ('seq', 'res'), pairs)  12.9 us
    ppermute x6, waiting for transfers between devices, block_phase(): got = lax.ppermute(src, ('seq', 'res'), pairs)  12.3 us
    pallas_call x2, Pallas kernels, outer_project(): pl.pallas_call(functools.partial(outer_project_kernel, scale), grid=(step...  9.71 us
    dot_general x2, matrix products, per_device(): jnp.einsum('hk,ihs->iks', homolog_shrink_weights, hidden, preferred_eleme...  3.06 us
    ppermute x2, starting transfers between devices, chan_stage(): return mine + lax.ppermute(other, 'chan', [(0, 1), (1, 0)])  2.2 us
    ppermute x2, starting transfers between devices, per_device(): lax.ppermute(r, 'res', [(0, 1), (1, 0)])  1.6 us
    reduce_sum x1, other arithmetic, apply_layer_norm_axis1(): mean = jnp.mean(values, axis=1, keepdims=True)  1.53 us
    ppermute x2, waiting for transfers between devices, chan_stage(): return mine + lax.ppermute(other, 'chan', [(0, 1), (1, 0)])  1.42 us
  transfers between devices with their start and end apart: 10, of which 5 were waited for; matrix products, arithmetic and copies ran while one was open for 10% of the time, Pallas kernels for 18%

profile of v10, /device:TPU:11, one launch (start us, length us, event | category | flops | bytes accessed | tf_op | source)
XLA Modules:
  0.0 54.2 jit_solution(3921692778313559237)
XLA Ops:
  0.6 0.0 copy-start
  0.7 1.5 %convert_reduce_fusion.1 = (f32[16,160]{1,0:T(8,128)S(1)}, f32[16,160]{1,0:T(8,128)S(1)}) fusion(bf16[32,64,160]{2,1,0:T(8,128)(2,1)} %bitcast.128), kind=kLoop, calls=%fused_computation.7 | loop fusion | flops 650240 | bytes 675840 | tf_op jit(solution)/shard_map/reduce_sum | solution.py:19
  2.2 0.4 fusion.26
  2.7 0.0 copy-start.5
  2.7 1.5 %convert_reduce_fusion.3 = (f32[16,160]{1,0:T(8,128)S(1)}, bf16[16,64,160]{2,1,0:T(8,128)(2,1)S(1)}) fusion(bf16[256,64]{0,1:T(8,128)(2,1)S(1)} %copy-done.7, f32[16,160]{1,0:T(8,128)S(1)} %add_rsqrt_fusion.3, f32[16,160]{1,0:T(8,128)S(1)} %get-tuple-element.27, bf16[32,64,160]{2,1,0:T(8,128)(2,1)S(1)} %bitcast.130, bf16[64,256]{1,0:T(8,128)(2,1)S(1)} %copy-done.8), kind=kOutput, calls=%fused_computation.17 | convolution fusion | flops 170554880 | bytes 1079296 | tf_op jit(solution)/shard_map/hk,ihs->iks/dot_general | solution.py:191
  4.2 0.2 fusion.30
  4.4 0.3 convolution_convert_fusion.1
  4.7 0.1 copy.30
  4.8 0.3 collective-permute-start.1
  5.2 1.5 %convert_reduce_fusion.2 = (f32[16,160]{1,0:T(8,128)S(1)}, bf16[16,64,160]{2,1,0:T(8,128)(2,1)S(1)}) fusion(bf16[256,64]{0,1:T(8,128)(2,1)S(1)} %copy-done.7, f32[16,160]{1,0:T(8,128)S(1)} %add_rsqrt_fusion.2, f32[16,160]{1,0:T(8,128)S(1)} %get-tuple-element.26, bf16[32,64,160]{2,1,0:T(8,128)(2,1)S(1)} %bitcast.131, bf16[64,256]{1,0:T(8,128)(2,1)S(1)} %copy-done.8), kind=kOutput, calls=%fused_computation.15 | convolution fusion | flops 170554880 | bytes 1079296 | tf_op jit(solution)/shard_map/hk,ihs->iks/dot_general | solution.py:191
  6.7 0.2 fusion.28
  6.9 0.0 copy-start.6
  6.9 0.3 convolution_convert_fusion
  7.2 0.1 copy.31
  7.3 1.3 %collective-permute-start.2 = (bf16[160,512]{1,0:T(8,128)(2,1)S(1)}, bf16[160,512]{1,0:T(8,128)(2,1)}, u32[]{:S(2)}, u32[]{:S(2)}) collective-permute-start(bf16[160,512]{1,0:T(8,128)(2,1)S(1)} %copy.31), channel_id=1, source_target_pairs={{0,2},{2,0},{1,3},{3,1},{4,6},{6,4},{5,7},{7,5},{8,10},{10,8},{9,1... | collective-permute-start | bytes 491528 | tf_op jit(solution)/shard_map/ppermute | solution.py:214
  8.6 0.3 fusion.19
  8.9 0.3 fusion.20
  9.2 0.0 copy-start.3
  9.2 0.1 pad_maximum_fusion
  9.3 0.3 copy.29
  9.6 0.6 %copy-done.3 = f32[1024,128]{1,0:T(8,128)S(1)} copy-done((f32[1024,128]{1,0:T(8,128)S(1)}, f32[1024,128]{1,0:T(8,128)}, u32[]{:S(2)}) %copy-start.3) | copy-done | bytes 524312
  10.2 0.1 fusion.36
  10.3 4.9 %shard_map.104 = f32[256,512]{1,0:T(8,128)S(1)} custom-call(bf16[1024,160]{1,0:T(8,128)(2,1)S(1)} %bitcast.122, bf16[160,1024]{1,0:T(8,128)(2,1)S(1)} %pad_maximum_fusion.1.r_ref, bf16[1024,128]{1,0:T(8,128)(2,1)S(1)} %get-tuple-element.15.wh_ref, bf16[1024,128]{1,0:T(8,128)(2,1)S(1)} %get-tuple-element.14.wl_ref), custom_call_target="tpu_custom_call" | custom-call | flops 3556769792 | bytes 1703936 | tf_op jit(solution)/shard_map/pallas_call | solution.py:88
  15.2 1.3 %collective-permute-start = (f32[2,64,512]{2,1,0:T(8,128)S(1)}, f32[2,64,512]{2,1,0:T(8,128)}, u32[]{:S(2)}, u32[]{:S(2)}) collective-permute-start(f32[2,64,512]{2,1,0:T(8,128)S(1)} %dynamic-slice_bitcast_fusion.1), channel_id=1, source_target_pairs={{0,1},{1,0},{2,3},{3,2},{4,5},{5,4},{6,7},{7,6},{8,9},{9,8},{10,11... | collective-permute-start | bytes 786440 | tf_op jit(solution)/shard_map/ppermute | solution.py:121
  16.5 1.0 %pad_maximum_fusion.2.r_ref = bf16[160,1024]{1,0:T(8,128)(2,1)S(1)} fusion(bf16[160,512]{1,0:T(8,128)(2,1)} %collective-permute-done.2, bf16[160,512]{1,0:T(8,128)(2,1)} %collective-permute-done.1), kind=kLoop, calls=%fused_computation.61 | loop fusion | flops 655360 | bytes 655360 | tf_op jit(solution)/shard_map/concatenate | solution.py:214
  17.5 0.3 collective-permute-done
  17.8 1.0 %bitcast_add_fusion.1 = f32[2,64,512]{2,1,0:T(8,128)S(1)} fusion(f32[2,64,512]{2,1,0:T(8,128)} %collective-permute-done, f32[2,2,64,512]{3,2,1,0:T(8,128)S(1)} %bitcast.125, s32[]{:T(128)S(6)} %select_n.56), kind=kLoop, calls=%fused_computation.63 | loop fusion | flops 65536 | bytes 786436 | tf_op jit(solution)/shard_map/add | solution.py:121
  18.8 3.2 %collective-permute-start.3 = (f32[64,512]{1,0:T(8,128)S(1)}, f32[64,512]{1,0:T(8,128)S(1)}, u32[]{:S(2)}, u32[]{:S(2)}) collective-permute-start(f32[64,512]{1,0:T(8,128)S(1)} %get-tuple-element.21), channel_id=1, source_target_pairs={{0,4},{6,10},{10,14},{12,0},{1,5},{7,11},{11,15},{13,1},{16,20},{2... | collective-permute-start | bytes 393224 | tf_op jit(solution)/shard_map/ppermute | solution.py:141
  22.0 2.3 %collective-permute-start.4 = (f32[64,512]{1,0:T(8,128)S(1)}, f32[64,512]{1,0:T(8,128)S(1)}, u32[]{:S(2)}, u32[]{:S(2)}) collective-permute-start(f32[64,512]{1,0:T(8,128)S(1)} %get-tuple-element.19), channel_id=1, source_target_pairs={{2,10},{6,14},{8,0},{12,4},{3,11},{7,15},{9,1},{13,5},{18,26},{22,... | collective-permute-start | bytes 393224 | tf_op jit(solution)/shard_map/ppermute | solution.py:141
  24.3 0.8 %collective-permute-start.5 = (f32[64,512]{1,0:T(8,128)S(1)}, f32[64,512]{1,0:T(8,128)S(1)}, u32[]{:S(2)}, u32[]{:S(2)}) collective-permute-start(f32[64,512]{1,0:T(8,128)S(1)} %get-tuple-element.20), channel_id=1, source_target_pairs={{2,14},{4,0},{8,4},{14,10},{3,15},{5,1},{9,5},{15,11},{18,30},{20,... | collective-permute-start | bytes 393224 | tf_op jit(solution)/shard_map/ppermute | solution.py:141
  25.2 4.9 %shard_map.105 = f32[256,512]{1,0:T(8,128)S(1)} custom-call(bf16[1024,160]{1,0:T(8,128)(2,1)S(1)} %bitcast.123, bf16[160,1024]{1,0:T(8,128)(2,1)S(1)} %pad_maximum_fusion.2.r_ref, bf16[1024,128]{1,0:T(8,128)(2,1)S(1)} %get-tuple-element.15.wh_ref, bf16[1024,128]{1,0:T(8,128)(2,1)S(1)} %get-tuple-element.14.wl_ref), custom_call_target="tpu_custom_call" | custom-call | flops 3556769792 | bytes 1703936 | tf_op jit(solution)/shard_map/pallas_call | solution.py:88
  30.1 3.2 %collective-permute-done.4 = f32[64,512]{1,0:T(8,128)S(1)} collective-permute-done((f32[64,512]{1,0:T(8,128)S(1)}, f32[64,512]{1,0:T(8,128)S(1)}, u32[]{:S(2)}, u32[]{:S(2)}) %collective-permute-start.4) | collective-permute-done | bytes 131104 | tf_op jit(solution)/shard_map/ppermute | solution.py:141
  33.4 0.9 %collective-permute-start.6 = (f32[2,64,512]{2,1,0:T(8,128)S(1)}, f32[2,64,512]{2,1,0:T(8,128)S(1)}, u32[]{:S(2)}, u32[]{:S(2)}) collective-permute-start(f32[2,64,512]{2,1,0:T(8,128)S(1)} %dynamic-slice_bitcast_fusion), channel_id=1, source_target_pairs={{0,1},{1,0},{2,3},{3,2},{4,5},{5,4},{6,7},{7,6},{8,9},{9,8},{10,11... | collective-permute-start | bytes 786440 | tf_op jit(solution)/shard_map/ppermute | solution.py:121
  34.3 1.2 %collective-permute-done.6 = f32[2,64,512]{2,1,0:T(8,128)S(1)} collective-permute-done((f32[2,64,512]{2,1,0:T(8,128)S(1)}, f32[2,64,512]{2,1,0:T(8,128)S(1)}, u32[]{:S(2)}, u32[]{:S(2)}) %collective-permute-start.6) | collective-permute-done | bytes 262176 | tf_op jit(solution)/shard_map/ppermute | solution.py:121
  35.5 1.3 %collective-permute-start.7 = (f32[64,512]{1,0:T(8,128)S(1)}, f32[64,512]{1,0:T(8,128)S(1)}, u32[]{:S(2)}, u32[]{:S(2)}) collective-permute-start(f32[64,512]{1,0:T(8,128)S(1)} %get-tuple-element.18), channel_id=1, source_target_pairs={{2,6},{4,8},{8,12},{14,2},{3,7},{5,9},{9,13},{15,3},{18,22},{20,24... | collective-permute-start | bytes 393224 | tf_op jit(solution)/shard_map/ppermute | solution.py:141
  36.8 1.3 %collective-permute-start.8 = (f32[64,512]{1,0:T(8,128)S(1)}, f32[64,512]{1,0:T(8,128)S(1)}, u32[]{:S(2)}, u32[]{:S(2)}) collective-permute-start(f32[64,512]{1,0:T(8,128)S(1)} %get-tuple-element.16), channel_id=1, source_target_pairs={{0,8},{4,12},{10,2},{14,6},{1,9},{5,13},{11,3},{15,7},{16,24},{20,... | collective-permute-start | bytes 393224 | tf_op jit(solution)/shard_map/ppermute | solution.py:141
  38.1 4.0 %collective-permute-start.9 = (f32[64,512]{1,0:T(8,128)S(1)}, f32[64,512]{1,0:T(8,128)S(1)}, u32[]{:S(2)}, u32[]{:S(2)}) collective-permute-start(f32[64,512]{1,0:T(8,128)S(1)} %get-tuple-element.17), channel_id=1, source_target_pairs={{0,12},{6,2},{10,6},{12,8},{1,13},{7,3},{11,7},{13,9},{16,28},{22,... | collective-permute-start | bytes 393224 | tf_op jit(solution)/shard_map/ppermute | solution.py:141
  42.1 1.1 %maximum_bitcast_fusion = bf16[160,32,64]{0,2,1:T(8,128)(2,1)} fusion(bf16[16,64,160]{2,1,0:T(8,128)(2,1)S(1)} %get-tuple-element.23, bf16[16,64,160]{2,1,0:T(8,128)(2,1)S(1)} %get-tuple-element.25), kind=kLoop, calls=%fused_computation.49 | loop fusion | flops 327680 | bytes 1310720 | tf_op jit(solution)/shard_map/transpose | solution.py:203
  43.3 3.0 %collective-permute-done.8 = f32[64,512]{1,0:T(8,128)S(1)} collective-permute-done((f32[64,512]{1,0:T(8,128)S(1)}, f32[64,512]{1,0:T(8,128)S(1)}, u32[]{:S(2)}, u32[]{:S(2)}) %collective-permute-start.8) | collective-permute-done | bytes 131104 | tf_op jit(solution)/shard_map/ppermute | solution.py:141
  46.3 6.0 %collective-permute-done.9 = f32[64,512]{1,0:T(8,128)S(1)} collective-permute-done((f32[64,512]{1,0:T(8,128)S(1)}, f32[64,512]{1,0:T(8,128)S(1)}, u32[]{:S(2)}, u32[]{:S(2)}) %collective-permute-start.9) | collective-permute-done | bytes 131104 | tf_op jit(solution)/shard_map/ppermute | solution.py:141
  52.3 0.1 fusion.54
  52.4 0.1 fusion.59
  52.6 0.2 multiply_reduce_fusion
  52.8 0.1 copy.37
  52.9 0.1 copy.38
  52.9 0.1 rsqrt.48
  53.0 0.1 div.52
  53.1 1.1 %fusion.23 = f32[32,8,128]{2,1,0:T(8,128)} fusion(bf16[512,128]{1,0:T(8,128)(2,1)S(1)} %copy-done, bf16[128,512]{1,0:T(8,128)(2,1)S(1)} %copy-done.4, f32[256,128]{1,0:T(8,128)S(1)} %bitcast.138, f32[32,8,128]{2,1,0:T(8,128)S(1)} %copy-done.2, f32[256]{0:T(256)S(1)} %rsqrt.48, f32[256]{0:T(256)S(1)} %div.52), kind=kOutput, calls=%fused_computation.40 | convolution fusion | flops 67567616 | bytes 657408 | tf_op jit(solution)/shard_map/dot_general | solution.py:250
  (37 shorter events, 0.4 us)
Async XLA Ops:
  0.6 52.5 %copy-start = (bf16[512,128]{1,0:T(8,128)(2,1)S(1)}, bf16[512,128]{1,0:T(8,128)(2,1)}, u32[]{:S(2)}) copy-start(bf16[512,128]{1,0:T(8,128)(2,1)} %param.17) | copy-start | bytes 393220
  0.6 1.6 %copy-start.1 = (bf16[160,32,64]{0,2,1:T(8,128)(2,1)S(1)}, bf16[160,32,64]{0,2,1:T(8,128)(2,1)}, u32[]{:S(2)}) copy-start(bf16[160,32,64]{0,2,1:T(8,128)(2,1)} %param.9) | copy-start | bytes 1966084
  0.7 2.0 %copy-start.7 = (bf16[256,64]{0,1:T(8,128)(2,1)S(1)}, bf16[256,64]{0,1:T(8,128)(2,1)}, u32[]{:S(2)}) copy-start(bf16[256,64]{0,1:T(8,128)(2,1)} %param.12) | copy-start | bytes 98308
  0.7 2.0 %copy-start.8 = (bf16[64,256]{1,0:T(8,128)(2,1)S(1)}, bf16[64,256]{1,0:T(8,128)(2,1)}, u32[]{:S(2)}) copy-start(bf16[64,256]{1,0:T(8,128)(2,1)} %param.11) | copy-start | bytes 98308
  2.7 1.8 %copy-start.5 = (bf16[64,32]{0,1:T(8,128)(2,1)S(1)}, bf16[64,32]{0,1:T(8,128)(2,1)}, u32[]{:S(2)}) copy-start(bf16[64,32]{0,1:T(8,128)(2,1)} %param.14) | copy-start | bytes 12292
  4.8 11.7 %collective-permute-start.1 = (bf16[160,512]{1,0:T(8,128)(2,1)S(1)}, bf16[160,512]{1,0:T(8,128)(2,1)}, u32[]{:S(2)}, u32[]{:S(2)}) collective-permute-start(bf16[160,512]{1,0:T(8,128)(2,1)S(1)} %copy.30), channel_id=1, source_target_pairs={{0,2},{2,0},{1,3},{3,1},{4,6},{6,4},{5,7},{7,5},{8,10},{10,8},{9,1... | collective-permute-start | bytes 491528 | tf_op jit(solution)/shard_map/ppermute | solution.py:214
  6.9 1.7 %copy-start.6 = (bf16[64,32]{0,1:T(8,128)(2,1)S(1)}, bf16[64,32]{0,1:T(8,128)(2,1)}, u32[]{:S(2)}) copy-start(bf16[64,32]{0,1:T(8,128)(2,1)} %param.13) | copy-start | bytes 12292
  7.3 9.2 %collective-permute-start.2 = (bf16[160,512]{1,0:T(8,128)(2,1)S(1)}, bf16[160,512]{1,0:T(8,128)(2,1)}, u32[]{:S(2)}, u32[]{:S(2)}) collective-permute-start(bf16[160,512]{1,0:T(8,128)(2,1)S(1)} %copy.31), channel_id=1, source_target_pairs={{0,2},{2,0},{1,3},{3,1},{4,6},{6,4},{5,7},{7,5},{8,10},{10,8},{9,1... | collective-permute-start | bytes 491528 | tf_op jit(solution)/shard_map/ppermute | solution.py:214
  9.2 1.0 %copy-start.3 = (f32[1024,128]{1,0:T(8,128)S(1)}, f32[1024,128]{1,0:T(8,128)}, u32[]{:S(2)}) copy-start(f32[1024,128]{1,0:T(8,128)} %param.15) | copy-start | bytes 1572868
  15.2 2.6 %collective-permute-start = (f32[2,64,512]{2,1,0:T(8,128)S(1)}, f32[2,64,512]{2,1,0:T(8,128)}, u32[]{:S(2)}, u32[]{:S(2)}) collective-permute-start(f32[2,64,512]{2,1,0:T(8,128)S(1)} %dynamic-slice_bitcast_fusion.1), channel_id=1, source_target_pairs={{0,1},{1,0},{2,3},{3,2},{4,5},{5,4},{6,7},{7,6},{8,9},{9,8},{10,11... | collective-permute-start | bytes 786440 | tf_op jit(solution)/shard_map/ppermute | solution.py:121
  18.8 11.3 %collective-permute-start.3 = (f32[64,512]{1,0:T(8,128)S(1)}, f32[64,512]{1,0:T(8,128)S(1)}, u32[]{:S(2)}, u32[]{:S(2)}) collective-permute-start(f32[64,512]{1,0:T(8,128)S(1)} %get-tuple-element.21), channel_id=1, source_target_pairs={{0,4},{6,10},{10,14},{12,0},{1,5},{7,11},{11,15},{13,1},{16,20},{2... | collective-permute-start | bytes 393224 | tf_op jit(solution)/shard_map/ppermute | solution.py:141
  22.0 11.3 %collective-permute-start.4 = (f32[64,512]{1,0:T(8,128)S(1)}, f32[64,512]{1,0:T(8,128)S(1)}, u32[]{:S(2)}, u32[]{:S(2)}) collective-permute-start(f32[64,512]{1,0:T(8,128)S(1)} %get-tuple-element.19), channel_id=1, source_target_pairs={{2,10},{6,14},{8,0},{12,4},{3,11},{7,15},{9,1},{13,5},{18,26},{22,... | collective-permute-start | bytes 393224 | tf_op jit(solution)/shard_map/ppermute | solution.py:141
  24.3 9.0 %collective-permute-start.5 = (f32[64,512]{1,0:T(8,128)S(1)}, f32[64,512]{1,0:T(8,128)S(1)}, u32[]{:S(2)}, u32[]{:S(2)}) collective-permute-start(f32[64,512]{1,0:T(8,128)S(1)} %get-tuple-element.20), channel_id=1, source_target_pairs={{2,14},{4,0},{8,4},{14,10},{3,15},{5,1},{9,5},{15,11},{18,30},{20,... | collective-permute-start | bytes 393224 | tf_op jit(solution)/shard_map/ppermute | solution.py:141
  33.4 2.1 %collective-permute-start.6 = (f32[2,64,512]{2,1,0:T(8,128)S(1)}, f32[2,64,512]{2,1,0:T(8,128)S(1)}, u32[]{:S(2)}, u32[]{:S(2)}) collective-permute-start(f32[2,64,512]{2,1,0:T(8,128)S(1)} %dynamic-slice_bitcast_fusion), channel_id=1, source_target_pairs={{0,1},{1,0},{2,3},{3,2},{4,5},{5,4},{6,7},{7,6},{8,9},{9,8},{10,11... | collective-permute-start | bytes 786440 | tf_op jit(solution)/shard_map/ppermute | solution.py:121
  35.5 7.7 %collective-permute-start.7 = (f32[64,512]{1,0:T(8,128)S(1)}, f32[64,512]{1,0:T(8,128)S(1)}, u32[]{:S(2)}, u32[]{:S(2)}) collective-permute-start(f32[64,512]{1,0:T(8,128)S(1)} %get-tuple-element.18), channel_id=1, source_target_pairs={{2,6},{4,8},{8,12},{14,2},{3,7},{5,9},{9,13},{15,3},{18,22},{20,24... | collective-permute-start | bytes 393224 | tf_op jit(solution)/shard_map/ppermute | solution.py:141
  36.8 9.5 %collective-permute-start.8 = (f32[64,512]{1,0:T(8,128)S(1)}, f32[64,512]{1,0:T(8,128)S(1)}, u32[]{:S(2)}, u32[]{:S(2)}) collective-permute-start(f32[64,512]{1,0:T(8,128)S(1)} %get-tuple-element.16), channel_id=1, source_target_pairs={{0,8},{4,12},{10,2},{14,6},{1,9},{5,13},{11,3},{15,7},{16,24},{20,... | collective-permute-start | bytes 393224 | tf_op jit(solution)/shard_map/ppermute | solution.py:141
  38.1 14.2 %collective-permute-start.9 = (f32[64,512]{1,0:T(8,128)S(1)}, f32[64,512]{1,0:T(8,128)S(1)}, u32[]{:S(2)}, u32[]{:S(2)}) collective-permute-start(f32[64,512]{1,0:T(8,128)S(1)} %get-tuple-element.17), channel_id=1, source_target_pairs={{0,12},{6,2},{10,6},{12,8},{1,13},{7,3},{11,7},{13,9},{16,28},{22,... | collective-permute-start | bytes 393224 | tf_op jit(solution)/shard_map/ppermute | solution.py:141
  43.3 9.2 %copy-start.2 = (f32[32,8,128]{2,1,0:T(8,128)S(1)}, f32[32,8,128]{2,1,0:T(8,128)}, u32[]{:S(2)}) copy-start(f32[32,8,128]{2,1,0:T(8,128)} %param.10) | copy-start | bytes 393220
  43.3 9.9 %copy-start.4 = (bf16[128,512]{1,0:T(8,128)(2,1)S(1)}, bf16[128,512]{1,0:T(8,128)(2,1)}, u32[]{:S(2)}) copy-start(bf16[128,512]{1,0:T(8,128)(2,1)} %param.16) | copy-start | bytes 393220

commit v11 on v7

--- a/solution.py
+++ b/solution.py
@@ -27,11 +27,14 @@
 JB = 4
 
 
-def outer_project_kernel(scale, lt_ref, r_ref, wh_ref, wl_ref, o_ref, vh_ref, vl_ref):
+def outer_project_kernel(scale, nparts, *refs):
+    lt_ref = refs[0]
+    r_refs = refs[1 : 1 + nparts]
+    wh_ref, wl_ref, o_ref, vh_ref, vl_ref = refs[1 + nparts :]
     width = wh_ref.shape[0] // (C_HI * C_LO)
     rows_i = lt_ref.shape[0] // (C_HI * C_LO)
     lanes = JB * width
-    nja = r_ref.shape[1] // lanes
+    nja = sum(r.shape[1] for r in r_refs) // lanes
     dd = wh_ref.shape[1]
 
     @pl.when(pl.program_id(0) == 0)
@@ -61,7 +64,9 @@
     acc = jnp.zeros(o_ref.shape, jnp.float32)
     block = C_LO * rows_i
     for c_hi in range(C_HI):
-        x = jnp.dot(lt_ref[c_hi * block : (c_hi + 1) * block, :], r_ref[...], preferred_element_type=jnp.float32)
+        lt_blk = lt_ref[c_hi * block : (c_hi + 1) * block, :]
+        xs = [jnp.dot(lt_blk, r[...], preferred_element_type=jnp.float32) for r in r_refs]
+        x = xs[0] if nparts == 1 else jnp.concatenate(xs, axis=1)
         xh = x.astype(jnp.bfloat16)
         xl = (x - xh.astype(jnp.float32)).astype(jnp.bfloat16)
         lh = rearrange(xh)
@@ -73,12 +78,16 @@
     o_ref[...] = acc * scale
 
 
-def outer_project(lt, r_all, wh, wl, scale):
+def outer_project(lt, r_parts, wh, wl, scale):
+    nparts = len(r_parts)
+    r_all = r_parts[0]
     rows_i = lt.shape[0] // (C_HI * C_LO)
     width = wh.shape[0] // (C_HI * C_LO)
     lanes = JB * width
-    total_lanes = r_all.shape[1]
+    total_lanes = sum(r.shape[1] for r in r_parts)
     chunk = min(total_lanes, 16 * lanes)
+    if nparts > 1:
+        assert chunk == total_lanes
     steps = total_lanes // chunk
     nja_chunk = chunk // lanes
     out_rows = (total_lanes // lanes) * rows_i
@@ -86,11 +95,15 @@
     s = lt.shape[1]
     flops = 2 * lt.shape[0] * s * total_lanes + 3 * 2 * out_rows * (C_LO * lanes) * (JB * d) * C_HI
     return pl.pallas_call(
-        functools.partial(outer_project_kernel, scale),
+        functools.partial(outer_project_kernel, scale, nparts),
         grid=(steps,),
         in_specs=[
             pl.BlockSpec(lt.shape, lambda q: (0, 0)),
-            pl.BlockSpec((s, chunk), lambda q: (0, q)),
+            *(
+                [pl.BlockSpec((s, chunk), lambda q: (0, q))]
+                if nparts == 1
+                else [pl.BlockSpec(r.shape, lambda q: (0, 0)) for r in r_parts]
+            ),
             pl.BlockSpec(wh.shape, lambda q: (0, 0)),
             pl.BlockSpec(wl.shape, lambda q: (0, 0)),
         ],
@@ -106,9 +119,9 @@
         cost_estimate=pl.CostEstimate(
             flops=flops,
             transcendentals=0,
-            bytes_accessed=lt.size * 2 + r_all.size * 2 + wh.size * 4 + out_rows * JB * d * 4,
-        ),
-    )(lt, r_all, wh, wl)
+            bytes_accessed=lt.size * 2 + total_lanes * s * 2 + wh.size * 4 + out_rows * JB * d * 4,
+        ),
+    )(lt, *r_parts, wh, wl)
 
 
 def chan_stage(block, chunk):
@@ -189,9 +202,8 @@
     w_lo = (moment_coupling_weights - w_hi_f32).astype(jnp.bfloat16)
     nres = lax.axis_size("res")
     if nres == 2:
-        r_other = jnp.concatenate([lax.ppermute(r, "res", [(0, 1), (1, 0)]) for r in right_parts], axis=1)
-        r_own = jnp.concatenate(right_parts, axis=1)
-        p_own = outer_project(lt, r_own, w_hi, w_lo, 1.0 / depth_total)
+        r_other = [lax.ppermute(r, "res", [(0, 1), (1, 0)]) for r in right_parts]
+        p_own = outer_project(lt, right_parts, w_hi, w_lo, 1.0 / depth_total)
         chunk = 2 * p_own.shape[0] // (lax.axis_size("seq") * lax.axis_size("chan"))
         part_own = chan_stage(p_own, chunk)
         p_other = outer_project(lt, r_other, w_hi, w_lo, 1.0 / depth_total)
@@ -203,7 +215,7 @@
         pair_update = seq_stage(part)
     else:
         r_all = lax.all_gather(jnp.concatenate(right_parts, axis=1), "res", axis=1, tiled=True)
-        partial_value = outer_project(lt, r_all, w_hi, w_lo, 1.0 / depth_total)
+        partial_value = outer_project(lt, [r_all], w_hi, w_lo, 1.0 / depth_total)
         pair_update = reduce_over_sequences(partial_value)
     nja_local = block_cols // JB
     pair_update = (

time: 43.9 us -> 42.4 us (0.966)
  other arithmetic: 6.02 us -> 5.05 us
  local copies, waits for them, and re-layouts: 2.42 us -> 1.75 us
    concatenate x2 -> x0, other arithmetic: 0.97 us -> none  [the longest x1 0.94 us: per_device(): jnp.concatenate([lax.ppermute(r, 'res', [(0, 1), (1, 0)]) for r in right_...]
    squeeze x2, local copies, waits for them, and re-layouts: 0.75 us -> 0.05 us  [chan_stage(): other = lax.dynamic_index_in_dim(xs, 1 - c, axis=1, keepdims=False)]
  transfers between devices with their start and end apart: 7 -> 7, of which waited for: 4 -> 4; matrix products, arithmetic and copies ran while one was open for 16% -> 13% of each run, Pallas kernels for 22% -> 23%
where the time goes in v11:
time: 42.4 us; the launch traced here: 42.1 us
  waiting for transfers between devices  10.5 us (25%)
  Pallas kernels  9.74 us (23%)
  starting transfers between devices  8.89 us (21%)
  matrix products  5.15 us (12%)
  other arithmetic  5.05 us (12%)
  local copies, waits for them, and re-layouts  1.75 us (4%)
  between operations  1.06 us (2%)
    ppermute x3, waiting for transfers between devices, seq_stage(): lax.ppermute(src, 'seq', [(q, (q + k) % nseq) for q in range(nseq)])  10.3 us
    pallas_call x2, Pallas kernels, outer_project(): pl.pallas_call(functools.partial(outer_project_kernel, scale, nparts), gr...  9.74 us
    ppermute x3, starting transfers between devices, seq_stage(): lax.ppermute(src, 'seq', [(q, (q + k) % nseq) for q in range(nseq)])  5.18 us
    ppermute x2, starting transfers between devices, per_device(): r_other = [lax.ppermute(r, 'res', [(0, 1), (1, 0)]) for r in right_parts]  3.08 us
    dot_general x2, matrix products, per_device(): jnp.einsum('hk,ihs->iks', homolog_shrink_weights, hidden, preferred_eleme...  3.07 us
    reduce_sum x1, other arithmetic, apply_layer_norm_axis1(): mean = jnp.mean(values, axis=1, keepdims=True)  1.53 us
    transpose x1, other arithmetic, per_device(): jnp.transpose(jnp.concatenate(refreshed_parts, axis=0), (2, 0, 1))  1.14 us
    dot_general x1, matrix products, per_device(): jnp.dot(pair_hidden, coupling_shrink_weights, preferred_element_type=jnp....  1.06 us
  transfers between devices with their start and end apart: 7, of which 4 were waited for; matrix products, arithmetic and copies ran while one was open for 13% of the time, Pallas kernels for 23%

profile of v11, /device:TPU:0, one launch (start us, length us, event | category | flops | bytes accessed | tf_op | source)
XLA Modules:
  0.0 42.1 jit_solution(12933929866525521218)
XLA Ops:
  0.6 0.0 copy-start
  0.7 1.5 %convert_reduce_fusion.1 = (f32[16,160]{1,0:T(8,128)S(1)}, f32[16,160]{1,0:T(8,128)S(1)}) fusion(bf16[32,64,160]{2,1,0:T(8,128)(2,1)} %bitcast.124), kind=kLoop, calls=%fused_computation.7 | loop fusion | flops 650240 | bytes 675840 | tf_op jit(solution)/shard_map/reduce_sum | solution.py:19
  2.2 0.0 copy-done.3
  2.2 0.4 fusion.26
  2.7 0.0 copy-start.7
  2.7 1.5 %convert_reduce_fusion.2 = (f32[16,160]{1,0:T(8,128)S(1)}, bf16[16,64,160]{2,1,0:T(8,128)(2,1)S(1)}) fusion(bf16[256,64]{0,1:T(8,128)(2,1)S(1)} %copy-done.9, f32[16,160]{1,0:T(8,128)S(1)} %add_rsqrt_fusion.2, f32[16,160]{1,0:T(8,128)S(1)} %get-tuple-element.15, bf16[32,64,160]{2,1,0:T(8,128)(2,1)S(1)} %bitcast.126, bf16[64,256]{1,0:T(8,128)(2,1)S(1)} %copy-done.10), kind=kOutput, calls=%fused_computation.15 | convolution fusion | flops 170554880 | bytes 1079296 | tf_op jit(solution)/shard_map/hk,ihs->iks/dot_general | solution.py:182
  4.2 0.2 fusion.28
  4.4 0.3 convolution_convert_fusion
  4.7 0.1 copy.31.refs_2_
  4.8 3.0 %collective-permute-start.2 = (bf16[160,512]{1,0:T(8,128)(2,1)S(1)}, bf16[160,512]{1,0:T(8,128)(2,1)S(1)}, u32[]{:S(2)}, u32[]{:S(2)}) collective-permute-start(bf16[160,512]{1,0:T(8,128)(2,1)S(1)} %copy.31.refs_2_), channel_id=1, source_target_pairs={{0,2},{2,0},{1,3},{3,1},{4,6},{6,4},{5,7},{7,5},{8,10},{10,8},{9,1... | collective-permute-start | bytes 491528 | tf_op jit(solution)/shard_map/ppermute | solution.py:205
  7.8 1.5 %convert_reduce_fusion.3 = (f32[16,160]{1,0:T(8,128)S(1)}, bf16[16,64,160]{2,1,0:T(8,128)(2,1)S(1)}) fusion(bf16[256,64]{0,1:T(8,128)(2,1)S(1)} %copy-done.9, f32[16,160]{1,0:T(8,128)S(1)} %add_rsqrt_fusion.3, f32[16,160]{1,0:T(8,128)S(1)} %get-tuple-element.16, bf16[32,64,160]{2,1,0:T(8,128)(2,1)S(1)} %bitcast.127, bf16[64,256]{1,0:T(8,128)(2,1)S(1)} %copy-done.10), kind=kOutput, calls=%fused_computation.17 | convolution fusion | flops 170554880 | bytes 1079296 | tf_op jit(solution)/shard_map/hk,ihs->iks/dot_general | solution.py:182
  9.4 0.0 copy-start.1
  9.4 0.0 copy-start.8
  9.4 0.2 fusion.30
  9.6 0.3 convolution_convert_fusion.1
  9.9 0.1 copy.30.refs_1_
  10.0 0.1 collective-permute-start.1
  10.1 0.0 copy-done.8
  10.1 0.3 fusion.20
  10.4 0.3 fusion.19
  10.7 0.0 copy-start.5
  10.7 0.1 pad_maximum_fusion
  10.8 0.3 copy.29
  11.1 0.6 %copy-done.5 = f32[1024,128]{1,0:T(8,128)S(1)} copy-done((f32[1024,128]{1,0:T(8,128)S(1)}, f32[1024,128]{1,0:T(8,128)}, u32[]{:S(2)}) %copy-start.5) | copy-done | bytes 524312
  11.7 0.1 fusion.36
  11.8 4.9 %shard_map.104 = f32[256,512]{1,0:T(8,128)S(1)} custom-call(bf16[1024,160]{1,0:T(8,128)(2,1)S(1)} %bitcast.122, bf16[160,512]{1,0:T(8,128)(2,1)S(1)} %copy.30.refs_1_, bf16[160,512]{1,0:T(8,128)(2,1)S(1)} %copy.31.refs_2_, bf16[1024,128]{1,0:T(8,128)(2,1)S(1)} %get-tuple-element.10.refs_3_, bf16[1024,128]{1,0:T(8,128)(2,1)S(1)} %get-tuple-element.9.refs_4_), custom_call_target="tpu_custom_call" | custom-call | flops 3556769792 | bytes 1703936 | tf_op jit(solution)/shard_map/pallas_call | solution.py:97
  16.7 0.1 collective-permute-start
  16.8 0.0 collective-permute-done.1.refs_1_
  16.8 4.9 %shard_map.105 = f32[256,512]{1,0:T(8,128)S(1)} custom-call(bf16[1024,160]{1,0:T(8,128)(2,1)S(1)} %bitcast.123, bf16[160,512]{1,0:T(8,128)(2,1)S(1)} %collective-permute-done.1.refs_1_, bf16[160,512]{1,0:T(8,128)(2,1)S(1)} %collective-permute-done.2.refs_2_, bf16[1024,128]{1,0:T(8,128)(2,1)S(1)} %get-tuple-element.10.refs_3_, ...), custom_call_target="tpu_custom_call" | custom-call | flops 3556769792 | bytes 1703936 | tf_op jit(solution)/shard_map/pallas_call | solution.py:97
  21.7 0.6 %collective-permute-start.3 = (f32[2,64,512]{2,1,0:T(8,128)S(1)}, f32[2,64,512]{2,1,0:T(8,128)S(1)}, u32[]{:S(2)}, u32[]{:S(2)}) collective-permute-start(f32[2,64,512]{2,1,0:T(8,128)S(1)} %dynamic-slice_bitcast_fusion), channel_id=1, source_target_pairs={{0,1},{1,0},{2,3},{3,2},{4,5},{5,4},{6,7},{7,6},{8,9},{9,8},{10,11... | collective-permute-start | bytes 786440 | tf_op jit(solution)/shard_map/ppermute | solution.py:134
  22.3 0.0 collective-permute-done
  22.3 1.0 %bitcast_add_fusion.1 = f32[2,64,512]{2,1,0:T(8,128)S(1)} fusion(f32[2,64,512]{2,1,0:T(8,128)} %collective-permute-done, f32[2,2,64,512]{3,2,1,0:T(8,128)S(1)} %bitcast.119, s32[]{:T(128)S(6)} %select_n.46), kind=kLoop, calls=%fused_computation.62 | loop fusion | flops 65536 | bytes 786436 | tf_op jit(solution)/shard_map/add | solution.py:134
  23.3 0.2 collective-permute-done.3
  23.5 0.0 copy-start.2
  23.6 2.1 %collective-permute-start.4 = (f32[64,512]{1,0:T(8,128)S(1)}, f32[64,512]{1,0:T(8,128)S(1)}, u32[]{:S(2)}, u32[]{:S(2)}) collective-permute-start(f32[64,512]{1,0:T(8,128)S(1)} %get-tuple-element.6), channel_id=1, source_target_pairs={{0,4},{4,8},{8,12},{12,0},{1,5},{5,9},{9,13},{13,1},{2,6},{6,10},{... | collective-permute-start | bytes 393224 | tf_op jit(solution)/shard_map/ppermute | solution.py:146
  25.7 2.1 %collective-permute-start.6 = (f32[64,512]{1,0:T(8,128)S(1)}, f32[64,512]{1,0:T(8,128)S(1)}, u32[]{:S(2)}, u32[]{:S(2)}) collective-permute-start(f32[64,512]{1,0:T(8,128)S(1)} %get-tuple-element.7), channel_id=1, source_target_pairs={{0,12},{4,0},{8,4},{12,8},{1,13},{5,1},{9,5},{13,9},{2,14},{6,2},{... | collective-permute-start | bytes 393224 | tf_op jit(solution)/shard_map/ppermute | solution.py:146
  27.8 0.9 %collective-permute-start.5 = (f32[64,512]{1,0:T(8,128)S(1)}, f32[64,512]{1,0:T(8,128)S(1)}, u32[]{:S(2)}, u32[]{:S(2)}) collective-permute-start(f32[64,512]{1,0:T(8,128)S(1)} %get-tuple-element.8), channel_id=1, source_target_pairs={{0,8},{4,12},{8,0},{12,4},{1,9},{5,13},{9,1},{13,5},{2,10},{6,14},... | collective-permute-start | bytes 393224 | tf_op jit(solution)/shard_map/ppermute | solution.py:146
  28.8 1.1 %maximum_bitcast_fusion = bf16[160,32,64]{0,2,1:T(8,128)(2,1)} fusion(bf16[16,64,160]{2,1,0:T(8,128)(2,1)S(1)} %get-tuple-element.12, bf16[16,64,160]{2,1,0:T(8,128)(2,1)S(1)} %copy-done.2), kind=kLoop, calls=%fused_computation.49 | loop fusion | flops 327680 | bytes 1310720 | tf_op jit(solution)/shard_map/transpose | solution.py:194
  29.9 2.2 %collective-permute-done.4 = f32[64,512]{1,0:T(8,128)S(1)} collective-permute-done((f32[64,512]{1,0:T(8,128)S(1)}, f32[64,512]{1,0:T(8,128)S(1)}, u32[]{:S(2)}, u32[]{:S(2)}) %collective-permute-start.4) | collective-permute-done | bytes 131104 | tf_op jit(solution)/shard_map/ppermute | solution.py:146
  32.1 1.9 %collective-permute-done.6 = f32[64,512]{1,0:T(8,128)S(1)} collective-permute-done((f32[64,512]{1,0:T(8,128)S(1)}, f32[64,512]{1,0:T(8,128)S(1)}, u32[]{:S(2)}, u32[]{:S(2)}) %collective-permute-start.6) | collective-permute-done | bytes 131104 | tf_op jit(solution)/shard_map/ppermute | solution.py:146
  34.0 6.2 %collective-permute-done.5 = f32[64,512]{1,0:T(8,128)S(1)} collective-permute-done((f32[64,512]{1,0:T(8,128)S(1)}, f32[64,512]{1,0:T(8,128)S(1)}, u32[]{:S(2)}, u32[]{:S(2)}) %collective-permute-start.5) | collective-permute-done | bytes 131104 | tf_op jit(solution)/shard_map/ppermute | solution.py:146
  40.3 0.1 fusion.60
  40.5 0.2 multiply_reduce_fusion
  40.7 0.1 copy.37
  40.7 0.1 copy.38
  40.8 0.1 rsqrt.48
  40.9 0.1 div.41
  41.0 1.1 %fusion.23 = f32[32,8,128]{2,1,0:T(8,128)} fusion(bf16[512,128]{1,0:T(8,128)(2,1)S(1)} %copy-done, bf16[128,512]{1,0:T(8,128)(2,1)S(1)} %copy-done.6, f32[256,128]{1,0:T(8,128)S(1)} %bitcast.134, f32[32,8,128]{2,1,0:T(8,128)S(1)} %copy-done.4, f32[256]{0:T(256)S(1)} %rsqrt.48, f32[256]{0:T(256)S(1)} %div.41), kind=kOutput, calls=%fused_computation.40 | convolution fusion | flops 67567616 | bytes 657408 | tf_op jit(solution)/shard_map/dot_general | solution.py:231
  (32 shorter events, 0.4 us)
Async XLA Ops:
  0.6 40.4 %copy-start = (bf16[512,128]{1,0:T(8,128)(2,1)S(1)}, bf16[512,128]{1,0:T(8,128)(2,1)}, u32[]{:S(2)}) copy-start(bf16[512,128]{1,0:T(8,128)(2,1)} %param.17) | copy-start | bytes 393220
  0.6 1.6 %copy-start.3 = (bf16[160,32,64]{0,2,1:T(8,128)(2,1)S(1)}, bf16[160,32,64]{0,2,1:T(8,128)(2,1)}, u32[]{:S(2)}) copy-start(bf16[160,32,64]{0,2,1:T(8,128)(2,1)} %param.9) | copy-start | bytes 1966084
  0.7 2.0 %copy-start.9 = (bf16[256,64]{0,1:T(8,128)(2,1)S(1)}, bf16[256,64]{0,1:T(8,128)(2,1)}, u32[]{:S(2)}) copy-start(bf16[256,64]{0,1:T(8,128)(2,1)} %param.12) | copy-start | bytes 98308
  0.7 2.0 %copy-start.10 = (bf16[64,256]{1,0:T(8,128)(2,1)S(1)}, bf16[64,256]{1,0:T(8,128)(2,1)}, u32[]{:S(2)}) copy-start(bf16[64,256]{1,0:T(8,128)(2,1)} %param.11) | copy-start | bytes 98308
  2.7 1.8 %copy-start.7 = (bf16[64,32]{0,1:T(8,128)(2,1)S(1)}, bf16[64,32]{0,1:T(8,128)(2,1)}, u32[]{:S(2)}) copy-start(bf16[64,32]{0,1:T(8,128)(2,1)} %param.14) | copy-start | bytes 12292
  4.8 12.0 %collective-permute-start.2 = (bf16[160,512]{1,0:T(8,128)(2,1)S(1)}, bf16[160,512]{1,0:T(8,128)(2,1)S(1)}, u32[]{:S(2)}, u32[]{:S(2)}) collective-permute-start(bf16[160,512]{1,0:T(8,128)(2,1)S(1)} %copy.31.refs_2_), channel_id=1, source_target_pairs={{0,2},{2,0},{1,3},{3,1},{4,6},{6,4},{5,7},{7,5},{8,10},{10,8},{9,1... | collective-permute-start | bytes 491528 | tf_op jit(solution)/shard_map/ppermute | solution.py:205
  9.4 1.0 %copy-start.1 = (bf16[16,64,160]{2,1,0:T(8,128)(2,1)}, bf16[16,64,160]{2,1,0:T(8,128)(2,1)S(1)}, u32[]{:S(2)}) copy-start(bf16[16,64,160]{2,1,0:T(8,128)(2,1)S(1)} %get-tuple-element.14) | copy-start | bytes 983044
  9.4 0.7 %copy-start.8 = (bf16[64,32]{0,1:T(8,128)(2,1)S(1)}, bf16[64,32]{0,1:T(8,128)(2,1)}, u32[]{:S(2)}) copy-start(bf16[64,32]{0,1:T(8,128)(2,1)} %param.13) | copy-start | bytes 12292
  10.0 6.8 %collective-permute-start.1 = (bf16[160,512]{1,0:T(8,128)(2,1)S(1)}, bf16[160,512]{1,0:T(8,128)(2,1)S(1)}, u32[]{:S(2)}, u32[]{:S(2)}) collective-permute-start(bf16[160,512]{1,0:T(8,128)(2,1)S(1)} %copy.30.refs_1_), channel_id=1, source_target_pairs={{0,2},{2,0},{1,3},{3,1},{4,6},{6,4},{5,7},{7,5},{8,10},{10,8},{9,1... | collective-permute-start | bytes 491528 | tf_op jit(solution)/shard_map/ppermute | solution.py:205
  10.7 1.0 %copy-start.5 = (f32[1024,128]{1,0:T(8,128)S(1)}, f32[1024,128]{1,0:T(8,128)}, u32[]{:S(2)}) copy-start(f32[1024,128]{1,0:T(8,128)} %param.15) | copy-start | bytes 1572868
  16.7 5.6 %collective-permute-start = (f32[2,64,512]{2,1,0:T(8,128)S(1)}, f32[2,64,512]{2,1,0:T(8,128)}, u32[]{:S(2)}, u32[]{:S(2)}) collective-permute-start(f32[2,64,512]{2,1,0:T(8,128)S(1)} %dynamic-slice_bitcast_fusion.1), channel_id=1, source_target_pairs={{0,1},{1,0},{2,3},{3,2},{4,5},{5,4},{6,7},{7,6},{8,9},{9,8},{10,11... | collective-permute-start | bytes 786440 | tf_op jit(solution)/shard_map/ppermute | solution.py:134
  21.7 1.7 %collective-permute-start.3 = (f32[2,64,512]{2,1,0:T(8,128)S(1)}, f32[2,64,512]{2,1,0:T(8,128)S(1)}, u32[]{:S(2)}, u32[]{:S(2)}) collective-permute-start(f32[2,64,512]{2,1,0:T(8,128)S(1)} %dynamic-slice_bitcast_fusion), channel_id=1, source_target_pairs={{0,1},{1,0},{2,3},{3,2},{4,5},{5,4},{6,7},{7,6},{8,9},{9,8},{10,11... | collective-permute-start | bytes 786440 | tf_op jit(solution)/shard_map/ppermute | solution.py:134
  23.5 5.3 %copy-start.2 = (bf16[16,64,160]{2,1,0:T(8,128)(2,1)S(1)}, bf16[16,64,160]{2,1,0:T(8,128)(2,1)}, u32[]{:S(2)}) copy-start(bf16[16,64,160]{2,1,0:T(8,128)(2,1)} %copy-done.1) | copy-start | bytes 983044
  23.6 8.6 %collective-permute-start.4 = (f32[64,512]{1,0:T(8,128)S(1)}, f32[64,512]{1,0:T(8,128)S(1)}, u32[]{:S(2)}, u32[]{:S(2)}) collective-permute-start(f32[64,512]{1,0:T(8,128)S(1)} %get-tuple-element.6), channel_id=1, source_target_pairs={{0,4},{4,8},{8,12},{12,0},{1,5},{5,9},{9,13},{13,1},{2,6},{6,10},{... | collective-permute-start | bytes 393224 | tf_op jit(solution)/shard_map/ppermute | solution.py:146
  25.7 8.3 %collective-permute-start.6 = (f32[64,512]{1,0:T(8,128)S(1)}, f32[64,512]{1,0:T(8,128)S(1)}, u32[]{:S(2)}, u32[]{:S(2)}) collective-permute-start(f32[64,512]{1,0:T(8,128)S(1)} %get-tuple-element.7), channel_id=1, source_target_pairs={{0,12},{4,0},{8,4},{12,8},{1,13},{5,1},{9,5},{13,9},{2,14},{6,2},{... | collective-permute-start | bytes 393224 | tf_op jit(solution)/shard_map/ppermute | solution.py:146
  27.8 12.4 %collective-permute-start.5 = (f32[64,512]{1,0:T(8,128)S(1)}, f32[64,512]{1,0:T(8,128)S(1)}, u32[]{:S(2)}, u32[]{:S(2)}) collective-permute-start(f32[64,512]{1,0:T(8,128)S(1)} %get-tuple-element.8), channel_id=1, source_target_pairs={{0,8},{4,12},{8,0},{12,4},{1,9},{5,13},{9,1},{13,5},{2,10},{6,14},... | collective-permute-start | bytes 393224 | tf_op jit(solution)/shard_map/ppermute | solution.py:146
  29.9 10.4 %copy-start.4 = (f32[32,8,128]{2,1,0:T(8,128)S(1)}, f32[32,8,128]{2,1,0:T(8,128)}, u32[]{:S(2)}) copy-start(f32[32,8,128]{2,1,0:T(8,128)} %param.10) | copy-start | bytes 393220
  29.9 11.1 %copy-start.6 = (bf16[128,512]{1,0:T(8,128)(2,1)S(1)}, bf16[128,512]{1,0:T(8,128)(2,1)}, u32[]{:S(2)}) copy-start(bf16[128,512]{1,0:T(8,128)(2,1)} %param.16) | copy-start | bytes 393220

commit v12 on v11

--- a/solution.py
+++ b/solution.py
@@ -128,9 +128,9 @@
     nchan = lax.axis_size("chan")
     rows, cols = block.shape
     xs = block.reshape(rows // (chunk * nchan), nchan, chunk, cols)
-    c = lax.axis_index("chan")
-    mine = lax.dynamic_index_in_dim(xs, c, axis=1, keepdims=False)
-    other = lax.dynamic_index_in_dim(xs, 1 - c, axis=1, keepdims=False)
+    first = lax.axis_index("chan") == 0
+    mine = jnp.where(first, xs[:, 0], xs[:, 1])
+    other = jnp.where(first, xs[:, 1], xs[:, 0])
     return mine + lax.ppermute(other, "chan", [(0, 1), (1, 0)])
 
 
@@ -143,6 +143,25 @@
     acc = lax.dynamic_index_in_dim(part, me, axis=0, keepdims=False)
     for k in range(1, nseq):
         src = lax.dynamic_index_in_dim(part, (me + k) % nseq, axis=0, keepdims=False)
+        acc = acc + lax.ppermute(src, "seq", [(q, (q + k) % nseq) for q in range(nseq)])
+    return acc
+
+
+def seq_stage_blocks(part_own, part_other):
+    nseq = lax.axis_size("seq")
+    half = part_own.shape[0]
+    me = lax.axis_index("seq")
+    r = lax.axis_index("res")
+
+    def entry(t):
+        q = t % half
+        own = lax.dynamic_index_in_dim(part_own, q, axis=0, keepdims=False)
+        other = lax.dynamic_index_in_dim(part_other, q, axis=0, keepdims=False)
+        return jnp.where(t // half == r, own, other)
+
+    acc = entry(me)
+    for k in range(1, nseq):
+        src = entry((me + k) % nseq)
         acc = acc + lax.ppermute(src, "seq", [(q, (q + k) % nseq) for q in range(nseq)])
     return acc
 
@@ -208,11 +227,7 @@
         part_own = chan_stage(p_own, chunk)
         p_other = outer_project(lt, r_other, w_hi, w_lo, 1.0 / depth_total)
         part_other = chan_stage(p_other, chunk)
-        first = lax.axis_index("res") == 0
-        part = jnp.where(
-            first, jnp.concatenate([part_own, part_other], axis=0), jnp.concatenate([part_other, part_own], axis=0)
-        )
-        pair_update = seq_stage(part)
+        pair_update = seq_stage_blocks(part_own, part_other)
     else:
         r_all = lax.all_gather(jnp.concatenate(right_parts, axis=1), "res", axis=1, tiled=True)
         partial_value = outer_project(lt, [r_all], w_hi, w_lo, 1.0 / depth_total)

time: 42.4 us -> 42.8 us (level)
  waiting for transfers between devices: 10.5 us -> 11.4 us
    ppermute x2, waiting for transfers between devices: 0.17 us -> 1.09 us  [chan_stage(): return mine + lax.ppermute(other, 'chan', [(0, 1), (1, 0)])]
    add x2, other arithmetic: 1.02 us -> 0.11 us  [chan_stage(): return mine + lax.ppermute(other, 'chan', [(0, 1), (1, 0)])]
    select_n x1 -> x3, other arithmetic: 0.04 us -> 0.83 us  [the longest x2 0.77 us: chan_stage(): other = jnp.where(first, xs[:, 1], xs[:, 0])]
  transfers between devices with their start and end apart: 7 -> 7, of which waited for: 4 -> 4; matrix products, arithmetic and copies ran while one was open for 13% -> 12% of each run, Pallas kernels for 23% -> 23%
where the time goes in v12:
time: 42.8 us; the launch traced here: 42.6 us
  waiting for transfers between devices  11.4 us (27%)
  Pallas kernels  9.74 us (23%)
  starting transfers between devices  8.85 us (21%)
  matrix products  5.15 us (12%)
  other arithmetic  4.93 us (12%)
  local copies, waits for them, and re-layouts  1.49 us (3%)
  between operations  1.02 us (2%)
    ppermute x3, waiting for transfers between devices, seq_stage_blocks(): lax.ppermute(src, 'seq', [(q, (q + k) % nseq) for q in range(nseq)])  10.3 us
    pallas_call x2, Pallas kernels, outer_project(): pl.pallas_call(functools.partial(outer_project_kernel, scale, nparts), gr...  9.74 us
    ppermute x3, starting transfers between devices, seq_stage_blocks(): lax.ppermute(src, 'seq', [(q, (q + k) % nseq) for q in range(nseq)])  5.18 us
    ppermute x2, starting transfers between devices, per_device(): r_other = [lax.ppermute(r, 'res', [(0, 1), (1, 0)]) for r in right_parts]  3.08 us
    dot_general x2, matrix products, per_device(): jnp.einsum('hk,ihs->iks', homolog_shrink_weights, hidden, preferred_eleme...  3.07 us
    reduce_sum x1, other arithmetic, apply_layer_norm_axis1(): mean = jnp.mean(values, axis=1, keepdims=True)  1.53 us
    transpose x1, other arithmetic, per_device(): jnp.transpose(jnp.concatenate(refreshed_parts, axis=0), (2, 0, 1))  1.14 us
    ppermute x2, waiting for transfers between devices, chan_stage(): return mine + lax.ppermute(other, 'chan', [(0, 1), (1, 0)])  1.09 us
  transfers between devices with their start and end apart: 7, of which 4 were waited for; matrix products, arithmetic and copies ran while one was open for 12% of the time, Pallas kernels for 23%

profile of v12, /device:TPU:0, one launch (start us, length us, event | category | flops | bytes accessed | tf_op | source)
XLA Modules:
  0.0 42.6 jit_solution(8178757926415216191)
XLA Ops:
  0.6 0.0 copy-start
  0.7 1.5 %convert_reduce_fusion.1 = (f32[16,160]{1,0:T(8,128)S(1)}, f32[16,160]{1,0:T(8,128)S(1)}) fusion(bf16[32,64,160]{2,1,0:T(8,128)(2,1)} %bitcast.152), kind=kLoop, calls=%fused_computation.7 | loop fusion | flops 650240 | bytes 675840 | tf_op jit(solution)/shard_map/reduce_sum | solution.py:19
  2.2 0.4 fusion.26
  2.7 0.0 copy-start.7
  2.7 1.5 %convert_reduce_fusion.2 = (f32[16,160]{1,0:T(8,128)S(1)}, bf16[16,64,160]{2,1,0:T(8,128)(2,1)S(1)}) fusion(bf16[256,64]{0,1:T(8,128)(2,1)S(1)} %copy-done.9, f32[16,160]{1,0:T(8,128)S(1)} %add_rsqrt_fusion.3, f32[16,160]{1,0:T(8,128)S(1)} %get-tuple-element.17, bf16[32,64,160]{2,1,0:T(8,128)(2,1)S(1)} %bitcast.154, bf16[64,256]{1,0:T(8,128)(2,1)S(1)} %copy-done.10), kind=kOutput, calls=%fused_computation.15 | convolution fusion | flops 170554880 | bytes 1079296 | tf_op jit(solution)/shard_map/hk,ihs->iks/dot_general | solution.py:201
  4.2 0.2 fusion.28
  4.4 0.3 convolution_convert_fusion
  4.7 0.1 copy.23.refs_2_
  4.8 3.0 %collective-permute-start.2 = (bf16[160,512]{1,0:T(8,128)(2,1)S(1)}, bf16[160,512]{1,0:T(8,128)(2,1)S(1)}, u32[]{:S(2)}, u32[]{:S(2)}) collective-permute-start(bf16[160,512]{1,0:T(8,128)(2,1)S(1)} %copy.23.refs_2_), channel_id=1, source_target_pairs={{0,2},{2,0},{1,3},{3,1},{4,6},{6,4},{5,7},{7,5},{8,10},{10,8},{9,1... | collective-permute-start | bytes 491528 | tf_op jit(solution)/shard_map/ppermute | solution.py:224
  7.8 1.5 %convert_reduce_fusion.3 = (f32[16,160]{1,0:T(8,128)S(1)}, bf16[16,64,160]{2,1,0:T(8,128)(2,1)S(1)}) fusion(bf16[256,64]{0,1:T(8,128)(2,1)S(1)} %copy-done.9, f32[16,160]{1,0:T(8,128)S(1)} %add_rsqrt_fusion.4, f32[16,160]{1,0:T(8,128)S(1)} %get-tuple-element.18, bf16[32,64,160]{2,1,0:T(8,128)(2,1)S(1)} %bitcast.155, bf16[64,256]{1,0:T(8,128)(2,1)S(1)} %copy-done.10), kind=kOutput, calls=%fused_computation.17 | convolution fusion | flops 170554880 | bytes 1079296 | tf_op jit(solution)/shard_map/hk,ihs->iks/dot_general | solution.py:201
  9.4 0.0 copy-start.1
  9.4 0.0 copy-start.8
  9.4 0.2 fusion.30
  9.6 0.3 convolution_convert_fusion.1
  9.9 0.1 copy.22.refs_1_
  10.0 0.1 collective-permute-start.1
  10.1 0.0 copy-done.8
  10.1 0.3 fusion.20
  10.4 0.3 fusion.19
  10.7 0.0 copy-start.5
  10.7 0.1 pad_maximum_fusion
  10.8 0.3 copy.21
  11.1 0.6 %copy-done.5 = f32[1024,128]{1,0:T(8,128)S(1)} copy-done((f32[1024,128]{1,0:T(8,128)S(1)}, f32[1024,128]{1,0:T(8,128)}, u32[]{:S(2)}) %copy-start.5) | copy-done | bytes 524312
  11.7 0.1 fusion.36
  11.8 4.9 %shard_map.104 = f32[256,512]{1,0:T(8,128)S(1)} custom-call(bf16[1024,160]{1,0:T(8,128)(2,1)S(1)} %bitcast.150, bf16[160,512]{1,0:T(8,128)(2,1)S(1)} %copy.22.refs_1_, bf16[160,512]{1,0:T(8,128)(2,1)S(1)} %copy.23.refs_2_, bf16[1024,128]{1,0:T(8,128)(2,1)S(1)} %get-tuple-element.12.refs_3_, bf16[1024,128]{1,0:T(8,128)(2,1)S(1)} %get-tuple-element.11.refs_4_), custom_call_target="tpu_custom_call" | custom-call | flops 3556769792 | bytes 1703936 | tf_op jit(solution)/shard_map/pallas_call | solution.py:97
  16.7 0.7 %select_bitcast_fusion.1 = f32[2,64,512]{2,1,0:T(8,128)} fusion(f32[2,2,64,512]{3,2,1,0:T(8,128)S(1)} %bitcast.146, pred[]{:T(512)S(6)} %eq.25), kind=kLoop, calls=%fused_computation.68 | loop fusion | flops 65536 | bytes 786433 | tf_op jit(solution)/shard_map/jit(_where)/select_n | solution.py:133
  17.4 0.0 collective-permute-start
  17.4 0.0 collective-permute-done.2.refs_2_
  17.4 0.0 collective-permute-done.1.refs_1_
  17.4 4.9 %shard_map.105 = f32[256,512]{1,0:T(8,128)S(1)} custom-call(bf16[1024,160]{1,0:T(8,128)(2,1)S(1)} %bitcast.151, bf16[160,512]{1,0:T(8,128)(2,1)S(1)} %collective-permute-done.1.refs_1_, bf16[160,512]{1,0:T(8,128)(2,1)S(1)} %collective-permute-done.2.refs_2_, bf16[1024,128]{1,0:T(8,128)(2,1)S(1)} %get-tuple-element.12.refs_3_, ...), custom_call_target="tpu_custom_call" | custom-call | flops 3556769792 | bytes 1703936 | tf_op jit(solution)/shard_map/pallas_call | solution.py:97
  22.3 0.6 %collective-permute-start.3 = (f32[2,64,512]{2,1,0:T(8,128)S(1)}, f32[2,64,512]{2,1,0:T(8,128)S(1)}, u32[]{:S(2)}, u32[]{:S(2)}) collective-permute-start(f32[2,64,512]{2,1,0:T(8,128)S(1)} %select_bitcast_fusion), channel_id=1, source_target_pairs={{0,1},{1,0},{2,3},{3,2},{4,5},{5,4},{6,7},{7,6},{8,9},{9,8},{10,11... | collective-permute-start | bytes 786440 | tf_op jit(solution)/shard_map/ppermute | solution.py:134
  22.9 0.1 bitcast_add_fusion
  23.0 0.0 copy-start.2
  23.0 1.1 %collective-permute-done.3 = f32[2,64,512]{2,1,0:T(8,128)S(1)} collective-permute-done((f32[2,64,512]{2,1,0:T(8,128)S(1)}, f32[2,64,512]{2,1,0:T(8,128)S(1)}, u32[]{:S(2)}, u32[]{:S(2)}) %collective-permute-start.3) | collective-permute-done | bytes 262176 | tf_op jit(solution)/shard_map/ppermute | solution.py:134
  24.1 0.1 fusion.54
  24.1 0.1 select_bitcast_fusion.4
  24.2 2.1 %collective-permute-start.4 = (f32[64,512]{1,0:T(8,128)S(1)}, f32[64,512]{1,0:T(8,128)S(1)}, u32[]{:S(2)}, u32[]{:S(2)}) collective-permute-start(f32[64,512]{1,0:T(8,128)S(1)} %get-tuple-element.8), channel_id=1, source_target_pairs={{0,4},{4,8},{8,12},{12,0},{1,5},{5,9},{9,13},{13,1},{2,6},{6,10},{... | collective-permute-start | bytes 393224 | tf_op jit(solution)/shard_map/ppermute | solution.py:165
  26.3 2.1 %collective-permute-start.6 = (f32[64,512]{1,0:T(8,128)S(1)}, f32[64,512]{1,0:T(8,128)S(1)}, u32[]{:S(2)}, u32[]{:S(2)}) collective-permute-start(f32[64,512]{1,0:T(8,128)S(1)} %get-tuple-element.9), channel_id=1, source_target_pairs={{0,12},{4,0},{8,4},{12,8},{1,13},{5,1},{9,5},{13,9},{2,14},{6,2},{... | collective-permute-start | bytes 393224 | tf_op jit(solution)/shard_map/ppermute | solution.py:165
  28.4 0.9 %collective-permute-start.5 = (f32[64,512]{1,0:T(8,128)S(1)}, f32[64,512]{1,0:T(8,128)S(1)}, u32[]{:S(2)}, u32[]{:S(2)}) collective-permute-start(f32[64,512]{1,0:T(8,128)S(1)} %get-tuple-element.10), channel_id=1, source_target_pairs={{0,8},{4,12},{8,0},{12,4},{1,9},{5,13},{9,1},{13,5},{2,10},{6,14},... | collective-permute-start | bytes 393224 | tf_op jit(solution)/shard_map/ppermute | solution.py:165
  29.4 1.1 %maximum_bitcast_fusion = bf16[160,32,64]{0,2,1:T(8,128)(2,1)} fusion(bf16[16,64,160]{2,1,0:T(8,128)(2,1)S(1)} %get-tuple-element.14, bf16[16,64,160]{2,1,0:T(8,128)(2,1)S(1)} %copy-done.2), kind=kLoop, calls=%fused_computation.49 | loop fusion | flops 327680 | bytes 1310720 | tf_op jit(solution)/shard_map/transpose | solution.py:213
  30.5 2.2 %collective-permute-done.4 = f32[64,512]{1,0:T(8,128)S(1)} collective-permute-done((f32[64,512]{1,0:T(8,128)S(1)}, f32[64,512]{1,0:T(8,128)S(1)}, u32[]{:S(2)}, u32[]{:S(2)}) %collective-permute-start.4) | collective-permute-done | bytes 131104 | tf_op jit(solution)/shard_map/ppermute | solution.py:165
  32.8 1.9 %collective-permute-done.6 = f32[64,512]{1,0:T(8,128)S(1)} collective-permute-done((f32[64,512]{1,0:T(8,128)S(1)}, f32[64,512]{1,0:T(8,128)S(1)}, u32[]{:S(2)}, u32[]{:S(2)}) %collective-permute-start.6) | collective-permute-done | bytes 131104 | tf_op jit(solution)/shard_map/ppermute | solution.py:165
  34.6 6.2 %collective-permute-done.5 = f32[64,512]{1,0:T(8,128)S(1)} collective-permute-done((f32[64,512]{1,0:T(8,128)S(1)}, f32[64,512]{1,0:T(8,128)S(1)}, u32[]{:S(2)}, u32[]{:S(2)}) %collective-permute-start.5) | collective-permute-done | bytes 131104 | tf_op jit(solution)/shard_map/ppermute | solution.py:165
  41.0 0.1 fusion.75
  41.1 0.1 div.82
  41.2 0.2 multiply_reduce_fusion
  41.4 0.1 rsqrt.48
  41.5 1.1 %fusion.23 = f32[32,8,128]{2,1,0:T(8,128)} fusion(bf16[512,128]{1,0:T(8,128)(2,1)S(1)} %copy-done, bf16[128,512]{1,0:T(8,128)(2,1)S(1)} %copy-done.6, f32[256,128]{1,0:T(8,128)S(1)} %bitcast.157, f32[32,8,128]{2,1,0:T(8,128)S(1)} %copy-done.4, f32[256]{0:T(256)S(1)} %rsqrt.48, f32[256]{0:T(256)S(1)} %div.82), kind=kOutput, calls=%fused_computation.40 | convolution fusion | flops 67567616 | bytes 657408 | tf_op jit(solution)/shard_map/dot_general | solution.py:246
  (28 shorter events, 0.2 us)
Async XLA Ops:
  0.6 40.8 %copy-start = (bf16[512,128]{1,0:T(8,128)(2,1)S(1)}, bf16[512,128]{1,0:T(8,128)(2,1)}, u32[]{:S(2)}) copy-start(bf16[512,128]{1,0:T(8,128)(2,1)} %param.17) | copy-start | bytes 393220
  0.6 1.6 %copy-start.3 = (bf16[160,32,64]{0,2,1:T(8,128)(2,1)S(1)}, bf16[160,32,64]{0,2,1:T(8,128)(2,1)}, u32[]{:S(2)}) copy-start(bf16[160,32,64]{0,2,1:T(8,128)(2,1)} %param.9) | copy-start | bytes 1966084
  0.7 2.0 %copy-start.9 = (bf16[256,64]{0,1:T(8,128)(2,1)S(1)}, bf16[256,64]{0,1:T(8,128)(2,1)}, u32[]{:S(2)}) copy-start(bf16[256,64]{0,1:T(8,128)(2,1)} %param.12) | copy-start | bytes 98308
  0.7 2.0 %copy-start.10 = (bf16[64,256]{1,0:T(8,128)(2,1)S(1)}, bf16[64,256]{1,0:T(8,128)(2,1)}, u32[]{:S(2)}) copy-start(bf16[64,256]{1,0:T(8,128)(2,1)} %param.11) | copy-start | bytes 98308
  2.7 1.8 %copy-start.7 = (bf16[64,32]{0,1:T(8,128)(2,1)S(1)}, bf16[64,32]{0,1:T(8,128)(2,1)}, u32[]{:S(2)}) copy-start(bf16[64,32]{0,1:T(8,128)(2,1)} %param.14) | copy-start | bytes 12292
  4.8 12.6 %collective-permute-start.2 = (bf16[160,512]{1,0:T(8,128)(2,1)S(1)}, bf16[160,512]{1,0:T(8,128)(2,1)S(1)}, u32[]{:S(2)}, u32[]{:S(2)}) collective-permute-start(bf16[160,512]{1,0:T(8,128)(2,1)S(1)} %copy.23.refs_2_), channel_id=1, source_target_pairs={{0,2},{2,0},{1,3},{3,1},{4,6},{6,4},{5,7},{7,5},{8,10},{10,8},{9,1... | collective-permute-start | bytes 491528 | tf_op jit(solution)/shard_map/ppermute | solution.py:224
  9.4 1.0 %copy-start.1 = (bf16[16,64,160]{2,1,0:T(8,128)(2,1)}, bf16[16,64,160]{2,1,0:T(8,128)(2,1)S(1)}, u32[]{:S(2)}) copy-start(bf16[16,64,160]{2,1,0:T(8,128)(2,1)S(1)} %get-tuple-element.16) | copy-start | bytes 983044
  9.4 0.7 %copy-start.8 = (bf16[64,32]{0,1:T(8,128)(2,1)S(1)}, bf16[64,32]{0,1:T(8,128)(2,1)}, u32[]{:S(2)}) copy-start(bf16[64,32]{0,1:T(8,128)(2,1)} %param.13) | copy-start | bytes 12292
  10.0 7.4 %collective-permute-start.1 = (bf16[160,512]{1,0:T(8,128)(2,1)S(1)}, bf16[160,512]{1,0:T(8,128)(2,1)S(1)}, u32[]{:S(2)}, u32[]{:S(2)}) collective-permute-start(bf16[160,512]{1,0:T(8,128)(2,1)S(1)} %copy.22.refs_1_), channel_id=1, source_target_pairs={{0,2},{2,0},{1,3},{3,1},{4,6},{6,4},{5,7},{7,5},{8,10},{10,8},{9,1... | collective-permute-start | bytes 491528 | tf_op jit(solution)/shard_map/ppermute | solution.py:224
  10.7 1.0 %copy-start.5 = (f32[1024,128]{1,0:T(8,128)S(1)}, f32[1024,128]{1,0:T(8,128)}, u32[]{:S(2)}) copy-start(f32[1024,128]{1,0:T(8,128)} %param.15) | copy-start | bytes 1572868
  17.4 5.5 %collective-permute-start = (f32[2,64,512]{2,1,0:T(8,128)}, f32[2,64,512]{2,1,0:T(8,128)S(1)}, u32[]{:S(2)}, u32[]{:S(2)}) collective-permute-start(f32[2,64,512]{2,1,0:T(8,128)} %select_bitcast_fusion.1), channel_id=1, source_target_pairs={{0,1},{1,0},{2,3},{3,2},{4,5},{5,4},{6,7},{7,6},{8,9},{9,8},{10,11... | collective-permute-start | bytes 786440 | tf_op jit(solution)/shard_map/ppermute | solution.py:134
  22.3 1.7 %collective-permute-start.3 = (f32[2,64,512]{2,1,0:T(8,128)S(1)}, f32[2,64,512]{2,1,0:T(8,128)S(1)}, u32[]{:S(2)}, u32[]{:S(2)}) collective-permute-start(f32[2,64,512]{2,1,0:T(8,128)S(1)} %select_bitcast_fusion), channel_id=1, source_target_pairs={{0,1},{1,0},{2,3},{3,2},{4,5},{5,4},{6,7},{7,6},{8,9},{9,8},{10,11... | collective-permute-start | bytes 786440 | tf_op jit(solution)/shard_map/ppermute | solution.py:134
  23.0 6.4 %copy-start.2 = (bf16[16,64,160]{2,1,0:T(8,128)(2,1)S(1)}, bf16[16,64,160]{2,1,0:T(8,128)(2,1)}, u32[]{:S(2)}) copy-start(bf16[16,64,160]{2,1,0:T(8,128)(2,1)} %copy-done.1) | copy-start | bytes 983044
  24.2 8.6 %collective-permute-start.4 = (f32[64,512]{1,0:T(8,128)S(1)}, f32[64,512]{1,0:T(8,128)S(1)}, u32[]{:S(2)}, u32[]{:S(2)}) collective-permute-start(f32[64,512]{1,0:T(8,128)S(1)} %get-tuple-element.8), channel_id=1, source_target_pairs={{0,4},{4,8},{8,12},{12,0},{1,5},{5,9},{9,13},{13,1},{2,6},{6,10},{... | collective-permute-start | bytes 393224 | tf_op jit(solution)/shard_map/ppermute | solution.py:165
  26.3 8.3 %collective-permute-start.6 = (f32[64,512]{1,0:T(8,128)S(1)}, f32[64,512]{1,0:T(8,128)S(1)}, u32[]{:S(2)}, u32[]{:S(2)}) collective-permute-start(f32[64,512]{1,0:T(8,128)S(1)} %get-tuple-element.9), channel_id=1, source_target_pairs={{0,12},{4,0},{8,4},{12,8},{1,13},{5,1},{9,5},{13,9},{2,14},{6,2},{... | collective-permute-start | bytes 393224 | tf_op jit(solution)/shard_map/ppermute | solution.py:165
  28.4 12.4 %collective-permute-start.5 = (f32[64,512]{1,0:T(8,128)S(1)}, f32[64,512]{1,0:T(8,128)S(1)}, u32[]{:S(2)}, u32[]{:S(2)}) collective-permute-start(f32[64,512]{1,0:T(8,128)S(1)} %get-tuple-element.10), channel_id=1, source_target_pairs={{0,8},{4,12},{8,0},{12,4},{1,9},{5,13},{9,1},{13,5},{2,10},{6,14},... | collective-permute-start | bytes 393224 | tf_op jit(solution)/shard_map/ppermute | solution.py:165
  30.5 10.4 %copy-start.4 = (f32[32,8,128]{2,1,0:T(8,128)S(1)}, f32[32,8,128]{2,1,0:T(8,128)}, u32[]{:S(2)}) copy-start(f32[32,8,128]{2,1,0:T(8,128)} %param.10) | copy-start | bytes 393220
  30.5 10.9 %copy-start.6 = (bf16[128,512]{1,0:T(8,128)(2,1)S(1)}, bf16[128,512]{1,0:T(8,128)(2,1)}, u32[]{:S(2)}) copy-start(bf16[128,512]{1,0:T(8,128)(2,1)} %param.16) | copy-start | bytes 393220

commit v13 on v11

--- a/solution.py
+++ b/solution.py
@@ -27,12 +27,12 @@
 JB = 4
 
 
-def outer_project_kernel(scale, nparts, *refs):
-    lt_ref = refs[0]
-    r_refs = refs[1 : 1 + nparts]
-    wh_ref, wl_ref, o_ref, vh_ref, vl_ref = refs[1 + nparts :]
+def outer_project_kernel(scale, nlt, nparts, *refs):
+    lt_refs = refs[:nlt]
+    r_refs = refs[nlt : nlt + nparts]
+    wh_ref, wl_ref, o_ref, vh_ref, vl_ref = refs[nlt + nparts :]
     width = wh_ref.shape[0] // (C_HI * C_LO)
-    rows_i = lt_ref.shape[0] // (C_HI * C_LO)
+    rows_i = sum(t.shape[1] for t in lt_refs)
     lanes = JB * width
     nja = sum(r.shape[1] for r in r_refs) // lanes
     dd = wh_ref.shape[1]
@@ -64,7 +64,9 @@
     acc = jnp.zeros(o_ref.shape, jnp.float32)
     block = C_LO * rows_i
     for c_hi in range(C_HI):
-        lt_blk = lt_ref[c_hi * block : (c_hi + 1) * block, :]
+        lt_blk = jnp.concatenate(
+            [t[c_hi * C_LO + c_lo] for c_lo in range(C_LO) for t in lt_refs], axis=0
+        )
         xs = [jnp.dot(lt_blk, r[...], preferred_element_type=jnp.float32) for r in r_refs]
         x = xs[0] if nparts == 1 else jnp.concatenate(xs, axis=1)
         xh = x.astype(jnp.bfloat16)
@@ -78,10 +80,11 @@
     o_ref[...] = acc * scale
 
 
-def outer_project(lt, r_parts, wh, wl, scale):
+def outer_project(lt_parts, r_parts, wh, wl, scale):
     nparts = len(r_parts)
+    nlt = len(lt_parts)
     r_all = r_parts[0]
-    rows_i = lt.shape[0] // (C_HI * C_LO)
+    rows_i = sum(t.shape[1] for t in lt_parts)
     width = wh.shape[0] // (C_HI * C_LO)
     lanes = JB * width
     total_lanes = sum(r.shape[1] for r in r_parts)
@@ -92,13 +95,13 @@
     nja_chunk = chunk // lanes
     out_rows = (total_lanes // lanes) * rows_i
     d = wh.shape[1]
-    s = lt.shape[1]
-    flops = 2 * lt.shape[0] * s * total_lanes + 3 * 2 * out_rows * (C_LO * lanes) * (JB * d) * C_HI
+    s = lt_parts[0].shape[2]
+    flops = 2 * C_HI * C_LO * rows_i * s * total_lanes + 3 * 2 * out_rows * (C_LO * lanes) * (JB * d) * C_HI
     return pl.pallas_call(
-        functools.partial(outer_project_kernel, scale, nparts),
+        functools.partial(outer_project_kernel, scale, nlt, nparts),
         grid=(steps,),
         in_specs=[
-            pl.BlockSpec(lt.shape, lambda q: (0, 0)),
+            *[pl.BlockSpec(t.shape, lambda q: (0, 0, 0)) for t in lt_parts],
             *(
                 [pl.BlockSpec((s, chunk), lambda q: (0, q))]
                 if nparts == 1
@@ -119,9 +122,9 @@
         cost_estimate=pl.CostEstimate(
             flops=flops,
             transcendentals=0,
-            bytes_accessed=lt.size * 2 + total_lanes * s * 2 + wh.size * 4 + out_rows * JB * d * 4,
-        ),
-    )(lt, *r_parts, wh, wl)
+            bytes_accessed=C_HI * C_LO * rows_i * s * 2 + total_lanes * s * 2 + wh.size * 4 + out_rows * JB * d * 4,
+        ),
+    )(*lt_parts, *r_parts, wh, wl)
 
 
 def chan_stage(block, chunk):
@@ -192,7 +195,6 @@
             jnp.einsum("kc,iks->cis", lhs_projector, n2, preferred_element_type=jnp.float32).astype(jnp.bfloat16)
         )
     homolog_refreshed = jnp.transpose(jnp.concatenate(refreshed_parts, axis=0), (2, 0, 1))
-    lt = jnp.concatenate(lt_parts, axis=1).reshape(proj_width * sites_local_share, homologs_local_share)
     owners = lax.axis_size(("seq", "chan"))
     depth_total = float(homologs_local_share * owners)
     block_cols = coupling_embedding.shape[1]
@@ -203,10 +205,10 @@
     nres = lax.axis_size("res")
     if nres == 2:
         r_other = [lax.ppermute(r, "res", [(0, 1), (1, 0)]) for r in right_parts]
-        p_own = outer_project(lt, right_parts, w_hi, w_lo, 1.0 / depth_total)
+        p_own = outer_project(lt_parts, right_parts, w_hi, w_lo, 1.0 / depth_total)
         chunk = 2 * p_own.shape[0] // (lax.axis_size("seq") * lax.axis_size("chan"))
         part_own = chan_stage(p_own, chunk)
-        p_other = outer_project(lt, r_other, w_hi, w_lo, 1.0 / depth_total)
+        p_other = outer_project(lt_parts, r_other, w_hi, w_lo, 1.0 / depth_total)
         part_other = chan_stage(p_other, chunk)
         first = lax.axis_index("res") == 0
         part = jnp.where(
@@ -215,7 +217,7 @@
         pair_update = seq_stage(part)
     else:
         r_all = lax.all_gather(jnp.concatenate(right_parts, axis=1), "res", axis=1, tiled=True)
-        partial_value = outer_project(lt, [r_all], w_hi, w_lo, 1.0 / depth_total)
+        partial_value = outer_project(lt_parts, [r_all], w_hi, w_lo, 1.0 / depth_total)
         pair_update = reduce_over_sequences(partial_value)
     nja_local = block_cols // JB
     pair_update = (

time: 42.4 us -> 42.1 us (level)
  transfers between devices with their start and end apart: 7 -> 7, of which waited for: 4 -> 4; matrix products, arithmetic and copies ran while one was open for 13% -> 12% of each run, Pallas kernels for 23% -> 23%
where the time goes in v13:
time: 42.1 us; the launch traced here: 41.8 us
  waiting for transfers between devices  10.5 us (25%)
  Pallas kernels  9.74 us (23%)
  starting transfers between devices  8.88 us (21%)
  matrix products  5.15 us (12%)
  other arithmetic  4.96 us (12%)
  local copies, waits for them, and re-layouts  1.58 us (4%)
  between operations  1.06 us (3%)
    ppermute x3, waiting for transfers between devices, seq_stage(): lax.ppermute(src, 'seq', [(q, (q + k) % nseq) for q in range(nseq)])  10.3 us
    pallas_call x2, Pallas kernels, outer_project(): pl.pallas_call(functools.partial(outer_project_kernel, scale, nlt, nparts...  9.74 us
    ppermute x3, starting transfers between devices, seq_stage(): lax.ppermute(src, 'seq', [(q, (q + k) % nseq) for q in range(nseq)])  5.17 us
    ppermute x2, starting transfers between devices, per_device(): r_other = [lax.ppermute(r, 'res', [(0, 1), (1, 0)]) for r in right_parts]  3.08 us
    dot_general x2, matrix products, per_device(): jnp.einsum('hk,ihs->iks', homolog_shrink_weights, hidden, preferred_eleme...  3.07 us
    reduce_sum x1, other arithmetic, apply_layer_norm_axis1(): mean = jnp.mean(values, axis=1, keepdims=True)  1.53 us
    transpose x1, other arithmetic, per_device(): jnp.transpose(jnp.concatenate(refreshed_parts, axis=0), (2, 0, 1))  1.14 us
    dot_general x1, matrix products, per_device(): jnp.dot(pair_hidden, coupling_shrink_weights, preferred_element_type=jnp....  1.06 us
  transfers between devices with their start and end apart: 7, of which 4 were waited for; matrix products, arithmetic and copies ran while one was open for 12% of the time, Pallas kernels for 23%

profile of v13, /device:TPU:0, one launch (start us, length us, event | category | flops | bytes accessed | tf_op | source)
XLA Modules:
  0.0 41.8 jit_solution(1994489101665769468)
XLA Ops:
  0.6 0.0 copy-start
  0.7 1.5 %convert_reduce_fusion.1 = (f32[16,160]{1,0:T(8,128)S(1)}, f32[16,160]{1,0:T(8,128)S(1)}) fusion(bf16[32,64,160]{2,1,0:T(8,128)(2,1)} %bitcast.127), kind=kLoop, calls=%fused_computation.7 | loop fusion | flops 650240 | bytes 675840 | tf_op jit(solution)/shard_map/reduce_sum | solution.py:19
  2.2 0.0 copy-done.3
  2.2 0.4 fusion.24
  2.7 0.0 copy-start.7
  2.7 1.5 %convert_reduce_fusion.2 = (f32[16,160]{1,0:T(8,128)S(1)}, bf16[16,64,160]{2,1,0:T(8,128)(2,1)S(1)}) fusion(bf16[256,64]{0,1:T(8,128)(2,1)S(1)} %copy-done.9, f32[16,160]{1,0:T(8,128)S(1)} %add_rsqrt_fusion.2, f32[16,160]{1,0:T(8,128)S(1)} %get-tuple-element.15, bf16[32,64,160]{2,1,0:T(8,128)(2,1)S(1)} %bitcast.129, bf16[64,256]{1,0:T(8,128)(2,1)S(1)} %copy-done.10), kind=kOutput, calls=%fused_computation.15 | convolution fusion | flops 170554880 | bytes 1079296 | tf_op jit(solution)/shard_map/hk,ihs->iks/dot_general | solution.py:185
  4.2 0.2 fusion.26
  4.4 0.3 convolution_convert_fusion
  4.7 0.1 copy.35.refs_3_
  4.8 3.0 %collective-permute-start.2 = (bf16[160,512]{1,0:T(8,128)(2,1)S(1)}, bf16[160,512]{1,0:T(8,128)(2,1)S(1)}, u32[]{:S(2)}, u32[]{:S(2)}) collective-permute-start(bf16[160,512]{1,0:T(8,128)(2,1)S(1)} %copy.35.refs_3_), channel_id=1, source_target_pairs={{0,2},{2,0},{1,3},{3,1},{4,6},{6,4},{5,7},{7,5},{8,10},{10,8},{9,1... | collective-permute-start | bytes 491528 | tf_op jit(solution)/shard_map/ppermute | solution.py:207
  7.8 1.5 %convert_reduce_fusion.3 = (f32[16,160]{1,0:T(8,128)S(1)}, bf16[16,64,160]{2,1,0:T(8,128)(2,1)S(1)}) fusion(bf16[256,64]{0,1:T(8,128)(2,1)S(1)} %copy-done.9, f32[16,160]{1,0:T(8,128)S(1)} %add_rsqrt_fusion.3, f32[16,160]{1,0:T(8,128)S(1)} %get-tuple-element.16, bf16[32,64,160]{2,1,0:T(8,128)(2,1)S(1)} %bitcast.130, bf16[64,256]{1,0:T(8,128)(2,1)S(1)} %copy-done.10), kind=kOutput, calls=%fused_computation.17 | convolution fusion | flops 170554880 | bytes 1079296 | tf_op jit(solution)/shard_map/hk,ihs->iks/dot_general | solution.py:185
  9.4 0.0 copy-start.1
  9.4 0.0 copy-start.8
  9.4 0.2 fusion.28
  9.6 0.3 convolution_convert_fusion.1
  9.9 0.1 copy.34.refs_2_
  10.0 0.1 collective-permute-start.1
  10.1 0.0 copy-done.8
  10.1 0.3 fusion.50
  10.4 0.0 copy-start.5
  10.4 0.3 fusion.47
  10.7 0.2 copy.55
  10.8 0.2 copy.54
  11.0 0.5 %copy-done.5 = f32[1024,128]{1,0:T(8,128)S(1)} copy-done((f32[1024,128]{1,0:T(8,128)S(1)}, f32[1024,128]{1,0:T(8,128)}, u32[]{:S(2)}) %copy-start.5) | copy-done | bytes 524312
  11.4 0.1 fusion.34
  11.5 4.9 %shard_map.104 = f32[256,512]{1,0:T(8,128)S(1)} custom-call(bf16[32,16,160]{2,1,0:T(8,128)(2,1)S(1)} %bitcast.125, bf16[32,16,160]{2,1,0:T(8,128)(2,1)S(1)} %bitcast.123, bf16[160,512]{1,0:T(8,128)(2,1)S(1)} %copy.34.refs_2_, bf16[160,512]{1,0:T(8,128)(2,1)S(1)} %copy.35.refs_3_, bf16[1024,128]{1,0:T(8,128)(2,1)S(1)} %get-tuple-element.10.refs_4_, ...), custom_call_target="tpu_custom_call" | custom-call | flops 3556769792 | bytes 1703936 | tf_op jit(solution)/shard_map/pallas_call | solution.py:100
  16.4 0.1 collective-permute-start
  16.5 0.0 collective-permute-done.1.refs_2_
  16.5 4.9 %shard_map.105 = f32[256,512]{1,0:T(8,128)S(1)} custom-call(bf16[32,16,160]{2,1,0:T(8,128)(2,1)S(1)} %bitcast.126, bf16[32,16,160]{2,1,0:T(8,128)(2,1)S(1)} %bitcast.124, bf16[160,512]{1,0:T(8,128)(2,1)S(1)} %collective-permute-done.1.refs_2_, bf16[160,512]{1,0:T(8,128)(2,1)S(1)} %collective-permute-done.2.refs_3_, ...), custom_call_target="tpu_custom_call" | custom-call | flops 3556769792 | bytes 1703936 | tf_op jit(solution)/shard_map/pallas_call | solution.py:100
  21.5 0.5 %collective-permute-start.3 = (f32[2,64,512]{2,1,0:T(8,128)S(1)}, f32[2,64,512]{2,1,0:T(8,128)S(1)}, u32[]{:S(2)}, u32[]{:S(2)}) collective-permute-start(f32[2,64,512]{2,1,0:T(8,128)S(1)} %dynamic-slice_bitcast_fusion), channel_id=1, source_target_pairs={{0,1},{1,0},{2,3},{3,2},{4,5},{5,4},{6,7},{7,6},{8,9},{9,8},{10,11... | collective-permute-start | bytes 786440 | tf_op jit(solution)/shard_map/ppermute | solution.py:137
  22.0 0.0 collective-permute-done
  22.0 1.0 %bitcast_add_fusion.1 = f32[2,64,512]{2,1,0:T(8,128)S(1)} fusion(f32[2,64,512]{2,1,0:T(8,128)} %collective-permute-done, f32[2,2,64,512]{3,2,1,0:T(8,128)S(1)} %bitcast.120, s32[]{:T(128)S(6)} %select_n.46), kind=kLoop, calls=%fused_computation.63 | loop fusion | flops 65536 | bytes 786436 | tf_op jit(solution)/shard_map/add | solution.py:137
  23.0 0.2 collective-permute-done.3
  23.2 0.0 copy-start.2
  23.3 2.1 %collective-permute-start.4 = (f32[64,512]{1,0:T(8,128)S(1)}, f32[64,512]{1,0:T(8,128)S(1)}, u32[]{:S(2)}, u32[]{:S(2)}) collective-permute-start(f32[64,512]{1,0:T(8,128)S(1)} %get-tuple-element.6), channel_id=1, source_target_pairs={{0,4},{4,8},{8,12},{12,0},{1,5},{5,9},{9,13},{13,1},{2,6},{6,10},{... | collective-permute-start | bytes 393224 | tf_op jit(solution)/shard_map/ppermute | solution.py:149
  25.4 2.1 %collective-permute-start.6 = (f32[64,512]{1,0:T(8,128)S(1)}, f32[64,512]{1,0:T(8,128)S(1)}, u32[]{:S(2)}, u32[]{:S(2)}) collective-permute-start(f32[64,512]{1,0:T(8,128)S(1)} %get-tuple-element.7), channel_id=1, source_target_pairs={{0,12},{4,0},{8,4},{12,8},{1,13},{5,1},{9,5},{13,9},{2,14},{6,2},{... | collective-permute-start | bytes 393224 | tf_op jit(solution)/shard_map/ppermute | solution.py:149
  27.5 0.9 %collective-permute-start.5 = (f32[64,512]{1,0:T(8,128)S(1)}, f32[64,512]{1,0:T(8,128)S(1)}, u32[]{:S(2)}, u32[]{:S(2)}) collective-permute-start(f32[64,512]{1,0:T(8,128)S(1)} %get-tuple-element.8), channel_id=1, source_target_pairs={{0,8},{4,12},{8,0},{12,4},{1,9},{5,13},{9,1},{13,5},{2,10},{6,14},... | collective-permute-start | bytes 393224 | tf_op jit(solution)/shard_map/ppermute | solution.py:149
  28.5 1.1 %maximum_bitcast_fusion = bf16[160,32,64]{0,2,1:T(8,128)(2,1)} fusion(bf16[16,64,160]{2,1,0:T(8,128)(2,1)S(1)} %get-tuple-element.14, bf16[16,64,160]{2,1,0:T(8,128)(2,1)S(1)} %copy-done.2), kind=kLoop, calls=%fused_computation.45 | loop fusion | flops 327680 | bytes 1310720 | tf_op jit(solution)/shard_map/transpose | solution.py:197
  29.6 2.2 %collective-permute-done.4 = f32[64,512]{1,0:T(8,128)S(1)} collective-permute-done((f32[64,512]{1,0:T(8,128)S(1)}, f32[64,512]{1,0:T(8,128)S(1)}, u32[]{:S(2)}, u32[]{:S(2)}) %collective-permute-start.4) | collective-permute-done | bytes 131104 | tf_op jit(solution)/shard_map/ppermute | solution.py:149
  31.9 1.9 %collective-permute-done.6 = f32[64,512]{1,0:T(8,128)S(1)} collective-permute-done((f32[64,512]{1,0:T(8,128)S(1)}, f32[64,512]{1,0:T(8,128)S(1)}, u32[]{:S(2)}, u32[]{:S(2)}) %collective-permute-start.6) | collective-permute-done | bytes 131104 | tf_op jit(solution)/shard_map/ppermute | solution.py:149
  33.7 6.2 %collective-permute-done.5 = f32[64,512]{1,0:T(8,128)S(1)} collective-permute-done((f32[64,512]{1,0:T(8,128)S(1)}, f32[64,512]{1,0:T(8,128)S(1)}, u32[]{:S(2)}, u32[]{:S(2)}) %collective-permute-start.5) | collective-permute-done | bytes 131104 | tf_op jit(solution)/shard_map/ppermute | solution.py:149
  40.1 0.1 fusion.62
  40.2 0.2 multiply_reduce_fusion
  40.4 0.1 copy.41
  40.5 0.1 copy.42
  40.6 0.1 rsqrt.48
  40.7 0.1 div.41
  40.8 1.1 %fusion.21 = f32[32,8,128]{2,1,0:T(8,128)} fusion(bf16[512,128]{1,0:T(8,128)(2,1)S(1)} %copy-done, bf16[128,512]{1,0:T(8,128)(2,1)S(1)} %copy-done.6, f32[256,128]{1,0:T(8,128)S(1)} %bitcast.137, f32[32,8,128]{2,1,0:T(8,128)S(1)} %copy-done.4, f32[256]{0:T(256)S(1)} %rsqrt.48, f32[256]{0:T(256)S(1)} %div.41), kind=kOutput, calls=%fused_computation.36 | convolution fusion | flops 67567616 | bytes 657408 | tf_op jit(solution)/shard_map/dot_general | solution.py:233
  (32 shorter events, 0.4 us)
Async XLA Ops:
  0.6 40.1 %copy-start = (bf16[512,128]{1,0:T(8,128)(2,1)S(1)}, bf16[512,128]{1,0:T(8,128)(2,1)}, u32[]{:S(2)}) copy-start(bf16[512,128]{1,0:T(8,128)(2,1)} %param.17) | copy-start | bytes 393220
  0.6 1.6 %copy-start.3 = (bf16[160,32,64]{0,2,1:T(8,128)(2,1)S(1)}, bf16[160,32,64]{0,2,1:T(8,128)(2,1)}, u32[]{:S(2)}) copy-start(bf16[160,32,64]{0,2,1:T(8,128)(2,1)} %param.9) | copy-start | bytes 1966084
  0.7 2.0 %copy-start.9 = (bf16[256,64]{0,1:T(8,128)(2,1)S(1)}, bf16[256,64]{0,1:T(8,128)(2,1)}, u32[]{:S(2)}) copy-start(bf16[256,64]{0,1:T(8,128)(2,1)} %param.12) | copy-start | bytes 98308
  0.7 2.0 %copy-start.10 = (bf16[64,256]{1,0:T(8,128)(2,1)S(1)}, bf16[64,256]{1,0:T(8,128)(2,1)}, u32[]{:S(2)}) copy-start(bf16[64,256]{1,0:T(8,128)(2,1)} %param.11) | copy-start | bytes 98308
  2.7 1.8 %copy-start.7 = (bf16[64,32]{0,1:T(8,128)(2,1)S(1)}, bf16[64,32]{0,1:T(8,128)(2,1)}, u32[]{:S(2)}) copy-start(bf16[64,32]{0,1:T(8,128)(2,1)} %param.14) | copy-start | bytes 12292
  4.8 11.7 %collective-permute-start.2 = (bf16[160,512]{1,0:T(8,128)(2,1)S(1)}, bf16[160,512]{1,0:T(8,128)(2,1)S(1)}, u32[]{:S(2)}, u32[]{:S(2)}) collective-permute-start(bf16[160,512]{1,0:T(8,128)(2,1)S(1)} %copy.35.refs_3_), channel_id=1, source_target_pairs={{0,2},{2,0},{1,3},{3,1},{4,6},{6,4},{5,7},{7,5},{8,10},{10,8},{9,1... | collective-permute-start | bytes 491528 | tf_op jit(solution)/shard_map/ppermute | solution.py:207
  9.4 1.0 %copy-start.1 = (bf16[16,64,160]{2,1,0:T(8,128)(2,1)}, bf16[16,64,160]{2,1,0:T(8,128)(2,1)S(1)}, u32[]{:S(2)}) copy-start(bf16[16,64,160]{2,1,0:T(8,128)(2,1)S(1)} %get-tuple-element.12) | copy-start | bytes 983044
  9.4 0.7 %copy-start.8 = (bf16[64,32]{0,1:T(8,128)(2,1)S(1)}, bf16[64,32]{0,1:T(8,128)(2,1)}, u32[]{:S(2)}) copy-start(bf16[64,32]{0,1:T(8,128)(2,1)} %param.13) | copy-start | bytes 12292
  10.0 6.5 %collective-permute-start.1 = (bf16[160,512]{1,0:T(8,128)(2,1)S(1)}, bf16[160,512]{1,0:T(8,128)(2,1)S(1)}, u32[]{:S(2)}, u32[]{:S(2)}) collective-permute-start(bf16[160,512]{1,0:T(8,128)(2,1)S(1)} %copy.34.refs_2_), channel_id=1, source_target_pairs={{0,2},{2,0},{1,3},{3,1},{4,6},{6,4},{5,7},{7,5},{8,10},{10,8},{9,1... | collective-permute-start | bytes 491528 | tf_op jit(solution)/shard_map/ppermute | solution.py:207
  10.4 1.0 %copy-start.5 = (f32[1024,128]{1,0:T(8,128)S(1)}, f32[1024,128]{1,0:T(8,128)}, u32[]{:S(2)}) copy-start(f32[1024,128]{1,0:T(8,128)} %param.15) | copy-start | bytes 1572868
  16.4 5.6 %collective-permute-start = (f32[2,64,512]{2,1,0:T(8,128)S(1)}, f32[2,64,512]{2,1,0:T(8,128)}, u32[]{:S(2)}, u32[]{:S(2)}) collective-permute-start(f32[2,64,512]{2,1,0:T(8,128)S(1)} %dynamic-slice_bitcast_fusion.1), channel_id=1, source_target_pairs={{0,1},{1,0},{2,3},{3,2},{4,5},{5,4},{6,7},{7,6},{8,9},{9,8},{10,11... | collective-permute-start | bytes 786440 | tf_op jit(solution)/shard_map/ppermute | solution.py:137
  21.5 1.7 %collective-permute-start.3 = (f32[2,64,512]{2,1,0:T(8,128)S(1)}, f32[2,64,512]{2,1,0:T(8,128)S(1)}, u32[]{:S(2)}, u32[]{:S(2)}) collective-permute-start(f32[2,64,512]{2,1,0:T(8,128)S(1)} %dynamic-slice_bitcast_fusion), channel_id=1, source_target_pairs={{0,1},{1,0},{2,3},{3,2},{4,5},{5,4},{6,7},{7,6},{8,9},{9,8},{10,11... | collective-permute-start | bytes 786440 | tf_op jit(solution)/shard_map/ppermute | solution.py:137
  23.2 5.3 %copy-start.2 = (bf16[16,64,160]{2,1,0:T(8,128)(2,1)S(1)}, bf16[16,64,160]{2,1,0:T(8,128)(2,1)}, u32[]{:S(2)}) copy-start(bf16[16,64,160]{2,1,0:T(8,128)(2,1)} %copy-done.1) | copy-start | bytes 983044
  23.3 8.5 %collective-permute-start.4 = (f32[64,512]{1,0:T(8,128)S(1)}, f32[64,512]{1,0:T(8,128)S(1)}, u32[]{:S(2)}, u32[]{:S(2)}) collective-permute-start(f32[64,512]{1,0:T(8,128)S(1)} %get-tuple-element.6), channel_id=1, source_target_pairs={{0,4},{4,8},{8,12},{12,0},{1,5},{5,9},{9,13},{13,1},{2,6},{6,10},{... | collective-permute-start | bytes 393224 | tf_op jit(solution)/shard_map/ppermute | solution.py:149
  25.4 8.3 %collective-permute-start.6 = (f32[64,512]{1,0:T(8,128)S(1)}, f32[64,512]{1,0:T(8,128)S(1)}, u32[]{:S(2)}, u32[]{:S(2)}) collective-permute-start(f32[64,512]{1,0:T(8,128)S(1)} %get-tuple-element.7), channel_id=1, source_target_pairs={{0,12},{4,0},{8,4},{12,8},{1,13},{5,1},{9,5},{13,9},{2,14},{6,2},{... | collective-permute-start | bytes 393224 | tf_op jit(solution)/shard_map/ppermute | solution.py:149
  27.5 12.4 %collective-permute-start.5 = (f32[64,512]{1,0:T(8,128)S(1)}, f32[64,512]{1,0:T(8,128)S(1)}, u32[]{:S(2)}, u32[]{:S(2)}) collective-permute-start(f32[64,512]{1,0:T(8,128)S(1)} %get-tuple-element.8), channel_id=1, source_target_pairs={{0,8},{4,12},{8,0},{12,4},{1,9},{5,13},{9,1},{13,5},{2,10},{6,14},... | collective-permute-start | bytes 393224 | tf_op jit(solution)/shard_map/ppermute | solution.py:149
  29.6 10.4 %copy-start.4 = (f32[32,8,128]{2,1,0:T(8,128)S(1)}, f32[32,8,128]{2,1,0:T(8,128)}, u32[]{:S(2)}) copy-start(f32[32,8,128]{2,1,0:T(8,128)} %param.10) | copy-start | bytes 393220
  29.6 11.1 %copy-start.6 = (bf16[128,512]{1,0:T(8,128)(2,1)S(1)}, bf16[128,512]{1,0:T(8,128)(2,1)}, u32[]{:S(2)}) copy-start(bf16[128,512]{1,0:T(8,128)(2,1)} %param.16) | copy-start | bytes 393220

commit v14 on v13

--- a/solution.py
+++ b/solution.py
@@ -143,6 +143,16 @@
         gathered = lax.all_to_all(part, "seq", 0, 0, tiled=False)
         return gathered.sum(axis=0)
     me = lax.axis_index("seq")
+    if nseq == 4:
+        pairs = part.reshape(2, 2, *part.shape[1:])
+        lo = me % 2
+        keep = lax.dynamic_index_in_dim(pairs, lo, axis=1, keepdims=False)
+        send = lax.dynamic_index_in_dim(pairs, 1 - lo, axis=1, keepdims=False)
+        half = keep + lax.ppermute(send, "seq", [(q, q ^ 1) for q in range(4)])
+        hi = me // 2
+        keep2 = lax.dynamic_index_in_dim(half, hi, axis=0, keepdims=False)
+        send2 = lax.dynamic_index_in_dim(half, 1 - hi, axis=0, keepdims=False)
+        return keep2 + lax.ppermute(send2, "seq", [(q, q ^ 2) for q in range(4)])
     acc = lax.dynamic_index_in_dim(part, me, axis=0, keepdims=False)
     for k in range(1, nseq):
         src = lax.dynamic_index_in_dim(part, (me + k) % nseq, axis=0, keepdims=False)

time: 42.1 us -> 43.5 us (1.033)
  waiting for transfers between devices: 10.5 us -> 12 us
    ppermute x3 -> x2, waiting for transfers between devices: 10.3 us -> 11.8 us  [the longest x1 6.83 us: seq_stage(): half = keep + lax.ppermute(send, 'seq', [(q, q ^ 1) for q in range(4)])]
    ppermute x3 -> x2, starting transfers between devices: 5.17 us -> 4.96 us  [the longest x1 2.82 us: seq_stage(): return keep2 + lax.ppermute(send2, 'seq', [(q, q ^ 2) for q in range(4)])]
  transfers between devices with their start and end apart: 7 -> 6, of which waited for: 4 -> 3; matrix products, arithmetic and copies ran while one was open for 12% -> 12% of each run, Pallas kernels for 23% -> 23%
where the time goes in v14:
time: 43.5 us; the launch traced here: 43.2 us
  waiting for transfers between devices  12 us (28%)
  Pallas kernels  9.74 us (22%)
  starting transfers between devices  8.67 us (20%)
  matrix products  5.15 us (12%)
  other arithmetic  4.97 us (11%)
  local copies, waits for them, and re-layouts  1.59 us (4%)
  between operations  1.07 us (2%)
    pallas_call x2, Pallas kernels, outer_project(): pl.pallas_call(functools.partial(outer_project_kernel, scale, nlt, nparts...  9.74 us
    ppermute x1, waiting for transfers between devices, seq_stage(): half = keep + lax.ppermute(send, 'seq', [(q, q ^ 1) for q in range(4)])  6.83 us
    ppermute x1, waiting for transfers between devices, seq_stage(): return keep2 + lax.ppermute(send2, 'seq', [(q, q ^ 2) for q in range(4)])  5 us
    ppermute x2, starting transfers between devices, per_device(): r_other = [lax.ppermute(r, 'res', [(0, 1), (1, 0)]) for r in right_parts]  3.08 us
    dot_general x2, matrix products, per_device(): jnp.einsum('hk,ihs->iks', homolog_shrink_weights, hidden, preferred_eleme...  3.07 us
    ppermute x1, starting transfers between devices, seq_stage(): return keep2 + lax.ppermute(send2, 'seq', [(q, q ^ 2) for q in range(4)])  2.82 us
    ppermute x1, starting transfers between devices, seq_stage(): half = keep + lax.ppermute(send, 'seq', [(q, q ^ 1) for q in range(4)])  2.15 us
    reduce_sum x1, other arithmetic, apply_layer_norm_axis1(): mean = jnp.mean(values, axis=1, keepdims=True)  1.53 us
  transfers between devices with their start and end apart: 6, of which 3 were waited for; matrix products, arithmetic and copies ran while one was open for 12% of the time, Pallas kernels for 23%

profile of v14, /device:TPU:0, one launch (start us, length us, event | category | flops | bytes accessed | tf_op | source)
XLA Modules:
  0.0 43.2 jit_solution(1941526047092297553)
XLA Ops:
  0.6 0.0 copy-start
  0.6 0.0 copy-start.3
  0.7 1.5 %convert_reduce_fusion.1 = (f32[16,160]{1,0:T(8,128)S(1)}, f32[16,160]{1,0:T(8,128)S(1)}) fusion(bf16[32,64,160]{2,1,0:T(8,128)(2,1)} %bitcast.124), kind=kLoop, calls=%fused_computation.7 | loop fusion | flops 650240 | bytes 675840 | tf_op jit(solution)/shard_map/reduce_sum | solution.py:19
  2.2 0.0 copy-done.3
  2.2 0.4 fusion.24
  2.7 0.0 copy-start.7
  2.7 1.5 %convert_reduce_fusion.2 = (f32[16,160]{1,0:T(8,128)S(1)}, bf16[16,64,160]{2,1,0:T(8,128)(2,1)S(1)}) fusion(bf16[256,64]{0,1:T(8,128)(2,1)S(1)} %copy-done.9, f32[16,160]{1,0:T(8,128)S(1)} %add_rsqrt_fusion.2, f32[16,160]{1,0:T(8,128)S(1)} %get-tuple-element.12, bf16[32,64,160]{2,1,0:T(8,128)(2,1)S(1)} %bitcast.126, bf16[64,256]{1,0:T(8,128)(2,1)S(1)} %copy-done.10), kind=kOutput, calls=%fused_computation.15 | convolution fusion | flops 170554880 | bytes 1079296 | tf_op jit(solution)/shard_map/hk,ihs->iks/dot_general | solution.py:195
  4.2 0.2 fusion.26
  4.4 0.3 convolution_convert_fusion
  4.7 0.1 copy.35.refs_3_
  4.8 3.0 %collective-permute-start.2 = (bf16[160,512]{1,0:T(8,128)(2,1)S(1)}, bf16[160,512]{1,0:T(8,128)(2,1)S(1)}, u32[]{:S(2)}, u32[]{:S(2)}) collective-permute-start(bf16[160,512]{1,0:T(8,128)(2,1)S(1)} %copy.35.refs_3_), channel_id=1, source_target_pairs={{0,2},{2,0},{1,3},{3,1},{4,6},{6,4},{5,7},{7,5},{8,10},{10,8},{9,1... | collective-permute-start | bytes 491528 | tf_op jit(solution)/shard_map/ppermute | solution.py:217
  7.8 1.5 %convert_reduce_fusion.3 = (f32[16,160]{1,0:T(8,128)S(1)}, bf16[16,64,160]{2,1,0:T(8,128)(2,1)S(1)}) fusion(bf16[256,64]{0,1:T(8,128)(2,1)S(1)} %copy-done.9, f32[16,160]{1,0:T(8,128)S(1)} %add_rsqrt_fusion.3, f32[16,160]{1,0:T(8,128)S(1)} %get-tuple-element.13, bf16[32,64,160]{2,1,0:T(8,128)(2,1)S(1)} %bitcast.127, bf16[64,256]{1,0:T(8,128)(2,1)S(1)} %copy-done.10), kind=kOutput, calls=%fused_computation.17 | convolution fusion | flops 170554880 | bytes 1079296 | tf_op jit(solution)/shard_map/hk,ihs->iks/dot_general | solution.py:195
  9.4 0.0 copy-start.1
  9.4 0.0 copy-start.8
  9.4 0.2 fusion.28
  9.6 0.3 convolution_convert_fusion.1
  9.9 0.1 copy.34.refs_2_
  10.0 0.1 collective-permute-start.1
  10.1 0.0 copy-done.8
  10.1 0.3 fusion.50
  10.4 0.0 copy-start.5
  10.4 0.3 fusion.47
  10.7 0.2 copy.55
  10.8 0.2 copy.54
  11.0 0.5 %copy-done.5 = f32[1024,128]{1,0:T(8,128)S(1)} copy-done((f32[1024,128]{1,0:T(8,128)S(1)}, f32[1024,128]{1,0:T(8,128)}, u32[]{:S(2)}) %copy-start.5) | copy-done | bytes 524312
  11.4 0.1 fusion.34
  11.5 4.9 %shard_map.104 = f32[256,512]{1,0:T(8,128)S(1)} custom-call(bf16[32,16,160]{2,1,0:T(8,128)(2,1)S(1)} %bitcast.122, bf16[32,16,160]{2,1,0:T(8,128)(2,1)S(1)} %bitcast.120, bf16[160,512]{1,0:T(8,128)(2,1)S(1)} %copy.34.refs_2_, bf16[160,512]{1,0:T(8,128)(2,1)S(1)} %copy.35.refs_3_, bf16[1024,128]{1,0:T(8,128)(2,1)S(1)} %get-tuple-element.7.refs_4_, ...), custom_call_target="tpu_custom_call" | custom-call | flops 3556769792 | bytes 1703936 | tf_op jit(solution)/shard_map/pallas_call | solution.py:100
  16.4 0.1 collective-permute-start
  16.5 0.0 collective-permute-done.2.refs_3_
  16.5 0.0 collective-permute-done.1.refs_2_
  16.5 4.9 %shard_map.105 = f32[256,512]{1,0:T(8,128)S(1)} custom-call(bf16[32,16,160]{2,1,0:T(8,128)(2,1)S(1)} %bitcast.123, bf16[32,16,160]{2,1,0:T(8,128)(2,1)S(1)} %bitcast.121, bf16[160,512]{1,0:T(8,128)(2,1)S(1)} %collective-permute-done.1.refs_2_, bf16[160,512]{1,0:T(8,128)(2,1)S(1)} %collective-permute-done.2.refs_3_, ...), custom_call_target="tpu_custom_call" | custom-call | flops 3556769792 | bytes 1703936 | tf_op jit(solution)/shard_map/pallas_call | solution.py:100
  21.5 0.5 %collective-permute-start.3 = (f32[2,64,512]{2,1,0:T(8,128)S(1)}, f32[2,64,512]{2,1,0:T(8,128)S(1)}, u32[]{:S(2)}, u32[]{:S(2)}) collective-permute-start(f32[2,64,512]{2,1,0:T(8,128)S(1)} %dynamic-slice_bitcast_fusion.1), channel_id=1, source_target_pairs={{0,1},{1,0},{2,3},{3,2},{4,5},{5,4},{6,7},{7,6},{8,9},{9,8},{10,11... | collective-permute-start | bytes 786440 | tf_op jit(solution)/shard_map/ppermute | solution.py:137
  22.0 0.0 collective-permute-done
  22.0 1.0 %bitcast_add_fusion.2 = f32[2,64,512]{2,1,0:T(8,128)S(1)} fusion(f32[2,64,512]{2,1,0:T(8,128)} %collective-permute-done, f32[2,2,64,512]{3,2,1,0:T(8,128)S(1)} %bitcast.117, s32[]{:T(128)S(6)} %select_n.46), kind=kLoop, calls=%fused_computation.64 | loop fusion | flops 65536 | bytes 786436 | tf_op jit(solution)/shard_map/add | solution.py:137
  23.0 0.2 collective-permute-done.3
  23.3 0.0 copy-start.2
  23.3 2.1 %collective-permute-start.4 = (f32[2,64,512]{2,1,0:T(8,128)S(1)}, f32[2,64,512]{2,1,0:T(8,128)S(1)}, u32[]{:S(2)}, u32[]{:S(2)}) collective-permute-start(f32[2,64,512]{2,1,0:T(8,128)S(1)} %dynamic-slice_bitcast_fusion), channel_id=1, source_target_pairs={{0,4},{4,0},{8,12},{12,8},{1,5},{5,1},{9,13},{13,9},{2,6},{6,2},{1... | collective-permute-start | bytes 786440 | tf_op jit(solution)/shard_map/ppermute | solution.py:151
  25.4 6.8 %collective-permute-done.4 = f32[2,64,512]{2,1,0:T(8,128)S(1)} collective-permute-done((f32[2,64,512]{2,1,0:T(8,128)S(1)}, f32[2,64,512]{2,1,0:T(8,128)S(1)}, u32[]{:S(2)}, u32[]{:S(2)}) %collective-permute-start.4) | collective-permute-done | bytes 262176 | tf_op jit(solution)/shard_map/ppermute | solution.py:151
  32.3 2.8 %collective-permute-start.5 = (f32[64,512]{1,0:T(8,128)S(1)}, f32[64,512]{1,0:T(8,128)S(1)}, u32[]{:S(2)}, u32[]{:S(2)}) collective-permute-start(f32[64,512]{1,0:T(8,128)S(1)} %dynamic-slice_bitcast_fusion.3), channel_id=1, source_target_pairs={{0,8},{4,12},{8,0},{12,4},{1,9},{5,13},{9,1},{13,5},{2,10},{6,14},... | collective-permute-start | bytes 393224 | tf_op jit(solution)/shard_map/ppermute | solution.py:155
  35.2 1.1 %maximum_bitcast_fusion = bf16[160,32,64]{0,2,1:T(8,128)(2,1)} fusion(bf16[16,64,160]{2,1,0:T(8,128)(2,1)S(1)} %get-tuple-element.11, bf16[16,64,160]{2,1,0:T(8,128)(2,1)S(1)} %copy-done.2), kind=kLoop, calls=%fused_computation.45 | loop fusion | flops 327680 | bytes 1310720 | tf_op jit(solution)/shard_map/transpose | solution.py:207
  36.3 5.0 %collective-permute-done.5 = f32[64,512]{1,0:T(8,128)S(1)} collective-permute-done((f32[64,512]{1,0:T(8,128)S(1)}, f32[64,512]{1,0:T(8,128)S(1)}, u32[]{:S(2)}, u32[]{:S(2)}) %collective-permute-start.5) | collective-permute-done | bytes 131104 | tf_op jit(solution)/shard_map/ppermute | solution.py:155
  41.5 0.1 fusion.60
  41.6 0.2 multiply_reduce_fusion
  41.8 0.1 copy.41
  41.9 0.1 copy.42
  41.9 0.1 rsqrt.48
  42.0 0.1 div.52
  42.1 1.1 %fusion.21 = f32[32,8,128]{2,1,0:T(8,128)} fusion(bf16[512,128]{1,0:T(8,128)(2,1)S(1)} %copy-done, bf16[128,512]{1,0:T(8,128)(2,1)S(1)} %copy-done.6, f32[256,128]{1,0:T(8,128)S(1)} %bitcast.136, f32[32,8,128]{2,1,0:T(8,128)S(1)} %copy-done.4, f32[256]{0:T(256)S(1)} %rsqrt.48, f32[256]{0:T(256)S(1)} %div.52), kind=kOutput, calls=%fused_computation.36 | convolution fusion | flops 67567616 | bytes 657408 | tf_op jit(solution)/shard_map/dot_general | solution.py:243
  (32 shorter events, 0.4 us)
Async XLA Ops:
  0.6 41.5 %copy-start = (bf16[512,128]{1,0:T(8,128)(2,1)S(1)}, bf16[512,128]{1,0:T(8,128)(2,1)}, u32[]{:S(2)}) copy-start(bf16[512,128]{1,0:T(8,128)(2,1)} %param.17) | copy-start | bytes 393220
  0.6 1.6 %copy-start.3 = (bf16[160,32,64]{0,2,1:T(8,128)(2,1)S(1)}, bf16[160,32,64]{0,2,1:T(8,128)(2,1)}, u32[]{:S(2)}) copy-start(bf16[160,32,64]{0,2,1:T(8,128)(2,1)} %param.9) | copy-start | bytes 1966084
  0.7 2.0 %copy-start.9 = (bf16[256,64]{0,1:T(8,128)(2,1)S(1)}, bf16[256,64]{0,1:T(8,128)(2,1)}, u32[]{:S(2)}) copy-start(bf16[256,64]{0,1:T(8,128)(2,1)} %param.12) | copy-start | bytes 98308
  0.7 2.0 %copy-start.10 = (bf16[64,256]{1,0:T(8,128)(2,1)S(1)}, bf16[64,256]{1,0:T(8,128)(2,1)}, u32[]{:S(2)}) copy-start(bf16[64,256]{1,0:T(8,128)(2,1)} %param.11) | copy-start | bytes 98308
  2.7 1.8 %copy-start.7 = (bf16[64,32]{0,1:T(8,128)(2,1)S(1)}, bf16[64,32]{0,1:T(8,128)(2,1)}, u32[]{:S(2)}) copy-start(bf16[64,32]{0,1:T(8,128)(2,1)} %param.14) | copy-start | bytes 12292
  4.8 11.7 %collective-permute-start.2 = (bf16[160,512]{1,0:T(8,128)(2,1)S(1)}, bf16[160,512]{1,0:T(8,128)(2,1)S(1)}, u32[]{:S(2)}, u32[]{:S(2)}) collective-permute-start(bf16[160,512]{1,0:T(8,128)(2,1)S(1)} %copy.35.refs_3_), channel_id=1, source_target_pairs={{0,2},{2,0},{1,3},{3,1},{4,6},{6,4},{5,7},{7,5},{8,10},{10,8},{9,1... | collective-permute-start | bytes 491528 | tf_op jit(solution)/shard_map/ppermute | solution.py:217
  9.4 1.0 %copy-start.1 = (bf16[16,64,160]{2,1,0:T(8,128)(2,1)}, bf16[16,64,160]{2,1,0:T(8,128)(2,1)S(1)}, u32[]{:S(2)}) copy-start(bf16[16,64,160]{2,1,0:T(8,128)(2,1)S(1)} %get-tuple-element.9) | copy-start | bytes 983044
  9.4 0.7 %copy-start.8 = (bf16[64,32]{0,1:T(8,128)(2,1)S(1)}, bf16[64,32]{0,1:T(8,128)(2,1)}, u32[]{:S(2)}) copy-start(bf16[64,32]{0,1:T(8,128)(2,1)} %param.13) | copy-start | bytes 12292
  10.0 6.5 %collective-permute-start.1 = (bf16[160,512]{1,0:T(8,128)(2,1)S(1)}, bf16[160,512]{1,0:T(8,128)(2,1)S(1)}, u32[]{:S(2)}, u32[]{:S(2)}) collective-permute-start(bf16[160,512]{1,0:T(8,128)(2,1)S(1)} %copy.34.refs_2_), channel_id=1, source_target_pairs={{0,2},{2,0},{1,3},{3,1},{4,6},{6,4},{5,7},{7,5},{8,10},{10,8},{9,1... | collective-permute-start | bytes 491528 | tf_op jit(solution)/shard_map/ppermute | solution.py:217
  10.4 1.0 %copy-start.5 = (f32[1024,128]{1,0:T(8,128)S(1)}, f32[1024,128]{1,0:T(8,128)}, u32[]{:S(2)}) copy-start(f32[1024,128]{1,0:T(8,128)} %param.15) | copy-start | bytes 1572868
  16.4 5.6 %collective-permute-start = (f32[2,64,512]{2,1,0:T(8,128)S(1)}, f32[2,64,512]{2,1,0:T(8,128)}, u32[]{:S(2)}, u32[]{:S(2)}) collective-permute-start(f32[2,64,512]{2,1,0:T(8,128)S(1)} %dynamic-slice_bitcast_fusion.2), channel_id=1, source_target_pairs={{0,1},{1,0},{2,3},{3,2},{4,5},{5,4},{6,7},{7,6},{8,9},{9,8},{10,11... | collective-permute-start | bytes 786440 | tf_op jit(solution)/shard_map/ppermute | solution.py:137
  21.5 1.7 %collective-permute-start.3 = (f32[2,64,512]{2,1,0:T(8,128)S(1)}, f32[2,64,512]{2,1,0:T(8,128)S(1)}, u32[]{:S(2)}, u32[]{:S(2)}) collective-permute-start(f32[2,64,512]{2,1,0:T(8,128)S(1)} %dynamic-slice_bitcast_fusion.1), channel_id=1, source_target_pairs={{0,1},{1,0},{2,3},{3,2},{4,5},{5,4},{6,7},{7,6},{8,9},{9,8},{10,11... | collective-permute-start | bytes 786440 | tf_op jit(solution)/shard_map/ppermute | solution.py:137
  23.3 11.9 %copy-start.2 = (bf16[16,64,160]{2,1,0:T(8,128)(2,1)S(1)}, bf16[16,64,160]{2,1,0:T(8,128)(2,1)}, u32[]{:S(2)}) copy-start(bf16[16,64,160]{2,1,0:T(8,128)(2,1)} %copy-done.1) | copy-start | bytes 983044
  23.3 9.0 %collective-permute-start.4 = (f32[2,64,512]{2,1,0:T(8,128)S(1)}, f32[2,64,512]{2,1,0:T(8,128)S(1)}, u32[]{:S(2)}, u32[]{:S(2)}) collective-permute-start(f32[2,64,512]{2,1,0:T(8,128)S(1)} %dynamic-slice_bitcast_fusion), channel_id=1, source_target_pairs={{0,4},{4,0},{8,12},{12,8},{1,5},{5,1},{9,13},{13,9},{2,6},{6,2},{1... | collective-permute-start | bytes 786440 | tf_op jit(solution)/shard_map/ppermute | solution.py:151
  32.3 9.0 %collective-permute-start.5 = (f32[64,512]{1,0:T(8,128)S(1)}, f32[64,512]{1,0:T(8,128)S(1)}, u32[]{:S(2)}, u32[]{:S(2)}) collective-permute-start(f32[64,512]{1,0:T(8,128)S(1)} %dynamic-slice_bitcast_fusion.3), channel_id=1, source_target_pairs={{0,8},{4,12},{8,0},{12,4},{1,9},{5,13},{9,1},{13,5},{2,10},{6,14},... | collective-permute-start | bytes 393224 | tf_op jit(solution)/shard_map/ppermute | solution.py:155
  36.3 5.1 %copy-start.4 = (f32[32,8,128]{2,1,0:T(8,128)S(1)}, f32[32,8,128]{2,1,0:T(8,128)}, u32[]{:S(2)}) copy-start(f32[32,8,128]{2,1,0:T(8,128)} %param.10) | copy-start | bytes 393220
  36.3 5.8 %copy-start.6 = (bf16[128,512]{1,0:T(8,128)(2,1)S(1)}, bf16[128,512]{1,0:T(8,128)(2,1)}, u32[]{:S(2)}) copy-start(bf16[128,512]{1,0:T(8,128)(2,1)} %param.16) | copy-start | bytes 393220

commit v15 on v13

--- a/solution.py
+++ b/solution.py
@@ -63,19 +63,19 @@
 
     acc = jnp.zeros(o_ref.shape, jnp.float32)
     block = C_LO * rows_i
+    lt_all = jnp.concatenate([t[c] for c in range(C_HI * C_LO) for t in lt_refs], axis=0)
+    xs = [jnp.dot(lt_all, r[...], preferred_element_type=jnp.float32) for r in r_refs]
+    x_all = xs[0] if nparts == 1 else jnp.concatenate(xs, axis=1)
+    n = acc.shape[0]
     for c_hi in range(C_HI):
-        lt_blk = jnp.concatenate(
-            [t[c_hi * C_LO + c_lo] for c_lo in range(C_LO) for t in lt_refs], axis=0
-        )
-        xs = [jnp.dot(lt_blk, r[...], preferred_element_type=jnp.float32) for r in r_refs]
-        x = xs[0] if nparts == 1 else jnp.concatenate(xs, axis=1)
+        x = x_all[c_hi * block : (c_hi + 1) * block]
         xh = x.astype(jnp.bfloat16)
         xl = (x - xh.astype(jnp.float32)).astype(jnp.bfloat16)
         lh = rearrange(xh)
         ll = rearrange(xl)
-        vh = vh_ref[c_hi]
-        acc = acc + jnp.dot(lh, vh, preferred_element_type=jnp.float32)
-        acc = acc + jnp.dot(ll, vh, preferred_element_type=jnp.float32)
+        both = jnp.dot(jnp.concatenate([lh, ll], axis=0), vh_ref[c_hi], preferred_element_type=jnp.float32)
+        acc = acc + both[:n]
+        acc = acc + both[n:]
         acc = acc + jnp.dot(lh, vl_ref[c_hi], preferred_element_type=jnp.float32)
     o_ref[...] = acc * scale
 

time: 42.1 us -> 40.9 us (0.971)
  Pallas kernels: 9.74 us -> 8.53 us
    pallas_call x2, Pallas kernels: 9.74 us -> 8.53 us  [outer_project(): pl.pallas_call(functools.partial(outer_project_kernel, scale, nlt, nparts...]
  transfers between devices with their start and end apart: 7 -> 7, of which waited for: 4 -> 4; matrix products, arithmetic and copies ran while one was open for 12% -> 13% of each run, Pallas kernels for 23% -> 21%
where the time goes in v15:
time: 40.9 us; the launch traced here: 40.6 us
  waiting for transfers between devices  10.5 us (26%)
  starting transfers between devices  8.88 us (22%)
  Pallas kernels  8.53 us (21%)
  matrix products  5.15 us (13%)
  other arithmetic  4.96 us (12%)
  local copies, waits for them, and re-layouts  1.58 us (4%)
  between operations  1.06 us (3%)
    ppermute x3, waiting for transfers between devices, seq_stage(): lax.ppermute(src, 'seq', [(q, (q + k) % nseq) for q in range(nseq)])  10.3 us
    pallas_call x2, Pallas kernels, outer_project(): pl.pallas_call(functools.partial(outer_project_kernel, scale, nlt, nparts...  8.53 us
    ppermute x3, starting transfers between devices, seq_stage(): lax.ppermute(src, 'seq', [(q, (q + k) % nseq) for q in range(nseq)])  5.18 us
    ppermute x2, starting transfers between devices, per_device(): r_other = [lax.ppermute(r, 'res', [(0, 1), (1, 0)]) for r in right_parts]  3.08 us
    dot_general x2, matrix products, per_device(): jnp.einsum('hk,ihs->iks', homolog_shrink_weights, hidden, preferred_eleme...  3.07 us
    reduce_sum x1, other arithmetic, apply_layer_norm_axis1(): mean = jnp.mean(values, axis=1, keepdims=True)  1.53 us
    transpose x1, other arithmetic, per_device(): jnp.transpose(jnp.concatenate(refreshed_parts, axis=0), (2, 0, 1))  1.14 us
    dot_general x1, matrix products, per_device(): jnp.dot(pair_hidden, coupling_shrink_weights, preferred_element_type=jnp....  1.06 us
  transfers between devices with their start and end apart: 7, of which 4 were waited for; matrix products, arithmetic and copies ran while one was open for 13% of the time, Pallas kernels for 21%

profile of v15, /device:TPU:0, one launch (start us, length us, event | category | flops | bytes accessed | tf_op | source)
XLA Modules:
  0.0 40.6 jit_solution(3178987709242265832)
XLA Ops:
  0.6 0.0 copy-start
  0.7 1.5 %convert_reduce_fusion.1 = (f32[16,160]{1,0:T(8,128)S(1)}, f32[16,160]{1,0:T(8,128)S(1)}) fusion(bf16[32,64,160]{2,1,0:T(8,128)(2,1)} %bitcast.127), kind=kLoop, calls=%fused_computation.7 | loop fusion | flops 650240 | bytes 675840 | tf_op jit(solution)/shard_map/reduce_sum | solution.py:19
  2.2 0.0 copy-done.3
  2.2 0.4 fusion.24
  2.7 0.0 copy-start.7
  2.7 1.5 %convert_reduce_fusion.2 = (f32[16,160]{1,0:T(8,128)S(1)}, bf16[16,64,160]{2,1,0:T(8,128)(2,1)S(1)}) fusion(bf16[256,64]{0,1:T(8,128)(2,1)S(1)} %copy-done.9, f32[16,160]{1,0:T(8,128)S(1)} %add_rsqrt_fusion.2, f32[16,160]{1,0:T(8,128)S(1)} %get-tuple-element.15, bf16[32,64,160]{2,1,0:T(8,128)(2,1)S(1)} %bitcast.129, bf16[64,256]{1,0:T(8,128)(2,1)S(1)} %copy-done.10), kind=kOutput, calls=%fused_computation.15 | convolution fusion | flops 170554880 | bytes 1079296 | tf_op jit(solution)/shard_map/hk,ihs->iks/dot_general | solution.py:185
  4.2 0.2 fusion.26
  4.4 0.3 convolution_convert_fusion
  4.7 0.1 copy.35.refs_3_
  4.8 3.0 %collective-permute-start.2 = (bf16[160,512]{1,0:T(8,128)(2,1)S(1)}, bf16[160,512]{1,0:T(8,128)(2,1)S(1)}, u32[]{:S(2)}, u32[]{:S(2)}) collective-permute-start(bf16[160,512]{1,0:T(8,128)(2,1)S(1)} %copy.35.refs_3_), channel_id=1, source_target_pairs={{0,2},{2,0},{1,3},{3,1},{4,6},{6,4},{5,7},{7,5},{8,10},{10,8},{9,1... | collective-permute-start | bytes 491528 | tf_op jit(solution)/shard_map/ppermute | solution.py:207
  7.8 1.5 %convert_reduce_fusion.3 = (f32[16,160]{1,0:T(8,128)S(1)}, bf16[16,64,160]{2,1,0:T(8,128)(2,1)S(1)}) fusion(bf16[256,64]{0,1:T(8,128)(2,1)S(1)} %copy-done.9, f32[16,160]{1,0:T(8,128)S(1)} %add_rsqrt_fusion.3, f32[16,160]{1,0:T(8,128)S(1)} %get-tuple-element.16, bf16[32,64,160]{2,1,0:T(8,128)(2,1)S(1)} %bitcast.130, bf16[64,256]{1,0:T(8,128)(2,1)S(1)} %copy-done.10), kind=kOutput, calls=%fused_computation.17 | convolution fusion | flops 170554880 | bytes 1079296 | tf_op jit(solution)/shard_map/hk,ihs->iks/dot_general | solution.py:185
  9.4 0.0 copy-start.1
  9.4 0.0 copy-start.8
  9.4 0.2 fusion.28
  9.6 0.3 convolution_convert_fusion.1
  9.9 0.1 copy.34.refs_2_
  10.0 0.1 collective-permute-start.1
  10.1 0.0 copy-done.8
  10.1 0.3 fusion.50
  10.4 0.0 copy-start.5
  10.4 0.3 fusion.47
  10.7 0.2 copy.55
  10.8 0.2 copy.54
  11.0 0.5 %copy-done.5 = f32[1024,128]{1,0:T(8,128)S(1)} copy-done((f32[1024,128]{1,0:T(8,128)S(1)}, f32[1024,128]{1,0:T(8,128)}, u32[]{:S(2)}) %copy-start.5) | copy-done | bytes 524312
  11.4 0.1 fusion.34
  11.5 4.3 %shard_map.104 = f32[256,512]{1,0:T(8,128)S(1)} custom-call(bf16[32,16,160]{2,1,0:T(8,128)(2,1)S(1)} %bitcast.125, bf16[32,16,160]{2,1,0:T(8,128)(2,1)S(1)} %bitcast.123, bf16[160,512]{1,0:T(8,128)(2,1)S(1)} %copy.34.refs_2_, bf16[160,512]{1,0:T(8,128)(2,1)S(1)} %copy.35.refs_3_, bf16[1024,128]{1,0:T(8,128)(2,1)S(1)} %get-tuple-element.10.refs_4_, ...), custom_call_target="tpu_custom_call" | custom-call | flops 3556769792 | bytes 1703936 | tf_op jit(solution)/shard_map/pallas_call | solution.py:100
  15.8 0.1 collective-permute-start
  15.9 0.0 collective-permute-done.2.refs_3_
  15.9 4.3 %shard_map.105 = f32[256,512]{1,0:T(8,128)S(1)} custom-call(bf16[32,16,160]{2,1,0:T(8,128)(2,1)S(1)} %bitcast.126, bf16[32,16,160]{2,1,0:T(8,128)(2,1)S(1)} %bitcast.124, bf16[160,512]{1,0:T(8,128)(2,1)S(1)} %collective-permute-done.1.refs_2_, bf16[160,512]{1,0:T(8,128)(2,1)S(1)} %collective-permute-done.2.refs_3_, ...), custom_call_target="tpu_custom_call" | custom-call | flops 3556769792 | bytes 1703936 | tf_op jit(solution)/shard_map/pallas_call | solution.py:100
  20.2 0.5 %collective-permute-start.3 = (f32[2,64,512]{2,1,0:T(8,128)S(1)}, f32[2,64,512]{2,1,0:T(8,128)S(1)}, u32[]{:S(2)}, u32[]{:S(2)}) collective-permute-start(f32[2,64,512]{2,1,0:T(8,128)S(1)} %dynamic-slice_bitcast_fusion), channel_id=1, source_target_pairs={{0,1},{1,0},{2,3},{3,2},{4,5},{5,4},{6,7},{7,6},{8,9},{9,8},{10,11... | collective-permute-start | bytes 786440 | tf_op jit(solution)/shard_map/ppermute | solution.py:137
  20.8 0.0 collective-permute-done
  20.8 1.0 %bitcast_add_fusion.1 = f32[2,64,512]{2,1,0:T(8,128)S(1)} fusion(f32[2,64,512]{2,1,0:T(8,128)} %collective-permute-done, f32[2,2,64,512]{3,2,1,0:T(8,128)S(1)} %bitcast.120, s32[]{:T(128)S(6)} %select_n.46), kind=kLoop, calls=%fused_computation.63 | loop fusion | flops 65536 | bytes 786436 | tf_op jit(solution)/shard_map/add | solution.py:137
  21.8 0.2 collective-permute-done.3
  22.0 0.0 copy-start.2
  22.1 2.1 %collective-permute-start.4 = (f32[64,512]{1,0:T(8,128)S(1)}, f32[64,512]{1,0:T(8,128)S(1)}, u32[]{:S(2)}, u32[]{:S(2)}) collective-permute-start(f32[64,512]{1,0:T(8,128)S(1)} %get-tuple-element.6), channel_id=1, source_target_pairs={{0,4},{4,8},{8,12},{12,0},{1,5},{5,9},{9,13},{13,1},{2,6},{6,10},{... | collective-permute-start | bytes 393224 | tf_op jit(solution)/shard_map/ppermute | solution.py:149
  24.2 2.1 %collective-permute-start.6 = (f32[64,512]{1,0:T(8,128)S(1)}, f32[64,512]{1,0:T(8,128)S(1)}, u32[]{:S(2)}, u32[]{:S(2)}) collective-permute-start(f32[64,512]{1,0:T(8,128)S(1)} %get-tuple-element.7), channel_id=1, source_target_pairs={{0,12},{4,0},{8,4},{12,8},{1,13},{5,1},{9,5},{13,9},{2,14},{6,2},{... | collective-permute-start | bytes 393224 | tf_op jit(solution)/shard_map/ppermute | solution.py:149
  26.3 0.9 %collective-permute-start.5 = (f32[64,512]{1,0:T(8,128)S(1)}, f32[64,512]{1,0:T(8,128)S(1)}, u32[]{:S(2)}, u32[]{:S(2)}) collective-permute-start(f32[64,512]{1,0:T(8,128)S(1)} %get-tuple-element.8), channel_id=1, source_target_pairs={{0,8},{4,12},{8,0},{12,4},{1,9},{5,13},{9,1},{13,5},{2,10},{6,14},... | collective-permute-start | bytes 393224 | tf_op jit(solution)/shard_map/ppermute | solution.py:149
  27.3 1.1 %maximum_bitcast_fusion = bf16[160,32,64]{0,2,1:T(8,128)(2,1)} fusion(bf16[16,64,160]{2,1,0:T(8,128)(2,1)S(1)} %get-tuple-element.14, bf16[16,64,160]{2,1,0:T(8,128)(2,1)S(1)} %copy-done.2), kind=kLoop, calls=%fused_computation.45 | loop fusion | flops 327680 | bytes 1310720 | tf_op jit(solution)/shard_map/transpose | solution.py:197
  28.4 2.2 %collective-permute-done.4 = f32[64,512]{1,0:T(8,128)S(1)} collective-permute-done((f32[64,512]{1,0:T(8,128)S(1)}, f32[64,512]{1,0:T(8,128)S(1)}, u32[]{:S(2)}, u32[]{:S(2)}) %collective-permute-start.4) | collective-permute-done | bytes 131104 | tf_op jit(solution)/shard_map/ppermute | solution.py:149
  30.6 1.9 %collective-permute-done.6 = f32[64,512]{1,0:T(8,128)S(1)} collective-permute-done((f32[64,512]{1,0:T(8,128)S(1)}, f32[64,512]{1,0:T(8,128)S(1)}, u32[]{:S(2)}, u32[]{:S(2)}) %collective-permute-start.6) | collective-permute-done | bytes 131104 | tf_op jit(solution)/shard_map/ppermute | solution.py:149
  32.5 6.2 %collective-permute-done.5 = f32[64,512]{1,0:T(8,128)S(1)} collective-permute-done((f32[64,512]{1,0:T(8,128)S(1)}, f32[64,512]{1,0:T(8,128)S(1)}, u32[]{:S(2)}, u32[]{:S(2)}) %collective-permute-start.5) | collective-permute-done | bytes 131104 | tf_op jit(solution)/shard_map/ppermute | solution.py:149
  38.9 0.1 fusion.62
  39.0 0.2 multiply_reduce_fusion
  39.2 0.1 copy.41
  39.3 0.1 copy.42
  39.3 0.1 rsqrt.48
  39.4 0.1 div.41
  39.5 1.1 %fusion.21 = f32[32,8,128]{2,1,0:T(8,128)} fusion(bf16[512,128]{1,0:T(8,128)(2,1)S(1)} %copy-done, bf16[128,512]{1,0:T(8,128)(2,1)S(1)} %copy-done.6, f32[256,128]{1,0:T(8,128)S(1)} %bitcast.137, f32[32,8,128]{2,1,0:T(8,128)S(1)} %copy-done.4, f32[256]{0:T(256)S(1)} %rsqrt.48, f32[256]{0:T(256)S(1)} %div.41), kind=kOutput, calls=%fused_computation.36 | convolution fusion | flops 67567616 | bytes 657408 | tf_op jit(solution)/shard_map/dot_general | solution.py:233
  (32 shorter events, 0.4 us)
Async XLA Ops:
  0.6 38.9 %copy-start = (bf16[512,128]{1,0:T(8,128)(2,1)S(1)}, bf16[512,128]{1,0:T(8,128)(2,1)}, u32[]{:S(2)}) copy-start(bf16[512,128]{1,0:T(8,128)(2,1)} %param.17) | copy-start | bytes 393220
  0.6 1.6 %copy-start.3 = (bf16[160,32,64]{0,2,1:T(8,128)(2,1)S(1)}, bf16[160,32,64]{0,2,1:T(8,128)(2,1)}, u32[]{:S(2)}) copy-start(bf16[160,32,64]{0,2,1:T(8,128)(2,1)} %param.9) | copy-start | bytes 1966084
  0.7 2.0 %copy-start.9 = (bf16[256,64]{0,1:T(8,128)(2,1)S(1)}, bf16[256,64]{0,1:T(8,128)(2,1)}, u32[]{:S(2)}) copy-start(bf16[256,64]{0,1:T(8,128)(2,1)} %param.12) | copy-start | bytes 98308
  0.7 2.0 %copy-start.10 = (bf16[64,256]{1,0:T(8,128)(2,1)S(1)}, bf16[64,256]{1,0:T(8,128)(2,1)}, u32[]{:S(2)}) copy-start(bf16[64,256]{1,0:T(8,128)(2,1)} %param.11) | copy-start | bytes 98308
  2.7 1.8 %copy-start.7 = (bf16[64,32]{0,1:T(8,128)(2,1)S(1)}, bf16[64,32]{0,1:T(8,128)(2,1)}, u32[]{:S(2)}) copy-start(bf16[64,32]{0,1:T(8,128)(2,1)} %param.14) | copy-start | bytes 12292
  4.8 11.1 %collective-permute-start.2 = (bf16[160,512]{1,0:T(8,128)(2,1)S(1)}, bf16[160,512]{1,0:T(8,128)(2,1)S(1)}, u32[]{:S(2)}, u32[]{:S(2)}) collective-permute-start(bf16[160,512]{1,0:T(8,128)(2,1)S(1)} %copy.35.refs_3_), channel_id=1, source_target_pairs={{0,2},{2,0},{1,3},{3,1},{4,6},{6,4},{5,7},{7,5},{8,10},{10,8},{9,1... | collective-permute-start | bytes 491528 | tf_op jit(solution)/shard_map/ppermute | solution.py:207
  9.4 1.0 %copy-start.1 = (bf16[16,64,160]{2,1,0:T(8,128)(2,1)}, bf16[16,64,160]{2,1,0:T(8,128)(2,1)S(1)}, u32[]{:S(2)}) copy-start(bf16[16,64,160]{2,1,0:T(8,128)(2,1)S(1)} %get-tuple-element.12) | copy-start | bytes 983044
  9.4 0.7 %copy-start.8 = (bf16[64,32]{0,1:T(8,128)(2,1)S(1)}, bf16[64,32]{0,1:T(8,128)(2,1)}, u32[]{:S(2)}) copy-start(bf16[64,32]{0,1:T(8,128)(2,1)} %param.13) | copy-start | bytes 12292
  10.0 5.9 %collective-permute-start.1 = (bf16[160,512]{1,0:T(8,128)(2,1)S(1)}, bf16[160,512]{1,0:T(8,128)(2,1)S(1)}, u32[]{:S(2)}, u32[]{:S(2)}) collective-permute-start(bf16[160,512]{1,0:T(8,128)(2,1)S(1)} %copy.34.refs_2_), channel_id=1, source_target_pairs={{0,2},{2,0},{1,3},{3,1},{4,6},{6,4},{5,7},{7,5},{8,10},{10,8},{9,1... | collective-permute-start | bytes 491528 | tf_op jit(solution)/shard_map/ppermute | solution.py:207
  10.4 1.0 %copy-start.5 = (f32[1024,128]{1,0:T(8,128)S(1)}, f32[1024,128]{1,0:T(8,128)}, u32[]{:S(2)}) copy-start(f32[1024,128]{1,0:T(8,128)} %param.15) | copy-start | bytes 1572868
  15.8 5.0 %collective-permute-start = (f32[2,64,512]{2,1,0:T(8,128)S(1)}, f32[2,64,512]{2,1,0:T(8,128)}, u32[]{:S(2)}, u32[]{:S(2)}) collective-permute-start(f32[2,64,512]{2,1,0:T(8,128)S(1)} %dynamic-slice_bitcast_fusion.1), channel_id=1, source_target_pairs={{0,1},{1,0},{2,3},{3,2},{4,5},{5,4},{6,7},{7,6},{8,9},{9,8},{10,11... | collective-permute-start | bytes 786440 | tf_op jit(solution)/shard_map/ppermute | solution.py:137
  20.2 1.7 %collective-permute-start.3 = (f32[2,64,512]{2,1,0:T(8,128)S(1)}, f32[2,64,512]{2,1,0:T(8,128)S(1)}, u32[]{:S(2)}, u32[]{:S(2)}) collective-permute-start(f32[2,64,512]{2,1,0:T(8,128)S(1)} %dynamic-slice_bitcast_fusion), channel_id=1, source_target_pairs={{0,1},{1,0},{2,3},{3,2},{4,5},{5,4},{6,7},{7,6},{8,9},{9,8},{10,11... | collective-permute-start | bytes 786440 | tf_op jit(solution)/shard_map/ppermute | solution.py:137
  22.0 5.3 %copy-start.2 = (bf16[16,64,160]{2,1,0:T(8,128)(2,1)S(1)}, bf16[16,64,160]{2,1,0:T(8,128)(2,1)}, u32[]{:S(2)}) copy-start(bf16[16,64,160]{2,1,0:T(8,128)(2,1)} %copy-done.1) | copy-start | bytes 983044
  22.1 8.6 %collective-permute-start.4 = (f32[64,512]{1,0:T(8,128)S(1)}, f32[64,512]{1,0:T(8,128)S(1)}, u32[]{:S(2)}, u32[]{:S(2)}) collective-permute-start(f32[64,512]{1,0:T(8,128)S(1)} %get-tuple-element.6), channel_id=1, source_target_pairs={{0,4},{4,8},{8,12},{12,0},{1,5},{5,9},{9,13},{13,1},{2,6},{6,10},{... | collective-permute-start | bytes 393224 | tf_op jit(solution)/shard_map/ppermute | solution.py:149
  24.2 8.3 %collective-permute-start.6 = (f32[64,512]{1,0:T(8,128)S(1)}, f32[64,512]{1,0:T(8,128)S(1)}, u32[]{:S(2)}, u32[]{:S(2)}) collective-permute-start(f32[64,512]{1,0:T(8,128)S(1)} %get-tuple-element.7), channel_id=1, source_target_pairs={{0,12},{4,0},{8,4},{12,8},{1,13},{5,1},{9,5},{13,9},{2,14},{6,2},{... | collective-permute-start | bytes 393224 | tf_op jit(solution)/shard_map/ppermute | solution.py:149
  26.3 12.4 %collective-permute-start.5 = (f32[64,512]{1,0:T(8,128)S(1)}, f32[64,512]{1,0:T(8,128)S(1)}, u32[]{:S(2)}, u32[]{:S(2)}) collective-permute-start(f32[64,512]{1,0:T(8,128)S(1)} %get-tuple-element.8), channel_id=1, source_target_pairs={{0,8},{4,12},{8,0},{12,4},{1,9},{5,13},{9,1},{13,5},{2,10},{6,14},... | collective-permute-start | bytes 393224 | tf_op jit(solution)/shard_map/ppermute | solution.py:149
  28.4 10.4 %copy-start.4 = (f32[32,8,128]{2,1,0:T(8,128)S(1)}, f32[32,8,128]{2,1,0:T(8,128)}, u32[]{:S(2)}) copy-start(f32[32,8,128]{2,1,0:T(8,128)} %param.10) | copy-start | bytes 393220
  28.4 11.1 %copy-start.6 = (bf16[128,512]{1,0:T(8,128)(2,1)S(1)}, bf16[128,512]{1,0:T(8,128)(2,1)}, u32[]{:S(2)}) copy-start(bf16[128,512]{1,0:T(8,128)(2,1)} %param.16) | copy-start | bytes 393220

commit v16 on v15

--- a/solution.py
+++ b/solution.py
@@ -67,16 +67,20 @@
     xs = [jnp.dot(lt_all, r[...], preferred_element_type=jnp.float32) for r in r_refs]
     x_all = xs[0] if nparts == 1 else jnp.concatenate(xs, axis=1)
     n = acc.shape[0]
+    lhs_hi, lhs_lo = [], []
     for c_hi in range(C_HI):
         x = x_all[c_hi * block : (c_hi + 1) * block]
         xh = x.astype(jnp.bfloat16)
         xl = (x - xh.astype(jnp.float32)).astype(jnp.bfloat16)
-        lh = rearrange(xh)
-        ll = rearrange(xl)
-        both = jnp.dot(jnp.concatenate([lh, ll], axis=0), vh_ref[c_hi], preferred_element_type=jnp.float32)
-        acc = acc + both[:n]
-        acc = acc + both[n:]
-        acc = acc + jnp.dot(lh, vl_ref[c_hi], preferred_element_type=jnp.float32)
+        lhs_hi.append(rearrange(xh))
+        lhs_lo.append(rearrange(xl))
+    lh = jnp.concatenate(lhs_hi, axis=1)
+    ll = jnp.concatenate(lhs_lo, axis=1)
+    vh = vh_ref[...].reshape(C_HI * vh_ref.shape[1], vh_ref.shape[2])
+    vl = vl_ref[...].reshape(C_HI * vl_ref.shape[1], vl_ref.shape[2])
+    both = jnp.dot(jnp.concatenate([lh, ll], axis=0), vh, preferred_element_type=jnp.float32)
+    acc = both[:n] + both[n:]
+    acc = acc + jnp.dot(lh, vl, preferred_element_type=jnp.float32)
     o_ref[...] = acc * scale
 
 

time: 40.9 us -> 40.8 us (level)
  no operation moved by 1% of the time
where the time goes in v16:
time: 40.8 us; the launch traced here: 40.6 us
  waiting for transfers between devices  10.5 us (26%)
  starting transfers between devices  8.89 us (22%)
  Pallas kernels  8.47 us (21%)
  matrix products  5.15 us (13%)
  other arithmetic  4.96 us (12%)
  local copies, waits for them, and re-layouts  1.58 us (4%)
  between operations  1.06 us (3%)
    ppermute x3, waiting for transfers between devices, seq_stage(): lax.ppermute(src, 'seq', [(q, (q + k) % nseq) for q in range(nseq)])  10.3 us
    pallas_call x2, Pallas kernels, outer_project(): pl.pallas_call(functools.partial(outer_project_kernel, scale, nlt, nparts...  8.47 us
    ppermute x3, starting transfers between devices, seq_stage(): lax.ppermute(src, 'seq', [(q, (q + k) % nseq) for q in range(nseq)])  5.18 us
    ppermute x2, starting transfers between devices, per_device(): r_other = [lax.ppermute(r, 'res', [(0, 1), (1, 0)]) for r in right_parts]  3.08 us
    dot_general x2, matrix products, per_device(): jnp.einsum('hk,ihs->iks', homolog_shrink_weights, hidden, preferred_eleme...  3.07 us
    reduce_sum x1, other arithmetic, apply_layer_norm_axis1(): mean = jnp.mean(values, axis=1, keepdims=True)  1.53 us
    transpose x1, other arithmetic, per_device(): jnp.transpose(jnp.concatenate(refreshed_parts, axis=0), (2, 0, 1))  1.14 us
    dot_general x1, matrix products, per_device(): jnp.dot(pair_hidden, coupling_shrink_weights, preferred_element_type=jnp....  1.06 us
  transfers between devices with their start and end apart: 7, of which 4 were waited for; matrix products, arithmetic and copies ran while one was open for 13% of the time, Pallas kernels for 21%

profile of v16, /device:TPU:0, one launch (start us, length us, event | category | flops | bytes accessed | tf_op | source)
XLA Modules:
  0.0 40.6 jit_solution(3839607075383833514)
XLA Ops:
  0.6 0.0 copy-start
  0.7 1.5 %convert_reduce_fusion.1 = (f32[16,160]{1,0:T(8,128)S(1)}, f32[16,160]{1,0:T(8,128)S(1)}) fusion(bf16[32,64,160]{2,1,0:T(8,128)(2,1)} %bitcast.127), kind=kLoop, calls=%fused_computation.7 | loop fusion | flops 650240 | bytes 675840 | tf_op jit(solution)/shard_map/reduce_sum | solution.py:19
  2.2 0.4 fusion.24
  2.7 0.0 copy-start.7
  2.7 1.5 %convert_reduce_fusion.2 = (f32[16,160]{1,0:T(8,128)S(1)}, bf16[16,64,160]{2,1,0:T(8,128)(2,1)S(1)}) fusion(bf16[256,64]{0,1:T(8,128)(2,1)S(1)} %copy-done.9, f32[16,160]{1,0:T(8,128)S(1)} %add_rsqrt_fusion.2, f32[16,160]{1,0:T(8,128)S(1)} %get-tuple-element.15, bf16[32,64,160]{2,1,0:T(8,128)(2,1)S(1)} %bitcast.129, bf16[64,256]{1,0:T(8,128)(2,1)S(1)} %copy-done.10), kind=kOutput, calls=%fused_computation.15 | convolution fusion | flops 170554880 | bytes 1079296 | tf_op jit(solution)/shard_map/hk,ihs->iks/dot_general | solution.py:189
  4.2 0.2 fusion.26
  4.4 0.3 convolution_convert_fusion
  4.7 0.1 copy.35.refs_3_
  4.8 3.0 %collective-permute-start.2 = (bf16[160,512]{1,0:T(8,128)(2,1)S(1)}, bf16[160,512]{1,0:T(8,128)(2,1)S(1)}, u32[]{:S(2)}, u32[]{:S(2)}) collective-permute-start(bf16[160,512]{1,0:T(8,128)(2,1)S(1)} %copy.35.refs_3_), channel_id=1, source_target_pairs={{0,2},{2,0},{1,3},{3,1},{4,6},{6,4},{5,7},{7,5},{8,10},{10,8},{9,1... | collective-permute-start | bytes 491528 | tf_op jit(solution)/shard_map/ppermute | solution.py:211
  7.8 1.5 %convert_reduce_fusion.3 = (f32[16,160]{1,0:T(8,128)S(1)}, bf16[16,64,160]{2,1,0:T(8,128)(2,1)S(1)}) fusion(bf16[256,64]{0,1:T(8,128)(2,1)S(1)} %copy-done.9, f32[16,160]{1,0:T(8,128)S(1)} %add_rsqrt_fusion.3, f32[16,160]{1,0:T(8,128)S(1)} %get-tuple-element.16, bf16[32,64,160]{2,1,0:T(8,128)(2,1)S(1)} %bitcast.130, bf16[64,256]{1,0:T(8,128)(2,1)S(1)} %copy-done.10), kind=kOutput, calls=%fused_computation.17 | convolution fusion | flops 170554880 | bytes 1079296 | tf_op jit(solution)/shard_map/hk,ihs->iks/dot_general | solution.py:189
  9.4 0.0 copy-start.1
  9.4 0.0 copy-start.8
  9.4 0.2 fusion.28
  9.6 0.3 convolution_convert_fusion.1
  9.9 0.1 copy.34.refs_2_
  10.0 0.1 collective-permute-start.1
  10.1 0.0 copy-done.8
  10.1 0.3 fusion.50
  10.4 0.0 copy-start.5
  10.4 0.3 fusion.47
  10.7 0.2 copy.55
  10.8 0.2 copy.54
  11.0 0.5 %copy-done.5 = f32[1024,128]{1,0:T(8,128)S(1)} copy-done((f32[1024,128]{1,0:T(8,128)S(1)}, f32[1024,128]{1,0:T(8,128)}, u32[]{:S(2)}) %copy-start.5) | copy-done | bytes 524312
  11.4 0.1 fusion.34
  11.5 4.2 %shard_map.104 = f32[256,512]{1,0:T(8,128)S(1)} custom-call(bf16[32,16,160]{2,1,0:T(8,128)(2,1)S(1)} %bitcast.125, bf16[32,16,160]{2,1,0:T(8,128)(2,1)S(1)} %bitcast.123, bf16[160,512]{1,0:T(8,128)(2,1)S(1)} %copy.34.refs_2_, bf16[160,512]{1,0:T(8,128)(2,1)S(1)} %copy.35.refs_3_, bf16[1024,128]{1,0:T(8,128)(2,1)S(1)} %get-tuple-element.10.refs_4_, ...), custom_call_target="tpu_custom_call" | custom-call | flops 3556769792 | bytes 1703936 | tf_op jit(solution)/shard_map/pallas_call | solution.py:104
  15.8 0.1 collective-permute-start
  15.9 0.0 collective-permute-done.2.refs_3_
  15.9 0.0 collective-permute-done.1.refs_2_
  15.9 4.2 %shard_map.105 = f32[256,512]{1,0:T(8,128)S(1)} custom-call(bf16[32,16,160]{2,1,0:T(8,128)(2,1)S(1)} %bitcast.126, bf16[32,16,160]{2,1,0:T(8,128)(2,1)S(1)} %bitcast.124, bf16[160,512]{1,0:T(8,128)(2,1)S(1)} %collective-permute-done.1.refs_2_, bf16[160,512]{1,0:T(8,128)(2,1)S(1)} %collective-permute-done.2.refs_3_, ...), custom_call_target="tpu_custom_call" | custom-call | flops 3556769792 | bytes 1703936 | tf_op jit(solution)/shard_map/pallas_call | solution.py:104
  20.2 0.5 %collective-permute-start.3 = (f32[2,64,512]{2,1,0:T(8,128)S(1)}, f32[2,64,512]{2,1,0:T(8,128)S(1)}, u32[]{:S(2)}, u32[]{:S(2)}) collective-permute-start(f32[2,64,512]{2,1,0:T(8,128)S(1)} %dynamic-slice_bitcast_fusion), channel_id=1, source_target_pairs={{0,1},{1,0},{2,3},{3,2},{4,5},{5,4},{6,7},{7,6},{8,9},{9,8},{10,11... | collective-permute-start | bytes 786440 | tf_op jit(solution)/shard_map/ppermute | solution.py:141
  20.7 0.0 collective-permute-done
  20.7 1.0 %bitcast_add_fusion.1 = f32[2,64,512]{2,1,0:T(8,128)S(1)} fusion(f32[2,64,512]{2,1,0:T(8,128)} %collective-permute-done, f32[2,2,64,512]{3,2,1,0:T(8,128)S(1)} %bitcast.120, s32[]{:T(128)S(6)} %select_n.46), kind=kLoop, calls=%fused_computation.63 | loop fusion | flops 65536 | bytes 786436 | tf_op jit(solution)/shard_map/add | solution.py:141
  21.7 0.2 collective-permute-done.3
  21.9 0.0 copy-start.2
  22.0 2.1 %collective-permute-start.4 = (f32[64,512]{1,0:T(8,128)S(1)}, f32[64,512]{1,0:T(8,128)S(1)}, u32[]{:S(2)}, u32[]{:S(2)}) collective-permute-start(f32[64,512]{1,0:T(8,128)S(1)} %get-tuple-element.6), channel_id=1, source_target_pairs={{0,4},{4,8},{8,12},{12,0},{1,5},{5,9},{9,13},{13,1},{2,6},{6,10},{... | collective-permute-start | bytes 393224 | tf_op jit(solution)/shard_map/ppermute | solution.py:153
  24.2 2.1 %collective-permute-start.6 = (f32[64,512]{1,0:T(8,128)S(1)}, f32[64,512]{1,0:T(8,128)S(1)}, u32[]{:S(2)}, u32[]{:S(2)}) collective-permute-start(f32[64,512]{1,0:T(8,128)S(1)} %get-tuple-element.7), channel_id=1, source_target_pairs={{0,12},{4,0},{8,4},{12,8},{1,13},{5,1},{9,5},{13,9},{2,14},{6,2},{... | collective-permute-start | bytes 393224 | tf_op jit(solution)/shard_map/ppermute | solution.py:153
  26.3 0.9 %collective-permute-start.5 = (f32[64,512]{1,0:T(8,128)S(1)}, f32[64,512]{1,0:T(8,128)S(1)}, u32[]{:S(2)}, u32[]{:S(2)}) collective-permute-start(f32[64,512]{1,0:T(8,128)S(1)} %get-tuple-element.8), channel_id=1, source_target_pairs={{0,8},{4,12},{8,0},{12,4},{1,9},{5,13},{9,1},{13,5},{2,10},{6,14},... | collective-permute-start | bytes 393224 | tf_op jit(solution)/shard_map/ppermute | solution.py:153
  27.2 1.1 %maximum_bitcast_fusion = bf16[160,32,64]{0,2,1:T(8,128)(2,1)} fusion(bf16[16,64,160]{2,1,0:T(8,128)(2,1)S(1)} %get-tuple-element.14, bf16[16,64,160]{2,1,0:T(8,128)(2,1)S(1)} %copy-done.2), kind=kLoop, calls=%fused_computation.45 | loop fusion | flops 327680 | bytes 1310720 | tf_op jit(solution)/shard_map/transpose | solution.py:201
  28.4 2.2 %collective-permute-done.4 = f32[64,512]{1,0:T(8,128)S(1)} collective-permute-done((f32[64,512]{1,0:T(8,128)S(1)}, f32[64,512]{1,0:T(8,128)S(1)}, u32[]{:S(2)}, u32[]{:S(2)}) %collective-permute-start.4) | collective-permute-done | bytes 131104 | tf_op jit(solution)/shard_map/ppermute | solution.py:153
  30.6 1.9 %collective-permute-done.6 = f32[64,512]{1,0:T(8,128)S(1)} collective-permute-done((f32[64,512]{1,0:T(8,128)S(1)}, f32[64,512]{1,0:T(8,128)S(1)}, u32[]{:S(2)}, u32[]{:S(2)}) %collective-permute-start.6) | collective-permute-done | bytes 131104 | tf_op jit(solution)/shard_map/ppermute | solution.py:153
  32.5 6.2 %collective-permute-done.5 = f32[64,512]{1,0:T(8,128)S(1)} collective-permute-done((f32[64,512]{1,0:T(8,128)S(1)}, f32[64,512]{1,0:T(8,128)S(1)}, u32[]{:S(2)}, u32[]{:S(2)}) %collective-permute-start.5) | collective-permute-done | bytes 131104 | tf_op jit(solution)/shard_map/ppermute | solution.py:153
  38.8 0.1 fusion.62
  38.9 0.2 multiply_reduce_fusion
  39.1 0.1 copy.41
  39.2 0.1 copy.42
  39.3 0.1 rsqrt.48
  39.4 0.1 div.41
  39.5 1.1 %fusion.21 = f32[32,8,128]{2,1,0:T(8,128)} fusion(bf16[512,128]{1,0:T(8,128)(2,1)S(1)} %copy-done, bf16[128,512]{1,0:T(8,128)(2,1)S(1)} %copy-done.6, f32[256,128]{1,0:T(8,128)S(1)} %bitcast.137, f32[32,8,128]{2,1,0:T(8,128)S(1)} %copy-done.4, f32[256]{0:T(256)S(1)} %rsqrt.48, f32[256]{0:T(256)S(1)} %div.41), kind=kOutput, calls=%fused_computation.36 | convolution fusion | flops 67567616 | bytes 657408 | tf_op jit(solution)/shard_map/dot_general | solution.py:237
  (32 shorter events, 0.4 us)
Async XLA Ops:
  0.6 38.8 %copy-start = (bf16[512,128]{1,0:T(8,128)(2,1)S(1)}, bf16[512,128]{1,0:T(8,128)(2,1)}, u32[]{:S(2)}) copy-start(bf16[512,128]{1,0:T(8,128)(2,1)} %param.17) | copy-start | bytes 393220
  0.6 1.6 %copy-start.3 = (bf16[160,32,64]{0,2,1:T(8,128)(2,1)S(1)}, bf16[160,32,64]{0,2,1:T(8,128)(2,1)}, u32[]{:S(2)}) copy-start(bf16[160,32,64]{0,2,1:T(8,128)(2,1)} %param.9) | copy-start | bytes 1966084
  0.7 2.0 %copy-start.9 = (bf16[256,64]{0,1:T(8,128)(2,1)S(1)}, bf16[256,64]{0,1:T(8,128)(2,1)}, u32[]{:S(2)}) copy-start(bf16[256,64]{0,1:T(8,128)(2,1)} %param.12) | copy-start | bytes 98308
  0.7 2.0 %copy-start.10 = (bf16[64,256]{1,0:T(8,128)(2,1)S(1)}, bf16[64,256]{1,0:T(8,128)(2,1)}, u32[]{:S(2)}) copy-start(bf16[64,256]{1,0:T(8,128)(2,1)} %param.11) | copy-start | bytes 98308
  2.7 1.8 %copy-start.7 = (bf16[64,32]{0,1:T(8,128)(2,1)S(1)}, bf16[64,32]{0,1:T(8,128)(2,1)}, u32[]{:S(2)}) copy-start(bf16[64,32]{0,1:T(8,128)(2,1)} %param.14) | copy-start | bytes 12292
  4.8 11.1 %collective-permute-start.2 = (bf16[160,512]{1,0:T(8,128)(2,1)S(1)}, bf16[160,512]{1,0:T(8,128)(2,1)S(1)}, u32[]{:S(2)}, u32[]{:S(2)}) collective-permute-start(bf16[160,512]{1,0:T(8,128)(2,1)S(1)} %copy.35.refs_3_), channel_id=1, source_target_pairs={{0,2},{2,0},{1,3},{3,1},{4,6},{6,4},{5,7},{7,5},{8,10},{10,8},{9,1... | collective-permute-start | bytes 491528 | tf_op jit(solution)/shard_map/ppermute | solution.py:211
  9.4 1.0 %copy-start.1 = (bf16[16,64,160]{2,1,0:T(8,128)(2,1)}, bf16[16,64,160]{2,1,0:T(8,128)(2,1)S(1)}, u32[]{:S(2)}) copy-start(bf16[16,64,160]{2,1,0:T(8,128)(2,1)S(1)} %get-tuple-element.12) | copy-start | bytes 983044
  9.4 0.7 %copy-start.8 = (bf16[64,32]{0,1:T(8,128)(2,1)S(1)}, bf16[64,32]{0,1:T(8,128)(2,1)}, u32[]{:S(2)}) copy-start(bf16[64,32]{0,1:T(8,128)(2,1)} %param.13) | copy-start | bytes 12292
  10.0 5.9 %collective-permute-start.1 = (bf16[160,512]{1,0:T(8,128)(2,1)S(1)}, bf16[160,512]{1,0:T(8,128)(2,1)S(1)}, u32[]{:S(2)}, u32[]{:S(2)}) collective-permute-start(bf16[160,512]{1,0:T(8,128)(2,1)S(1)} %copy.34.refs_2_), channel_id=1, source_target_pairs={{0,2},{2,0},{1,3},{3,1},{4,6},{6,4},{5,7},{7,5},{8,10},{10,8},{9,1... | collective-permute-start | bytes 491528 | tf_op jit(solution)/shard_map/ppermute | solution.py:211
  10.4 1.0 %copy-start.5 = (f32[1024,128]{1,0:T(8,128)S(1)}, f32[1024,128]{1,0:T(8,128)}, u32[]{:S(2)}) copy-start(f32[1024,128]{1,0:T(8,128)} %param.15) | copy-start | bytes 1572868
  15.8 4.9 %collective-permute-start = (f32[2,64,512]{2,1,0:T(8,128)S(1)}, f32[2,64,512]{2,1,0:T(8,128)}, u32[]{:S(2)}, u32[]{:S(2)}) collective-permute-start(f32[2,64,512]{2,1,0:T(8,128)S(1)} %dynamic-slice_bitcast_fusion.1), channel_id=1, source_target_pairs={{0,1},{1,0},{2,3},{3,2},{4,5},{5,4},{6,7},{7,6},{8,9},{9,8},{10,11... | collective-permute-start | bytes 786440 | tf_op jit(solution)/shard_map/ppermute | solution.py:141
  20.2 1.7 %collective-permute-start.3 = (f32[2,64,512]{2,1,0:T(8,128)S(1)}, f32[2,64,512]{2,1,0:T(8,128)S(1)}, u32[]{:S(2)}, u32[]{:S(2)}) collective-permute-start(f32[2,64,512]{2,1,0:T(8,128)S(1)} %dynamic-slice_bitcast_fusion), channel_id=1, source_target_pairs={{0,1},{1,0},{2,3},{3,2},{4,5},{5,4},{6,7},{7,6},{8,9},{9,8},{10,11... | collective-permute-start | bytes 786440 | tf_op jit(solution)/shard_map/ppermute | solution.py:141
  21.9 5.3 %copy-start.2 = (bf16[16,64,160]{2,1,0:T(8,128)(2,1)S(1)}, bf16[16,64,160]{2,1,0:T(8,128)(2,1)}, u32[]{:S(2)}) copy-start(bf16[16,64,160]{2,1,0:T(8,128)(2,1)} %copy-done.1) | copy-start | bytes 983044
  22.0 8.6 %collective-permute-start.4 = (f32[64,512]{1,0:T(8,128)S(1)}, f32[64,512]{1,0:T(8,128)S(1)}, u32[]{:S(2)}, u32[]{:S(2)}) collective-permute-start(f32[64,512]{1,0:T(8,128)S(1)} %get-tuple-element.6), channel_id=1, source_target_pairs={{0,4},{4,8},{8,12},{12,0},{1,5},{5,9},{9,13},{13,1},{2,6},{6,10},{... | collective-permute-start | bytes 393224 | tf_op jit(solution)/shard_map/ppermute | solution.py:153
  24.2 8.3 %collective-permute-start.6 = (f32[64,512]{1,0:T(8,128)S(1)}, f32[64,512]{1,0:T(8,128)S(1)}, u32[]{:S(2)}, u32[]{:S(2)}) collective-permute-start(f32[64,512]{1,0:T(8,128)S(1)} %get-tuple-element.7), channel_id=1, source_target_pairs={{0,12},{4,0},{8,4},{12,8},{1,13},{5,1},{9,5},{13,9},{2,14},{6,2},{... | collective-permute-start | bytes 393224 | tf_op jit(solution)/shard_map/ppermute | solution.py:153
  26.3 12.4 %collective-permute-start.5 = (f32[64,512]{1,0:T(8,128)S(1)}, f32[64,512]{1,0:T(8,128)S(1)}, u32[]{:S(2)}, u32[]{:S(2)}) collective-permute-start(f32[64,512]{1,0:T(8,128)S(1)} %get-tuple-element.8), channel_id=1, source_target_pairs={{0,8},{4,12},{8,0},{12,4},{1,9},{5,13},{9,1},{13,5},{2,10},{6,14},... | collective-permute-start | bytes 393224 | tf_op jit(solution)/shard_map/ppermute | solution.py:153
  28.4 10.4 %copy-start.4 = (f32[32,8,128]{2,1,0:T(8,128)S(1)}, f32[32,8,128]{2,1,0:T(8,128)}, u32[]{:S(2)}) copy-start(f32[32,8,128]{2,1,0:T(8,128)} %param.10) | copy-start | bytes 393220
  28.4 11.1 %copy-start.6 = (bf16[128,512]{1,0:T(8,128)(2,1)S(1)}, bf16[128,512]{1,0:T(8,128)(2,1)}, u32[]{:S(2)}) copy-start(bf16[128,512]{1,0:T(8,128)(2,1)} %param.16) | copy-start | bytes 393220
